TPU v7x, 32 devices: a whole 2x2x4 slice. The times are simulated.
32 devices in a mesh: seq: 8 (over z, x), head: 4 (over y, core).
Axes of the slice: x: 2, y: 2, z: 4, core: 2. Of those that a mesh axis runs over, the one named last changes fastest.
Arguments:
- queries: float32 [8192, 2048], P('seq', 'head')
- keys: float32 [8192, 2048], P('seq', 'head')
- values: float32 [8192, 2048], P('seq', 'head'), may hold values from -6 to 6
- positions: int32 [8192], P('seq'), may hold values from 0 to 8191, as said below
- cluster: int32 [8192], P('seq'), may hold values from 0 to 7, as said below
- slot: int32 [8192], P('seq'), may hold values from 0 to 1023, as said below
- out_weight: float32 [2048, 4096], P('head'), may hold values from -0.5 to 0.5
Outputs:
- projected: float32 [8192, 4096], P('seq', 'head')
Inputs may be any that keep to these rules, and one draw needn't show every extreme that they name: Every cluster holds exactly 1024 tokens. Of the tokens of one index of seq, at most 192 have cluster ids in one range k * 1 to (k + 1) - 1. Within each cluster every slot is taken once, in increasing order of position. `positions`: each position is taken by exactly one token.
All inputs are finite; a program needn't handle non-finite values.
Results may differ from a plain program's by a relative error of at most 0.0003.
Values sent between devices are 32-bit elements; how exact they have to be, the bound alone decides.
No kernel may reach another device: no remote copies, remote signals or barrier semaphores. Data moves between devices by JAX's collectives and lax.ppermute only.
A program may use at most 128 MiB of HBM per device.

v0:
```python
import math

import jax
import jax.numpy as jnp
from jax import lax
from jax.sharding import PartitionSpec as P

DH = 128
CS = 1024
CL_DEV = 1


ROPE_BASE = 500000.0
ORIG_CONTEXT = 8192.0
STRETCH = 4.0
BETA_FAST = 32.0
BETA_SLOW = 1.0


def yarn_tables(token_pos, width):
    half_width = width // 2
    expo = jnp.arange(half_width, dtype=jnp.float32) * 2.0 / width
    theta = jnp.exp(-expo * math.log(ROPE_BASE))
    ratio = ORIG_CONTEXT * theta / (2.0 * math.pi)
    ramp = jnp.clip((ratio - BETA_SLOW) / (BETA_FAST - BETA_SLOW), 0.0, 1.0)
    freq = theta * (ramp + (1.0 - ramp) / STRETCH)
    angle = token_pos.astype(jnp.float32)[:, None] * freq[None, :]
    mscale = 0.1 * math.log(STRETCH) + 1.0
    cos_table = jnp.concatenate([jnp.cos(angle), jnp.cos(angle)], -1) * mscale
    sin_table = jnp.concatenate([jnp.sin(angle), jnp.sin(angle)], -1) * mscale
    return (cos_table[:, None, :], sin_table[:, None, :])


def rotate(field, cos_table, sin_table):
    half_width = field.shape[-1] // 2
    turned = jnp.concatenate([-field[..., half_width:], field[..., :half_width]], -1)
    return field * cos_table + turned * sin_table


def cluster_attention(triple):
    query_c, key_c, value_c = triple
    length = query_c.shape[0]
    scores = jnp.einsum(
        "qhd,khd->hqk", query_c, key_c, precision=lax.Precision.HIGHEST
    ) / math.sqrt(query_c.shape[-1])
    causal = jnp.arange(length)[:, None] >= jnp.arange(length)[None, :]
    scores = jnp.where(causal[None], scores, -jnp.inf)
    peak = jnp.max(scores, -1, keepdims=True)
    weights = jnp.exp(scores - peak)
    total = jnp.sum(weights, -1, keepdims=True)
    summed = jnp.einsum("hqk,khd->qhd", weights, value_c, precision=lax.Precision.HIGHEST)
    return summed / jnp.transpose(total, (1, 0, 2))


def attend_local(query_all, key_all, value_all):
    row_count, head_count, width = query_all.shape
    grouped = (
        query_all.reshape(row_count // CS, CS, head_count, width),
        key_all.reshape(row_count // CS, CS, head_count, width),
        value_all.reshape(row_count // CS, CS, head_count, width),
    )
    return lax.map(cluster_attention, grouped).reshape(row_count, head_count, width)


def per_device(queries, keys, values, positions, cluster, slot, out_weight):
    seq_count = lax.axis_size("seq")
    row_count = queries.shape[0]
    capacity = 3 * row_count // (2 * seq_count)
    buffer_rows = seq_count * capacity
    heads_here = queries.shape[1] // DH
    owner_ids = cluster // CL_DEV
    target_row = cluster % CL_DEV * CS + slot
    one_hot = (owner_ids[:, None] == jnp.arange(seq_count)[None, :]).astype(jnp.int32)
    token_rank = jnp.sum(jnp.cumsum(one_hot, 0) * one_hot, 1) - 1
    send_row = owner_ids * capacity + token_rank
    source_token = (
        jnp.full((buffer_rows,), row_count, jnp.int32)
        .at[send_row]
        .set(jnp.arange(row_count, dtype=jnp.int32))
    )
    cos_table, sin_table = yarn_tables(positions, DH)
    shaped = (row_count, heads_here, DH)
    rot_q = rotate(queries.reshape(shaped), cos_table, sin_table)
    rot_k = rotate(keys.reshape(shaped), cos_table, sin_table)
    stacked = jnp.concatenate([rot_q, rot_k, values.reshape(shaped)], 1)
    stacked = jnp.concatenate([stacked, jnp.zeros((1, 3 * heads_here, DH), jnp.float32)], 0)
    send_all = stacked[source_token]
    send_q = send_all[:, :heads_here]
    send_k = send_all[:, heads_here : 2 * heads_here]
    send_v = send_all[:, 2 * heads_here :]
    slot_rows = jnp.full((buffer_rows,), row_count, jnp.int32).at[send_row].set(target_row)
    arrived = lax.all_to_all(slot_rows, "seq", split_axis=0, concat_axis=0, tiled=True)
    picked = jnp.minimum(arrived, row_count - 1)
    where_from = (
        jnp.zeros((row_count,), jnp.int32)
        .at[arrived]
        .set(jnp.arange(buffer_rows, dtype=jnp.int32), mode="drop")
    )

    def place(pieces):
        return pieces[where_from]

    received = (
        lax.all_to_all(send_q, "seq", split_axis=0, concat_axis=0, tiled=True),
        lax.all_to_all(send_k, "seq", split_axis=0, concat_axis=0, tiled=True),
        lax.all_to_all(send_v, "seq", split_axis=0, concat_axis=0, tiled=True),
    )
    result = attend_local(place(received[0]), place(received[1]), place(received[2]))
    returned = lax.all_to_all(result[picked], "seq", split_axis=0, concat_axis=0, tiled=True)
    mixed = returned[send_row].reshape(row_count, heads_here * DH)
    partial_term = jnp.dot(
        mixed, out_weight, precision=lax.Precision.HIGHEST, preferred_element_type=jnp.float32
    )
    projected = lax.psum_scatter(partial_term, "head", scatter_dimension=1, tiled=True)
    return projected


def solution(mesh):
    in_specs = (
        P("seq", "head"),
        P("seq", "head"),
        P("seq", "head"),
        P("seq"),
        P("seq"),
        P("seq"),
        P("head", None),
    )
    out_specs = P("seq", "head")
    return jax.shard_map(
        per_device, mesh=mesh, in_specs=in_specs, out_specs=out_specs, check_vma=False
    )
```

profile of v0, /device:TPU:0, one launch (start us, length us, event | category | flops | bytes accessed | tf_op | source)
XLA Modules:
  0.0 574.2 jit_solution(1708298302698836180)
XLA Ops:
  11.4 4.5 scatter_custom_fusion.1
  16.6 7.3 %all-to-all-start.1 = ((s32[8,192,1]{1,2,0:T(1,128)}), s32[8,192,1]{1,2,0:T(1,128)S(1)}, u32[]{:S(2)}, u32[]{:S(2)}) async-start(s32[8,192,1]{1,2,0:T(1,128)} %all_to_all.27), calls=%async_computation.1 | async-start | bytes 16384 | tf_op jit(solution)/shard_map/all_to_all | solution.py:92
  24.5 4.5 scatter_custom_fusion
  41.6 3.0 fusion.10
  44.7 5.3 select_maximum_fusion
  49.9 12.0 %gather_fusion = f32[1536,12,128]{2,1,0:T(8,128)} fusion(f32[1025,12,128]{2,1,0:T(8,128)} %select_maximum_fusion, s32[2048]{0:T(1024)S(1)} %pad_clamp_fusion.1), kind=kCustom, calls=%fused_computation | custom fusion | bytes 18880512 | tf_op jit(solution)/shard_map/gather | solution.py:87
  61.9 10.4 %fusion.32 = (f32[1536,4,128]{2,1,0:T(4,128)}, f32[1536,4,128]{2,1,0:T(4,128)}, f32[1536,4,128]{2,1,0:T(4,128)S(1)}) fusion(f32[1536,12,128]{2,1,0:T(8,128)} %gather_fusion), kind=kLoop, calls=%fused_computation.68 | loop fusion | bytes 18874368 | tf_op jit(solution)/shard_map/slice | solution.py:90
  72.4 76.4 %all_to_all.33 = f32[1536,4,128]{2,1,0:T(4,128)} all-to-all(f32[1536,4,128]{2,1,0:T(4,128)} %get-tuple-element.25), channel_id=1, replica_groups=mesh['seq'=8,'head'=4] {'seq'}, dimensions={0} | all-to-all | bytes 6291456 | tf_op jit(solution)/shard_map/all_to_all | solution.py:104
  148.7 73.7 %all_to_all.34 = f32[1536,4,128]{2,1,0:T(4,128)} all-to-all(f32[1536,4,128]{2,1,0:T(4,128)S(1)} %get-tuple-element.26), channel_id=1, replica_groups=mesh['seq'=8,'head'=4] {'seq'}, dimensions={0} | all-to-all | bytes 6291456 | tf_op jit(solution)/shard_map/all_to_all | solution.py:105
  222.4 4.4 all-to-all-start
  227.4 6.2 %scatter_custom_fusion.2 = s32[1024]{0:T(1024)S(1)} fusion(s32[1536]{0:T(1024)S(1)} %get-tuple-element.14, s32[1536]{0:T(1024)S(1)} %iota.38, s32[]{:T(128)} %constant.85.clone.1), kind=kCustom, calls=%fused_computation.63 | custom fusion | bytes 4100 | tf_op jit(solution)/shard_map/scatter | solution.py:97
  233.6 5.4 gather_fusion.2
  239.1 9.8 %gather_fusion.3 = f32[1024,4,128]{2,1,0:T(4,128)} fusion(f32[1536,4,128]{2,1,0:T(4,128)} %all_to_all.34, s32[1024]{0:T(1024)S(1)} %fusion.23), kind=kCustom, calls=%fused_computation.3 | custom fusion | bytes 4198400 | tf_op jit(solution)/shard_map/gather | solution.py:101
  248.9 17.5 %fusion = (f32[4,1024]{1,0:T(4,128)S(1)}, f32[4,1024,1024]{1,2,0:T(8,128)S(1)}) fusion(pred[1024,1024]{0,1:T(8,128)(4,1)S(1)} %iota_compare_fusion.1, f32[1024,4,128]{2,1,0:T(4,128)} %gather_fusion.3, f32[1024,4,128]{2,1,0:T(4,128)S(1)} %gather_fusion.2), kind=kOutput, calls=%fused_computation.11 | convolution fusion | flops 6455029760 | bytes 22036480 | tf_op jit(solution)/shard_map/while/body/eval_jaxpr/qhd,khd->hqk/dot_general | solution.py:43
  266.4 5.7 copy-done
  272.1 3.6 fusion.1
  275.8 20.8 %all-to-all-done = f32[1536,4,128]{2,1,0:T(4,128)} async-done(((f32[1536,4,128]{2,1,0:T(4,128)}), f32[1536,4,128]{2,1,0:T(4,128)}, u32[]{:S(2)}, u32[]{:S(2)}) %all-to-all-start) | async-done | bytes 3145760 | tf_op jit(solution)/shard_map/all_to_all | solution.py:106
  296.6 5.4 gather_fusion.1
  302.0 17.9 %bitcast_divide_fusion = f32[1024,4,128]{0,2,1:T(8,128)} fusion(f32[1024,4]{0,1:T(4,128)S(1)} %bitcast.34, f32[4,1024,1024]{1,2,0:T(8,128)} %copy-done, f32[4,1024]{1,0:T(4,128)S(1)} %get-tuple-element.35, pred[1024,1024]{0,1:T(8,128)(4,1)S(1)} %iota_compare_fusion.1, f32[1024,4,128]{2,1,0:T(4,128)S(1)} %gather_fusion.1), kind=kOutput, calls=%fused_computation.31 | convolution fusion | flops 6455558144 | bytes 22052864 | tf_op jit(solution)/shard_map/while/body/eval_jaxpr/hqk,khd->qhd/dot_general | solution.py:51
  322.0 5.7 gather_fusion.4
  327.7 74.5 %all_to_all.35 = f32[1536,4,128]{2,1,0:T(4,128)S(1)} all-to-all(f32[1536,4,128]{2,1,0:T(4,128)} %gather_fusion.4), channel_id=1, replica_groups=mesh['seq'=8,'head'=4] {'seq'}, dimensions={0} | all-to-all | bytes 6291456 | tf_op jit(solution)/shard_map/all_to_all | solution.py:109
  402.1 7.9 %gather_fusion.5 = f32[1024,4,128]{2,1,0:T(4,128)} fusion(f32[1536,4,128]{2,1,0:T(4,128)S(1)} %all_to_all.35, s32[1024]{0:T(1024)S(1)} %get-tuple-element.20), kind=kCustom, calls=%fused_computation.5 | custom fusion | bytes 4198400 | tf_op jit(solution)/shard_map/gather | solution.py:110
  410.1 31.7 %fusion.7 = f32[1024,4096]{1,0:T(8,128)} fusion(f32[512,4096]{1,0:T(8,128)} %param.13, f32[128,8,4,128]{3,2,1,0:T(4,128)} %bitcast.31), kind=kOutput, calls=%fused_computation.22 | convolution fusion | flops 25769803776 | bytes 27262976 | tf_op jit(solution)/shard_map/dot_general | solution.py:111
  441.8 125.3 %reduce-scatter.2.cloned.1.call-done = f32[1024,1024]{1,0:T(8,128)} async-done(((f32[1024,4096]{1,0:T(8,128)}), f32[1024,1024]{1,0:T(8,128)}) %reduce-scatter.2.cloned.1.call-update) | async-done | bytes 4194320 | tf_op jit(solution)/shard_map/reduce_scatter | solution.py:114
  (35 shorter events, 21.3 us)
Async XLA Ops:
  16.6 55.8 %all-to-all-start.1 = ((s32[8,192,1]{1,2,0:T(1,128)}), s32[8,192,1]{1,2,0:T(1,128)S(1)}, u32[]{:S(2)}, u32[]{:S(2)}) async-start(s32[8,192,1]{1,2,0:T(1,128)} %all_to_all.27), calls=%async_computation.1 | async-start | bytes 16384 | tf_op jit(solution)/shard_map/all_to_all | solution.py:92
  36.9 2.2 copy-start.1
  41.6 3.1 copy-start.2
  222.4 74.1 %all-to-all-start = ((f32[1536,4,128]{2,1,0:T(4,128)}), f32[1536,4,128]{2,1,0:T(4,128)}, u32[]{:S(2)}, u32[]{:S(2)}) async-start(f32[1536,4,128]{2,1,0:T(4,128)} %get-tuple-element.24), calls=%async_computation | async-start | bytes 6291456 | tf_op jit(solution)/shard_map/all_to_all | solution.py:106
  226.9 340.2 %reduce-scatter.2.cloned.1.call-start = ((), (), s32[]{:S(2)}) async-start(), calls=%async_computation.6 | async-start | bytes 20971520 | tf_op jit(solution)/shard_map/reduce_scatter | solution.py:114
  266.4 5.7 copy-start
Sparse Core Ops, SparseCore 0:
  441.9 125.1 reduce-scatter.1
where the time goes:
time: 578 us; the launch traced here: 574 us
  blocking collectives  225 us (39%)
  waiting for transfers between devices  146 us (25%)
  local copies, waits for them, and re-layouts  88.4 us (15%)
  matrix products  67.1 us (12%)
  other arithmetic  22.3 us (4%)
  between operations  13.8 us (2%)
  starting transfers between devices  11.7 us (2%)
    reduce_scatter x1, waiting for transfers between devices, per_device(): lax.psum_scatter(partial_term, 'head', scatter_dimension=1, tiled=True)  125 us
    all_to_all x1, blocking collectives, per_device(): lax.all_to_all(send_q, 'seq', split_axis=0, concat_axis=0, tiled=True)  76.4 us
    all_to_all x1, blocking collectives, per_device(): lax.all_to_all(result[picked], 'seq', split_axis=0, concat_axis=0, tiled=...  74.5 us
    all_to_all x1, blocking collectives, per_device(): lax.all_to_all(send_k, 'seq', split_axis=0, concat_axis=0, tiled=True)  73.7 us
    dot_general x1, matrix products, per_device(): jnp.dot(mixed, out_weight, precision=lax.Precision.HIGHEST, preferred_ele...  31.7 us
    all_to_all x1, waiting for transfers between devices, per_device(): lax.all_to_all(send_v, 'seq', split_axis=0, concat_axis=0, tiled=True)  20.8 us
    gather x3, local copies, waits for them, and re-layouts, place(): return pieces[where_from]  20.7 us
    dot_general x1, matrix products, cluster_attention(): jnp.einsum('hqk,khd->qhd', weights, value_c, precision=lax.Precision.HIGH...  17.9 us
  transfers between devices with their start and end apart: 3, of which 2 were waited for; matrix products, arithmetic and copies ran while one was open for 16% of the time, Pallas kernels for 0%

commit v1 on v0

--- a/solution.py
+++ b/solution.py
@@ -64,6 +64,25 @@
 
 def per_device(queries, keys, values, positions, cluster, slot, out_weight):
     seq_count = lax.axis_size("seq")
+    head_count = lax.axis_size("head")
+    head_index = lax.axis_index("head")
+    col_width = out_weight.shape[1] // head_count
+    weight_blocks = out_weight.reshape(out_weight.shape[0], head_count, col_width)
+    weight_parts = [None] * head_count
+    for shift in range(head_count):
+        if shift == 0:
+            piece = weight_blocks[:, head_index]
+        else:
+            dest = (head_index + shift) % head_count
+            piece = lax.ppermute(
+                jnp.take(weight_blocks, dest, axis=1),
+                "head",
+                [(src, (src + shift) % head_count) for src in range(head_count)],
+            )
+        weight_parts[shift] = piece
+    stacked_w = jnp.stack(weight_parts, 0)
+    order = (head_index - jnp.arange(head_count)) % head_count
+    weight_cols = stacked_w[order].reshape(head_count * out_weight.shape[0], col_width)
     row_count = queries.shape[0]
     capacity = 3 * row_count // (2 * seq_count)
     buffer_rows = seq_count * capacity
@@ -106,12 +125,13 @@
         lax.all_to_all(send_v, "seq", split_axis=0, concat_axis=0, tiled=True),
     )
     result = attend_local(place(received[0]), place(received[1]), place(received[2]))
+    result, weight_cols = lax.optimization_barrier((result, weight_cols))
     returned = lax.all_to_all(result[picked], "seq", split_axis=0, concat_axis=0, tiled=True)
     mixed = returned[send_row].reshape(row_count, heads_here * DH)
-    partial_term = jnp.dot(
-        mixed, out_weight, precision=lax.Precision.HIGHEST, preferred_element_type=jnp.float32
+    gathered = lax.all_gather(mixed, "head", axis=1, tiled=True)
+    projected = jnp.dot(
+        gathered, weight_cols, precision=lax.Precision.HIGHEST, preferred_element_type=jnp.float32
     )
-    projected = lax.psum_scatter(partial_term, "head", scatter_dimension=1, tiled=True)
     return projected
 
 

time: 578 us -> 622 us (1.076)
  blocking collectives: 225 us -> 151 us
  waiting for transfers between devices: 146 us -> 196 us
  other arithmetic: 22.3 us -> 55.2 us
  local copies, waits for them, and re-layouts: 88.4 us -> 113 us
    reduce_scatter x1 -> x0, waiting for transfers between devices: 125 us -> none  [per_device(): lax.psum_scatter(partial_term, 'head', scatter_dimension=1, tiled=True)]
    ppermute x0 -> x3, waiting for transfers between devices: none -> 79 us  [per_device(): lax.ppermute(jnp.take(weight_blocks, dest, axis=1), 'head', [(src, (src +...]
    all_to_all x1 -> x0, blocking collectives: 76.4 us -> none  [per_device(): lax.all_to_all(send_q, 'seq', split_axis=0, concat_axis=0, tiled=True)]
    all_to_all x0 -> x1, waiting for transfers between devices: none -> 59.2 us  [per_device(): lax.all_to_all(send_q, 'seq', split_axis=0, concat_axis=0, tiled=True)]
    all_gather x0 -> x1, waiting for transfers between devices: none -> 57.5 us  [per_device(): gathered = lax.all_gather(mixed, 'head', axis=1, tiled=True)]
    all_to_all x1, waiting for transfers between devices: 20.8 us -> 0.01 us  [per_device(): lax.all_to_all(send_v, 'seq', split_axis=0, concat_axis=0, tiled=True)]
    dynamic_slice x0 -> x1, other arithmetic: none -> 20 us  [per_device(): piece = weight_blocks[:, head_index]]
    reshape x0 -> x1, local copies, waits for them, and re-layouts: none -> 10.8 us  [per_device(): out_weight.reshape(out_weight.shape[0], head_count, col_width)]
  transfers between devices with their start and end apart: 3 -> 7, of which waited for: 2 -> 5; matrix products, arithmetic and copies ran while one was open for 16% -> 24% of each run, Pallas kernels for 0% -> 0%
where the time goes in v1:
time: 622 us; the launch traced here: 618 us
  waiting for transfers between devices  196 us (32%)
  blocking collectives  151 us (24%)
  local copies, waits for them, and re-layouts  113 us (18%)
  matrix products  70.6 us (11%)
  other arithmetic  55.2 us (9%)
  starting transfers between devices  17.4 us (3%)
  between operations  13.9 us (2%)
    ppermute x3, waiting for transfers between devices, per_device(): lax.ppermute(jnp.take(weight_blocks, dest, axis=1), 'head', [(src, (src +...  79 us
    all_to_all x1, blocking collectives, per_device(): lax.all_to_all(send_k, 'seq', split_axis=0, concat_axis=0, tiled=True)  76.2 us
    all_to_all x1, blocking collectives, per_device(): lax.all_to_all(result[picked], 'seq', split_axis=0, concat_axis=0, tiled=...  75.1 us
    all_to_all x1, waiting for transfers between devices, per_device(): lax.all_to_all(send_q, 'seq', split_axis=0, concat_axis=0, tiled=True)  59.2 us
    all_gather x1, waiting for transfers between devices, per_device(): gathered = lax.all_gather(mixed, 'head', axis=1, tiled=True)  57.5 us
    dot_general x1, matrix products, per_device(): jnp.dot(gathered, weight_cols, precision=lax.Precision.HIGHEST, preferred...  31.8 us
    gather x3, local copies, waits for them, and re-layouts, place(): return pieces[where_from]  20.7 us
    dot_general x1, matrix products, cluster_attention(): jnp.einsum('qhd,khd->hqk', query_c, key_c, precision=lax.Precision.HIGHEST)  20.7 us
  transfers between devices with their start and end apart: 7, of which 5 were waited for; matrix products, arithmetic and copies ran while one was open for 24% of the time, Pallas kernels for 0%

profile of v1, /device:TPU:0, one launch (start us, length us, event | category | flops | bytes accessed | tf_op | source)
XLA Modules:
  0.0 617.5 jit_solution(9982841143723869538)
XLA Ops:
  16.6 7.3 %all-to-all-start.1 = ((s32[8,192,1]{1,2,0:T(1,128)}), s32[8,192,1]{1,2,0:T(1,128)S(1)}, u32[]{:S(2)}, u32[]{:S(2)}) async-start(s32[8,192,1]{1,2,0:T(1,128)} %all_to_all.27), calls=%async_computation.1 | async-start | bytes 16384 | tf_op jit(solution)/shard_map/all_to_all | solution.py:111
  46.2 5.3 select_maximum_fusion
  51.5 12.0 %gather_fusion = f32[1536,12,128]{2,1,0:T(8,128)} fusion(f32[1025,12,128]{2,1,0:T(8,128)} %select_maximum_fusion, s32[2048]{0:T(1024)S(1)} %pad_clamp_fusion.1), kind=kCustom, calls=%fused_computation | custom fusion | bytes 18880512 | tf_op jit(solution)/shard_map/gather | solution.py:106
  63.5 10.0 %fusion.33 = (f32[1536,4,128]{2,1,0:T(4,128)}, f32[1536,4,128]{2,1,0:T(4,128)}, f32[1536,4,128]{2,1,0:T(4,128)S(1)}) fusion(f32[1536,12,128]{2,1,0:T(8,128)} %gather_fusion), kind=kLoop, calls=%fused_computation.85 | loop fusion | bytes 18874368 | tf_op jit(solution)/shard_map/slice | solution.py:109
  73.4 76.2 %all_to_all.33 = f32[1536,4,128]{2,1,0:T(4,128)} all-to-all(f32[1536,4,128]{2,1,0:T(4,128)S(1)} %get-tuple-element.42), channel_id=1, replica_groups=mesh['seq'=8,'head'=4] {'seq'}, dimensions={0} | all-to-all | bytes 6291456 | tf_op jit(solution)/shard_map/all_to_all | solution.py:124
  153.6 10.8 %reshape.231 = f32[512,4,1024]{2,1,0:T(4,128)} reshape(f32[512,4096]{1,0:T(8,128)} %param.15) | data formatting | bytes 16777216 | tf_op jit(solution)/shard_map/reshape | solution.py:70
  164.4 59.2 %all-to-all-done.2 = f32[1536,4,128]{2,1,0:T(4,128)S(1)} async-done(((f32[1536,4,128]{2,1,0:T(4,128)}), f32[1536,4,128]{2,1,0:T(4,128)S(1)}, u32[]{:S(2)}, u32[]{:S(2)}) %all-to-all-start.2) | async-done | bytes 3145760 | tf_op jit(solution)/shard_map/all_to_all | solution.py:123
  229.8 20.0 %constant_dynamic-slice_fusion.2 = (f32[512,1,1024]{2,1,0:T(1,128)}, f32[512,1,1024]{2,1,0:T(1,128)S(1)}, f32[512,1,1024]{2,1,0:T(1,128)S(1)}, f32[512,1,1024]{2,1,0:T(1,128)}) fusion(f32[512,4,1024]{2,1,0:T(4,128)} %reshape.231, s32[]{:T(128)S(6)} %select_n.98, s32[]{:T(128)S(6)} %select_n.115, s32[]{:T(128)S(6)} %select_n.119, pred[]{:T(512)S(6)} %and.53, ...), kind=kLoop, calls=%fused_computation.79 | loop fusion | flops 524288 | bytes 16777232 | tf_op jit(solution)/shard_map/dynamic_slice | solution.py:74
  259.7 6.2 %scatter_custom_fusion.2 = s32[1024]{0:T(1024)S(1)} fusion(s32[1536]{0:T(1024)S(1)} %get-tuple-element.37, s32[1536]{0:T(1024)S(1)} %iota.42, s32[]{:T(128)} %constant.129.clone.1), kind=kCustom, calls=%fused_computation.74 | custom fusion | bytes 4100 | tf_op jit(solution)/shard_map/scatter | solution.py:116
  265.9 27.5 %collective-permute-done.2 = f32[512,1024]{1,0:T(8,128)} collective-permute-done((f32[512,1024]{1,0:T(8,128)}, f32[512,1024]{1,0:T(8,128)}, u32[]{:S(2)}, u32[]{:S(2)}) %collective-permute-start.2) | collective-permute-done | bytes 2097184 | tf_op jit(solution)/shard_map/ppermute | solution.py:77
  293.4 47.9 %collective-permute-done.1 = f32[512,1024]{1,0:T(8,128)} collective-permute-done((f32[512,1024]{1,0:T(8,128)}, f32[512,1024]{1,0:T(8,128)}, u32[]{:S(2)}, u32[]{:S(2)}) %collective-permute-start.1) | collective-permute-done | bytes 2097184 | tf_op jit(solution)/shard_map/ppermute | solution.py:77
  344.9 6.0 pad_maximum_fusion
  350.9 7.7 %gather_fusion.4 = f32[4,512,1024]{2,1,0:T(8,128)} fusion(f32[4,512,1024]{2,1,0:T(8,128)} %pad_maximum_fusion, s32[1024]{0:T(1024)S(1)} %pad_clamp_fusion.2), kind=kCustom, calls=%fused_computation.4 | custom fusion | bytes 16777232 | tf_op jit(solution)/shard_map/gather | solution.py:85
  358.6 5.4 gather_fusion.3
  364.0 9.8 %gather_fusion.2 = f32[1024,4,128]{2,1,0:T(4,128)} fusion(f32[1536,4,128]{2,1,0:T(4,128)} %copy-done.2, s32[1024]{0:T(1024)S(1)} %fusion.22), kind=kCustom, calls=%fused_computation.2 | custom fusion | bytes 4198400 | tf_op jit(solution)/shard_map/gather | solution.py:120
  373.9 20.7 %fusion = (f32[4,1024]{1,0:T(4,128)S(1)}, f32[4,1024,1024]{1,2,0:T(8,128)S(1)}) fusion(pred[1024,1024]{0,1:T(8,128)(4,1)S(1)} %iota_compare_fusion.1, f32[1024,4,128]{2,1,0:T(4,128)S(1)} %gather_fusion.3, f32[1024,4,128]{2,1,0:T(4,128)} %gather_fusion.2), kind=kOutput, calls=%fused_computation.12 | convolution fusion | flops 6455029760 | bytes 22036480 | tf_op jit(solution)/shard_map/while/body/eval_jaxpr/qhd,khd->hqk/dot_general | solution.py:43
  394.5 5.7 copy-done
  403.9 5.4 gather_fusion.1
  409.3 18.1 %bitcast_divide_fusion = f32[1024,4,128]{0,2,1:T(8,128)} fusion(f32[1024,4]{0,1:T(4,128)S(1)} %bitcast.51, f32[4,1024,1024]{1,2,0:T(8,128)} %copy-done, f32[4,1024]{1,0:T(4,128)S(1)} %get-tuple-element.55, pred[1024,1024]{0,1:T(8,128)(4,1)S(1)} %iota_compare_fusion.1, f32[1024,4,128]{2,1,0:T(4,128)S(1)} %gather_fusion.1), kind=kOutput, calls=%fused_computation.38 | convolution fusion | flops 6455558144 | bytes 22052864 | tf_op jit(solution)/shard_map/while/body/eval_jaxpr/hqk,khd->qhd/dot_general | solution.py:51
  429.5 5.5 gather_fusion.5
  435.0 75.1 %all_to_all.34 = f32[1536,4,128]{2,1,0:T(4,128)S(1)} all-to-all(f32[1536,4,128]{2,1,0:T(4,128)} %gather_fusion.5), channel_id=1, replica_groups=mesh['seq'=8,'head'=4] {'seq'}, dimensions={0} | all-to-all | bytes 6291456 | tf_op jit(solution)/shard_map/all_to_all | solution.py:129
  510.0 7.9 %gather_fusion.6 = f32[1024,4,128]{2,1,0:T(4,128)} fusion(f32[1536,4,128]{2,1,0:T(4,128)S(1)} %all_to_all.34, s32[1024]{0:T(1024)S(1)} %get-tuple-element.38), kind=kCustom, calls=%fused_computation.6 | custom fusion | bytes 4198400 | tf_op jit(solution)/shard_map/gather | solution.py:130
  521.1 57.5 %all-gather.2.cloned.1.call-done = f32[1024,2048]{1,0:T(8,128)} async-done(((f32[1024,512]{1,0:T(8,128)}), f32[1024,2048]{1,0:T(8,128)}) %all-gather.2.cloned.1.call-update) | async-done | bytes 8388624 | tf_op jit(solution)/shard_map/all_gather | solution.py:131
  578.6 31.8 %fusion.34 = f32[1024,1024]{1,0:T(8,128)} fusion(f32[1024,2048]{1,0:T(8,128)} %all-gather.2.cloned.1.call-done, f32[2048,1024]{1,0:T(8,128)} %bitcast.45), kind=kOutput, calls=%fused_computation.86 | convolution fusion | flops 25769803776 | bytes 20971520 | tf_op jit(solution)/shard_map/dot_general | solution.py:132
  (59 shorter events, 64.7 us)
Async XLA Ops:
  16.6 56.9 %all-to-all-start.1 = ((s32[8,192,1]{1,2,0:T(1,128)}), s32[8,192,1]{1,2,0:T(1,128)S(1)}, u32[]{:S(2)}, u32[]{:S(2)}) async-start(s32[8,192,1]{1,2,0:T(1,128)} %all_to_all.27), calls=%async_computation.1 | async-start | bytes 16384 | tf_op jit(solution)/shard_map/all_to_all | solution.py:111
  28.7 3.0 copy-start.5
  40.9 2.2 copy-start.1
  43.1 3.1 copy-start.3
  149.6 73.9 %all-to-all-start.2 = ((f32[1536,4,128]{2,1,0:T(4,128)}), f32[1536,4,128]{2,1,0:T(4,128)S(1)}, u32[]{:S(2)}, u32[]{:S(2)}) async-start(f32[1536,4,128]{2,1,0:T(4,128)} %get-tuple-element.41), calls=%async_computation.2 | async-start | bytes 6291456 | tf_op jit(solution)/shard_map/all_to_all | solution.py:123
  223.5 1.7 copy-start.2
  225.3 178.6 %all-to-all-start = ((f32[1536,4,128]{2,1,0:T(4,128)}), f32[1536,4,128]{2,1,0:T(4,128)}, u32[]{:S(2)}, u32[]{:S(2)}) async-start(f32[1536,4,128]{2,1,0:T(4,128)} %get-tuple-element.40), calls=%async_computation | async-start | bytes 6291456 | tf_op jit(solution)/shard_map/all_to_all | solution.py:125
  229.8 348.8 %all-gather.2.cloned.1.call-start = ((), (), s32[]{:S(2)}) async-start(), calls=%async_computation.5 | async-start | bytes 10485760 | tf_op jit(solution)/shard_map/all_gather | solution.py:131
  251.6 41.7 %collective-permute-start.2 = (f32[512,1024]{1,0:T(8,128)}, f32[512,1024]{1,0:T(8,128)}, u32[]{:S(2)}, u32[]{:S(2)}) collective-permute-start(f32[512,1024]{1,0:T(8,128)} %bitcast.42), channel_id=1, source_target_pairs={{0,3},{1,0},{2,1},{3,2},{4,7},{5,4},{6,5},{7,6},{8,11},{9,8},{10,9... | collective-permute-start | bytes 6291464 | tf_op jit(solution)/shard_map/ppermute | solution.py:77
  255.1 86.2 %collective-permute-start.1 = (f32[512,1024]{1,0:T(8,128)}, f32[512,1024]{1,0:T(8,128)}, u32[]{:S(2)}, u32[]{:S(2)}) collective-permute-start(f32[512,1024]{1,0:T(8,128)} %fusion.9), channel_id=1, source_target_pairs={{0,2},{1,3},{2,0},{3,1},{4,6},{5,7},{6,4},{7,5},{8,10},{9,11},{10,... | collective-permute-start | bytes 6291464 | tf_op jit(solution)/shard_map/ppermute | solution.py:77
  256.6 2.1 copy-start.4
  258.5 86.4 %collective-permute-start = (f32[512,1024]{1,0:T(8,128)}, f32[512,1024]{1,0:T(8,128)}, u32[]{:S(2)}, u32[]{:S(2)}) collective-permute-start(f32[512,1024]{1,0:T(8,128)} %fusion.10), channel_id=1, source_target_pairs={{0,1},{1,2},{2,3},{3,0},{4,5},{5,6},{6,7},{7,4},{8,9},{9,10},{10,1... | collective-permute-start | bytes 6291464 | tf_op jit(solution)/shard_map/ppermute | solution.py:77
  394.5 5.7 copy-start
Sparse Core Ops, SparseCore 0:
  521.3 57.3 all-gather.1

commit v2 on v0

--- a/solution.py
+++ b/solution.py
@@ -64,6 +64,7 @@
 
 def per_device(queries, keys, values, positions, cluster, slot, out_weight):
     seq_count = lax.axis_size("seq")
+    weight_cols = lax.all_to_all(out_weight, "head", split_axis=1, concat_axis=0, tiled=True)
     row_count = queries.shape[0]
     capacity = 3 * row_count // (2 * seq_count)
     buffer_rows = seq_count * capacity
@@ -106,12 +107,13 @@
         lax.all_to_all(send_v, "seq", split_axis=0, concat_axis=0, tiled=True),
     )
     result = attend_local(place(received[0]), place(received[1]), place(received[2]))
+    result, weight_cols = lax.optimization_barrier((result, weight_cols))
     returned = lax.all_to_all(result[picked], "seq", split_axis=0, concat_axis=0, tiled=True)
     mixed = returned[send_row].reshape(row_count, heads_here * DH)
-    partial_term = jnp.dot(
-        mixed, out_weight, precision=lax.Precision.HIGHEST, preferred_element_type=jnp.float32
+    gathered = lax.all_gather(mixed, "head", axis=1, tiled=True)
+    projected = jnp.dot(
+        gathered, weight_cols, precision=lax.Precision.HIGHEST, preferred_element_type=jnp.float32
     )
-    projected = lax.psum_scatter(partial_term, "head", scatter_dimension=1, tiled=True)
     return projected
 
 

time: 578 us -> 600 us (1.038)
  local copies, waits for them, and re-layouts: 88.4 us -> 113 us
  waiting for transfers between devices: 146 us -> 133 us
    reduce_scatter x1 -> x0, waiting for transfers between devices: 125 us -> none  [per_device(): lax.psum_scatter(partial_term, 'head', scatter_dimension=1, tiled=True)]
    all_gather x0 -> x1, waiting for transfers between devices: none -> 56.6 us  [per_device(): gathered = lax.all_gather(mixed, 'head', axis=1, tiled=True)]
    all_to_all x1, waiting for transfers between devices: 20.8 us -> 61 us  [per_device(): lax.all_to_all(send_v, 'seq', split_axis=0, concat_axis=0, tiled=True)]
    all_to_all x0 -> x1, waiting for transfers between devices: none -> 15.4 us  [per_device(): lax.all_to_all(out_weight, 'head', split_axis=1, concat_axis=0, tiled=True)]
    gather x3, local copies, waits for them, and re-layouts: 20.7 us -> 29.5 us  [place(): return pieces[where_from]]
    all_to_all x0 -> x1, local copies, waits for them, and re-layouts: none -> 8.74 us  [per_device(): lax.all_to_all(out_weight, 'head', split_axis=1, concat_axis=0, tiled=True)]
    unnamed x6 -> x10, local copies, waits for them, and re-layouts: 5.72 us -> 13.8 us
    all_to_all x0 -> x1, starting transfers between devices: none -> 6.06 us  [per_device(): lax.all_to_all(out_weight, 'head', split_axis=1, concat_axis=0, tiled=True)]
  transfers between devices with their start and end apart: 3 -> 4, of which waited for: 2 -> 3; matrix products, arithmetic and copies ran while one was open for 16% -> 23% of each run, Pallas kernels for 0% -> 0%
where the time goes in v2:
time: 600 us; the launch traced here: 595 us
  blocking collectives  224 us (37%)
  waiting for transfers between devices  133 us (22%)
  local copies, waits for them, and re-layouts  113 us (19%)
  matrix products  69.5 us (12%)
  other arithmetic  24 us (4%)
  starting transfers between devices  17 us (3%)
  between operations  13.8 us (2%)
    all_to_all x1, blocking collectives, per_device(): lax.all_to_all(send_q, 'seq', split_axis=0, concat_axis=0, tiled=True)  76.4 us
    all_to_all x1, blocking collectives, per_device(): lax.all_to_all(result[picked], 'seq', split_axis=0, concat_axis=0, tiled=...  74.3 us
    all_to_all x1, blocking collectives, per_device(): lax.all_to_all(send_k, 'seq', split_axis=0, concat_axis=0, tiled=True)  73.7 us
    all_to_all x1, waiting for transfers between devices, per_device(): lax.all_to_all(send_v, 'seq', split_axis=0, concat_axis=0, tiled=True)  61 us
    all_gather x1, waiting for transfers between devices, per_device(): gathered = lax.all_gather(mixed, 'head', axis=1, tiled=True)  56.6 us
    dot_general x1, matrix products, per_device(): jnp.dot(gathered, weight_cols, precision=lax.Precision.HIGHEST, preferred...  31.8 us
    gather x3, local copies, waits for them, and re-layouts, place(): return pieces[where_from]  29.5 us
    dot_general x1, matrix products, cluster_attention(): jnp.einsum('qhd,khd->hqk', query_c, key_c, precision=lax.Precision.HIGHEST)  21.3 us
  transfers between devices with their start and end apart: 4, of which 3 were waited for; matrix products, arithmetic and copies ran while one was open for 23% of the time, Pallas kernels for 0%

profile of v2, /device:TPU:0, one launch (start us, length us, event | category | flops | bytes accessed | tf_op | source)
XLA Modules:
  0.0 595.2 jit_solution(10736772374302047272)
XLA Ops:
  16.6 7.3 %all-to-all-start.1 = ((s32[8,192,1]{1,2,0:T(1,128)}), s32[8,192,1]{1,2,0:T(1,128)S(1)}, u32[]{:S(2)}, u32[]{:S(2)}) async-start(s32[8,192,1]{1,2,0:T(1,128)} %all_to_all.45), calls=%async_computation.1 | async-start | bytes 16384 | tf_op jit(solution)/shard_map/all_to_all | solution.py:93
  31.6 4.5 scatter_custom_fusion
  36.2 4.6 slice_negate_fusion
  46.2 5.3 select_maximum_fusion
  51.4 12.0 %gather_fusion = f32[1536,12,128]{2,1,0:T(8,128)} fusion(f32[1025,12,128]{2,1,0:T(8,128)} %select_maximum_fusion, s32[2048]{0:T(1024)S(1)} %pad_clamp_fusion.1), kind=kCustom, calls=%fused_computation | custom fusion | bytes 18880512 | tf_op jit(solution)/shard_map/gather | solution.py:88
  63.4 10.0 %fusion.29 = (f32[1536,4,128]{2,1,0:T(4,128)}, f32[1536,4,128]{2,1,0:T(4,128)}, f32[1536,4,128]{2,1,0:T(4,128)S(1)}) fusion(f32[1536,12,128]{2,1,0:T(8,128)} %gather_fusion), kind=kLoop, calls=%fused_computation.66 | loop fusion | bytes 18874368 | tf_op jit(solution)/shard_map/slice | solution.py:91
  73.4 76.4 %all_to_all.52 = f32[1536,4,128]{2,1,0:T(4,128)} all-to-all(f32[1536,4,128]{2,1,0:T(4,128)} %get-tuple-element.29), channel_id=1, replica_groups=mesh['seq'=8,'head'=4] {'seq'}, dimensions={0} | all-to-all | bytes 6291456 | tf_op jit(solution)/shard_map/all_to_all | solution.py:105
  149.8 73.7 %all_to_all.53 = f32[1536,4,128]{2,1,0:T(4,128)} all-to-all(f32[1536,4,128]{2,1,0:T(4,128)S(1)} %get-tuple-element.30), channel_id=1, replica_groups=mesh['seq'=8,'head'=4] {'seq'}, dimensions={0} | all-to-all | bytes 6291456 | tf_op jit(solution)/shard_map/all_to_all | solution.py:106
  227.1 9.0 %copy.26 = f32[512,4096]{0,1:T(8,128)} copy(f32[512,4096]{1,0:T(8,128)} %param.13) | data formatting | bytes 16777216 | tf_op args[6]
  236.1 61.0 %all-to-all-done = f32[1536,4,128]{2,1,0:T(4,128)S(1)} async-done(((f32[1536,4,128]{2,1,0:T(4,128)}), f32[1536,4,128]{2,1,0:T(4,128)S(1)}, u32[]{:S(2)}, u32[]{:S(2)}) %all-to-all-start) | async-done | bytes 3145760 | tf_op jit(solution)/shard_map/all_to_all | solution.py:107
  298.8 6.1 %all-to-all-start.4 = ((f32[512,4,1024]{0,2,1:T(8,128)}), f32[512,4,1024]{0,2,1:T(8,128)}, u32[]{:S(2)}, u32[]{:S(2)}) async-start(f32[512,4,1024]{0,2,1:T(8,128)} %bitcast.32), calls=%async_computation.4 | async-start | bytes 16777216 | tf_op jit(solution)/shard_map/all_to_all | solution.py:67
  305.4 6.2 %scatter_custom_fusion.2 = s32[1024]{0:T(1024)S(1)} fusion(s32[1536]{0:T(1024)S(1)} %get-tuple-element.25, s32[1536]{0:T(1024)S(1)} %iota.38, s32[]{:T(128)} %constant.85.clone.1), kind=kCustom, calls=%fused_computation.61 | custom fusion | bytes 4100 | tf_op jit(solution)/shard_map/scatter | solution.py:98
  311.7 9.8 %gather_fusion.2 = f32[1024,4,128]{2,1,0:T(4,128)} fusion(f32[1536,4,128]{2,1,0:T(4,128)} %all_to_all.52, s32[1024]{0:T(1024)S(1)} %fusion.20), kind=kCustom, calls=%fused_computation.2 | custom fusion | bytes 4198400 | tf_op jit(solution)/shard_map/gather | solution.py:102
  321.5 9.8 %gather_fusion.3 = f32[1024,4,128]{2,1,0:T(4,128)} fusion(f32[1536,4,128]{2,1,0:T(4,128)} %all_to_all.53, s32[1024]{0:T(1024)S(1)} %fusion.20), kind=kCustom, calls=%fused_computation.3 | custom fusion | bytes 4198400 | tf_op jit(solution)/shard_map/gather | solution.py:102
  331.3 9.9 %gather_fusion.1 = f32[1024,4,128]{2,1,0:T(4,128)} fusion(f32[1536,4,128]{2,1,0:T(4,128)} %copy-done.1, s32[1024]{0:T(1024)S(1)} %fusion.20), kind=kCustom, calls=%fused_computation.1 | custom fusion | bytes 4198400 | tf_op jit(solution)/shard_map/gather | solution.py:102
  341.1 21.3 %fusion = (f32[4,1024]{1,0:T(4,128)S(1)}, f32[4,1024,1024]{1,2,0:T(8,128)S(1)}) fusion(pred[1024,1024]{0,1:T(8,128)(4,1)S(1)} %iota_compare_fusion.1, f32[1024,4,128]{2,1,0:T(4,128)} %gather_fusion.3, f32[1024,4,128]{2,1,0:T(4,128)} %gather_fusion.2), kind=kOutput, calls=%fused_computation.11 | convolution fusion | flops 6455029760 | bytes 22036480 | tf_op jit(solution)/shard_map/while/body/eval_jaxpr/qhd,khd->hqk/dot_general | solution.py:43
  366.3 16.3 %bitcast_divide_fusion = f32[1024,4,128]{0,2,1:T(8,128)} fusion(f32[1024,4]{0,1:T(4,128)S(1)} %bitcast.38, f32[4,1024,1024]{1,2,0:T(8,128)S(1)} %get-tuple-element.40, f32[4,1024]{1,0:T(4,128)S(1)} %get-tuple-element.39, pred[1024,1024]{0,1:T(8,128)(4,1)S(1)} %iota_compare_fusion.1, f32[1024,4,128]{2,1,0:T(4,128)} %gather_fusion.1), kind=kOutput, calls=%fused_computation.29 | convolution fusion | flops 6455558144 | bytes 22052864 | tf_op jit(solution)/shard_map/while/body/eval_jaxpr/hqk,khd->qhd/dot_general | solution.py:51
  382.6 15.4 %all-to-all-done.4 = f32[512,4,1024]{0,2,1:T(8,128)} async-done(((f32[512,4,1024]{0,2,1:T(8,128)}), f32[512,4,1024]{0,2,1:T(8,128)}, u32[]{:S(2)}, u32[]{:S(2)}) %all-to-all-start.4) | async-done | bytes 8388640 | tf_op jit(solution)/shard_map/all_to_all | solution.py:67
  398.1 8.7 %copy.27 = f32[4,512,1024]{2,1,0:T(8,128)} copy(f32[4,512,1024]{1,2,0:T(8,128)} %bitcast.7) | data formatting | bytes 16777216 | tf_op jit(solution)/shard_map/all_to_all | solution.py:67
  408.9 5.5 gather_fusion.4
  414.3 74.3 %all_to_all.54 = f32[1536,4,128]{2,1,0:T(4,128)S(1)} all-to-all(f32[1536,4,128]{2,1,0:T(4,128)} %gather_fusion.4), channel_id=1, replica_groups=mesh['seq'=8,'head'=4] {'seq'}, dimensions={0} | all-to-all | bytes 6291456 | tf_op jit(solution)/shard_map/all_to_all | solution.py:111
  488.7 7.9 %gather_fusion.5 = f32[1024,4,128]{2,1,0:T(4,128)} fusion(f32[1536,4,128]{2,1,0:T(4,128)S(1)} %all_to_all.54, s32[1024]{0:T(1024)S(1)} %get-tuple-element.26), kind=kCustom, calls=%fused_computation.5 | custom fusion | bytes 4198400 | tf_op jit(solution)/shard_map/gather | solution.py:112
  499.7 56.6 %all-gather.2.cloned.1.call-done = f32[1024,2048]{1,0:T(8,128)} async-done(((f32[1024,512]{1,0:T(8,128)}), f32[1024,2048]{1,0:T(8,128)}) %all-gather.2.cloned.1.call-update) | async-done | bytes 8388624 | tf_op jit(solution)/shard_map/all_gather | solution.py:113
  556.3 31.8 %fusion.30 = f32[1024,1024]{1,0:T(8,128)} fusion(f32[1024,2048]{1,0:T(8,128)} %all-gather.2.cloned.1.call-done, f32[2048,1024]{1,0:T(8,128)} %bitcast.34), kind=kOutput, calls=%fused_computation.67 | convolution fusion | flops 25769803776 | bytes 20971520 | tf_op jit(solution)/shard_map/dot_general | solution.py:114
  (42 shorter events, 37.9 us)
Async XLA Ops:
  16.6 56.8 %all-to-all-start.1 = ((s32[8,192,1]{1,2,0:T(1,128)}), s32[8,192,1]{1,2,0:T(1,128)S(1)}, u32[]{:S(2)}, u32[]{:S(2)}) async-start(s32[8,192,1]{1,2,0:T(1,128)} %all_to_all.45), calls=%async_computation.1 | async-start | bytes 16384 | tf_op jit(solution)/shard_map/all_to_all | solution.py:93
  25.8 3.0 copy-start.3
  40.8 2.2 copy-start
  43.1 3.1 copy-start.2
  223.5 73.7 %all-to-all-start = ((f32[1536,4,128]{2,1,0:T(4,128)}), f32[1536,4,128]{2,1,0:T(4,128)S(1)}, u32[]{:S(2)}, u32[]{:S(2)}) async-start(f32[1536,4,128]{2,1,0:T(4,128)} %get-tuple-element.28), calls=%async_computation | async-start | bytes 6291456 | tf_op jit(solution)/shard_map/all_to_all | solution.py:107
  297.2 1.7 copy-start.1
  298.8 99.2 %all-to-all-start.4 = ((f32[512,4,1024]{0,2,1:T(8,128)}), f32[512,4,1024]{0,2,1:T(8,128)}, u32[]{:S(2)}, u32[]{:S(2)}) async-start(f32[512,4,1024]{0,2,1:T(8,128)} %bitcast.32), calls=%async_computation.4 | async-start | bytes 16777216 | tf_op jit(solution)/shard_map/all_to_all | solution.py:67
  304.9 251.4 %all-gather.2.cloned.1.call-start = ((), (), s32[]{:S(2)}) async-start(), calls=%async_computation.6 | async-start | bytes 10485760 | tf_op jit(solution)/shard_map/all_gather | solution.py:113
Sparse Core Ops, SparseCore 0:
  499.9 56.4 all-gather.1

commit v3 on v0

--- a/solution.py
+++ b/solution.py
@@ -41,14 +41,14 @@
     query_c, key_c, value_c = triple
     length = query_c.shape[0]
     scores = jnp.einsum(
-        "qhd,khd->hqk", query_c, key_c, precision=lax.Precision.HIGHEST
+        "qhd,khd->hqk", query_c, key_c, precision=lax.Precision.HIGH
     ) / math.sqrt(query_c.shape[-1])
     causal = jnp.arange(length)[:, None] >= jnp.arange(length)[None, :]
     scores = jnp.where(causal[None], scores, -jnp.inf)
     peak = jnp.max(scores, -1, keepdims=True)
     weights = jnp.exp(scores - peak)
     total = jnp.sum(weights, -1, keepdims=True)
-    summed = jnp.einsum("hqk,khd->qhd", weights, value_c, precision=lax.Precision.HIGHEST)
+    summed = jnp.einsum("hqk,khd->qhd", weights, value_c, precision=lax.Precision.HIGH)
     return summed / jnp.transpose(total, (1, 0, 2))
 
 
@@ -108,11 +108,36 @@
     result = attend_local(place(received[0]), place(received[1]), place(received[2]))
     returned = lax.all_to_all(result[picked], "seq", split_axis=0, concat_axis=0, tiled=True)
     mixed = returned[send_row].reshape(row_count, heads_here * DH)
-    partial_term = jnp.dot(
-        mixed, out_weight, precision=lax.Precision.HIGHEST, preferred_element_type=jnp.float32
+    return project_scatter(mixed, out_weight)
+
+
+def swap_pairs(count, bit):
+    return [(index, index ^ bit) for index in range(count)]
+
+
+def project_scatter(mixed, out_weight):
+    head_count = lax.axis_size("head")
+    head_index = lax.axis_index("head")
+    core = head_index % 2
+    y_half = head_index // 2
+    in_rows, total_cols = out_weight.shape
+    width = total_cols // head_count
+    blocks = out_weight.reshape(in_rows, head_count // 2, 2, width)
+    other_w = jnp.where(core == 0, blocks[:, :, 1], blocks[:, :, 0])
+    own_w = jnp.where(core == 0, blocks[:, :, 0], blocks[:, :, 1])
+    other_w = other_w.reshape(in_rows, total_cols // 2)
+    own_w = own_w.reshape(in_rows, total_cols // 2)
+    dot = lambda a, b: jnp.dot(
+        a, b, precision=lax.Precision.HIGH, preferred_element_type=jnp.float32
     )
-    projected = lax.psum_scatter(partial_term, "head", scatter_dimension=1, tiled=True)
-    return projected
+    to_partner = dot(mixed, other_w)
+    from_partner = lax.ppermute(to_partner, "head", swap_pairs(head_count, 1))
+    chip_sum = dot(mixed, own_w) + from_partner
+    halves = chip_sum.reshape(chip_sum.shape[0], head_count // 2, width)
+    send_half = jnp.where(y_half == 0, halves[:, 1], halves[:, 0])
+    keep_half = jnp.where(y_half == 0, halves[:, 0], halves[:, 1])
+    from_across = lax.ppermute(send_half, "head", swap_pairs(head_count, 2))
+    return keep_half + from_across
 
 
 def solution(mesh):

time: 578 us -> 561 us (0.971)
  blocking collectives: 225 us -> 150 us
  local copies, waits for them, and re-layouts: 88.4 us -> 129 us
  other arithmetic: 22.3 us -> 62.3 us
  matrix products: 67.1 us -> 46.8 us
  between operations: 13.8 us -> 0.54 us
  starting transfers between devices: 11.7 us -> 18.2 us
    reduce_scatter x1 -> x0, waiting for transfers between devices: 125 us -> none  [per_device(): lax.psum_scatter(partial_term, 'head', scatter_dimension=1, tiled=True)]
    ppermute x0 -> x2, waiting for transfers between devices: none -> 98.5 us  [the longest x1 91.1 us: project_scatter(): from_across = lax.ppermute(send_half, 'head', swap_pairs(head_count, 2))]
    all_to_all x1 -> x0, blocking collectives: 74.5 us -> none  [per_device(): lax.all_to_all(result[picked], 'seq', split_axis=0, concat_axis=0, tiled=...]
    select_n x0 -> x2, other arithmetic: none -> 33.8 us  [the longest x1 31.7 us: project_scatter(): own_w = jnp.where(core == 0, blocks[:, :, 0], blocks[:, :, 1])]
    reshape x0 -> x2, local copies, waits for them, and re-layouts: none -> 23.5 us  [the longest x1 11.7 us: project_scatter(): halves = chip_sum.reshape(chip_sum.shape[0], head_count // 2, width)]
    all_to_all x0 -> x1, waiting for transfers between devices: none -> 22.8 us  [per_device(): lax.all_to_all(result[picked], 'seq', split_axis=0, concat_axis=0, tiled=...]
    dot_general x3 -> x4, matrix products: 67.1 us -> 46.8 us  [the longest x2 23.3 us: project_scatter(): jnp.dot(a, b, precision=lax.Precision.HIGH, preferred_element_type=jnp.fl...]
    slice x1 -> x2, local copies, waits for them, and re-layouts: 0.28 us -> 10.9 us  [the longest x1 10.6 us: project_scatter(): keep_half = jnp.where(y_half == 0, halves[:, 0], halves[:, 1])]
  transfers between devices with their start and end apart: 3 -> 5, of which waited for: 2 -> 4; matrix products, arithmetic and copies ran while one was open for 16% -> 25% of each run, Pallas kernels for 0% -> 0%
where the time goes in v3:
time: 561 us; the launch traced here: 556 us
  blocking collectives  150 us (27%)
  waiting for transfers between devices  149 us (27%)
  local copies, waits for them, and re-layouts  129 us (23%)
  other arithmetic  62.3 us (11%)
  matrix products  46.8 us (8%)
  starting transfers between devices  18.2 us (3%)
    ppermute x1, waiting for transfers between devices, project_scatter(): from_across = lax.ppermute(send_half, 'head', swap_pairs(head_count, 2))  91.1 us
    all_to_all x1, blocking collectives, per_device(): lax.all_to_all(send_q, 'seq', split_axis=0, concat_axis=0, tiled=True)  76.4 us
    all_to_all x1, blocking collectives, per_device(): lax.all_to_all(send_k, 'seq', split_axis=0, concat_axis=0, tiled=True)  73.7 us
    select_n x1, other arithmetic, project_scatter(): own_w = jnp.where(core == 0, blocks[:, :, 0], blocks[:, :, 1])  31.7 us
    all_to_all x1, waiting for transfers between devices, per_device(): lax.all_to_all(send_v, 'seq', split_axis=0, concat_axis=0, tiled=True)  27.8 us
    dot_general x2, matrix products, project_scatter(): jnp.dot(a, b, precision=lax.Precision.HIGH, preferred_element_type=jnp.fl...  23.3 us
    all_to_all x1, waiting for transfers between devices, per_device(): lax.all_to_all(result[picked], 'seq', split_axis=0, concat_axis=0, tiled=...  22.8 us
    gather x3, local copies, waits for them, and re-layouts, place(): return pieces[where_from]  20.7 us
  transfers between devices with their start and end apart: 5, of which 4 were waited for; matrix products, arithmetic and copies ran while one was open for 25% of the time, Pallas kernels for 0%

profile of v3, /device:TPU:0, one launch (start us, length us, event | category | flops | bytes accessed | tf_op | source)
XLA Modules:
  0.0 556.3 jit_solution(11149987949480432386)
XLA Ops:
  10.0 7.3 %all-to-all-start.1 = ((s32[8,192,1]{1,2,0:T(1,128)}), s32[8,192,1]{1,2,0:T(1,128)S(1)}, u32[]{:S(2)}, u32[]{:S(2)}) async-start(s32[8,192,1]{1,2,0:T(1,128)} %all_to_all.27), calls=%async_computation.1 | async-start | bytes 16384 | tf_op jit(solution)/shard_map/all_to_all | solution.py:92
  44.9 12.0 %gather_fusion = f32[1536,12,128]{2,1,0:T(8,128)} fusion(f32[1025,12,128]{2,1,0:T(8,128)} %select_maximum_fusion, s32[2048]{0:T(1024)S(1)} %pad_clamp_fusion.1), kind=kCustom, calls=%fused_computation | custom fusion | bytes 18880512 | tf_op jit(solution)/shard_map/gather | solution.py:87
  56.9 10.0 %fusion.36 = (f32[1536,4,128]{2,1,0:T(4,128)}, f32[1536,4,128]{2,1,0:T(4,128)}, f32[1536,4,128]{2,1,0:T(4,128)S(1)}) fusion(f32[1536,12,128]{2,1,0:T(8,128)} %gather_fusion), kind=kLoop, calls=%fused_computation.77 | loop fusion | bytes 18874368 | tf_op jit(solution)/shard_map/slice | solution.py:90
  66.9 76.4 %all_to_all.33 = f32[1536,4,128]{2,1,0:T(4,128)} all-to-all(f32[1536,4,128]{2,1,0:T(4,128)} %get-tuple-element.27), channel_id=1, replica_groups=mesh['seq'=8,'head'=4] {'seq'}, dimensions={0} | all-to-all | bytes 6291456 | tf_op jit(solution)/shard_map/all_to_all | solution.py:104
  143.3 73.7 %all_to_all.34 = f32[1536,4,128]{2,1,0:T(4,128)} all-to-all(f32[1536,4,128]{2,1,0:T(4,128)S(1)} %get-tuple-element.28), channel_id=1, replica_groups=mesh['seq'=8,'head'=4] {'seq'}, dimensions={0} | all-to-all | bytes 6291456 | tf_op jit(solution)/shard_map/all_to_all | solution.py:105
  222.3 6.2 %scatter_custom_fusion.2 = s32[1024]{0:T(1024)S(1)} fusion(s32[1536]{0:T(1024)S(1)} %get-tuple-element.22, s32[1536]{0:T(1024)S(1)} %iota.38, s32[]{:T(128)} %constant.99.clone.1), kind=kCustom, calls=%fused_computation.72 | custom fusion | bytes 4100 | tf_op jit(solution)/shard_map/scatter | solution.py:97
  228.5 5.4 gather_fusion.2
  233.9 9.8 %gather_fusion.3 = f32[1024,4,128]{2,1,0:T(4,128)} fusion(f32[1536,4,128]{2,1,0:T(4,128)} %all_to_all.34, s32[1024]{0:T(1024)S(1)} %fusion.27), kind=kCustom, calls=%fused_computation.3 | custom fusion | bytes 4198400 | tf_op jit(solution)/shard_map/gather | solution.py:101
  243.8 10.5 %fusion = (f32[4,1024]{1,0:T(4,128)S(1)}, f32[4,1024,1024]{1,2,0:T(8,128)S(1)}) fusion(pred[1024,1024]{0,1:T(8,128)(4,1)S(1)} %iota_compare_fusion.1, f32[1024,4,128]{2,1,0:T(4,128)} %gather_fusion.3, f32[1024,4,128]{2,1,0:T(4,128)S(1)} %gather_fusion.2), kind=kOutput, calls=%fused_computation.11 | convolution fusion | flops 3233804288 | bytes 22036480 | tf_op jit(solution)/shard_map/while/body/eval_jaxpr/qhd,khd->hqk/dot_general | solution.py:43
  254.3 5.7 %copy-done = f32[4,1024,1024]{1,2,0:T(8,128)} copy-done((f32[4,1024,1024]{1,2,0:T(8,128)}, f32[4,1024,1024]{1,2,0:T(8,128)S(1)}, u32[]{:S(2)}) %copy-start) | copy-done | bytes 16777240
  263.6 27.8 %all-to-all-done = f32[1536,4,128]{2,1,0:T(4,128)} async-done(((f32[1536,4,128]{2,1,0:T(4,128)}), f32[1536,4,128]{2,1,0:T(4,128)}, u32[]{:S(2)}, u32[]{:S(2)}) %all-to-all-start) | async-done | bytes 3145760 | tf_op jit(solution)/shard_map/all_to_all | solution.py:106
  296.9 12.9 %bitcast_divide_fusion = f32[1024,4,128]{0,2,1:T(8,128)} fusion(f32[1024,4]{0,1:T(4,128)S(1)} %bitcast.47, f32[4,1024,1024]{1,2,0:T(8,128)} %copy-done, f32[4,1024]{1,0:T(4,128)S(1)} %get-tuple-element.39, pred[1024,1024]{0,1:T(8,128)(4,1)S(1)} %iota_compare_fusion.1, f32[1024,4,128]{2,1,0:T(4,128)S(1)} %gather_fusion.1), kind=kOutput, calls=%fused_computation.38 | convolution fusion | flops 3234332672 | bytes 22052864 | tf_op jit(solution)/shard_map/while/body/eval_jaxpr/hqk,khd->qhd/dot_general | solution.py:51
  311.9 5.5 gather_fusion.4
  321.9 11.7 %reshape.194 = f32[512,2,2,1024]{3,2,1,0:T(2,128)} reshape(f32[512,4096]{1,0:T(8,128)} %param.13) | data formatting | bytes 16777216 | tf_op jit(solution)/shard_map/reshape | solution.py:125
  333.6 31.7 %fusion.7 = (f32[512,2,1024]{2,1,0:T(2,128)}, f32[512,2,1024]{2,1,0:T(2,128)S(1)}) fusion(pred[]{:T(512)S(6)} %eq.43, f32[512,2,2,1024]{3,2,1,0:T(2,128)} %reshape.194), kind=kLoop, calls=%fused_computation.23 | loop fusion | flops 2097152 | bytes 16777216 | tf_op jit(solution)/shard_map/jit(_where)/select_n | solution.py:127
  369.3 22.8 %all-to-all-done.4 = f32[1536,4,128]{2,1,0:T(4,128)} async-done(((f32[1536,4,128]{2,1,0:T(4,128)}), f32[1536,4,128]{2,1,0:T(4,128)}, u32[]{:S(2)}, u32[]{:S(2)}) %all-to-all-start.4) | async-done | bytes 3145760 | tf_op jit(solution)/shard_map/all_to_all | solution.py:109
  392.0 5.4 gather_fusion.5
  397.5 10.7 %fusion.9 = f32[1024,2048]{1,0:T(8,128)} fusion(f32[512,2048]{1,0:T(8,128)} %bitcast.44, f32[128,8,4,128]{3,2,1,0:T(4,128)S(1)} %bitcast.39), kind=kOutput, calls=%fused_computation.29 | convolution fusion | flops 6442450944 | bytes 14680064 | tf_op jit(solution)/shard_map/dot_general | solution.py:130
  408.2 6.1 %copy.31 = f32[64,8,2,1024]{3,1,2,0:T(8,128)} copy(f32[64,8,2,1024]{3,2,1,0:T(2,128)} %bitcast.41) | data formatting | bytes 8388608
  414.3 7.4 %collective-permute-done = f32[1024,2048]{1,0:T(8,128)} collective-permute-done((f32[1024,2048]{1,0:T(8,128)}, f32[1024,2048]{1,0:T(8,128)}, u32[]{:S(2)}, u32[]{:S(2)}) %collective-permute-start) | collective-permute-done | bytes 8388640 | tf_op jit(solution)/shard_map/ppermute | solution.py:134
  421.7 12.6 %convolution_add_fusion = f32[1024,2048]{1,0:T(8,128)} fusion(f32[1024,2048]{1,0:T(8,128)} %collective-permute-done, f32[512,2048]{1,0:T(8,128)} %bitcast.43, f32[128,8,4,128]{3,2,1,0:T(4,128)S(1)} %bitcast.40), kind=kOutput, calls=%fused_computation.28 | convolution fusion | flops 6444548096 | bytes 23068672 | tf_op jit(solution)/shard_map/dot_general | solution.py:130
  434.3 11.7 %reshape.195 = f32[1024,2,1024]{2,1,0:T(2,128)} reshape(f32[1024,2048]{1,0:T(8,128)} %convolution_add_fusion) | data formatting | bytes 16777216 | tf_op jit(solution)/shard_map/reshape | solution.py:136
  446.0 10.6 %fusion.37 = (f32[1024,1,1024]{2,1,0:T(1,128)S(1)}, f32[1024,1,1024]{2,1,0:T(1,128)S(1)}) fusion(f32[1024,2,1024]{2,1,0:T(2,128)} %reshape.195), kind=kLoop, calls=%fused_computation.78 | loop fusion | bytes 16777216 | tf_op jit(solution)/shard_map/slice | solution.py:138
  460.3 91.1 %collective-permute-done.1 = f32[1024,1024]{1,0:T(8,128)S(1)} collective-permute-done((f32[1024,1024]{1,0:T(8,128)S(1)}, f32[1024,1024]{1,0:T(8,128)S(1)}, u32[]{:S(2)}, u32[]{:S(2)}) %collective-permute-start.1) | collective-permute-done | bytes 4194336 | tf_op jit(solution)/shard_map/ppermute | solution.py:139
  (48 shorter events, 70.6 us)
Async XLA Ops:
  10.0 56.8 %all-to-all-start.1 = ((s32[8,192,1]{1,2,0:T(1,128)}), s32[8,192,1]{1,2,0:T(1,128)S(1)}, u32[]{:S(2)}, u32[]{:S(2)}) async-start(s32[8,192,1]{1,2,0:T(1,128)} %all_to_all.27), calls=%async_computation.1 | async-start | bytes 16384 | tf_op jit(solution)/shard_map/all_to_all | solution.py:92
  19.3 3.0 copy-start.3
  34.3 2.2 copy-start.1
  36.5 3.1 copy-start.2
  217.0 74.5 %all-to-all-start = ((f32[1536,4,128]{2,1,0:T(4,128)}), f32[1536,4,128]{2,1,0:T(4,128)}, u32[]{:S(2)}, u32[]{:S(2)}) async-start(f32[1536,4,128]{2,1,0:T(4,128)} %get-tuple-element.26), calls=%async_computation | async-start | bytes 6291456 | tf_op jit(solution)/shard_map/all_to_all | solution.py:106
  254.3 5.7 %copy-start = (f32[4,1024,1024]{1,2,0:T(8,128)}, f32[4,1024,1024]{1,2,0:T(8,128)S(1)}, u32[]{:S(2)}) copy-start(f32[4,1024,1024]{1,2,0:T(8,128)S(1)} %get-tuple-element.40) | copy-start | bytes 50331652
  317.4 74.6 %all-to-all-start.4 = ((f32[1536,4,128]{2,1,0:T(4,128)}), f32[1536,4,128]{2,1,0:T(4,128)}, u32[]{:S(2)}, u32[]{:S(2)}) async-start(f32[1536,4,128]{2,1,0:T(4,128)} %gather_fusion.4), calls=%async_computation.4 | async-start | bytes 6291456 | tf_op jit(solution)/shard_map/all_to_all | solution.py:109
  408.2 13.5 %collective-permute-start = (f32[1024,2048]{1,0:T(8,128)}, f32[1024,2048]{1,0:T(8,128)}, u32[]{:S(2)}, u32[]{:S(2)}) collective-permute-start(f32[1024,2048]{1,0:T(8,128)} %fusion.9), channel_id=1, source_target_pairs={{0,1},{1,0},{2,3},{3,2},{4,5},{5,4},{6,7},{7,6},{8,9},{9,8},{10,11... | collective-permute-start | bytes 25165832 | tf_op jit(solution)/shard_map/ppermute | solution.py:134
  458.7 92.7 %collective-permute-start.1 = (f32[1024,1024]{1,0:T(8,128)S(1)}, f32[1024,1024]{1,0:T(8,128)S(1)}, u32[]{:S(2)}, u32[]{:S(2)}) collective-permute-start(f32[1024,1024]{1,0:T(8,128)S(1)} %select_bitcast_fusion), channel_id=1, source_target_pairs={{0,2},{1,3},{2,0},{3,1},{4,6},{5,7},{6,4},{7,5},{8,10},{9,11},{10,... | collective-permute-start | bytes 12582920 | tf_op jit(solution)/shard_map/ppermute | solution.py:139

commit v4 on v0

--- a/solution.py
+++ b/solution.py
@@ -41,14 +41,14 @@
     query_c, key_c, value_c = triple
     length = query_c.shape[0]
     scores = jnp.einsum(
-        "qhd,khd->hqk", query_c, key_c, precision=lax.Precision.HIGHEST
+        "qhd,khd->hqk", query_c, key_c, precision=lax.Precision.HIGH
     ) / math.sqrt(query_c.shape[-1])
     causal = jnp.arange(length)[:, None] >= jnp.arange(length)[None, :]
     scores = jnp.where(causal[None], scores, -jnp.inf)
     peak = jnp.max(scores, -1, keepdims=True)
     weights = jnp.exp(scores - peak)
     total = jnp.sum(weights, -1, keepdims=True)
-    summed = jnp.einsum("hqk,khd->qhd", weights, value_c, precision=lax.Precision.HIGHEST)
+    summed = jnp.einsum("hqk,khd->qhd", weights, value_c, precision=lax.Precision.HIGH)
     return summed / jnp.transpose(total, (1, 0, 2))
 
 
@@ -108,11 +108,33 @@
     result = attend_local(place(received[0]), place(received[1]), place(received[2]))
     returned = lax.all_to_all(result[picked], "seq", split_axis=0, concat_axis=0, tiled=True)
     mixed = returned[send_row].reshape(row_count, heads_here * DH)
-    partial_term = jnp.dot(
-        mixed, out_weight, precision=lax.Precision.HIGHEST, preferred_element_type=jnp.float32
-    )
-    projected = lax.psum_scatter(partial_term, "head", scatter_dimension=1, tiled=True)
-    return projected
+    return project_scatter(mixed, out_weight)
+
+
+def swap_pairs(count, bit):
+    return [(index, index ^ bit) for index in range(count)]
+
+
+def project_scatter(mixed, out_weight):
+    head_count = lax.axis_size("head")
+    me = lax.axis_index("head")
+    partner = me ^ 1
+    width = out_weight.shape[1] // head_count
+
+    def block(index):
+        return lax.dynamic_slice_in_dim(out_weight, index * width, width, axis=1)
+
+    def dot(weight):
+        return jnp.dot(
+            mixed, weight, precision=lax.Precision.HIGH, preferred_element_type=jnp.float32
+        )
+
+    for_partner_far = lax.ppermute(dot(block(partner ^ 2)), "head", swap_pairs(head_count, 1))
+    far_sum = dot(block(me ^ 2)) + for_partner_far
+    from_far = lax.ppermute(far_sum, "head", swap_pairs(head_count, 2))
+    for_partner_near = lax.ppermute(dot(block(partner)), "head", swap_pairs(head_count, 1))
+    near_sum = dot(block(me)) + for_partner_near
+    return near_sum + from_far
 
 
 def solution(mesh):

time: 578 us -> 522 us (0.903)
  blocking collectives: 225 us -> 150 us
  waiting for transfers between devices: 146 us -> 185 us
  matrix products: 67.1 us -> 49 us
  between operations: 13.8 us -> 0.44 us
  other arithmetic: 22.3 us -> 29.3 us
    reduce_scatter x1 -> x0, waiting for transfers between devices: 125 us -> none  [per_device(): lax.psum_scatter(partial_term, 'head', scatter_dimension=1, tiled=True)]
    ppermute x0 -> x3, waiting for transfers between devices: none -> 86.7 us  [the longest x1 86.2 us: project_scatter(): from_far = lax.ppermute(far_sum, 'head', swap_pairs(head_count, 2))]
    all_to_all x1 -> x0, blocking collectives: 74.5 us -> none  [per_device(): lax.all_to_all(result[picked], 'seq', split_axis=0, concat_axis=0, tiled=...]
    all_to_all x0 -> x1, waiting for transfers between devices: none -> 70.8 us  [per_device(): lax.all_to_all(result[picked], 'seq', split_axis=0, concat_axis=0, tiled=...]
    dot_general x3 -> x6, matrix products: 67.1 us -> 49 us  [the longest x4 25.6 us: dot(): jnp.dot(mixed, weight, precision=lax.Precision.HIGH, preferred_element_ty...]
    all_to_all x1, waiting for transfers between devices: 20.8 us -> 27.8 us  [per_device(): lax.all_to_all(send_v, 'seq', split_axis=0, concat_axis=0, tiled=True)]
    add x0 -> x1, other arithmetic: none -> 7.01 us  [project_scatter(): return near_sum + from_far]
  transfers between devices with their start and end apart: 3 -> 6, of which waited for: 2 -> 4; matrix products, arithmetic and copies ran while one was open for 16% -> 20% of each run, Pallas kernels for 0% -> 0%
where the time goes in v4:
time: 522 us; the launch traced here: 519 us
  waiting for transfers between devices  185 us (35%)
  blocking collectives  150 us (29%)
  local copies, waits for them, and re-layouts  87.3 us (17%)
  matrix products  49 us (9%)
  other arithmetic  29.3 us (6%)
  starting transfers between devices  17.4 us (3%)
    ppermute x1, waiting for transfers between devices, project_scatter(): from_far = lax.ppermute(far_sum, 'head', swap_pairs(head_count, 2))  86.2 us
    all_to_all x1, blocking collectives, per_device(): lax.all_to_all(send_q, 'seq', split_axis=0, concat_axis=0, tiled=True)  76.4 us
    all_to_all x1, blocking collectives, per_device(): lax.all_to_all(send_k, 'seq', split_axis=0, concat_axis=0, tiled=True)  73.7 us
    all_to_all x1, waiting for transfers between devices, per_device(): lax.all_to_all(result[picked], 'seq', split_axis=0, concat_axis=0, tiled=...  70.8 us
    all_to_all x1, waiting for transfers between devices, per_device(): lax.all_to_all(send_v, 'seq', split_axis=0, concat_axis=0, tiled=True)  27.8 us
    dot_general x4, matrix products, dot(): jnp.dot(mixed, weight, precision=lax.Precision.HIGH, preferred_element_ty...  25.6 us
    gather x3, local copies, waits for them, and re-layouts, place(): return pieces[where_from]  20.7 us
    dot_general x1, matrix products, cluster_attention(): jnp.einsum('hqk,khd->qhd', weights, value_c, precision=lax.Precision.HIGH)  12.9 us
  transfers between devices with their start and end apart: 6, of which 4 were waited for; matrix products, arithmetic and copies ran while one was open for 20% of the time, Pallas kernels for 0%

profile of v4, /device:TPU:0, one launch (start us, length us, event | category | flops | bytes accessed | tf_op | source)
XLA Modules:
  0.0 518.9 jit_solution(6452303594252034116)
XLA Ops:
  10.0 7.3 %all-to-all-start.1 = ((s32[8,192,1]{1,2,0:T(1,128)}), s32[8,192,1]{1,2,0:T(1,128)S(1)}, u32[]{:S(2)}, u32[]{:S(2)}) async-start(s32[8,192,1]{1,2,0:T(1,128)} %all_to_all.27), calls=%async_computation.1 | async-start | bytes 16384 | tf_op jit(solution)/shard_map/all_to_all | solution.py:92
  18.0 4.5 scatter_custom_fusion
  38.1 5.3 %select_maximum_fusion = f32[1025,12,128]{2,1,0:T(8,128)} fusion(f32[1024,4,128]{2,1,0:T(4,128)S(1)} %copy-done.3, f32[1024,4,128]{2,1,0:T(4,128)S(1)} %get-tuple-element.32, f32[1024,4,128]{2,1,0:T(4,128)S(1)} %get-tuple-element.31), kind=kLoop, calls=%fused_computation.14 | loop fusion | flops 9446400 | bytes 12589056 | tf_op jit(solution)/shard_map/concatenate | solution.py:85
  43.4 12.0 %gather_fusion = f32[1536,12,128]{2,1,0:T(8,128)} fusion(f32[1025,12,128]{2,1,0:T(8,128)} %select_maximum_fusion, s32[2048]{0:T(1024)S(1)} %pad_clamp_fusion.1), kind=kCustom, calls=%fused_computation | custom fusion | bytes 18880512 | tf_op jit(solution)/shard_map/gather | solution.py:87
  55.3 10.4 %fusion.48 = (f32[1536,4,128]{2,1,0:T(4,128)}, f32[1536,4,128]{2,1,0:T(4,128)}, f32[1536,4,128]{2,1,0:T(4,128)S(1)}) fusion(f32[1536,12,128]{2,1,0:T(8,128)} %gather_fusion), kind=kLoop, calls=%fused_computation.86 | loop fusion | bytes 18874368 | tf_op jit(solution)/shard_map/slice | solution.py:90
  65.7 76.4 %all_to_all.33 = f32[1536,4,128]{2,1,0:T(4,128)} all-to-all(f32[1536,4,128]{2,1,0:T(4,128)} %get-tuple-element.25), channel_id=1, replica_groups=mesh['seq'=8,'head'=4] {'seq'}, dimensions={0} | all-to-all | bytes 6291456 | tf_op jit(solution)/shard_map/all_to_all | solution.py:104
  142.1 73.7 %all_to_all.34 = f32[1536,4,128]{2,1,0:T(4,128)} all-to-all(f32[1536,4,128]{2,1,0:T(4,128)S(1)} %get-tuple-element.26), channel_id=1, replica_groups=mesh['seq'=8,'head'=4] {'seq'}, dimensions={0} | all-to-all | bytes 6291456 | tf_op jit(solution)/shard_map/all_to_all | solution.py:105
  220.7 6.2 %scatter_custom_fusion.2 = s32[1024]{0:T(1024)S(1)} fusion(s32[1536]{0:T(1024)S(1)} %get-tuple-element.14, s32[1536]{0:T(1024)S(1)} %iota.38, s32[]{:T(128)} %constant.91.clone.1), kind=kCustom, calls=%fused_computation.77 | custom fusion | bytes 4100 | tf_op jit(solution)/shard_map/scatter | solution.py:97
  227.0 5.4 %gather_fusion.2 = f32[1024,4,128]{2,1,0:T(4,128)S(1)} fusion(f32[1536,4,128]{2,1,0:T(4,128)} %all_to_all.33, s32[1024]{0:T(1024)S(1)} %fusion.35), kind=kCustom, calls=%fused_computation.2 | custom fusion | bytes 4198400 | tf_op jit(solution)/shard_map/gather | solution.py:101
  232.4 9.8 %gather_fusion.3 = f32[1024,4,128]{2,1,0:T(4,128)} fusion(f32[1536,4,128]{2,1,0:T(4,128)} %all_to_all.34, s32[1024]{0:T(1024)S(1)} %fusion.35), kind=kCustom, calls=%fused_computation.3 | custom fusion | bytes 4198400 | tf_op jit(solution)/shard_map/gather | solution.py:101
  242.2 10.5 %fusion = (f32[4,1024]{1,0:T(4,128)S(1)}, f32[4,1024,1024]{1,2,0:T(8,128)S(1)}) fusion(pred[1024,1024]{0,1:T(8,128)(4,1)S(1)} %iota_compare_fusion.1, f32[1024,4,128]{2,1,0:T(4,128)} %gather_fusion.3, f32[1024,4,128]{2,1,0:T(4,128)S(1)} %gather_fusion.2), kind=kOutput, calls=%fused_computation.11 | convolution fusion | flops 3233804288 | bytes 22036480 | tf_op jit(solution)/shard_map/while/body/eval_jaxpr/qhd,khd->hqk/dot_general | solution.py:43
  252.8 5.7 %copy-done = f32[4,1024,1024]{1,2,0:T(8,128)} copy-done((f32[4,1024,1024]{1,2,0:T(8,128)}, f32[4,1024,1024]{1,2,0:T(8,128)S(1)}, u32[]{:S(2)}) %copy-start) | copy-done | bytes 16777240
  262.1 27.8 %all-to-all-done = f32[1536,4,128]{2,1,0:T(4,128)} async-done(((f32[1536,4,128]{2,1,0:T(4,128)}), f32[1536,4,128]{2,1,0:T(4,128)}, u32[]{:S(2)}, u32[]{:S(2)}) %all-to-all-start) | async-done | bytes 3145760 | tf_op jit(solution)/shard_map/all_to_all | solution.py:106
  289.9 5.4 %gather_fusion.1 = f32[1024,4,128]{2,1,0:T(4,128)S(1)} fusion(f32[1536,4,128]{2,1,0:T(4,128)} %all-to-all-done, s32[1024]{0:T(1024)S(1)} %fusion.35), kind=kCustom, calls=%fused_computation.1 | custom fusion | bytes 4198400 | tf_op jit(solution)/shard_map/gather | solution.py:101
  295.4 12.9 %bitcast_divide_fusion = f32[1024,4,128]{0,2,1:T(8,128)} fusion(f32[1024,4]{0,1:T(4,128)S(1)} %bitcast.42, f32[4,1024,1024]{1,2,0:T(8,128)} %copy-done, f32[4,1024]{1,0:T(4,128)S(1)} %get-tuple-element.35, pred[1024,1024]{0,1:T(8,128)(4,1)S(1)} %iota_compare_fusion.1, f32[1024,4,128]{2,1,0:T(4,128)S(1)} %gather_fusion.1), kind=kOutput, calls=%fused_computation.37 | convolution fusion | flops 3234332672 | bytes 22052864 | tf_op jit(solution)/shard_map/while/body/eval_jaxpr/hqk,khd->qhd/dot_general | solution.py:51
  310.3 5.5 %gather_fusion.4 = f32[1536,4,128]{2,1,0:T(4,128)} fusion(f32[1024,4,128]{2,1,0:T(4,128)S(1)} %copy.19, s32[2048]{0:T(1024)S(1)} %pad_clamp_fusion), kind=kCustom, calls=%fused_computation.4 | custom fusion | bytes 6297600 | tf_op jit(solution)/shard_map/gather | solution.py:109
  319.5 70.8 %all-to-all-done.4 = f32[1536,4,128]{2,1,0:T(4,128)S(1)} async-done(((f32[1536,4,128]{2,1,0:T(4,128)}), f32[1536,4,128]{2,1,0:T(4,128)S(1)}, u32[]{:S(2)}, u32[]{:S(2)}) %all-to-all-start.4) | async-done | bytes 3145760 | tf_op jit(solution)/shard_map/all_to_all | solution.py:109
  392.0 5.4 %gather_fusion.5 = f32[1024,4,128]{2,1,0:T(4,128)S(1)} fusion(f32[1536,4,128]{2,1,0:T(4,128)} %copy-done.2, s32[1024]{0:T(1024)S(1)} %get-tuple-element.20), kind=kCustom, calls=%fused_computation.5 | custom fusion | bytes 4198400 | tf_op jit(solution)/shard_map/gather | solution.py:110
  397.4 6.6 %fusion.7 = f32[1024,1024]{1,0:T(8,128)} fusion(f32[512,4096]{1,0:T(8,128)} %param.13, s32[]{:T(128)S(6)} %select_n.68, f32[128,8,4,128]{3,2,1,0:T(4,128)S(1)} %bitcast.36), kind=kOutput, calls=%fused_computation.24 | convolution fusion | flops 3221225472 | bytes 8388612 | tf_op jit(solution)/shard_map/dot_general | solution.py:128
  404.0 6.6 %fusion.10 = f32[1024,1024]{1,0:T(8,128)} fusion(f32[512,4096]{1,0:T(8,128)} %param.13, s32[]{:T(128)S(6)} %select_n.66, f32[128,8,4,128]{3,2,1,0:T(4,128)S(1)} %bitcast.37), kind=kOutput, calls=%fused_computation.27 | convolution fusion | flops 3221225472 | bytes 8388612 | tf_op jit(solution)/shard_map/dot_general | solution.py:128
  411.5 7.3 %convolution_add_fusion = f32[1024,1024]{1,0:T(8,128)} fusion(f32[1024,1024]{1,0:T(8,128)} %collective-permute-done.1, f32[512,4096]{1,0:T(8,128)} %param.13, s32[]{:T(128)S(6)} %select_n.67, f32[128,8,4,128]{3,2,1,0:T(4,128)S(1)} %bitcast.38), kind=kOutput, calls=%fused_computation.23 | convolution fusion | flops 3222274048 | bytes 12582916 | tf_op jit(solution)/shard_map/dot_general | solution.py:128
  420.3 5.1 fusion.12
  425.5 86.2 %collective-permute-done.2 = f32[1024,1024]{1,0:T(8,128)} collective-permute-done((f32[1024,1024]{1,0:T(8,128)}, f32[1024,1024]{1,0:T(8,128)}, u32[]{:S(2)}, u32[]{:S(2)}) %collective-permute-start.2) | collective-permute-done | bytes 4194336 | tf_op jit(solution)/shard_map/ppermute | solution.py:134
  511.7 7.0 %add_add_fusion = f32[1024,1024]{1,0:T(8,128)} fusion(f32[1024,1024]{1,0:T(8,128)} %collective-permute-done.2, f32[1024,1024]{1,0:T(8,128)S(1)} %fusion.12, f32[1024,1024]{1,0:T(8,128)} %collective-permute-done), kind=kLoop, calls=%fused_computation.21 | loop fusion | flops 2097152 | bytes 16777216 | tf_op jit(solution)/shard_map/add | solution.py:137
  (45 shorter events, 44.6 us)
Async XLA Ops:
  10.0 55.7 %all-to-all-start.1 = ((s32[8,192,1]{1,2,0:T(1,128)}), s32[8,192,1]{1,2,0:T(1,128)S(1)}, u32[]{:S(2)}, u32[]{:S(2)}) async-start(s32[8,192,1]{1,2,0:T(1,128)} %all_to_all.27), calls=%async_computation.1 | async-start | bytes 16384 | tf_op jit(solution)/shard_map/all_to_all | solution.py:92
  30.3 2.2 copy-start.1
  35.0 3.1 copy-start.3
  215.8 74.1 %all-to-all-start = ((f32[1536,4,128]{2,1,0:T(4,128)}), f32[1536,4,128]{2,1,0:T(4,128)}, u32[]{:S(2)}, u32[]{:S(2)}) async-start(f32[1536,4,128]{2,1,0:T(4,128)} %get-tuple-element.24), calls=%async_computation | async-start | bytes 6291456 | tf_op jit(solution)/shard_map/all_to_all | solution.py:106
  252.7 5.7 %copy-start = (f32[4,1024,1024]{1,2,0:T(8,128)}, f32[4,1024,1024]{1,2,0:T(8,128)S(1)}, u32[]{:S(2)}) copy-start(f32[4,1024,1024]{1,2,0:T(8,128)S(1)} %get-tuple-element.36) | copy-start | bytes 50331652
  315.8 74.5 %all-to-all-start.4 = ((f32[1536,4,128]{2,1,0:T(4,128)}), f32[1536,4,128]{2,1,0:T(4,128)S(1)}, u32[]{:S(2)}, u32[]{:S(2)}) async-start(f32[1536,4,128]{2,1,0:T(4,128)} %gather_fusion.4), calls=%async_computation.4 | async-start | bytes 6291456 | tf_op jit(solution)/shard_map/all_to_all | solution.py:109
  390.3 1.7 copy-start.2
  404.0 7.5 %collective-permute-start.1 = (f32[1024,1024]{1,0:T(8,128)}, f32[1024,1024]{1,0:T(8,128)}, u32[]{:S(2)}, u32[]{:S(2)}) collective-permute-start(f32[1024,1024]{1,0:T(8,128)} %fusion.7), channel_id=1, source_target_pairs={{0,1},{1,0},{2,3},{3,2},{4,5},{5,4},{6,7},{7,6},{8,9},{9,8},{10,11... | collective-permute-start | bytes 12582920 | tf_op jit(solution)/shard_map/ppermute | solution.py:132
  410.6 14.8 %collective-permute-start = (f32[1024,1024]{1,0:T(8,128)}, f32[1024,1024]{1,0:T(8,128)}, u32[]{:S(2)}, u32[]{:S(2)}) collective-permute-start(f32[1024,1024]{1,0:T(8,128)} %fusion.10), channel_id=1, source_target_pairs={{0,1},{1,0},{2,3},{3,2},{4,5},{5,4},{6,7},{7,6},{8,9},{9,8},{10,11... | collective-permute-start | bytes 12582920 | tf_op jit(solution)/shard_map/ppermute | solution.py:135
  418.8 92.9 %collective-permute-start.2 = (f32[1024,1024]{1,0:T(8,128)}, f32[1024,1024]{1,0:T(8,128)}, u32[]{:S(2)}, u32[]{:S(2)}) collective-permute-start(f32[1024,1024]{1,0:T(8,128)} %convolution_add_fusion), channel_id=1, source_target_pairs={{0,2},{1,3},{2,0},{3,1},{4,6},{5,7},{6,4},{7,5},{8,10},{9,11},{10,... | collective-permute-start | bytes 12582920 | tf_op jit(solution)/shard_map/ppermute | solution.py:134

commit v5 on v0

--- a/solution.py
+++ b/solution.py
@@ -41,14 +41,14 @@
     query_c, key_c, value_c = triple
     length = query_c.shape[0]
     scores = jnp.einsum(
-        "qhd,khd->hqk", query_c, key_c, precision=lax.Precision.HIGHEST
+        "qhd,khd->hqk", query_c, key_c, precision=lax.Precision.HIGH
     ) / math.sqrt(query_c.shape[-1])
     causal = jnp.arange(length)[:, None] >= jnp.arange(length)[None, :]
     scores = jnp.where(causal[None], scores, -jnp.inf)
     peak = jnp.max(scores, -1, keepdims=True)
     weights = jnp.exp(scores - peak)
     total = jnp.sum(weights, -1, keepdims=True)
-    summed = jnp.einsum("hqk,khd->qhd", weights, value_c, precision=lax.Precision.HIGHEST)
+    summed = jnp.einsum("hqk,khd->qhd", weights, value_c, precision=lax.Precision.HIGH)
     return summed / jnp.transpose(total, (1, 0, 2))
 
 
@@ -100,19 +100,53 @@
     def place(pieces):
         return pieces[where_from]
 
+    far_weights = fetch_far_weights(out_weight)
+    first_arrived = lax.all_to_all(send_q, "seq", split_axis=0, concat_axis=0, tiled=True)
+    first_arrived, far_weights = lax.optimization_barrier((first_arrived, far_weights))
     received = (
-        lax.all_to_all(send_q, "seq", split_axis=0, concat_axis=0, tiled=True),
+        first_arrived,
         lax.all_to_all(send_k, "seq", split_axis=0, concat_axis=0, tiled=True),
         lax.all_to_all(send_v, "seq", split_axis=0, concat_axis=0, tiled=True),
     )
     result = attend_local(place(received[0]), place(received[1]), place(received[2]))
     returned = lax.all_to_all(result[picked], "seq", split_axis=0, concat_axis=0, tiled=True)
     mixed = returned[send_row].reshape(row_count, heads_here * DH)
-    partial_term = jnp.dot(
-        mixed, out_weight, precision=lax.Precision.HIGHEST, preferred_element_type=jnp.float32
+    return project_scatter(mixed, out_weight, far_weights)
+
+
+def swap_pairs(count, bit):
+    return [(index, index ^ bit) for index in range(count)]
+
+
+def weight_block(out_weight, index):
+    width = out_weight.shape[1] // lax.axis_size("head")
+    return lax.dynamic_slice_in_dim(out_weight, index * width, width, axis=1)
+
+
+def fetch_far_weights(out_weight):
+    head_count = lax.axis_size("head")
+    me = lax.axis_index("head")
+    outgoing = jnp.stack(
+        [weight_block(out_weight, me ^ 2), weight_block(out_weight, me ^ 3)], 0
     )
-    projected = lax.psum_scatter(partial_term, "head", scatter_dimension=1, tiled=True)
-    return projected
+    return lax.ppermute(outgoing, "head", swap_pairs(head_count, 2))
+
+
+def project_scatter(mixed, out_weight, far_weights):
+    head_count = lax.axis_size("head")
+    me = lax.axis_index("head")
+
+    def dot(lhs, weight):
+        return jnp.dot(
+            lhs, weight, precision=lax.Precision.HIGH, preferred_element_type=jnp.float32
+        )
+
+    far_mixed = lax.ppermute(mixed, "head", swap_pairs(head_count, 2))
+    near_partner = dot(mixed, weight_block(out_weight, me ^ 1))
+    for_partner = near_partner + dot(far_mixed, far_weights[1])
+    from_partner = lax.ppermute(for_partner, "head", swap_pairs(head_count, 1))
+    own = dot(mixed, weight_block(out_weight, me)) + dot(far_mixed, far_weights[0])
+    return own + from_partner
 
 
 def solution(mesh):

time: 578 us -> 474 us (0.82)
  blocking collectives: 225 us -> 151 us
  matrix products: 67.1 us -> 47.3 us
  waiting for transfers between devices: 146 us -> 132 us
  between operations: 13.8 us -> 0.51 us
  other arithmetic: 22.3 us -> 30.4 us
  starting transfers between devices: 11.7 us -> 18.4 us
    reduce_scatter x1 -> x0, waiting for transfers between devices: 125 us -> none  [per_device(): lax.psum_scatter(partial_term, 'head', scatter_dimension=1, tiled=True)]
    all_to_all x1 -> x0, blocking collectives: 73.7 us -> none  [per_device(): lax.all_to_all(send_k, 'seq', split_axis=0, concat_axis=0, tiled=True)]
    all_to_all x0 -> x1, waiting for transfers between devices: none -> 63.6 us  [per_device(): lax.all_to_all(send_k, 'seq', split_axis=0, concat_axis=0, tiled=True)]
    ppermute x0 -> x3, waiting for transfers between devices: none -> 53.4 us  [the longest x1 39.8 us: project_scatter(): far_mixed = lax.ppermute(mixed, 'head', swap_pairs(head_count, 2))]
    dot_general x3 -> x6, matrix products: 67.1 us -> 47.3 us  [the longest x4 23.9 us: dot(): jnp.dot(lhs, weight, precision=lax.Precision.HIGH, preferred_element_type...]
    all_to_all x1, waiting for transfers between devices: 20.8 us -> 14.7 us  [per_device(): lax.all_to_all(send_v, 'seq', split_axis=0, concat_axis=0, tiled=True)]
  transfers between devices with their start and end apart: 3 -> 6, of which waited for: 2 -> 4; matrix products, arithmetic and copies ran while one was open for 16% -> 22% of each run, Pallas kernels for 0% -> 0%
where the time goes in v5:
time: 474 us; the launch traced here: 471 us
  blocking collectives  151 us (32%)
  waiting for transfers between devices  132 us (28%)
  local copies, waits for them, and re-layouts  91.4 us (19%)
  matrix products  47.3 us (10%)
  other arithmetic  30.4 us (6%)
  starting transfers between devices  18.4 us (4%)
    all_to_all x1, blocking collectives, per_device(): lax.all_to_all(send_q, 'seq', split_axis=0, concat_axis=0, tiled=True)  76.2 us
    all_to_all x1, blocking collectives, per_device(): lax.all_to_all(result[picked], 'seq', split_axis=0, concat_axis=0, tiled=...  74.8 us
    all_to_all x1, waiting for transfers between devices, per_device(): lax.all_to_all(send_k, 'seq', split_axis=0, concat_axis=0, tiled=True)  63.6 us
    ppermute x1, waiting for transfers between devices, project_scatter(): far_mixed = lax.ppermute(mixed, 'head', swap_pairs(head_count, 2))  39.8 us
    dot_general x4, matrix products, dot(): jnp.dot(lhs, weight, precision=lax.Precision.HIGH, preferred_element_type...  23.9 us
    gather x3, local copies, waits for them, and re-layouts, place(): return pieces[where_from]  20.7 us
    all_to_all x1, waiting for transfers between devices, per_device(): lax.all_to_all(send_v, 'seq', split_axis=0, concat_axis=0, tiled=True)  14.7 us
    ppermute x1, waiting for transfers between devices, fetch_far_weights(): return lax.ppermute(outgoing, 'head', swap_pairs(head_count, 2))  13.6 us
  transfers between devices with their start and end apart: 6, of which 4 were waited for; matrix products, arithmetic and copies ran while one was open for 22% of the time, Pallas kernels for 0%

profile of v5, /device:TPU:0, one launch (start us, length us, event | category | flops | bytes accessed | tf_op | source)
XLA Modules:
  0.0 470.7 jit_solution(2325430893239760446)
XLA Ops:
  10.0 7.3 %all-to-all-start.1 = ((s32[8,192,1]{1,2,0:T(1,128)}), s32[8,192,1]{1,2,0:T(1,128)S(1)}, u32[]{:S(2)}, u32[]{:S(2)}) async-start(s32[8,192,1]{1,2,0:T(1,128)} %all_to_all.27), calls=%async_computation.1 | async-start | bytes 16384 | tf_op jit(solution)/shard_map/all_to_all | solution.py:92
  38.1 5.3 %select_maximum_fusion = f32[1025,12,128]{2,1,0:T(8,128)} fusion(f32[1024,4,128]{2,1,0:T(4,128)S(1)} %copy-done.3, f32[1024,4,128]{2,1,0:T(4,128)S(1)} %get-tuple-element.38, f32[1024,4,128]{2,1,0:T(4,128)S(1)} %get-tuple-element.37), kind=kLoop, calls=%fused_computation.14 | loop fusion | flops 9446400 | bytes 12589056 | tf_op jit(solution)/shard_map/concatenate | solution.py:85
  43.4 12.0 %gather_fusion = f32[1536,12,128]{2,1,0:T(8,128)} fusion(f32[1025,12,128]{2,1,0:T(8,128)} %select_maximum_fusion, s32[2048]{0:T(1024)S(1)} %pad_clamp_fusion.1), kind=kCustom, calls=%fused_computation | custom fusion | bytes 18880512 | tf_op jit(solution)/shard_map/gather | solution.py:87
  55.4 10.4 %fusion.40 = (f32[1536,4,128]{2,1,0:T(4,128)}, f32[1536,4,128]{2,1,0:T(4,128)S(1)}, f32[1536,4,128]{2,1,0:T(4,128)}) fusion(f32[1536,12,128]{2,1,0:T(8,128)} %gather_fusion), kind=kLoop, calls=%fused_computation.82 | loop fusion | bytes 18874368 | tf_op jit(solution)/shard_map/slice | solution.py:90
  65.8 76.2 %all_to_all.33 = f32[1536,4,128]{2,1,0:T(4,128)} all-to-all(f32[1536,4,128]{2,1,0:T(4,128)S(1)} %get-tuple-element.29), channel_id=1, replica_groups=mesh['seq'=8,'head'=4] {'seq'}, dimensions={0} | all-to-all | bytes 6291456 | tf_op jit(solution)/shard_map/all_to_all | solution.py:104
  152.0 63.6 %all-to-all-done.3 = f32[1536,4,128]{2,1,0:T(4,128)S(1)} async-done(((f32[1536,4,128]{2,1,0:T(4,128)}), f32[1536,4,128]{2,1,0:T(4,128)S(1)}, u32[]{:S(2)}, u32[]{:S(2)}) %all-to-all-start.3) | async-done | bytes 3145760 | tf_op jit(solution)/shard_map/all_to_all | solution.py:108
  222.3 6.2 %scatter_custom_fusion.2 = s32[1024]{0:T(1024)S(1)} fusion(s32[1536]{0:T(1024)S(1)} %get-tuple-element.25, s32[1536]{0:T(1024)S(1)} %iota.38, s32[]{:T(128)} %constant.92.clone.1), kind=kCustom, calls=%fused_computation.75 | custom fusion | bytes 4100 | tf_op jit(solution)/shard_map/scatter | solution.py:97
  228.5 13.6 %collective-permute-done = f32[2,512,1024]{2,1,0:T(8,128)} collective-permute-done((f32[2,512,1024]{2,1,0:T(8,128)}, f32[2,512,1024]{2,1,0:T(8,128)}, u32[]{:S(2)}, u32[]{:S(2)}) %collective-permute-start) | collective-permute-done | bytes 4194336 | tf_op jit(solution)/shard_map/ppermute | solution.py:132
  242.1 5.4 %gather_fusion.2 = f32[1024,4,128]{2,1,0:T(4,128)S(1)} fusion(f32[1536,4,128]{2,1,0:T(4,128)} %all_to_all.33, s32[1024]{0:T(1024)S(1)} %fusion.29), kind=kCustom, calls=%fused_computation.2 | custom fusion | bytes 4198400 | tf_op jit(solution)/shard_map/gather | solution.py:101
  247.6 9.8 %gather_fusion.3 = f32[1024,4,128]{2,1,0:T(4,128)} fusion(f32[1536,4,128]{2,1,0:T(4,128)} %copy-done.2, s32[1024]{0:T(1024)S(1)} %fusion.29), kind=kCustom, calls=%fused_computation.3 | custom fusion | bytes 4198400 | tf_op jit(solution)/shard_map/gather | solution.py:101
  257.4 10.5 %fusion = (f32[4,1024]{1,0:T(4,128)S(1)}, f32[4,1024,1024]{1,2,0:T(8,128)S(1)}) fusion(pred[1024,1024]{0,1:T(8,128)(4,1)S(1)} %iota_compare_fusion.1, f32[1024,4,128]{2,1,0:T(4,128)} %gather_fusion.3, f32[1024,4,128]{2,1,0:T(4,128)S(1)} %gather_fusion.2), kind=kOutput, calls=%fused_computation.11 | convolution fusion | flops 3233804288 | bytes 22036480 | tf_op jit(solution)/shard_map/while/body/eval_jaxpr/qhd,khd->hqk/dot_general | solution.py:43
  267.9 5.7 %copy-done = f32[4,1024,1024]{1,2,0:T(8,128)} copy-done((f32[4,1024,1024]{1,2,0:T(8,128)}, f32[4,1024,1024]{1,2,0:T(8,128)S(1)}, u32[]{:S(2)}) %copy-start) | copy-done | bytes 16777240
  277.2 14.7 %all-to-all-done = f32[1536,4,128]{2,1,0:T(4,128)} async-done(((f32[1536,4,128]{2,1,0:T(4,128)}), f32[1536,4,128]{2,1,0:T(4,128)}, u32[]{:S(2)}, u32[]{:S(2)}) %all-to-all-start) | async-done | bytes 3145760 | tf_op jit(solution)/shard_map/all_to_all | solution.py:109
  292.0 5.4 %gather_fusion.1 = f32[1024,4,128]{2,1,0:T(4,128)S(1)} fusion(f32[1536,4,128]{2,1,0:T(4,128)} %all-to-all-done, s32[1024]{0:T(1024)S(1)} %fusion.29), kind=kCustom, calls=%fused_computation.1 | custom fusion | bytes 4198400 | tf_op jit(solution)/shard_map/gather | solution.py:101
  297.4 12.9 %bitcast_divide_fusion = f32[1024,4,128]{0,2,1:T(8,128)} fusion(f32[1024,4]{0,1:T(4,128)S(1)} %bitcast.49, f32[4,1024,1024]{1,2,0:T(8,128)} %copy-done, f32[4,1024]{1,0:T(4,128)S(1)} %get-tuple-element.41, pred[1024,1024]{0,1:T(8,128)(4,1)S(1)} %iota_compare_fusion.1, f32[1024,4,128]{2,1,0:T(4,128)S(1)} %gather_fusion.1), kind=kOutput, calls=%fused_computation.35 | convolution fusion | flops 3234332672 | bytes 22052864 | tf_op jit(solution)/shard_map/while/body/eval_jaxpr/hqk,khd->qhd/dot_general | solution.py:51
  312.4 5.5 %gather_fusion.4 = f32[1536,4,128]{2,1,0:T(4,128)} fusion(f32[1024,4,128]{2,1,0:T(4,128)S(1)} %copy.19, s32[2048]{0:T(1024)S(1)} %pad_clamp_fusion), kind=kCustom, calls=%fused_computation.4 | custom fusion | bytes 6297600 | tf_op jit(solution)/shard_map/gather | solution.py:112
  317.8 74.8 %all_to_all.34 = f32[1536,4,128]{2,1,0:T(4,128)} all-to-all(f32[1536,4,128]{2,1,0:T(4,128)} %gather_fusion.4), channel_id=1, replica_groups=mesh['seq'=8,'head'=4] {'seq'}, dimensions={0} | all-to-all | bytes 6291456 | tf_op jit(solution)/shard_map/all_to_all | solution.py:112
  392.6 5.4 %gather_fusion.5 = f32[1024,4,128]{2,1,0:T(4,128)S(1)} fusion(f32[1536,4,128]{2,1,0:T(4,128)} %all_to_all.34, s32[1024]{0:T(1024)S(1)} %get-tuple-element.26), kind=kCustom, calls=%fused_computation.5 | custom fusion | bytes 4198400 | tf_op jit(solution)/shard_map/gather | solution.py:113
  401.0 5.1 %fusion.17 = f32[1024,1024]{1,0:T(8,128)S(1)} fusion(f32[512,4096]{1,0:T(8,128)} %param.13, s32[]{:T(128)S(6)} %select_n.68, f32[128,8,4,128]{3,2,1,0:T(4,128)S(1)} %bitcast.45), kind=kOutput, calls=%fused_computation.41 | convolution fusion | flops 3221225472 | bytes 8388612 | tf_op jit(solution)/shard_map/dot_general | solution.py:140
  406.1 39.8 %collective-permute-done.1 = f32[1024,512]{1,0:T(8,128)} collective-permute-done((f32[1024,512]{1,0:T(8,128)}, f32[1024,512]{1,0:T(8,128)}, u32[]{:S(2)}, u32[]{:S(2)}) %collective-permute-start.1) | collective-permute-done | bytes 2097184 | tf_op jit(solution)/shard_map/ppermute | solution.py:144
  445.9 7.7 %convolution_add_fusion = f32[1024,1024]{1,0:T(8,128)} fusion(f32[1024,1024]{1,0:T(8,128)S(1)} %fusion.17, f32[1024,512]{1,0:T(8,128)} %collective-permute-done.1, f32[2,512,1024]{2,1,0:T(8,128)} %collective-permute-done), kind=kOutput, calls=%fused_computation.24 | convolution fusion | flops 3222274048 | bytes 12582912 | tf_op jit(solution)/shard_map/dot_general | solution.py:140
  453.6 5.1 %fusion.20 = f32[1024,1024]{1,0:T(8,128)S(1)} fusion(f32[512,4096]{1,0:T(8,128)} %param.13, s32[]{:T(128)S(6)} %select_n.67, f32[128,8,4,128]{3,2,1,0:T(4,128)S(1)} %bitcast.46), kind=kOutput, calls=%fused_computation.44 | convolution fusion | flops 3221225472 | bytes 8388612 | tf_op jit(solution)/shard_map/dot_general | solution.py:140
  458.8 6.0 %fusion.10 = f32[1024,1024]{1,0:T(8,128)S(1)} fusion(f32[1024,512]{1,0:T(8,128)} %collective-permute-done.1, f32[2,512,1024]{2,1,0:T(8,128)} %collective-permute-done), kind=kOutput, calls=%fused_computation.33 | convolution fusion | flops 3221225472 | bytes 8388608 | tf_op jit(solution)/shard_map/dot_general | solution.py:140
  464.8 5.7 %add_add_fusion = f32[1024,1024]{1,0:T(8,128)} fusion(f32[1024,1024]{1,0:T(8,128)} %collective-permute-done.2, f32[1024,1024]{1,0:T(8,128)S(1)} %fusion.20, f32[1024,1024]{1,0:T(8,128)S(1)} %fusion.10), kind=kLoop, calls=%fused_computation.22 | loop fusion | flops 2097152 | bytes 16777216 | tf_op jit(solution)/shard_map/add | solution.py:149
  (48 shorter events, 56.1 us)
Async XLA Ops:
  10.0 55.8 %all-to-all-start.1 = ((s32[8,192,1]{1,2,0:T(1,128)}), s32[8,192,1]{1,2,0:T(1,128)S(1)}, u32[]{:S(2)}, u32[]{:S(2)}) async-start(s32[8,192,1]{1,2,0:T(1,128)} %all_to_all.27), calls=%async_computation.1 | async-start | bytes 16384 | tf_op jit(solution)/shard_map/all_to_all | solution.py:92
  30.3 2.2 copy-start.1
  35.0 3.1 copy-start.3
  142.0 73.7 %all-to-all-start.3 = ((f32[1536,4,128]{2,1,0:T(4,128)}), f32[1536,4,128]{2,1,0:T(4,128)S(1)}, u32[]{:S(2)}, u32[]{:S(2)}) async-start(f32[1536,4,128]{2,1,0:T(4,128)} %get-tuple-element.30), calls=%async_computation.3 | async-start | bytes 6291456 | tf_op jit(solution)/shard_map/all_to_all | solution.py:108
  150.5 91.6 %collective-permute-start = (f32[2,512,1024]{2,1,0:T(8,128)}, f32[2,512,1024]{2,1,0:T(8,128)}, u32[]{:S(2)}, u32[]{:S(2)}) collective-permute-start(f32[2,512,1024]{2,1,0:T(8,128)} %pad_maximum_fusion), channel_id=1, source_target_pairs={{0,2},{1,3},{2,0},{3,1},{4,6},{5,7},{6,4},{7,5},{8,10},{9,11},{10,... | collective-permute-start | bytes 12582920 | tf_op jit(solution)/shard_map/ppermute | solution.py:132
  215.6 1.7 copy-start.2
  217.3 74.6 %all-to-all-start = ((f32[1536,4,128]{2,1,0:T(4,128)}), f32[1536,4,128]{2,1,0:T(4,128)}, u32[]{:S(2)}, u32[]{:S(2)}) async-start(f32[1536,4,128]{2,1,0:T(4,128)} %get-tuple-element.28), calls=%async_computation | async-start | bytes 6291456 | tf_op jit(solution)/shard_map/all_to_all | solution.py:109
  267.9 5.7 %copy-start = (f32[4,1024,1024]{1,2,0:T(8,128)}, f32[4,1024,1024]{1,2,0:T(8,128)S(1)}, u32[]{:S(2)}) copy-start(f32[4,1024,1024]{1,2,0:T(8,128)S(1)} %get-tuple-element.42) | copy-start | bytes 50331652
  399.5 46.4 %collective-permute-start.1 = (f32[1024,512]{1,0:T(8,128)}, f32[1024,512]{1,0:T(8,128)}, u32[]{:S(2)}, u32[]{:S(2)}) collective-permute-start(f32[1024,512]{1,0:T(8,128)} %bitcast.39), channel_id=1, source_target_pairs={{0,2},{1,3},{2,0},{3,1},{4,6},{5,7},{6,4},{7,5},{8,10},{9,11},{10,... | collective-permute-start | bytes 6291464 | tf_op jit(solution)/shard_map/ppermute | solution.py:144
  453.6 11.2 %collective-permute-start.2 = (f32[1024,1024]{1,0:T(8,128)}, f32[1024,1024]{1,0:T(8,128)}, u32[]{:S(2)}, u32[]{:S(2)}) collective-permute-start(f32[1024,1024]{1,0:T(8,128)} %convolution_add_fusion), channel_id=1, source_target_pairs={{0,1},{1,0},{2,3},{3,2},{4,5},{5,4},{6,7},{7,6},{8,9},{9,8},{10,11... | collective-permute-start | bytes 12582920 | tf_op jit(solution)/shard_map/ppermute | solution.py:147

commit v6 on v5

--- a/solution.py
+++ b/solution.py
@@ -82,12 +82,10 @@
     shaped = (row_count, heads_here, DH)
     rot_q = rotate(queries.reshape(shaped), cos_table, sin_table)
     rot_k = rotate(keys.reshape(shaped), cos_table, sin_table)
-    stacked = jnp.concatenate([rot_q, rot_k, values.reshape(shaped)], 1)
-    stacked = jnp.concatenate([stacked, jnp.zeros((1, 3 * heads_here, DH), jnp.float32)], 0)
-    send_all = stacked[source_token]
-    send_q = send_all[:, :heads_here]
-    send_k = send_all[:, heads_here : 2 * heads_here]
-    send_v = send_all[:, 2 * heads_here :]
+    send_from = jnp.minimum(source_token, row_count - 1)
+    send_q = rot_q[send_from]
+    send_k = rot_k[send_from]
+    send_v = values.reshape(shaped)[send_from]
     slot_rows = jnp.full((buffer_rows,), row_count, jnp.int32).at[send_row].set(target_row)
     arrived = lax.all_to_all(slot_rows, "seq", split_axis=0, concat_axis=0, tiled=True)
     picked = jnp.minimum(arrived, row_count - 1)
@@ -109,9 +107,13 @@
         lax.all_to_all(send_v, "seq", split_axis=0, concat_axis=0, tiled=True),
     )
     result = attend_local(place(received[0]), place(received[1]), place(received[2]))
-    returned = lax.all_to_all(result[picked], "seq", split_axis=0, concat_axis=0, tiled=True)
-    mixed = returned[send_row].reshape(row_count, heads_here * DH)
-    return project_scatter(mixed, out_weight, far_weights)
+    outgoing = result[picked]
+    split = heads_here // 2
+    mixed_parts = []
+    for lo, hi in ((0, split), (split, heads_here)):
+        back = lax.all_to_all(outgoing[:, lo:hi], "seq", split_axis=0, concat_axis=0, tiled=True)
+        mixed_parts.append((back[send_row].reshape(row_count, (hi - lo) * DH), lo * DH, hi * DH))
+    return project_scatter(mixed_parts, out_weight, far_weights)
 
 
 def swap_pairs(count, bit):
@@ -132,20 +134,25 @@
     return lax.ppermute(outgoing, "head", swap_pairs(head_count, 2))
 
 
-def project_scatter(mixed, out_weight, far_weights):
+def project_scatter(mixed_parts, out_weight, far_weights):
     head_count = lax.axis_size("head")
     me = lax.axis_index("head")
+    partner_w = weight_block(out_weight, me ^ 1)
+    own_w = weight_block(out_weight, me)
 
     def dot(lhs, weight):
         return jnp.dot(
             lhs, weight, precision=lax.Precision.HIGH, preferred_element_type=jnp.float32
         )
 
-    far_mixed = lax.ppermute(mixed, "head", swap_pairs(head_count, 2))
-    near_partner = dot(mixed, weight_block(out_weight, me ^ 1))
-    for_partner = near_partner + dot(far_mixed, far_weights[1])
+    for_partner = 0.0
+    own = 0.0
+    for mixed, lo, hi in mixed_parts:
+        far_mixed = lax.ppermute(mixed, "head", swap_pairs(head_count, 2))
+        for_partner = for_partner + dot(mixed, partner_w[lo:hi])
+        for_partner = for_partner + dot(far_mixed, far_weights[1, lo:hi])
+        own = own + dot(mixed, own_w[lo:hi]) + dot(far_mixed, far_weights[0, lo:hi])
     from_partner = lax.ppermute(for_partner, "head", swap_pairs(head_count, 1))
-    own = dot(mixed, weight_block(out_weight, me)) + dot(far_mixed, far_weights[0])
     return own + from_partner
 
 

time: 474 us -> 453 us (0.956)
  blocking collectives: 151 us -> 40.5 us
  waiting for transfers between devices: 132 us -> 191 us
  starting transfers between devices: 18.4 us -> 31.7 us
  matrix products: 47.3 us -> 59.7 us
    all_to_all x2 -> x1, blocking collectives: 151 us -> 40.5 us  [per_device(): lax.all_to_all(outgoing[:, lo:hi], 'seq', split_axis=0, concat_axis=0, ti...]
    all_to_all x0 -> x2, waiting for transfers between devices: none -> 94.7 us  [the longest x1 64.6 us: per_device(): lax.all_to_all(send_q, 'seq', split_axis=0, concat_axis=0, tiled=True)]
    ppermute x1 -> x2, waiting for transfers between devices: 39.8 us -> 11.6 us  [project_scatter(): far_mixed = lax.ppermute(mixed, 'head', swap_pairs(head_count, 2))]
    dot_general x4 -> x8, matrix products: 23.9 us -> 36.2 us  [dot(): jnp.dot(lhs, weight, precision=lax.Precision.HIGH, preferred_element_type...]
    all_to_all x0 -> x2, starting transfers between devices: none -> 10.4 us  [the longest x1 6.13 us: per_device(): lax.all_to_all(send_q, 'seq', split_axis=0, concat_axis=0, tiled=True)]
    gather x3 -> x6, local copies, waits for them, and re-layouts: 22.9 us -> 31.9 us  [the longest x2 8.72 us: per_device(): back[send_row].reshape(row_count, (hi - lo) * DH)]
    all_to_all x1, waiting for transfers between devices: 63.6 us -> 56.3 us  [per_device(): lax.all_to_all(send_k, 'seq', split_axis=0, concat_axis=0, tiled=True)]
    concatenate x1 -> x0, other arithmetic: 5.28 us -> none  [per_device(): stacked = jnp.concatenate([rot_q, rot_k, values.reshape(shaped)], 1)]
  transfers between devices with their start and end apart: 6 -> 9, of which waited for: 4 -> 6; matrix products, arithmetic and copies ran while one was open for 22% -> 27% of each run, Pallas kernels for 0% -> 0%
where the time goes in v6:
time: 453 us; the launch traced here: 448 us
  waiting for transfers between devices  191 us (42%)
  local copies, waits for them, and re-layouts  92.3 us (20%)
  matrix products  59.7 us (13%)
  blocking collectives  40.5 us (9%)
  other arithmetic  32.7 us (7%)
  starting transfers between devices  31.7 us (7%)
    all_to_all x1, waiting for transfers between devices, per_device(): lax.all_to_all(send_q, 'seq', split_axis=0, concat_axis=0, tiled=True)  64.6 us
    all_to_all x1, waiting for transfers between devices, per_device(): lax.all_to_all(send_k, 'seq', split_axis=0, concat_axis=0, tiled=True)  56.3 us
    all_to_all x1, blocking collectives, per_device(): lax.all_to_all(outgoing[:, lo:hi], 'seq', split_axis=0, concat_axis=0, ti...  40.5 us
    dot_general x8, matrix products, dot(): jnp.dot(lhs, weight, precision=lax.Precision.HIGH, preferred_element_type...  36.2 us
    all_to_all x1, waiting for transfers between devices, per_device(): lax.all_to_all(outgoing[:, lo:hi], 'seq', split_axis=0, concat_axis=0, ti...  30.1 us
    gather x3, local copies, waits for them, and re-layouts, place(): return pieces[where_from]  20.6 us
    ppermute x1, waiting for transfers between devices, fetch_far_weights(): return lax.ppermute(outgoing, 'head', swap_pairs(head_count, 2))  15.3 us
    all_to_all x1, waiting for transfers between devices, per_device(): lax.all_to_all(send_v, 'seq', split_axis=0, concat_axis=0, tiled=True)  13.1 us
  transfers between devices with their start and end apart: 9, of which 6 were waited for; matrix products, arithmetic and copies ran while one was open for 27% of the time, Pallas kernels for 0%

profile of v6, /device:TPU:0, one launch (start us, length us, event | category | flops | bytes accessed | tf_op | source)
XLA Modules:
  0.0 448.4 jit_solution(3371589006255824643)
XLA Ops:
  10.0 7.3 %all-to-all-start.1 = ((s32[8,192,1]{1,2,0:T(1,128)}), s32[8,192,1]{1,2,0:T(1,128)S(1)}, u32[]{:S(2)}, u32[]{:S(2)}) async-start(s32[8,192,1]{1,2,0:T(1,128)} %all_to_all.31), calls=%async_computation.1 | async-start | bytes 16384 | tf_op jit(solution)/shard_map/all_to_all | solution.py:90
  38.2 6.6 %gather_fusion.2 = f32[1536,4,128]{2,1,0:T(4,128)} fusion(f32[1024,4,128]{2,1,0:T(4,128)} %get-tuple-element.36, s32[2048]{0:T(1024)S(1)} %pad_clamp_fusion.1), kind=kCustom, calls=%fused_computation.2 | custom fusion | bytes 6297600 | tf_op jit(solution)/shard_map/gather | solution.py:86
  44.7 6.1 %all-to-all-start.2 = ((f32[1536,4,128]{2,1,0:T(4,128)}), f32[1536,4,128]{2,1,0:T(4,128)}, u32[]{:S(2)}, u32[]{:S(2)}) async-start(f32[1536,4,128]{2,1,0:T(4,128)} %gather_fusion.2), calls=%async_computation.2 | async-start | bytes 6291456 | tf_op jit(solution)/shard_map/all_to_all | solution.py:102
  50.9 5.6 %gather_fusion.4 = f32[1536,4,128]{2,1,0:T(4,128)} fusion(f32[1024,4,128]{2,1,0:T(4,128)S(1)} %copy-done.3, s32[2048]{0:T(1024)S(1)} %pad_clamp_fusion.1), kind=kCustom, calls=%fused_computation.4 | custom fusion | bytes 6297600 | tf_op jit(solution)/shard_map/gather | solution.py:87
  56.5 64.6 %all-to-all-done.2 = f32[1536,4,128]{2,1,0:T(4,128)} async-done(((f32[1536,4,128]{2,1,0:T(4,128)}), f32[1536,4,128]{2,1,0:T(4,128)}, u32[]{:S(2)}, u32[]{:S(2)}) %all-to-all-start.2) | async-done | bytes 3145760 | tf_op jit(solution)/shard_map/all_to_all | solution.py:102
  134.4 5.6 %gather_fusion = f32[1536,4,128]{2,1,0:T(4,128)} fusion(f32[1024,4,128]{2,1,0:T(4,128)S(1)} %reshape.174, s32[2048]{0:T(1024)S(1)} %pad_clamp_fusion.1), kind=kCustom, calls=%fused_computation | custom fusion | bytes 6297600 | tf_op jit(solution)/shard_map/gather | solution.py:88
  140.0 56.3 %all-to-all-done.3 = f32[1536,4,128]{2,1,0:T(4,128)} async-done(((f32[1536,4,128]{2,1,0:T(4,128)}), f32[1536,4,128]{2,1,0:T(4,128)}, u32[]{:S(2)}, u32[]{:S(2)}) %all-to-all-start.3) | async-done | bytes 3145760 | tf_op jit(solution)/shard_map/all_to_all | solution.py:106
  201.2 6.2 %scatter_custom_fusion.2 = s32[1024]{0:T(1024)S(1)} fusion(s32[1536]{0:T(1024)S(1)} %get-tuple-element.25, s32[1536]{0:T(1024)S(1)} %iota.37, s32[]{:T(128)} %constant.52.clone.1), kind=kCustom, calls=%fused_computation.86 | custom fusion | bytes 4100 | tf_op jit(solution)/shard_map/scatter | solution.py:95
  207.4 15.3 %collective-permute-done = f32[2,512,1024]{2,1,0:T(8,128)} collective-permute-done((f32[2,512,1024]{2,1,0:T(8,128)}, f32[2,512,1024]{2,1,0:T(8,128)}, u32[]{:S(2)}, u32[]{:S(2)}) %collective-permute-start) | collective-permute-done | bytes 4194336 | tf_op jit(solution)/shard_map/ppermute | solution.py:134
  222.7 5.4 %gather_fusion.3 = f32[1024,4,128]{2,1,0:T(4,128)S(1)} fusion(f32[1536,4,128]{2,1,0:T(4,128)} %all-to-all-done.2, s32[1024]{0:T(1024)S(1)} %fusion.39), kind=kCustom, calls=%fused_computation.3 | custom fusion | bytes 4198400 | tf_op jit(solution)/shard_map/gather | solution.py:99
  228.2 9.8 %gather_fusion.5 = f32[1024,4,128]{2,1,0:T(4,128)} fusion(f32[1536,4,128]{2,1,0:T(4,128)} %all-to-all-done.3, s32[1024]{0:T(1024)S(1)} %fusion.39), kind=kCustom, calls=%fused_computation.5 | custom fusion | bytes 4198400 | tf_op jit(solution)/shard_map/gather | solution.py:99
  238.0 10.5 %fusion = (f32[4,1024]{1,0:T(4,128)S(1)}, f32[4,1024,1024]{1,2,0:T(8,128)S(1)}) fusion(pred[1024,1024]{0,1:T(8,128)(4,1)S(1)} %iota_compare_fusion, f32[1024,4,128]{2,1,0:T(4,128)} %gather_fusion.5, f32[1024,4,128]{2,1,0:T(4,128)S(1)} %gather_fusion.3), kind=kOutput, calls=%fused_computation.14 | convolution fusion | flops 3233804288 | bytes 22036480 | tf_op jit(solution)/shard_map/while/body/eval_jaxpr/qhd,khd->hqk/dot_general | solution.py:43
  248.5 5.7 %copy-done = f32[4,1024,1024]{1,2,0:T(8,128)} copy-done((f32[4,1024,1024]{1,2,0:T(8,128)}, f32[4,1024,1024]{1,2,0:T(8,128)S(1)}, u32[]{:S(2)}) %copy-start) | copy-done | bytes 16777240
  257.8 13.1 %all-to-all-done = f32[1536,4,128]{2,1,0:T(4,128)} async-done(((f32[1536,4,128]{2,1,0:T(4,128)}), f32[1536,4,128]{2,1,0:T(4,128)}, u32[]{:S(2)}, u32[]{:S(2)}) %all-to-all-start) | async-done | bytes 3145760 | tf_op jit(solution)/shard_map/all_to_all | solution.py:107
  270.9 5.4 %gather_fusion.1 = f32[1024,4,128]{2,1,0:T(4,128)S(1)} fusion(f32[1536,4,128]{2,1,0:T(4,128)} %all-to-all-done, s32[1024]{0:T(1024)S(1)} %fusion.39), kind=kCustom, calls=%fused_computation.1 | custom fusion | bytes 4198400 | tf_op jit(solution)/shard_map/gather | solution.py:99
  276.3 12.9 %bitcast_divide_fusion = f32[1024,4,128]{0,2,1:T(8,128)} fusion(f32[1024,4]{0,1:T(4,128)S(1)} %bitcast.64, f32[4,1024,1024]{1,2,0:T(8,128)} %copy-done, f32[4,1024]{1,0:T(4,128)S(1)} %get-tuple-element.40, pred[1024,1024]{0,1:T(8,128)(4,1)S(1)} %iota_compare_fusion, f32[1024,4,128]{2,1,0:T(4,128)S(1)} %gather_fusion.1), kind=kOutput, calls=%fused_computation.31 | convolution fusion | flops 3234332672 | bytes 22052864 | tf_op jit(solution)/shard_map/while/body/eval_jaxpr/hqk,khd->qhd/dot_general | solution.py:51
  291.3 5.5 %gather_fusion.6 = f32[1536,4,128]{2,1,0:T(4,128)} fusion(f32[1024,4,128]{2,1,0:T(4,128)S(1)} %copy.19, s32[2048]{0:T(1024)S(1)} %pad_clamp_fusion), kind=kCustom, calls=%fused_computation.6 | custom fusion | bytes 6297600 | tf_op jit(solution)/shard_map/gather | solution.py:110
  296.8 5.2 %fusion.50 = (f32[1536,2,128]{2,1,0:T(2,128)S(1)}, f32[1536,2,128]{2,1,0:T(2,128)}) fusion(f32[1536,4,128]{2,1,0:T(4,128)} %gather_fusion.6), kind=kLoop, calls=%fused_computation.93 | loop fusion | bytes 6291456 | tf_op jit(solution)/shard_map/slice | solution.py:114
  302.0 40.5 %all_to_all.38 = f32[1536,2,128]{2,1,0:T(2,128)S(1)} all-to-all(f32[1536,2,128]{2,1,0:T(2,128)S(1)} %get-tuple-element.30), channel_id=1, replica_groups=mesh['seq'=8,'head'=4] {'seq'}, dimensions={0} | all-to-all | bytes 3145728 | tf_op jit(solution)/shard_map/all_to_all | solution.py:114
  352.9 30.1 %all-to-all-done.5 = f32[1536,2,128]{2,1,0:T(2,128)} async-done(((f32[1536,2,128]{2,1,0:T(2,128)}), f32[1536,2,128]{2,1,0:T(2,128)}, u32[]{:S(2)}, u32[]{:S(2)}) %all-to-all-start.5) | async-done | bytes 1572896 | tf_op jit(solution)/shard_map/all_to_all | solution.py:114
  399.5 11.5 %collective-permute-done.2 = f32[1024,256]{1,0:T(8,128)S(1)} collective-permute-done((f32[1024,256]{1,0:T(8,128)S(1)}, f32[1024,256]{1,0:T(8,128)S(1)}, u32[]{:S(2)}, u32[]{:S(2)}) %collective-permute-start.2) | collective-permute-done | bytes 1048608 | tf_op jit(solution)/shard_map/ppermute | solution.py:151
  411.0 5.9 %add_add_fusion = f32[1024,1024]{1,0:T(8,128)} fusion(f32[1024,1024]{1,0:T(8,128)S(1)} %fusion.13, f32[1024,1024]{1,0:T(8,128)S(1)} %fusion.15, f32[1024,1024]{1,0:T(8,128)S(1)} %fusion.22, f32[1024,256]{1,0:T(8,128)S(1)} %collective-permute-done.2, f32[2,512,1024]{2,1,0:T(8,128)} %collective-permute-done), kind=kOutput, calls=%fused_computation.22 | convolution fusion | flops 1613758464 | bytes 18874368 | tf_op jit(solution)/shard_map/dot_general | solution.py:144
  427.0 5.6 %fusion.26 = f32[1024,1024]{1,0:T(8,128)} fusion(f32[1024,256]{1,0:T(8,128)} %collective-permute-done.1, f32[2,512,1024]{2,1,0:T(8,128)} %collective-permute-done), kind=kOutput, calls=%fused_computation.53 | convolution fusion | flops 1610612736 | bytes 6291456 | tf_op jit(solution)/shard_map/dot_general | solution.py:144
  437.7 10.4 %add_add_fusion.1 = f32[1024,1024]{1,0:T(8,128)} fusion(f32[1024,1024]{1,0:T(8,128)} %collective-permute-done.3, f32[1024,1024]{1,0:T(8,128)} %fusion.24, f32[1024,1024]{1,0:T(8,128)} %fusion.17, f32[1024,1024]{1,0:T(8,128)S(1)} %copy-done.2, f32[1024,1024]{1,0:T(8,128)} %fusion.26), kind=kLoop, calls=%fused_computation.23 | loop fusion | flops 4194304 | bytes 25165824 | tf_op jit(solution)/shard_map/add | solution.py:156
  (62 shorter events, 96.6 us)
Async XLA Ops:
  10.0 34.7 %all-to-all-start.1 = ((s32[8,192,1]{1,2,0:T(1,128)}), s32[8,192,1]{1,2,0:T(1,128)S(1)}, u32[]{:S(2)}, u32[]{:S(2)}) async-start(s32[8,192,1]{1,2,0:T(1,128)} %all_to_all.31), calls=%async_computation.1 | async-start | bytes 16384 | tf_op jit(solution)/shard_map/all_to_all | solution.py:90
  17.3 4.8 %copy-start.4 = (s32[1024]{0:T(1024)S(1)}, s32[1024]{0:T(1024)}, u32[]{:S(2)}) copy-start(s32[1024]{0:T(1024)} %param.10) | copy-start | bytes 12292
  31.4 2.2 copy-start.1
  44.7 6.1 %copy-start.3 = (f32[1024,4,128]{2,1,0:T(4,128)S(1)}, f32[1024,4,128]{2,1,0:T(4,128)}, u32[]{:S(2)}) copy-start(f32[1024,4,128]{2,1,0:T(4,128)} %get-tuple-element.37) | copy-start | bytes 6291460
  44.7 76.4 %all-to-all-start.2 = ((f32[1536,4,128]{2,1,0:T(4,128)}), f32[1536,4,128]{2,1,0:T(4,128)}, u32[]{:S(2)}, u32[]{:S(2)}) async-start(f32[1536,4,128]{2,1,0:T(4,128)} %gather_fusion.2), calls=%async_computation.2 | async-start | bytes 6291456 | tf_op jit(solution)/shard_map/all_to_all | solution.py:102
  121.1 75.2 %all-to-all-start.3 = ((f32[1536,4,128]{2,1,0:T(4,128)}), f32[1536,4,128]{2,1,0:T(4,128)}, u32[]{:S(2)}, u32[]{:S(2)}) async-start(f32[1536,4,128]{2,1,0:T(4,128)} %gather_fusion.4), calls=%async_computation.3 | async-start | bytes 6291456 | tf_op jit(solution)/shard_map/all_to_all | solution.py:106
  131.0 91.8 %collective-permute-start = (f32[2,512,1024]{2,1,0:T(8,128)}, f32[2,512,1024]{2,1,0:T(8,128)}, u32[]{:S(2)}, u32[]{:S(2)}) collective-permute-start(f32[2,512,1024]{2,1,0:T(8,128)} %pad_maximum_fusion), channel_id=1, source_target_pairs={{0,2},{1,3},{2,0},{3,1},{4,6},{5,7},{6,4},{7,5},{8,10},{9,11},{10,... | collective-permute-start | bytes 12582920 | tf_op jit(solution)/shard_map/ppermute | solution.py:134
  196.3 74.6 %all-to-all-start = ((f32[1536,4,128]{2,1,0:T(4,128)}), f32[1536,4,128]{2,1,0:T(4,128)}, u32[]{:S(2)}, u32[]{:S(2)}) async-start(f32[1536,4,128]{2,1,0:T(4,128)} %gather_fusion), calls=%async_computation | async-start | bytes 6291456 | tf_op jit(solution)/shard_map/all_to_all | solution.py:107
  248.5 5.7 %copy-start = (f32[4,1024,1024]{1,2,0:T(8,128)}, f32[4,1024,1024]{1,2,0:T(8,128)S(1)}, u32[]{:S(2)}) copy-start(f32[4,1024,1024]{1,2,0:T(8,128)S(1)} %get-tuple-element.41) | copy-start | bytes 50331652
  342.5 40.5 %all-to-all-start.5 = ((f32[1536,2,128]{2,1,0:T(2,128)}), f32[1536,2,128]{2,1,0:T(2,128)}, u32[]{:S(2)}, u32[]{:S(2)}) async-start(f32[1536,2,128]{2,1,0:T(2,128)} %get-tuple-element.31), calls=%async_computation.5 | async-start | bytes 3145728 | tf_op jit(solution)/shard_map/all_to_all | solution.py:114
  351.4 44.6 %collective-permute-start.1 = (f32[1024,256]{1,0:T(8,128)}, f32[1024,256]{1,0:T(8,128)}, u32[]{:S(2)}, u32[]{:S(2)}) collective-permute-start(f32[1024,256]{1,0:T(8,128)} %bitcast.53), channel_id=1, source_target_pairs={{0,2},{1,3},{2,0},{3,1},{4,6},{5,7},{6,4},{7,5},{8,10},{9,11},{10,... | collective-permute-start | bytes 3145736 | tf_op jit(solution)/shard_map/ppermute | solution.py:151
  388.3 22.7 %collective-permute-start.2 = (f32[1024,256]{1,0:T(8,128)S(1)}, f32[1024,256]{1,0:T(8,128)S(1)}, u32[]{:S(2)}, u32[]{:S(2)}) collective-permute-start(f32[1024,256]{1,0:T(8,128)S(1)} %bitcast.61), channel_id=1, source_target_pairs={{0,2},{1,3},{2,0},{3,1},{4,6},{5,7},{6,4},{7,5},{8,10},{9,11},{10,... | collective-permute-start | bytes 3145736 | tf_op jit(solution)/shard_map/ppermute | solution.py:151
  417.0 20.7 %collective-permute-start.3 = (f32[1024,1024]{1,0:T(8,128)}, f32[1024,1024]{1,0:T(8,128)}, u32[]{:S(2)}, u32[]{:S(2)}) collective-permute-start(f32[1024,1024]{1,0:T(8,128)} %add_add_fusion), channel_id=1, source_target_pairs={{0,1},{1,0},{2,3},{3,2},{4,5},{5,4},{6,7},{7,6},{8,9},{9,8},{10,11... | collective-permute-start | bytes 12582920 | tf_op jit(solution)/shard_map/ppermute | solution.py:155
  432.6 5.2 %copy-start.2 = (f32[1024,1024]{1,0:T(8,128)S(1)}, f32[1024,1024]{1,0:T(8,128)}, u32[]{:S(2)}) copy-start(f32[1024,1024]{1,0:T(8,128)} %fusion.19) | copy-start | bytes 12582916

commit v7 on v6

--- a/solution.py
+++ b/solution.py
@@ -99,19 +99,16 @@
         return pieces[where_from]
 
     far_weights = fetch_far_weights(out_weight)
-    first_arrived = lax.all_to_all(send_q, "seq", split_axis=0, concat_axis=0, tiled=True)
-    first_arrived, far_weights = lax.optimization_barrier((first_arrived, far_weights))
-    received = (
-        first_arrived,
-        lax.all_to_all(send_k, "seq", split_axis=0, concat_axis=0, tiled=True),
-        lax.all_to_all(send_v, "seq", split_axis=0, concat_axis=0, tiled=True),
-    )
-    result = attend_local(place(received[0]), place(received[1]), place(received[2]))
-    outgoing = result[picked]
+    arrived_v = lax.all_to_all(send_v, "seq", split_axis=0, concat_axis=0, tiled=True)
+    arrived_v, far_weights = lax.optimization_barrier((arrived_v, far_weights))
+    arrived_q = lax.all_to_all(send_q, "seq", split_axis=0, concat_axis=0, tiled=True)
+    arrived_k = lax.all_to_all(send_k, "seq", split_axis=0, concat_axis=0, tiled=True)
+    placed = (place(arrived_q), place(arrived_k), place(arrived_v))
     split = heads_here // 2
     mixed_parts = []
     for lo, hi in ((0, split), (split, heads_here)):
-        back = lax.all_to_all(outgoing[:, lo:hi], "seq", split_axis=0, concat_axis=0, tiled=True)
+        result = attend_local(*(piece[:, lo:hi] for piece in placed))
+        back = lax.all_to_all(result[picked], "seq", split_axis=0, concat_axis=0, tiled=True)
         mixed_parts.append((back[send_row].reshape(row_count, (hi - lo) * DH), lo * DH, hi * DH))
     return project_scatter(mixed_parts, out_weight, far_weights)
 
@@ -145,14 +142,19 @@
             lhs, weight, precision=lax.Precision.HIGH, preferred_element_type=jnp.float32
         )
 
-    for_partner = 0.0
-    own = 0.0
+    terms_partner = []
+    terms_own = []
     for mixed, lo, hi in mixed_parts:
         far_mixed = lax.ppermute(mixed, "head", swap_pairs(head_count, 2))
-        for_partner = for_partner + dot(mixed, partner_w[lo:hi])
-        for_partner = for_partner + dot(far_mixed, far_weights[1, lo:hi])
-        own = own + dot(mixed, own_w[lo:hi]) + dot(far_mixed, far_weights[0, lo:hi])
+        terms_partner += [(mixed, partner_w[lo:hi]), (far_mixed, far_weights[1, lo:hi])]
+        terms_own += [(mixed, own_w[lo:hi]), (far_mixed, far_weights[0, lo:hi])]
+    for_partner = dot(*terms_partner[0])
+    for term in terms_partner[1:]:
+        for_partner = for_partner + dot(*term)
     from_partner = lax.ppermute(for_partner, "head", swap_pairs(head_count, 1))
+    own = dot(*terms_own[0])
+    for term in terms_own[1:]:
+        own = own + dot(*term)
     return own + from_partner
 
 

time: 453 us -> 479 us (1.057)
  waiting for transfers between devices: 191 us -> 246 us
  blocking collectives: 40.5 us -> 0 us
  starting transfers between devices: 31.7 us -> 36.9 us
    ppermute x1, waiting for transfers between devices: 15.3 us -> 61.2 us  [fetch_far_weights(): return lax.ppermute(outgoing, 'head', swap_pairs(head_count, 2))]
    all_to_all x1 -> x0, blocking collectives: 40.5 us -> none  [per_device(): lax.all_to_all(outgoing[:, lo:hi], 'seq', split_axis=0, concat_axis=0, ti...]
    all_to_all x1 -> x2, waiting for transfers between devices: 30.1 us -> 45.4 us  [per_device(): lax.all_to_all(result[picked], 'seq', split_axis=0, concat_axis=0, tiled=...]
    all_to_all x1, waiting for transfers between devices: 13.1 us -> 0.01 us  [per_device(): lax.all_to_all(send_v, 'seq', split_axis=0, concat_axis=0, tiled=True)]
    all_to_all x1, waiting for transfers between devices: 56.3 us -> 62.7 us  [per_device(): lax.all_to_all(send_k, 'seq', split_axis=0, concat_axis=0, tiled=True)]
    all_to_all x1 -> x2, starting transfers between devices: 4.29 us -> 10 us  [per_device(): lax.all_to_all(result[picked], 'seq', split_axis=0, concat_axis=0, tiled=...]
    unnamed x12 -> x20, local copies, waits for them, and re-layouts: 6.83 us -> 1.23 us
    gather x1 -> x2, local copies, waits for them, and re-layouts: 5.49 us -> 10.4 us  [per_device(): result[picked]]
  transfers between devices with their start and end apart: 9 -> 10, of which waited for: 6 -> 6; matrix products, arithmetic and copies ran while one was open for 27% -> 28% of each run, Pallas kernels for 0% -> 0%
where the time goes in v7:
time: 479 us; the launch traced here: 475 us
  waiting for transfers between devices  246 us (51%)
  local copies, waits for them, and re-layouts  95.1 us (20%)
  matrix products  62.9 us (13%)
  starting transfers between devices  36.9 us (8%)
  other arithmetic  33.5 us (7%)
    all_to_all x1, waiting for transfers between devices, per_device(): lax.all_to_all(send_q, 'seq', split_axis=0, concat_axis=0, tiled=True)  64.8 us
    all_to_all x1, waiting for transfers between devices, per_device(): lax.all_to_all(send_k, 'seq', split_axis=0, concat_axis=0, tiled=True)  62.7 us
    ppermute x1, waiting for transfers between devices, fetch_far_weights(): return lax.ppermute(outgoing, 'head', swap_pairs(head_count, 2))  61.2 us
    all_to_all x2, waiting for transfers between devices, per_device(): lax.all_to_all(result[picked], 'seq', split_axis=0, concat_axis=0, tiled=...  45.4 us
    dot_general x8, matrix products, dot(): jnp.dot(lhs, weight, precision=lax.Precision.HIGH, preferred_element_type...  36.2 us
    gather x3, local copies, waits for them, and re-layouts, place(): return pieces[where_from]  20.7 us
    dot_general x2, matrix products, cluster_attention(): jnp.einsum('qhd,khd->hqk', query_c, key_c, precision=lax.Precision.HIGH)  13.6 us
    dot_general x2, matrix products, cluster_attention(): jnp.einsum('hqk,khd->qhd', weights, value_c, precision=lax.Precision.HIGH)  13.1 us
  transfers between devices with their start and end apart: 10, of which 6 were waited for; matrix products, arithmetic and copies ran while one was open for 28% of the time, Pallas kernels for 0%

profile of v7, /device:TPU:0, one launch (start us, length us, event | category | flops | bytes accessed | tf_op | source)
XLA Modules:
  0.0 475.1 jit_solution(10459165072919695314)
XLA Ops:
  10.0 7.3 %all-to-all-start.1 = ((s32[8,192,1]{1,2,0:T(1,128)}), s32[8,192,1]{1,2,0:T(1,128)S(1)}, u32[]{:S(2)}, u32[]{:S(2)}) async-start(s32[8,192,1]{1,2,0:T(1,128)} %all_to_all.31), calls=%async_computation.1 | async-start | bytes 16384 | tf_op jit(solution)/shard_map/all_to_all | solution.py:90
  38.0 6.6 %gather_fusion.2 = f32[1536,4,128]{2,1,0:T(4,128)} fusion(f32[1024,4,128]{2,1,0:T(4,128)} %get-tuple-element.57, s32[2048]{0:T(1024)S(1)} %pad_clamp_fusion.1), kind=kCustom, calls=%fused_computation.2 | custom fusion | bytes 6297600 | tf_op jit(solution)/shard_map/gather | solution.py:86
  44.5 6.1 %all-to-all-start.2 = ((f32[1536,4,128]{2,1,0:T(4,128)}), f32[1536,4,128]{2,1,0:T(4,128)}, u32[]{:S(2)}, u32[]{:S(2)}) async-start(f32[1536,4,128]{2,1,0:T(4,128)} %gather_fusion.2), calls=%async_computation.2 | async-start | bytes 6291456 | tf_op jit(solution)/shard_map/all_to_all | solution.py:104
  50.7 5.5 %gather_fusion.4 = f32[1536,4,128]{2,1,0:T(4,128)} fusion(f32[1024,4,128]{2,1,0:T(4,128)S(1)} %copy-done.2, s32[2048]{0:T(1024)S(1)} %pad_clamp_fusion.1), kind=kCustom, calls=%fused_computation.4 | custom fusion | bytes 6297600 | tf_op jit(solution)/shard_map/gather | solution.py:87
  56.2 64.8 %all-to-all-done.2 = f32[1536,4,128]{2,1,0:T(4,128)} async-done(((f32[1536,4,128]{2,1,0:T(4,128)}), f32[1536,4,128]{2,1,0:T(4,128)}, u32[]{:S(2)}, u32[]{:S(2)}) %all-to-all-start.2) | async-done | bytes 3145760 | tf_op jit(solution)/shard_map/all_to_all | solution.py:104
  127.3 5.6 %gather_fusion = f32[1536,4,128]{2,1,0:T(4,128)} fusion(f32[1024,4,128]{2,1,0:T(4,128)S(1)} %reshape.186, s32[2048]{0:T(1024)S(1)} %pad_clamp_fusion.1), kind=kCustom, calls=%fused_computation | custom fusion | bytes 6297600 | tf_op jit(solution)/shard_map/gather | solution.py:88
  132.9 62.7 %all-to-all-done.3 = f32[1536,4,128]{2,1,0:T(4,128)} async-done(((f32[1536,4,128]{2,1,0:T(4,128)}), f32[1536,4,128]{2,1,0:T(4,128)}, u32[]{:S(2)}, u32[]{:S(2)}) %all-to-all-start.3) | async-done | bytes 3145760 | tf_op jit(solution)/shard_map/all_to_all | solution.py:105
  206.9 6.6 %scatter_custom_fusion.2 = s32[1024]{0:T(1024)S(1)} fusion(s32[1536]{0:T(1024)S(1)} %get-tuple-element.40, s32[1536]{0:T(1024)S(1)} %iota.41, s32[]{:T(128)} %constant.96.clone.1), kind=kCustom, calls=%fused_computation.103 | custom fusion | bytes 4100 | tf_op jit(solution)/shard_map/scatter | solution.py:95
  213.5 9.8 %gather_fusion.3 = f32[1024,4,128]{2,1,0:T(4,128)} fusion(f32[1536,4,128]{2,1,0:T(4,128)} %all-to-all-done.2, s32[1024]{0:T(1024)S(1)} %fusion.56), kind=kCustom, calls=%fused_computation.3 | custom fusion | bytes 4198400 | tf_op jit(solution)/shard_map/gather | solution.py:99
  223.3 5.4 %gather_fusion.5 = f32[1024,4,128]{2,1,0:T(4,128)S(1)} fusion(f32[1536,4,128]{2,1,0:T(4,128)} %all-to-all-done.3, s32[1024]{0:T(1024)S(1)} %fusion.56), kind=kCustom, calls=%fused_computation.5 | custom fusion | bytes 4198400 | tf_op jit(solution)/shard_map/gather | solution.py:99
  235.4 61.2 %collective-permute-done = f32[2,512,1024]{2,1,0:T(8,128)} collective-permute-done((f32[2,512,1024]{2,1,0:T(8,128)}, f32[2,512,1024]{2,1,0:T(8,128)}, u32[]{:S(2)}, u32[]{:S(2)}) %collective-permute-start) | collective-permute-done | bytes 4194336 | tf_op jit(solution)/shard_map/ppermute | solution.py:131
  296.6 5.4 %gather_fusion.1 = f32[1024,4,128]{2,1,0:T(4,128)S(1)} fusion(f32[1536,4,128]{2,1,0:T(4,128)} %all-to-all-done, s32[1024]{0:T(1024)S(1)} %fusion.56), kind=kCustom, calls=%fused_computation.1 | custom fusion | bytes 4198400 | tf_op jit(solution)/shard_map/gather | solution.py:99
  308.5 9.0 %fusion.2 = (f32[2,1024]{1,0:T(2,128)S(1)}, f32[2,1024]{1,0:T(2,128)S(1)}, f32[2,1024,1024]{1,2,0:T(8,128)}) fusion(f32[2,1024,1024]{1,2,0:T(8,128)S(1)} %get-tuple-element.62, f32[2,1024]{1,0:T(2,128)S(1)} %get-tuple-element.61, pred[1024,1024]{0,1:T(8,128)(4,1)S(1)} %iota_compare_fusion, f32[1024,2,128]{2,1,0:T(2,128)S(1)} %copy-done.7, ...), kind=kOutput, calls=%fused_computation.19 | convolution fusion | flops 1625288704 | bytes 19947520 | tf_op jit(solution)/shard_map/while/body/eval_jaxpr/qhd,khd->hqk/dot_general | solution.py:43
  322.5 5.2 %gather_fusion.6 = f32[1536,2,128]{2,1,0:T(2,128)} fusion(f32[1024,2,128]{2,1,0:T(2,128)S(1)} %copy.25, s32[2048]{0:T(1024)S(1)} %pad_clamp_fusion), kind=kCustom, calls=%fused_computation.6 | custom fusion | bytes 3151872 | tf_op jit(solution)/shard_map/gather | solution.py:111
  327.7 5.7 %all-to-all-start.4 = ((f32[1536,2,128]{2,1,0:T(2,128)}), f32[1536,2,128]{2,1,0:T(2,128)S(1)}, u32[]{:S(2)}, u32[]{:S(2)}) async-start(f32[1536,2,128]{2,1,0:T(2,128)} %gather_fusion.6), calls=%async_computation.4 | async-start | bytes 3145728 | tf_op jit(solution)/shard_map/all_to_all | solution.py:111
  338.0 8.7 %fusion.48 = f32[1024,2,128]{0,2,1:T(8,128)} fusion(f32[2,1024,1024]{1,2,0:T(8,128)} %get-tuple-element.63, f32[2,1024]{1,0:T(2,128)S(1)} %get-tuple-element.33, pred[1024,1024]{0,1:T(8,128)(4,1)S(1)} %iota_compare_fusion, f32[1024,2,128]{2,1,0:T(2,128)S(1)} %copy-done.5, f32[1024,2]{0,1:T(2,128)S(1)} %bitcast.75), kind=kOutput, calls=%fused_computation.75 | convolution fusion | flops 1617166336 | bytes 11550720 | tf_op jit(solution)/shard_map/while/body/eval_jaxpr/hqk,khd->qhd/dot_general | solution.py:51
  348.2 5.2 %gather_fusion.8 = f32[1536,2,128]{2,1,0:T(2,128)} fusion(f32[1024,2,128]{2,1,0:T(2,128)S(1)} %copy.30, s32[2048]{0:T(1024)S(1)} %pad_clamp_fusion), kind=kCustom, calls=%fused_computation.8 | custom fusion | bytes 3151872 | tf_op jit(solution)/shard_map/gather | solution.py:111
  353.4 15.2 %all-to-all-done.4 = f32[1536,2,128]{2,1,0:T(2,128)S(1)} async-done(((f32[1536,2,128]{2,1,0:T(2,128)}), f32[1536,2,128]{2,1,0:T(2,128)S(1)}, u32[]{:S(2)}, u32[]{:S(2)}) %all-to-all-start.4) | async-done | bytes 1572896 | tf_op jit(solution)/shard_map/all_to_all | solution.py:111
  379.1 30.2 %all-to-all-done.5 = f32[1536,2,128]{2,1,0:T(2,128)} async-done(((f32[1536,2,128]{2,1,0:T(2,128)}), f32[1536,2,128]{2,1,0:T(2,128)}, u32[]{:S(2)}, u32[]{:S(2)}) %all-to-all-start.5) | async-done | bytes 1572896 | tf_op jit(solution)/shard_map/all_to_all | solution.py:111
  409.3 5.2 %gather_fusion.9 = f32[1024,2,128]{2,1,0:T(2,128)S(1)} fusion(f32[1536,2,128]{2,1,0:T(2,128)} %all-to-all-done.5, s32[1024]{0:T(1024)S(1)} %get-tuple-element.42), kind=kCustom, calls=%fused_computation.9 | custom fusion | bytes 2101248 | tf_op jit(solution)/shard_map/gather | solution.py:112
  425.8 12.0 %collective-permute-done.2 = f32[1024,256]{1,0:T(8,128)S(1)} collective-permute-done((f32[1024,256]{1,0:T(8,128)S(1)}, f32[1024,256]{1,0:T(8,128)S(1)}, u32[]{:S(2)}, u32[]{:S(2)}) %collective-permute-start.2) | collective-permute-done | bytes 1048608 | tf_op jit(solution)/shard_map/ppermute | solution.py:148
  437.8 5.9 %add_add_fusion = f32[1024,1024]{1,0:T(8,128)} fusion(f32[1024,1024]{1,0:T(8,128)S(1)} %fusion.18, f32[1024,1024]{1,0:T(8,128)S(1)} %fusion.20, f32[1024,1024]{1,0:T(8,128)S(1)} %fusion.35, f32[1024,256]{1,0:T(8,128)S(1)} %collective-permute-done.2, f32[2,512,1024]{2,1,0:T(8,128)} %collective-permute-done), kind=kOutput, calls=%fused_computation.24 | convolution fusion | flops 1613758464 | bytes 18874368 | tf_op jit(solution)/shard_map/dot_general | solution.py:141
  453.7 5.6 %fusion.39 = f32[1024,1024]{1,0:T(8,128)} fusion(f32[1024,256]{1,0:T(8,128)} %collective-permute-done.1, f32[2,512,1024]{2,1,0:T(8,128)} %collective-permute-done), kind=kOutput, calls=%fused_computation.68 | convolution fusion | flops 1610612736 | bytes 6291456 | tf_op jit(solution)/shard_map/dot_general | solution.py:141
  464.4 10.4 %add_add_fusion.1 = f32[1024,1024]{1,0:T(8,128)} fusion(f32[1024,1024]{1,0:T(8,128)} %collective-permute-done.3, f32[1024,1024]{1,0:T(8,128)} %fusion.37, f32[1024,1024]{1,0:T(8,128)} %fusion.22, f32[1024,1024]{1,0:T(8,128)S(1)} %copy-done.1, f32[1024,1024]{1,0:T(8,128)} %fusion.39), kind=kLoop, calls=%fused_computation.25 | loop fusion | flops 4194304 | bytes 25165824 | tf_op jit(solution)/shard_map/add | solution.py:158
  (77 shorter events, 109.3 us)
Async XLA Ops:
  10.0 34.5 %all-to-all-start.1 = ((s32[8,192,1]{1,2,0:T(1,128)}), s32[8,192,1]{1,2,0:T(1,128)S(1)}, u32[]{:S(2)}, u32[]{:S(2)}) async-start(s32[8,192,1]{1,2,0:T(1,128)} %all_to_all.31), calls=%async_computation.1 | async-start | bytes 16384 | tf_op jit(solution)/shard_map/all_to_all | solution.py:90
  17.3 4.8 %copy-start.8 = (s32[1024]{0:T(1024)S(1)}, s32[1024]{0:T(1024)}, u32[]{:S(2)}) copy-start(s32[1024]{0:T(1024)} %param.10) | copy-start | bytes 12292
  31.3 2.2 copy-start
  44.5 6.1 %copy-start.2 = (f32[1024,4,128]{2,1,0:T(4,128)S(1)}, f32[1024,4,128]{2,1,0:T(4,128)}, u32[]{:S(2)}) copy-start(f32[1024,4,128]{2,1,0:T(4,128)} %get-tuple-element.58) | copy-start | bytes 6291460
  44.5 76.4 %all-to-all-start.2 = ((f32[1536,4,128]{2,1,0:T(4,128)}), f32[1536,4,128]{2,1,0:T(4,128)}, u32[]{:S(2)}, u32[]{:S(2)}) async-start(f32[1536,4,128]{2,1,0:T(4,128)} %gather_fusion.2), calls=%async_computation.2 | async-start | bytes 6291456 | tf_op jit(solution)/shard_map/all_to_all | solution.py:104
  120.9 74.6 %all-to-all-start.3 = ((f32[1536,4,128]{2,1,0:T(4,128)}), f32[1536,4,128]{2,1,0:T(4,128)}, u32[]{:S(2)}, u32[]{:S(2)}) async-start(f32[1536,4,128]{2,1,0:T(4,128)} %gather_fusion.4), calls=%async_computation.3 | async-start | bytes 6291456 | tf_op jit(solution)/shard_map/all_to_all | solution.py:105
  195.6 101.0 %all-to-all-start = ((f32[1536,4,128]{2,1,0:T(4,128)}), f32[1536,4,128]{2,1,0:T(4,128)}, u32[]{:S(2)}, u32[]{:S(2)}) async-start(f32[1536,4,128]{2,1,0:T(4,128)} %gather_fusion), calls=%async_computation | async-start | bytes 6291456 | tf_op jit(solution)/shard_map/all_to_all | solution.py:102
  204.9 91.7 %collective-permute-start = (f32[2,512,1024]{2,1,0:T(8,128)}, f32[2,512,1024]{2,1,0:T(8,128)}, u32[]{:S(2)}, u32[]{:S(2)}) collective-permute-start(f32[2,512,1024]{2,1,0:T(8,128)} %pad_maximum_fusion), channel_id=1, source_target_pairs={{0,2},{1,3},{2,0},{3,1},{4,6},{5,7},{6,4},{7,5},{8,10},{9,11},{10,... | collective-permute-start | bytes 12582920 | tf_op jit(solution)/shard_map/ppermute | solution.py:131
  302.0 1.8 copy-start.3
  302.0 1.8 copy-start.4
  303.8 4.7 copy-start.6
  303.8 4.7 copy-start.7
  327.7 40.9 %all-to-all-start.4 = ((f32[1536,2,128]{2,1,0:T(2,128)}), f32[1536,2,128]{2,1,0:T(2,128)S(1)}, u32[]{:S(2)}, u32[]{:S(2)}) async-start(f32[1536,2,128]{2,1,0:T(2,128)} %gather_fusion.6), calls=%async_computation.4 | async-start | bytes 3145728 | tf_op jit(solution)/shard_map/all_to_all | solution.py:111
  333.4 4.6 copy-start.5
  368.6 40.7 %all-to-all-start.5 = ((f32[1536,2,128]{2,1,0:T(2,128)}), f32[1536,2,128]{2,1,0:T(2,128)}, u32[]{:S(2)}, u32[]{:S(2)}) async-start(f32[1536,2,128]{2,1,0:T(2,128)} %gather_fusion.8), calls=%async_computation.5 | async-start | bytes 3145728 | tf_op jit(solution)/shard_map/all_to_all | solution.py:111
  377.6 44.7 %collective-permute-start.1 = (f32[1024,256]{1,0:T(8,128)}, f32[1024,256]{1,0:T(8,128)}, u32[]{:S(2)}, u32[]{:S(2)}) collective-permute-start(f32[1024,256]{1,0:T(8,128)} %bitcast.64), channel_id=1, source_target_pairs={{0,2},{1,3},{2,0},{3,1},{4,6},{5,7},{6,4},{7,5},{8,10},{9,11},{10,... | collective-permute-start | bytes 3145736 | tf_op jit(solution)/shard_map/ppermute | solution.py:148
  414.6 23.2 %collective-permute-start.2 = (f32[1024,256]{1,0:T(8,128)S(1)}, f32[1024,256]{1,0:T(8,128)S(1)}, u32[]{:S(2)}, u32[]{:S(2)}) collective-permute-start(f32[1024,256]{1,0:T(8,128)S(1)} %bitcast.72), channel_id=1, source_target_pairs={{0,2},{1,3},{2,0},{3,1},{4,6},{5,7},{6,4},{7,5},{8,10},{9,11},{10,... | collective-permute-start | bytes 3145736 | tf_op jit(solution)/shard_map/ppermute | solution.py:148
  443.7 20.7 %collective-permute-start.3 = (f32[1024,1024]{1,0:T(8,128)}, f32[1024,1024]{1,0:T(8,128)}, u32[]{:S(2)}, u32[]{:S(2)}) collective-permute-start(f32[1024,1024]{1,0:T(8,128)} %add_add_fusion), channel_id=1, source_target_pairs={{0,1},{1,0},{2,3},{3,2},{4,5},{5,4},{6,7},{7,6},{8,9},{9,8},{10,11... | collective-permute-start | bytes 12582920 | tf_op jit(solution)/shard_map/ppermute | solution.py:154
  459.3 5.1 %copy-start.1 = (f32[1024,1024]{1,0:T(8,128)S(1)}, f32[1024,1024]{1,0:T(8,128)}, u32[]{:S(2)}) copy-start(f32[1024,1024]{1,0:T(8,128)} %fusion.24) | copy-start | bytes 12582916

commit v8 on v7

--- a/solution.py
+++ b/solution.py
@@ -99,10 +99,10 @@
         return pieces[where_from]
 
     far_weights = fetch_far_weights(out_weight)
+    arrived_q = lax.all_to_all(send_q, "seq", split_axis=0, concat_axis=0, tiled=True)
+    send_k, far_weights = lax.optimization_barrier((send_k, far_weights))
+    arrived_k = lax.all_to_all(send_k, "seq", split_axis=0, concat_axis=0, tiled=True)
     arrived_v = lax.all_to_all(send_v, "seq", split_axis=0, concat_axis=0, tiled=True)
-    arrived_v, far_weights = lax.optimization_barrier((arrived_v, far_weights))
-    arrived_q = lax.all_to_all(send_q, "seq", split_axis=0, concat_axis=0, tiled=True)
-    arrived_k = lax.all_to_all(send_k, "seq", split_axis=0, concat_axis=0, tiled=True)
     placed = (place(arrived_q), place(arrived_k), place(arrived_v))
     split = heads_here // 2
     mixed_parts = []

time: 479 us -> 479 us (level)
    ppermute x1, waiting for transfers between devices: 61.2 us -> 84.7 us  [fetch_far_weights(): return lax.ppermute(outgoing, 'head', swap_pairs(head_count, 2))]
    all_to_all x1, waiting for transfers between devices: 62.7 us -> 40.2 us  [per_device(): lax.all_to_all(send_k, 'seq', split_axis=0, concat_axis=0, tiled=True)]
where the time goes in v8:
time: 479 us; the launch traced here: 475 us
  waiting for transfers between devices  248 us (52%)
  local copies, waits for them, and re-layouts  94.1 us (20%)
  matrix products  62.9 us (13%)
  starting transfers between devices  36.4 us (8%)
  other arithmetic  33.6 us (7%)
    ppermute x1, waiting for transfers between devices, fetch_far_weights(): return lax.ppermute(outgoing, 'head', swap_pairs(head_count, 2))  84.7 us
    all_to_all x1, waiting for transfers between devices, per_device(): lax.all_to_all(send_q, 'seq', split_axis=0, concat_axis=0, tiled=True)  62.8 us
    all_to_all x2, waiting for transfers between devices, per_device(): lax.all_to_all(result[picked], 'seq', split_axis=0, concat_axis=0, tiled=...  47.6 us
    all_to_all x1, waiting for transfers between devices, per_device(): lax.all_to_all(send_k, 'seq', split_axis=0, concat_axis=0, tiled=True)  40.2 us
    dot_general x8, matrix products, dot(): jnp.dot(lhs, weight, precision=lax.Precision.HIGH, preferred_element_type...  36.2 us
    gather x3, local copies, waits for them, and re-layouts, place(): return pieces[where_from]  20.7 us
    dot_general x2, matrix products, cluster_attention(): jnp.einsum('qhd,khd->hqk', query_c, key_c, precision=lax.Precision.HIGH)  13.6 us
    dot_general x2, matrix products, cluster_attention(): jnp.einsum('hqk,khd->qhd', weights, value_c, precision=lax.Precision.HIGH)  13.1 us
  transfers between devices with their start and end apart: 10, of which 6 were waited for; matrix products, arithmetic and copies ran while one was open for 28% of the time, Pallas kernels for 0%

profile of v8, /device:TPU:0, one launch (start us, length us, event | category | flops | bytes accessed | tf_op | source)
XLA Modules:
  0.0 475.1 jit_solution(1640600356824040990)
XLA Ops:
  10.0 7.3 %all-to-all-start.1 = ((s32[8,192,1]{1,2,0:T(1,128)}), s32[8,192,1]{1,2,0:T(1,128)S(1)}, u32[]{:S(2)}, u32[]{:S(2)}) async-start(s32[8,192,1]{1,2,0:T(1,128)} %all_to_all.31), calls=%async_computation.1 | async-start | bytes 16384 | tf_op jit(solution)/shard_map/all_to_all | solution.py:90
  38.0 6.6 %gather_fusion.2 = f32[1536,4,128]{2,1,0:T(4,128)} fusion(f32[1024,4,128]{2,1,0:T(4,128)} %get-tuple-element.57, s32[2048]{0:T(1024)S(1)} %pad_clamp_fusion.1), kind=kCustom, calls=%fused_computation.2 | custom fusion | bytes 6297600 | tf_op jit(solution)/shard_map/gather | solution.py:86
  44.6 6.0 %all-to-all-start.2 = ((f32[1536,4,128]{2,1,0:T(4,128)}), f32[1536,4,128]{2,1,0:T(4,128)}, u32[]{:S(2)}, u32[]{:S(2)}) async-start(f32[1536,4,128]{2,1,0:T(4,128)} %gather_fusion.2), calls=%async_computation.2 | async-start | bytes 6291456 | tf_op jit(solution)/shard_map/all_to_all | solution.py:102
  52.5 5.5 %gather_fusion = f32[1536,4,128]{2,1,0:T(4,128)} fusion(f32[1024,4,128]{2,1,0:T(4,128)S(1)} %reshape.186, s32[2048]{0:T(1024)S(1)} %pad_clamp_fusion.1), kind=kCustom, calls=%fused_computation | custom fusion | bytes 6297600 | tf_op jit(solution)/shard_map/gather | solution.py:88
  58.1 62.8 %all-to-all-done.2 = f32[1536,4,128]{2,1,0:T(4,128)} async-done(((f32[1536,4,128]{2,1,0:T(4,128)}), f32[1536,4,128]{2,1,0:T(4,128)}, u32[]{:S(2)}, u32[]{:S(2)}) %all-to-all-start.2) | async-done | bytes 3145760 | tf_op jit(solution)/shard_map/all_to_all | solution.py:102
  132.2 5.5 %gather_fusion.4 = f32[1536,4,128]{2,1,0:T(4,128)} fusion(f32[1024,4,128]{2,1,0:T(4,128)S(1)} %copy-done.2, s32[2048]{0:T(1024)S(1)} %pad_clamp_fusion.1), kind=kCustom, calls=%fused_computation.4 | custom fusion | bytes 6297600 | tf_op jit(solution)/shard_map/gather | solution.py:87
  137.7 84.7 %collective-permute-done = f32[2,512,1024]{2,1,0:T(8,128)} collective-permute-done((f32[2,512,1024]{2,1,0:T(8,128)}, f32[2,512,1024]{2,1,0:T(8,128)}, u32[]{:S(2)}, u32[]{:S(2)}) %collective-permute-start) | collective-permute-done | bytes 4194336 | tf_op jit(solution)/shard_map/ppermute | solution.py:131
  222.4 5.7 %all-to-all-start.3 = ((f32[1536,4,128]{2,1,0:T(4,128)}), f32[1536,4,128]{2,1,0:T(4,128)}, u32[]{:S(2)}, u32[]{:S(2)}) async-start(f32[1536,4,128]{2,1,0:T(4,128)} %gather_fusion.4), calls=%async_computation.3 | async-start | bytes 6291456 | tf_op jit(solution)/shard_map/all_to_all | solution.py:104
  228.6 6.2 %scatter_custom_fusion.2 = s32[1024]{0:T(1024)S(1)} fusion(s32[1536]{0:T(1024)S(1)} %get-tuple-element.40, s32[1536]{0:T(1024)S(1)} %iota.41, s32[]{:T(128)} %constant.96.clone.1), kind=kCustom, calls=%fused_computation.103 | custom fusion | bytes 4100 | tf_op jit(solution)/shard_map/scatter | solution.py:95
  234.8 9.8 %gather_fusion.3 = f32[1024,4,128]{2,1,0:T(4,128)} fusion(f32[1536,4,128]{2,1,0:T(4,128)} %all-to-all-done.2, s32[1024]{0:T(1024)S(1)} %fusion.56), kind=kCustom, calls=%fused_computation.3 | custom fusion | bytes 4198400 | tf_op jit(solution)/shard_map/gather | solution.py:99
  244.6 5.4 %gather_fusion.1 = f32[1024,4,128]{2,1,0:T(4,128)S(1)} fusion(f32[1536,4,128]{2,1,0:T(4,128)} %all-to-all-done, s32[1024]{0:T(1024)S(1)} %fusion.56), kind=kCustom, calls=%fused_computation.1 | custom fusion | bytes 4198400 | tf_op jit(solution)/shard_map/gather | solution.py:99
  256.7 40.2 %all-to-all-done.3 = f32[1536,4,128]{2,1,0:T(4,128)} async-done(((f32[1536,4,128]{2,1,0:T(4,128)}), f32[1536,4,128]{2,1,0:T(4,128)}, u32[]{:S(2)}, u32[]{:S(2)}) %all-to-all-start.3) | async-done | bytes 3145760 | tf_op jit(solution)/shard_map/all_to_all | solution.py:104
  296.9 5.4 %gather_fusion.5 = f32[1024,4,128]{2,1,0:T(4,128)S(1)} fusion(f32[1536,4,128]{2,1,0:T(4,128)} %all-to-all-done.3, s32[1024]{0:T(1024)S(1)} %fusion.56), kind=kCustom, calls=%fused_computation.5 | custom fusion | bytes 4198400 | tf_op jit(solution)/shard_map/gather | solution.py:99
  308.2 9.0 %fusion.2 = (f32[2,1024]{1,0:T(2,128)S(1)}, f32[2,1024]{1,0:T(2,128)S(1)}, f32[2,1024,1024]{1,2,0:T(8,128)}) fusion(f32[2,1024,1024]{1,2,0:T(8,128)S(1)} %get-tuple-element.62, f32[2,1024]{1,0:T(2,128)S(1)} %get-tuple-element.61, pred[1024,1024]{0,1:T(8,128)(4,1)S(1)} %iota_compare_fusion, f32[1024,2,128]{2,1,0:T(2,128)S(1)} %get-tuple-element.52, ...), kind=kOutput, calls=%fused_computation.19 | convolution fusion | flops 1625288704 | bytes 19947520 | tf_op jit(solution)/shard_map/while/body/eval_jaxpr/qhd,khd->hqk/dot_general | solution.py:43
  322.1 5.2 %gather_fusion.6 = f32[1536,2,128]{2,1,0:T(2,128)} fusion(f32[1024,2,128]{2,1,0:T(2,128)S(1)} %copy.25, s32[2048]{0:T(1024)S(1)} %pad_clamp_fusion), kind=kCustom, calls=%fused_computation.6 | custom fusion | bytes 3151872 | tf_op jit(solution)/shard_map/gather | solution.py:111
  335.6 8.7 %fusion.48 = f32[1024,2,128]{0,2,1:T(8,128)} fusion(f32[2,1024,1024]{1,2,0:T(8,128)} %get-tuple-element.63, f32[2,1024]{1,0:T(2,128)S(1)} %get-tuple-element.33, pred[1024,1024]{0,1:T(8,128)(4,1)S(1)} %iota_compare_fusion, f32[1024,2,128]{2,1,0:T(2,128)S(1)} %copy-done.4, f32[1024,2]{0,1:T(2,128)S(1)} %bitcast.75), kind=kOutput, calls=%fused_computation.75 | convolution fusion | flops 1617166336 | bytes 11550720 | tf_op jit(solution)/shard_map/while/body/eval_jaxpr/hqk,khd->qhd/dot_general | solution.py:51
  345.8 5.2 %gather_fusion.8 = f32[1536,2,128]{2,1,0:T(2,128)} fusion(f32[1024,2,128]{2,1,0:T(2,128)S(1)} %copy.30, s32[2048]{0:T(1024)S(1)} %pad_clamp_fusion), kind=kCustom, calls=%fused_computation.8 | custom fusion | bytes 3151872 | tf_op jit(solution)/shard_map/gather | solution.py:111
  351.0 17.2 %all-to-all-done.4 = f32[1536,2,128]{2,1,0:T(2,128)S(1)} async-done(((f32[1536,2,128]{2,1,0:T(2,128)}), f32[1536,2,128]{2,1,0:T(2,128)S(1)}, u32[]{:S(2)}, u32[]{:S(2)}) %all-to-all-start.4) | async-done | bytes 1572896 | tf_op jit(solution)/shard_map/all_to_all | solution.py:111
  378.7 30.4 %all-to-all-done.5 = f32[1536,2,128]{2,1,0:T(2,128)} async-done(((f32[1536,2,128]{2,1,0:T(2,128)}), f32[1536,2,128]{2,1,0:T(2,128)}, u32[]{:S(2)}, u32[]{:S(2)}) %all-to-all-start.5) | async-done | bytes 1572896 | tf_op jit(solution)/shard_map/all_to_all | solution.py:111
  409.1 5.2 %gather_fusion.9 = f32[1024,2,128]{2,1,0:T(2,128)S(1)} fusion(f32[1536,2,128]{2,1,0:T(2,128)} %all-to-all-done.5, s32[1024]{0:T(1024)S(1)} %get-tuple-element.42), kind=kCustom, calls=%fused_computation.9 | custom fusion | bytes 2101248 | tf_op jit(solution)/shard_map/gather | solution.py:112
  425.5 12.3 %collective-permute-done.2 = f32[1024,256]{1,0:T(8,128)S(1)} collective-permute-done((f32[1024,256]{1,0:T(8,128)S(1)}, f32[1024,256]{1,0:T(8,128)S(1)}, u32[]{:S(2)}, u32[]{:S(2)}) %collective-permute-start.2) | collective-permute-done | bytes 1048608 | tf_op jit(solution)/shard_map/ppermute | solution.py:148
  437.8 5.9 %add_add_fusion = f32[1024,1024]{1,0:T(8,128)} fusion(f32[1024,1024]{1,0:T(8,128)S(1)} %fusion.18, f32[1024,1024]{1,0:T(8,128)S(1)} %fusion.20, f32[1024,1024]{1,0:T(8,128)S(1)} %fusion.35, f32[1024,256]{1,0:T(8,128)S(1)} %collective-permute-done.2, f32[2,512,1024]{2,1,0:T(8,128)} %collective-permute-done), kind=kOutput, calls=%fused_computation.24 | convolution fusion | flops 1613758464 | bytes 18874368 | tf_op jit(solution)/shard_map/dot_general | solution.py:141
  453.7 5.6 %fusion.39 = f32[1024,1024]{1,0:T(8,128)} fusion(f32[1024,256]{1,0:T(8,128)} %collective-permute-done.1, f32[2,512,1024]{2,1,0:T(8,128)} %collective-permute-done), kind=kOutput, calls=%fused_computation.68 | convolution fusion | flops 1610612736 | bytes 6291456 | tf_op jit(solution)/shard_map/dot_general | solution.py:141
  464.4 10.4 %add_add_fusion.1 = f32[1024,1024]{1,0:T(8,128)} fusion(f32[1024,1024]{1,0:T(8,128)} %collective-permute-done.3, f32[1024,1024]{1,0:T(8,128)} %fusion.37, f32[1024,1024]{1,0:T(8,128)} %fusion.22, f32[1024,1024]{1,0:T(8,128)S(1)} %copy-done.1, f32[1024,1024]{1,0:T(8,128)} %fusion.39), kind=kLoop, calls=%fused_computation.25 | loop fusion | flops 4194304 | bytes 25165824 | tf_op jit(solution)/shard_map/add | solution.py:158
  (75 shorter events, 108.4 us)
Async XLA Ops:
  10.0 34.6 %all-to-all-start.1 = ((s32[8,192,1]{1,2,0:T(1,128)}), s32[8,192,1]{1,2,0:T(1,128)S(1)}, u32[]{:S(2)}, u32[]{:S(2)}) async-start(s32[8,192,1]{1,2,0:T(1,128)} %all_to_all.31), calls=%async_computation.1 | async-start | bytes 16384 | tf_op jit(solution)/shard_map/all_to_all | solution.py:90
  17.3 4.8 %copy-start.7 = (s32[1024]{0:T(1024)S(1)}, s32[1024]{0:T(1024)}, u32[]{:S(2)}) copy-start(s32[1024]{0:T(1024)} %param.10) | copy-start | bytes 12292
  31.3 2.2 copy-start
  44.6 76.3 %all-to-all-start.2 = ((f32[1536,4,128]{2,1,0:T(4,128)}), f32[1536,4,128]{2,1,0:T(4,128)}, u32[]{:S(2)}, u32[]{:S(2)}) async-start(f32[1536,4,128]{2,1,0:T(4,128)} %gather_fusion.2), calls=%async_computation.2 | async-start | bytes 6291456 | tf_op jit(solution)/shard_map/all_to_all | solution.py:102
  120.9 101.5 %all-to-all-start = ((f32[1536,4,128]{2,1,0:T(4,128)}), f32[1536,4,128]{2,1,0:T(4,128)}, u32[]{:S(2)}, u32[]{:S(2)}) async-start(f32[1536,4,128]{2,1,0:T(4,128)} %gather_fusion), calls=%async_computation | async-start | bytes 6291456 | tf_op jit(solution)/shard_map/all_to_all | solution.py:105
  128.3 3.9 copy-start.2
  130.6 91.7 %collective-permute-start = (f32[2,512,1024]{2,1,0:T(8,128)}, f32[2,512,1024]{2,1,0:T(8,128)}, u32[]{:S(2)}, u32[]{:S(2)}) collective-permute-start(f32[2,512,1024]{2,1,0:T(8,128)} %pad_maximum_fusion), channel_id=1, source_target_pairs={{0,2},{1,3},{2,0},{3,1},{4,6},{5,7},{6,4},{7,5},{8,10},{9,11},{10,... | collective-permute-start | bytes 12582920 | tf_op jit(solution)/shard_map/ppermute | solution.py:131
  222.4 74.5 %all-to-all-start.3 = ((f32[1536,4,128]{2,1,0:T(4,128)}), f32[1536,4,128]{2,1,0:T(4,128)}, u32[]{:S(2)}, u32[]{:S(2)}) async-start(f32[1536,4,128]{2,1,0:T(4,128)} %gather_fusion.4), calls=%async_computation.3 | async-start | bytes 6291456 | tf_op jit(solution)/shard_map/all_to_all | solution.py:104
  302.3 1.2 copy-start.3
  303.5 4.7 copy-start.6
  308.2 9.0 %copy-start.5 = (f32[1024,2,128]{2,1,0:T(2,128)S(1)}, f32[1024,2,128]{2,1,0:T(2,128)}, u32[]{:S(2)}) copy-start(f32[1024,2,128]{2,1,0:T(2,128)} %get-tuple-element.47) | copy-start | bytes 3145732
  327.3 40.8 %all-to-all-start.4 = ((f32[1536,2,128]{2,1,0:T(2,128)}), f32[1536,2,128]{2,1,0:T(2,128)S(1)}, u32[]{:S(2)}, u32[]{:S(2)}) async-start(f32[1536,2,128]{2,1,0:T(2,128)} %gather_fusion.6), calls=%async_computation.4 | async-start | bytes 3145728 | tf_op jit(solution)/shard_map/all_to_all | solution.py:111
  331.0 4.6 copy-start.4
  368.2 40.9 %all-to-all-start.5 = ((f32[1536,2,128]{2,1,0:T(2,128)}), f32[1536,2,128]{2,1,0:T(2,128)}, u32[]{:S(2)}, u32[]{:S(2)}) async-start(f32[1536,2,128]{2,1,0:T(2,128)} %gather_fusion.8), calls=%async_computation.5 | async-start | bytes 3145728 | tf_op jit(solution)/shard_map/all_to_all | solution.py:111
  377.2 44.9 %collective-permute-start.1 = (f32[1024,256]{1,0:T(8,128)}, f32[1024,256]{1,0:T(8,128)}, u32[]{:S(2)}, u32[]{:S(2)}) collective-permute-start(f32[1024,256]{1,0:T(8,128)} %bitcast.64), channel_id=1, source_target_pairs={{0,2},{1,3},{2,0},{3,1},{4,6},{5,7},{6,4},{7,5},{8,10},{9,11},{10,... | collective-permute-start | bytes 3145736 | tf_op jit(solution)/shard_map/ppermute | solution.py:148
  414.4 23.4 %collective-permute-start.2 = (f32[1024,256]{1,0:T(8,128)S(1)}, f32[1024,256]{1,0:T(8,128)S(1)}, u32[]{:S(2)}, u32[]{:S(2)}) collective-permute-start(f32[1024,256]{1,0:T(8,128)S(1)} %bitcast.72), channel_id=1, source_target_pairs={{0,2},{1,3},{2,0},{3,1},{4,6},{5,7},{6,4},{7,5},{8,10},{9,11},{10,... | collective-permute-start | bytes 3145736 | tf_op jit(solution)/shard_map/ppermute | solution.py:148
  443.7 20.7 %collective-permute-start.3 = (f32[1024,1024]{1,0:T(8,128)}, f32[1024,1024]{1,0:T(8,128)}, u32[]{:S(2)}, u32[]{:S(2)}) collective-permute-start(f32[1024,1024]{1,0:T(8,128)} %add_add_fusion), channel_id=1, source_target_pairs={{0,1},{1,0},{2,3},{3,2},{4,5},{5,4},{6,7},{7,6},{8,9},{9,8},{10,11... | collective-permute-start | bytes 12582920 | tf_op jit(solution)/shard_map/ppermute | solution.py:154
  459.3 5.1 %copy-start.1 = (f32[1024,1024]{1,0:T(8,128)S(1)}, f32[1024,1024]{1,0:T(8,128)}, u32[]{:S(2)}) copy-start(f32[1024,1024]{1,0:T(8,128)} %fusion.24) | copy-start | bytes 12582916

commit v9 on v8

--- a/solution.py
+++ b/solution.py
@@ -99,8 +99,11 @@
         return pieces[where_from]
 
     far_weights = fetch_far_weights(out_weight)
+    far_own, far_partner = far_weights
     arrived_q = lax.all_to_all(send_q, "seq", split_axis=0, concat_axis=0, tiled=True)
-    send_k, far_weights = lax.optimization_barrier((send_k, far_weights))
+    arrived_q, far_own = lax.optimization_barrier((arrived_q, far_own))
+    send_k, far_partner = lax.optimization_barrier((send_k, far_partner))
+    far_weights = (far_own, far_partner)
     arrived_k = lax.all_to_all(send_k, "seq", split_axis=0, concat_axis=0, tiled=True)
     arrived_v = lax.all_to_all(send_v, "seq", split_axis=0, concat_axis=0, tiled=True)
     placed = (place(arrived_q), place(arrived_k), place(arrived_v))
@@ -125,10 +128,10 @@
 def fetch_far_weights(out_weight):
     head_count = lax.axis_size("head")
     me = lax.axis_index("head")
-    outgoing = jnp.stack(
-        [weight_block(out_weight, me ^ 2), weight_block(out_weight, me ^ 3)], 0
-    )
-    return lax.ppermute(outgoing, "head", swap_pairs(head_count, 2))
+    pairs = swap_pairs(head_count, 2)
+    for_own = lax.ppermute(weight_block(out_weight, me ^ 2), "head", pairs)
+    for_partner = lax.ppermute(weight_block(out_weight, me ^ 3), "head", pairs)
+    return for_own, for_partner
 
 
 def project_scatter(mixed_parts, out_weight, far_weights):
@@ -146,8 +149,8 @@
     terms_own = []
     for mixed, lo, hi in mixed_parts:
         far_mixed = lax.ppermute(mixed, "head", swap_pairs(head_count, 2))
-        terms_partner += [(mixed, partner_w[lo:hi]), (far_mixed, far_weights[1, lo:hi])]
-        terms_own += [(mixed, own_w[lo:hi]), (far_mixed, far_weights[0, lo:hi])]
+        terms_partner += [(mixed, partner_w[lo:hi]), (far_mixed, far_weights[1][lo:hi])]
+        terms_own += [(mixed, own_w[lo:hi]), (far_mixed, far_weights[0][lo:hi])]
     for_partner = dot(*terms_partner[0])
     for term in terms_partner[1:]:
         for_partner = for_partner + dot(*term)

time: 479 us -> 453 us (0.946)
  waiting for transfers between devices: 248 us -> 220 us
    all_to_all x1, waiting for transfers between devices: 40.2 us -> 1.43 us  [per_device(): lax.all_to_all(send_k, 'seq', split_axis=0, concat_axis=0, tiled=True)]
    all_to_all x1, waiting for transfers between devices: 0.01 us -> 18.5 us  [per_device(): lax.all_to_all(send_v, 'seq', split_axis=0, concat_axis=0, tiled=True)]
    ppermute x1 -> x2, waiting for transfers between devices: 84.7 us -> 78.1 us  [the longest x1 39.7 us: fetch_far_weights(): for_partner = lax.ppermute(weight_block(out_weight, me ^ 3), 'head', pairs)]
    dynamic_slice x0 -> x1, local copies, waits for them, and re-layouts: none -> 4.9 us  [weight_block(): return lax.dynamic_slice_in_dim(out_weight, index * width, width, axis=1)]
  transfers between devices with their start and end apart: 10 -> 11, of which waited for: 6 -> 8; matrix products, arithmetic and copies ran while one was open for 28% -> 30% of each run, Pallas kernels for 0% -> 0%
where the time goes in v9:
time: 453 us; the launch traced here: 449 us
  waiting for transfers between devices  220 us (49%)
  local copies, waits for them, and re-layouts  96.6 us (21%)
  matrix products  62.9 us (14%)
  starting transfers between devices  37.4 us (8%)
  other arithmetic  31.3 us (7%)
    all_to_all x1, waiting for transfers between devices, per_device(): lax.all_to_all(send_q, 'seq', split_axis=0, concat_axis=0, tiled=True)  62.7 us
    all_to_all x2, waiting for transfers between devices, per_device(): lax.all_to_all(result[picked], 'seq', split_axis=0, concat_axis=0, tiled=...  47 us
    ppermute x1, waiting for transfers between devices, fetch_far_weights(): for_partner = lax.ppermute(weight_block(out_weight, me ^ 3), 'head', pairs)  39.7 us
    ppermute x1, waiting for transfers between devices, fetch_far_weights(): for_own = lax.ppermute(weight_block(out_weight, me ^ 2), 'head', pairs)  38.4 us
    dot_general x8, matrix products, dot(): jnp.dot(lhs, weight, precision=lax.Precision.HIGH, preferred_element_type...  36.2 us
    gather x3, local copies, waits for them, and re-layouts, place(): return pieces[where_from]  20.7 us
    all_to_all x1, waiting for transfers between devices, per_device(): lax.all_to_all(send_v, 'seq', split_axis=0, concat_axis=0, tiled=True)  18.5 us
    dot_general x2, matrix products, cluster_attention(): jnp.einsum('qhd,khd->hqk', query_c, key_c, precision=lax.Precision.HIGH)  13.6 us
  transfers between devices with their start and end apart: 11, of which 8 were waited for; matrix products, arithmetic and copies ran while one was open for 30% of the time, Pallas kernels for 0%

profile of v9, /device:TPU:0, one launch (start us, length us, event | category | flops | bytes accessed | tf_op | source)
XLA Modules:
  0.0 448.8 jit_solution(5194015188982082197)
XLA Ops:
  10.0 7.3 %all-to-all-start.1 = ((s32[8,192,1]{1,2,0:T(1,128)}), s32[8,192,1]{1,2,0:T(1,128)S(1)}, u32[]{:S(2)}, u32[]{:S(2)}) async-start(s32[8,192,1]{1,2,0:T(1,128)} %all_to_all.31), calls=%async_computation.1 | async-start | bytes 16384 | tf_op jit(solution)/shard_map/all_to_all | solution.py:90
  38.0 6.6 %gather_fusion.2 = f32[1536,4,128]{2,1,0:T(4,128)} fusion(f32[1024,4,128]{2,1,0:T(4,128)} %get-tuple-element.61, s32[2048]{0:T(1024)S(1)} %pad_clamp_fusion.1), kind=kCustom, calls=%fused_computation.2 | custom fusion | bytes 6297600 | tf_op jit(solution)/shard_map/gather | solution.py:86
  44.6 6.0 %all-to-all-start.2 = ((f32[1536,4,128]{2,1,0:T(4,128)}), f32[1536,4,128]{2,1,0:T(4,128)}, u32[]{:S(2)}, u32[]{:S(2)}) async-start(f32[1536,4,128]{2,1,0:T(4,128)} %gather_fusion.2), calls=%async_computation.2 | async-start | bytes 6291456 | tf_op jit(solution)/shard_map/all_to_all | solution.py:103
  52.5 5.6 %gather_fusion = f32[1536,4,128]{2,1,0:T(4,128)} fusion(f32[1024,4,128]{2,1,0:T(4,128)S(1)} %reshape.186, s32[2048]{0:T(1024)S(1)} %pad_clamp_fusion.1), kind=kCustom, calls=%fused_computation | custom fusion | bytes 6297600 | tf_op jit(solution)/shard_map/gather | solution.py:88
  58.1 62.7 %all-to-all-done.2 = f32[1536,4,128]{2,1,0:T(4,128)} async-done(((f32[1536,4,128]{2,1,0:T(4,128)}), f32[1536,4,128]{2,1,0:T(4,128)}, u32[]{:S(2)}, u32[]{:S(2)}) %all-to-all-start.2) | async-done | bytes 3145760 | tf_op jit(solution)/shard_map/all_to_all | solution.py:103
  131.7 5.5 %gather_fusion.4 = f32[1536,4,128]{2,1,0:T(4,128)} fusion(f32[1024,4,128]{2,1,0:T(4,128)S(1)} %copy-done.2, s32[2048]{0:T(1024)S(1)} %pad_clamp_fusion.1), kind=kCustom, calls=%fused_computation.4 | custom fusion | bytes 6297600 | tf_op jit(solution)/shard_map/gather | solution.py:87
  137.2 39.7 %collective-permute-done.1 = f32[512,1024]{1,0:T(8,128)} collective-permute-done((f32[512,1024]{1,0:T(8,128)}, f32[512,1024]{1,0:T(8,128)}, u32[]{:S(2)}, u32[]{:S(2)}) %collective-permute-start.1) | collective-permute-done | bytes 2097184 | tf_op jit(solution)/shard_map/ppermute | solution.py:133
  177.0 18.5 %all-to-all-done = f32[1536,4,128]{2,1,0:T(4,128)} async-done(((f32[1536,4,128]{2,1,0:T(4,128)}), f32[1536,4,128]{2,1,0:T(4,128)}, u32[]{:S(2)}, u32[]{:S(2)}) %all-to-all-start) | async-done | bytes 3145760 | tf_op jit(solution)/shard_map/all_to_all | solution.py:108
  202.4 6.2 %scatter_custom_fusion.2 = s32[1024]{0:T(1024)S(1)} fusion(s32[1536]{0:T(1024)S(1)} %get-tuple-element.46, s32[1536]{0:T(1024)S(1)} %iota.41, s32[]{:T(128)} %constant.96.clone.1), kind=kCustom, calls=%fused_computation.96 | custom fusion | bytes 4100 | tf_op jit(solution)/shard_map/scatter | solution.py:95
  208.7 38.4 %collective-permute-done = f32[512,1024]{1,0:T(8,128)} collective-permute-done((f32[512,1024]{1,0:T(8,128)S(1)}, f32[512,1024]{1,0:T(8,128)}, u32[]{:S(2)}, u32[]{:S(2)}) %collective-permute-start) | collective-permute-done | bytes 2097184 | tf_op jit(solution)/shard_map/ppermute | solution.py:132
  247.0 9.8 %gather_fusion.3 = f32[1024,4,128]{2,1,0:T(4,128)} fusion(f32[1536,4,128]{2,1,0:T(4,128)} %all-to-all-done.2, s32[1024]{0:T(1024)S(1)} %fusion.52), kind=kCustom, calls=%fused_computation.3 | custom fusion | bytes 4198400 | tf_op jit(solution)/shard_map/gather | solution.py:99
  256.8 5.4 %gather_fusion.1 = f32[1024,4,128]{2,1,0:T(4,128)S(1)} fusion(f32[1536,4,128]{2,1,0:T(4,128)} %all-to-all-done, s32[1024]{0:T(1024)S(1)} %fusion.52), kind=kCustom, calls=%fused_computation.1 | custom fusion | bytes 4198400 | tf_op jit(solution)/shard_map/gather | solution.py:99
  270.5 5.4 %gather_fusion.5 = f32[1024,4,128]{2,1,0:T(4,128)S(1)} fusion(f32[1536,4,128]{2,1,0:T(4,128)} %all-to-all-done.3, s32[1024]{0:T(1024)S(1)} %fusion.52), kind=kCustom, calls=%fused_computation.5 | custom fusion | bytes 4198400 | tf_op jit(solution)/shard_map/gather | solution.py:99
  281.9 9.0 %fusion.2 = (f32[2,1024]{1,0:T(2,128)S(1)}, f32[2,1024]{1,0:T(2,128)S(1)}, f32[2,1024,1024]{1,2,0:T(8,128)}) fusion(f32[2,1024,1024]{1,2,0:T(8,128)S(1)} %get-tuple-element.66, f32[2,1024]{1,0:T(2,128)S(1)} %get-tuple-element.65, pred[1024,1024]{0,1:T(8,128)(4,1)S(1)} %iota_compare_fusion, f32[1024,2,128]{2,1,0:T(2,128)S(1)} %get-tuple-element.56, ...), kind=kOutput, calls=%fused_computation.19 | convolution fusion | flops 1625288704 | bytes 19947520 | tf_op jit(solution)/shard_map/while/body/eval_jaxpr/qhd,khd->hqk/dot_general | solution.py:43
  295.8 5.2 %gather_fusion.6 = f32[1536,2,128]{2,1,0:T(2,128)} fusion(f32[1024,2,128]{2,1,0:T(2,128)S(1)} %copy.25, s32[2048]{0:T(1024)S(1)} %pad_clamp_fusion), kind=kCustom, calls=%fused_computation.6 | custom fusion | bytes 3151872 | tf_op jit(solution)/shard_map/gather | solution.py:114
  309.9 8.7 %fusion.44 = f32[1024,2,128]{0,2,1:T(8,128)} fusion(f32[2,1024,1024]{1,2,0:T(8,128)} %get-tuple-element.67, f32[2,1024]{1,0:T(2,128)S(1)} %get-tuple-element.44, pred[1024,1024]{0,1:T(8,128)(4,1)S(1)} %iota_compare_fusion, f32[1024,2,128]{2,1,0:T(2,128)S(1)} %copy-done.5, f32[1024,2]{0,1:T(2,128)S(1)} %bitcast.59), kind=kOutput, calls=%fused_computation.68 | convolution fusion | flops 1617166336 | bytes 11550720 | tf_op jit(solution)/shard_map/while/body/eval_jaxpr/hqk,khd->qhd/dot_general | solution.py:51
  320.1 5.2 %gather_fusion.8 = f32[1536,2,128]{2,1,0:T(2,128)} fusion(f32[1024,2,128]{2,1,0:T(2,128)S(1)} %copy.30, s32[2048]{0:T(1024)S(1)} %pad_clamp_fusion), kind=kCustom, calls=%fused_computation.8 | custom fusion | bytes 3151872 | tf_op jit(solution)/shard_map/gather | solution.py:114
  325.3 16.5 %all-to-all-done.4 = f32[1536,2,128]{2,1,0:T(2,128)S(1)} async-done(((f32[1536,2,128]{2,1,0:T(2,128)}), f32[1536,2,128]{2,1,0:T(2,128)S(1)}, u32[]{:S(2)}, u32[]{:S(2)}) %all-to-all-start.4) | async-done | bytes 1572896 | tf_op jit(solution)/shard_map/all_to_all | solution.py:114
  352.3 30.5 %all-to-all-done.5 = f32[1536,2,128]{2,1,0:T(2,128)} async-done(((f32[1536,2,128]{2,1,0:T(2,128)}), f32[1536,2,128]{2,1,0:T(2,128)}, u32[]{:S(2)}, u32[]{:S(2)}) %all-to-all-start.5) | async-done | bytes 1572896 | tf_op jit(solution)/shard_map/all_to_all | solution.py:114
  382.8 5.2 %gather_fusion.9 = f32[1024,2,128]{2,1,0:T(2,128)S(1)} fusion(f32[1536,2,128]{2,1,0:T(2,128)} %all-to-all-done.5, s32[1024]{0:T(1024)S(1)} %get-tuple-element.47), kind=kCustom, calls=%fused_computation.9 | custom fusion | bytes 2101248 | tf_op jit(solution)/shard_map/gather | solution.py:115
  399.2 12.3 %collective-permute-done.3 = f32[1024,256]{1,0:T(8,128)S(1)} collective-permute-done((f32[1024,256]{1,0:T(8,128)S(1)}, f32[1024,256]{1,0:T(8,128)S(1)}, u32[]{:S(2)}, u32[]{:S(2)}) %collective-permute-start.3) | collective-permute-done | bytes 1048608 | tf_op jit(solution)/shard_map/ppermute | solution.py:151
  411.5 5.9 %add_add_fusion = f32[1024,1024]{1,0:T(8,128)} fusion(f32[1024,1024]{1,0:T(8,128)S(1)} %fusion.18, f32[1024,1024]{1,0:T(8,128)S(1)} %fusion.20, f32[1024,1024]{1,0:T(8,128)S(1)} %fusion.35, f32[1024,256]{1,0:T(8,128)S(1)} %collective-permute-done.3, f32[512,1024]{1,0:T(8,128)} %collective-permute-done.1), kind=kOutput, calls=%fused_computation.23 | convolution fusion | flops 1613758464 | bytes 18874368 | tf_op jit(solution)/shard_map/dot_general | solution.py:144
  427.4 5.6 %fusion.39 = f32[1024,1024]{1,0:T(8,128)} fusion(f32[1024,256]{1,0:T(8,128)} %collective-permute-done.2, f32[512,1024]{1,0:T(8,128)} %collective-permute-done), kind=kOutput, calls=%fused_computation.65 | convolution fusion | flops 1610612736 | bytes 6291456 | tf_op jit(solution)/shard_map/dot_general | solution.py:144
  438.1 10.4 %add_add_fusion.1 = f32[1024,1024]{1,0:T(8,128)} fusion(f32[1024,1024]{1,0:T(8,128)} %collective-permute-done.4, f32[1024,1024]{1,0:T(8,128)} %fusion.37, f32[1024,1024]{1,0:T(8,128)} %fusion.22, f32[1024,1024]{1,0:T(8,128)S(1)} %copy-done.1, f32[1024,1024]{1,0:T(8,128)} %fusion.39), kind=kLoop, calls=%fused_computation.24 | loop fusion | flops 4194304 | bytes 25165824 | tf_op jit(solution)/shard_map/add | solution.py:161
  (78 shorter events, 116.6 us)
Async XLA Ops:
  10.0 34.5 %all-to-all-start.1 = ((s32[8,192,1]{1,2,0:T(1,128)}), s32[8,192,1]{1,2,0:T(1,128)S(1)}, u32[]{:S(2)}, u32[]{:S(2)}) async-start(s32[8,192,1]{1,2,0:T(1,128)} %all_to_all.31), calls=%async_computation.1 | async-start | bytes 16384 | tf_op jit(solution)/shard_map/all_to_all | solution.py:90
  17.3 4.8 %copy-start.8 = (s32[1024]{0:T(1024)S(1)}, s32[1024]{0:T(1024)}, u32[]{:S(2)}) copy-start(s32[1024]{0:T(1024)} %param.10) | copy-start | bytes 12292
  31.3 2.2 copy-start
  44.6 76.3 %all-to-all-start.2 = ((f32[1536,4,128]{2,1,0:T(4,128)}), f32[1536,4,128]{2,1,0:T(4,128)}, u32[]{:S(2)}, u32[]{:S(2)}) async-start(f32[1536,4,128]{2,1,0:T(4,128)} %gather_fusion.2), calls=%async_computation.2 | async-start | bytes 6291456 | tf_op jit(solution)/shard_map/all_to_all | solution.py:103
  120.8 74.6 %all-to-all-start = ((f32[1536,4,128]{2,1,0:T(4,128)}), f32[1536,4,128]{2,1,0:T(4,128)}, u32[]{:S(2)}, u32[]{:S(2)}) async-start(f32[1536,4,128]{2,1,0:T(4,128)} %gather_fusion), calls=%async_computation | async-start | bytes 6291456 | tf_op jit(solution)/shard_map/all_to_all | solution.py:108
  125.3 6.4 %copy-start.2 = (f32[1024,4,128]{2,1,0:T(4,128)S(1)}, f32[1024,4,128]{2,1,0:T(4,128)}, u32[]{:S(2)}) copy-start(f32[1024,4,128]{2,1,0:T(4,128)} %get-tuple-element.62) | copy-start | bytes 6291460
  130.2 46.8 %collective-permute-start.1 = (f32[512,1024]{1,0:T(8,128)}, f32[512,1024]{1,0:T(8,128)}, u32[]{:S(2)}, u32[]{:S(2)}) collective-permute-start(f32[512,1024]{1,0:T(8,128)} %get-tuple-element.50), channel_id=1, source_target_pairs={{0,2},{1,3},{2,0},{3,1},{4,6},{5,7},{6,4},{7,5},{8,10},{9,11},{10,... | collective-permute-start | bytes 6291464 | tf_op jit(solution)/shard_map/ppermute | solution.py:133
  137.2 63.1 %copy-start.4 = (f32[512,1024]{1,0:T(8,128)S(1)}, f32[512,1024]{1,0:T(8,128)}, u32[]{:S(2)}) copy-start(f32[512,1024]{1,0:T(8,128)} %get-tuple-element.49) | copy-start | bytes 6291460
  195.5 75.0 %all-to-all-start.3 = ((f32[1536,4,128]{2,1,0:T(4,128)}), f32[1536,4,128]{2,1,0:T(4,128)}, u32[]{:S(2)}, u32[]{:S(2)}) async-start(f32[1536,4,128]{2,1,0:T(4,128)} %gather_fusion.4), calls=%async_computation.3 | async-start | bytes 6291456 | tf_op jit(solution)/shard_map/all_to_all | solution.py:107
  200.4 46.6 %collective-permute-start = (f32[512,1024]{1,0:T(8,128)S(1)}, f32[512,1024]{1,0:T(8,128)}, u32[]{:S(2)}, u32[]{:S(2)}) collective-permute-start(f32[512,1024]{1,0:T(8,128)S(1)} %copy-done.4), channel_id=1, source_target_pairs={{0,2},{1,3},{2,0},{3,1},{4,6},{5,7},{6,4},{7,5},{8,10},{9,11},{10,... | collective-permute-start | bytes 6291464 | tf_op jit(solution)/shard_map/ppermute | solution.py:132
  276.0 1.2 copy-start.3
  277.2 4.7 %copy-start.7 = (f32[1024,2,128]{2,1,0:T(2,128)S(1)}, f32[1024,2,128]{2,1,0:T(2,128)}, u32[]{:S(2)}) copy-start(f32[1024,2,128]{2,1,0:T(2,128)} %get-tuple-element.54) | copy-start | bytes 3145732
  281.9 9.0 %copy-start.6 = (f32[1024,2,128]{2,1,0:T(2,128)S(1)}, f32[1024,2,128]{2,1,0:T(2,128)}, u32[]{:S(2)}) copy-start(f32[1024,2,128]{2,1,0:T(2,128)} %get-tuple-element.51) | copy-start | bytes 3145732
  301.0 40.8 %all-to-all-start.4 = ((f32[1536,2,128]{2,1,0:T(2,128)}), f32[1536,2,128]{2,1,0:T(2,128)S(1)}, u32[]{:S(2)}, u32[]{:S(2)}) async-start(f32[1536,2,128]{2,1,0:T(2,128)} %gather_fusion.6), calls=%async_computation.4 | async-start | bytes 3145728 | tf_op jit(solution)/shard_map/all_to_all | solution.py:114
  305.3 4.6 %copy-start.5 = (f32[1024,2,128]{2,1,0:T(2,128)S(1)}, f32[1024,2,128]{2,1,0:T(2,128)}, u32[]{:S(2)}) copy-start(f32[1024,2,128]{2,1,0:T(2,128)} %get-tuple-element.52) | copy-start | bytes 3145732
  341.8 40.9 %all-to-all-start.5 = ((f32[1536,2,128]{2,1,0:T(2,128)}), f32[1536,2,128]{2,1,0:T(2,128)}, u32[]{:S(2)}, u32[]{:S(2)}) async-start(f32[1536,2,128]{2,1,0:T(2,128)} %gather_fusion.8), calls=%async_computation.5 | async-start | bytes 3145728 | tf_op jit(solution)/shard_map/all_to_all | solution.py:114
  350.7 45.0 %collective-permute-start.2 = (f32[1024,256]{1,0:T(8,128)}, f32[1024,256]{1,0:T(8,128)}, u32[]{:S(2)}, u32[]{:S(2)}) collective-permute-start(f32[1024,256]{1,0:T(8,128)} %bitcast.48), channel_id=1, source_target_pairs={{0,2},{1,3},{2,0},{3,1},{4,6},{5,7},{6,4},{7,5},{8,10},{9,11},{10,... | collective-permute-start | bytes 3145736 | tf_op jit(solution)/shard_map/ppermute | solution.py:151
  388.0 23.4 %collective-permute-start.3 = (f32[1024,256]{1,0:T(8,128)S(1)}, f32[1024,256]{1,0:T(8,128)S(1)}, u32[]{:S(2)}, u32[]{:S(2)}) collective-permute-start(f32[1024,256]{1,0:T(8,128)S(1)} %bitcast.56), channel_id=1, source_target_pairs={{0,2},{1,3},{2,0},{3,1},{4,6},{5,7},{6,4},{7,5},{8,10},{9,11},{10,... | collective-permute-start | bytes 3145736 | tf_op jit(solution)/shard_map/ppermute | solution.py:151
  417.4 20.7 %collective-permute-start.4 = (f32[1024,1024]{1,0:T(8,128)}, f32[1024,1024]{1,0:T(8,128)}, u32[]{:S(2)}, u32[]{:S(2)}) collective-permute-start(f32[1024,1024]{1,0:T(8,128)} %add_add_fusion), channel_id=1, source_target_pairs={{0,1},{1,0},{2,3},{3,2},{4,5},{5,4},{6,7},{7,6},{8,9},{9,8},{10,11... | collective-permute-start | bytes 12582920 | tf_op jit(solution)/shard_map/ppermute | solution.py:157
  433.0 5.2 %copy-start.1 = (f32[1024,1024]{1,0:T(8,128)S(1)}, f32[1024,1024]{1,0:T(8,128)}, u32[]{:S(2)}) copy-start(f32[1024,1024]{1,0:T(8,128)} %fusion.24) | copy-start | bytes 12582916

commit v10 on v6

--- a/solution.py
+++ b/solution.py
@@ -109,11 +109,37 @@
     result = attend_local(place(received[0]), place(received[1]), place(received[2]))
     outgoing = result[picked]
     split = heads_here // 2
-    mixed_parts = []
-    for lo, hi in ((0, split), (split, heads_here)):
+    head_count = lax.axis_size("head")
+    me = lax.axis_index("head")
+    partner_w = weight_block(out_weight, me ^ 1)
+    own_w = weight_block(out_weight, me)
+
+    def dot(lhs, weight):
+        return jnp.dot(
+            lhs, weight, precision=lax.Precision.HIGH, preferred_element_type=jnp.float32
+        )
+
+    def exchange(lo, hi):
         back = lax.all_to_all(outgoing[:, lo:hi], "seq", split_axis=0, concat_axis=0, tiled=True)
-        mixed_parts.append((back[send_row].reshape(row_count, (hi - lo) * DH), lo * DH, hi * DH))
-    return project_scatter(mixed_parts, out_weight, far_weights)
+        return back
+
+    def half_terms(back, lo, hi):
+        mixed = back[send_row].reshape(row_count, (hi - lo) * DH)
+        far_mixed = lax.ppermute(mixed, "head", swap_pairs(head_count, 2))
+        rows = slice(lo * DH, hi * DH)
+        to_partner = dot(mixed, partner_w[rows]) + dot(far_mixed, far_weights[1, rows])
+        to_own = dot(mixed, own_w[rows]) + dot(far_mixed, far_weights[0, rows])
+        return to_partner, to_own
+
+    first_partner, first_own = half_terms(exchange(0, split), 0, split)
+    second_back = exchange(split, heads_here)
+    second_back, first_partner, first_own = lax.optimization_barrier(
+        (second_back, first_partner, first_own)
+    )
+    second_partner, second_own = half_terms(second_back, split, heads_here)
+    for_partner = first_partner + second_partner
+    from_partner = lax.ppermute(for_partner, "head", swap_pairs(head_count, 1))
+    return first_own + second_own + from_partner
 
 
 def swap_pairs(count, bit):
@@ -134,28 +160,6 @@
     return lax.ppermute(outgoing, "head", swap_pairs(head_count, 2))
 
 
-def project_scatter(mixed_parts, out_weight, far_weights):
-    head_count = lax.axis_size("head")
-    me = lax.axis_index("head")
-    partner_w = weight_block(out_weight, me ^ 1)
-    own_w = weight_block(out_weight, me)
-
-    def dot(lhs, weight):
-        return jnp.dot(
-            lhs, weight, precision=lax.Precision.HIGH, preferred_element_type=jnp.float32
-        )
-
-    for_partner = 0.0
-    own = 0.0
-    for mixed, lo, hi in mixed_parts:
-        far_mixed = lax.ppermute(mixed, "head", swap_pairs(head_count, 2))
-        for_partner = for_partner + dot(mixed, partner_w[lo:hi])
-        for_partner = for_partner + dot(far_mixed, far_weights[1, lo:hi])
-        own = own + dot(mixed, own_w[lo:hi]) + dot(far_mixed, far_weights[0, lo:hi])
-    from_partner = lax.ppermute(for_partner, "head", swap_pairs(head_count, 1))
-    return own + from_partner
-
-
 def solution(mesh):
     in_specs = (
         P("seq", "head"),

time: 453 us -> 441 us (0.974); the launches traced: 448 us -> 442 us
  starting transfers between devices: 31.7 us -> 41.2 us
  matrix products: 59.7 us -> 53.3 us
  other arithmetic: 32.7 us -> 27 us
  waiting for transfers between devices: 191 us -> 186 us
    all_to_all x1, waiting for transfers between devices: 30.1 us -> 0.01 us  [exchange(): lax.all_to_all(outgoing[:, lo:hi], 'seq', split_axis=0, concat_axis=0, ti...]
    ppermute x3, waiting for transfers between devices: 11.6 us -> 36.7 us  [the longest x2 35.7 us: half_terms(): far_mixed = lax.ppermute(mixed, 'head', swap_pairs(head_count, 2))]
    all_to_all x1, starting transfers between devices: 4.97 us -> 14.7 us  [per_device(): lax.all_to_all(send_k, 'seq', split_axis=0, concat_axis=0, tiled=True)]
    dot_general x8, matrix products: 36.2 us -> 29.9 us  [dot(): jnp.dot(lhs, weight, precision=lax.Precision.HIGH, preferred_element_type...]
  transfers between devices with their start and end apart: 9 -> 9, of which waited for: 6 -> 7; matrix products, arithmetic and copies ran while one was open for 27% -> 25% of each run, Pallas kernels for 0% -> 0%
where the time goes in v10:
time: 441 us; the launch traced here: 442 us
  waiting for transfers between devices  186 us (42%)
  local copies, waits for them, and re-layouts  93.3 us (21%)
  matrix products  53.3 us (12%)
  starting transfers between devices  41.2 us (9%)
  blocking collectives  40.7 us (9%)
  other arithmetic  27 us (6%)
    all_to_all x1, waiting for transfers between devices, per_device(): lax.all_to_all(send_q, 'seq', split_axis=0, concat_axis=0, tiled=True)  64.6 us
    all_to_all x1, waiting for transfers between devices, per_device(): lax.all_to_all(send_k, 'seq', split_axis=0, concat_axis=0, tiled=True)  56.1 us
    all_to_all x1, blocking collectives, exchange(): lax.all_to_all(outgoing[:, lo:hi], 'seq', split_axis=0, concat_axis=0, ti...  40.7 us
    ppermute x2, waiting for transfers between devices, half_terms(): far_mixed = lax.ppermute(mixed, 'head', swap_pairs(head_count, 2))  35.7 us
    dot_general x8, matrix products, dot(): jnp.dot(lhs, weight, precision=lax.Precision.HIGH, preferred_element_type...  29.9 us
    gather x3, local copies, waits for them, and re-layouts, place(): return pieces[where_from]  20.7 us
    ppermute x1, waiting for transfers between devices, fetch_far_weights(): return lax.ppermute(outgoing, 'head', swap_pairs(head_count, 2))  15.2 us
    all_to_all x1, starting transfers between devices, per_device(): lax.all_to_all(send_k, 'seq', split_axis=0, concat_axis=0, tiled=True)  14.7 us
  transfers between devices with their start and end apart: 9, of which 7 were waited for; matrix products, arithmetic and copies ran while one was open for 25% of the time, Pallas kernels for 0%

profile of v10, /device:TPU:0, one launch (start us, length us, event | category | flops | bytes accessed | tf_op | source)
XLA Modules:
  0.0 441.6 jit_solution(5675911694001803825)
XLA Ops:
  10.0 7.3 %all-to-all-start.1 = ((s32[8,192,1]{1,2,0:T(1,128)}), s32[8,192,1]{1,2,0:T(1,128)S(1)}, u32[]{:S(2)}, u32[]{:S(2)}) async-start(s32[8,192,1]{1,2,0:T(1,128)} %all_to_all.31), calls=%async_computation.1 | async-start | bytes 16384 | tf_op jit(solution)/shard_map/all_to_all | solution.py:90
  36.7 6.6 %gather_fusion.2 = f32[1536,4,128]{2,1,0:T(4,128)} fusion(f32[1024,4,128]{2,1,0:T(4,128)} %get-tuple-element.42, s32[2048]{0:T(1024)S(1)} %pad_clamp_fusion.1), kind=kCustom, calls=%fused_computation.2 | custom fusion | bytes 6297600 | tf_op jit(solution)/shard_map/gather | solution.py:86
  43.2 6.1 %all-to-all-start.2 = ((f32[1536,4,128]{2,1,0:T(4,128)}), f32[1536,4,128]{2,1,0:T(4,128)}, u32[]{:S(2)}, u32[]{:S(2)}) async-start(f32[1536,4,128]{2,1,0:T(4,128)} %gather_fusion.2), calls=%async_computation.2 | async-start | bytes 6291456 | tf_op jit(solution)/shard_map/all_to_all | solution.py:102
  49.4 5.6 %gather_fusion.4 = f32[1536,4,128]{2,1,0:T(4,128)} fusion(f32[1024,4,128]{2,1,0:T(4,128)S(1)} %copy-done.4, s32[2048]{0:T(1024)S(1)} %pad_clamp_fusion.1), kind=kCustom, calls=%fused_computation.4 | custom fusion | bytes 6297600 | tf_op jit(solution)/shard_map/gather | solution.py:87
  55.0 64.6 %all-to-all-done.2 = f32[1536,4,128]{2,1,0:T(4,128)} async-done(((f32[1536,4,128]{2,1,0:T(4,128)}), f32[1536,4,128]{2,1,0:T(4,128)}, u32[]{:S(2)}, u32[]{:S(2)}) %all-to-all-start.2) | async-done | bytes 3145760 | tf_op jit(solution)/shard_map/all_to_all | solution.py:102
  119.6 14.7 %all-to-all-start.3 = ((f32[1536,4,128]{2,1,0:T(4,128)}), f32[1536,4,128]{2,1,0:T(4,128)}, u32[]{:S(2)}, u32[]{:S(2)}) async-start(f32[1536,4,128]{2,1,0:T(4,128)} %gather_fusion.4), calls=%async_computation.3 | async-start | bytes 6291456 | tf_op jit(solution)/shard_map/all_to_all | solution.py:106
  142.7 5.6 %gather_fusion = f32[1536,4,128]{2,1,0:T(4,128)} fusion(f32[1024,4,128]{2,1,0:T(4,128)S(1)} %reshape.174, s32[2048]{0:T(1024)S(1)} %pad_clamp_fusion.1), kind=kCustom, calls=%fused_computation | custom fusion | bytes 6297600 | tf_op jit(solution)/shard_map/gather | solution.py:88
  148.3 56.1 %all-to-all-done.3 = f32[1536,4,128]{2,1,0:T(4,128)} async-done(((f32[1536,4,128]{2,1,0:T(4,128)}), f32[1536,4,128]{2,1,0:T(4,128)}, u32[]{:S(2)}, u32[]{:S(2)}) %all-to-all-start.3) | async-done | bytes 3145760 | tf_op jit(solution)/shard_map/all_to_all | solution.py:106
  209.3 6.2 %scatter_custom_fusion.2 = s32[1024]{0:T(1024)S(1)} fusion(s32[1536]{0:T(1024)S(1)} %get-tuple-element.31, s32[1536]{0:T(1024)S(1)} %iota.37, s32[]{:T(128)} %constant.52.clone.1), kind=kCustom, calls=%fused_computation.86 | custom fusion | bytes 4100 | tf_op jit(solution)/shard_map/scatter | solution.py:95
  215.5 15.2 %collective-permute-done = f32[2,512,1024]{2,1,0:T(8,128)} collective-permute-done((f32[2,512,1024]{2,1,0:T(8,128)}, f32[2,512,1024]{2,1,0:T(8,128)}, u32[]{:S(2)}, u32[]{:S(2)}) %collective-permute-start) | collective-permute-done | bytes 4194336 | tf_op jit(solution)/shard_map/ppermute | solution.py:160
  230.7 5.4 %gather_fusion.3 = f32[1024,4,128]{2,1,0:T(4,128)S(1)} fusion(f32[1536,4,128]{2,1,0:T(4,128)} %all-to-all-done.2, s32[1024]{0:T(1024)S(1)} %fusion.37), kind=kCustom, calls=%fused_computation.3 | custom fusion | bytes 4198400 | tf_op jit(solution)/shard_map/gather | solution.py:99
  236.1 9.8 %gather_fusion.5 = f32[1024,4,128]{2,1,0:T(4,128)} fusion(f32[1536,4,128]{2,1,0:T(4,128)} %all-to-all-done.3, s32[1024]{0:T(1024)S(1)} %fusion.37), kind=kCustom, calls=%fused_computation.5 | custom fusion | bytes 4198400 | tf_op jit(solution)/shard_map/gather | solution.py:99
  245.9 10.5 %fusion = (f32[4,1024]{1,0:T(4,128)S(1)}, f32[4,1024,1024]{1,2,0:T(8,128)S(1)}) fusion(pred[1024,1024]{0,1:T(8,128)(4,1)S(1)} %iota_compare_fusion, f32[1024,4,128]{2,1,0:T(4,128)} %gather_fusion.5, f32[1024,4,128]{2,1,0:T(4,128)S(1)} %gather_fusion.3), kind=kOutput, calls=%fused_computation.14 | convolution fusion | flops 3233804288 | bytes 22036480 | tf_op jit(solution)/shard_map/while/body/eval_jaxpr/qhd,khd->hqk/dot_general | solution.py:43
  256.5 5.7 %copy-done = f32[4,1024,1024]{1,2,0:T(8,128)} copy-done((f32[4,1024,1024]{1,2,0:T(8,128)}, f32[4,1024,1024]{1,2,0:T(8,128)S(1)}, u32[]{:S(2)}) %copy-start) | copy-done | bytes 16777240
  265.8 13.0 %all-to-all-done = f32[1536,4,128]{2,1,0:T(4,128)} async-done(((f32[1536,4,128]{2,1,0:T(4,128)}), f32[1536,4,128]{2,1,0:T(4,128)}, u32[]{:S(2)}, u32[]{:S(2)}) %all-to-all-start) | async-done | bytes 3145760 | tf_op jit(solution)/shard_map/all_to_all | solution.py:107
  278.8 5.4 %gather_fusion.1 = f32[1024,4,128]{2,1,0:T(4,128)S(1)} fusion(f32[1536,4,128]{2,1,0:T(4,128)} %all-to-all-done, s32[1024]{0:T(1024)S(1)} %fusion.37), kind=kCustom, calls=%fused_computation.1 | custom fusion | bytes 4198400 | tf_op jit(solution)/shard_map/gather | solution.py:99
  284.3 12.9 %bitcast_divide_fusion = f32[1024,4,128]{0,2,1:T(8,128)} fusion(f32[1024,4]{0,1:T(4,128)S(1)} %bitcast.66, f32[4,1024,1024]{1,2,0:T(8,128)} %copy-done, f32[4,1024]{1,0:T(4,128)S(1)} %get-tuple-element.46, pred[1024,1024]{0,1:T(8,128)(4,1)S(1)} %iota_compare_fusion, f32[1024,4,128]{2,1,0:T(4,128)S(1)} %gather_fusion.1), kind=kOutput, calls=%fused_computation.33 | convolution fusion | flops 3234332672 | bytes 22052864 | tf_op jit(solution)/shard_map/while/body/eval_jaxpr/hqk,khd->qhd/dot_general | solution.py:51
  299.2 5.5 %gather_fusion.6 = f32[1536,4,128]{2,1,0:T(4,128)} fusion(f32[1024,4,128]{2,1,0:T(4,128)S(1)} %copy.19, s32[2048]{0:T(1024)S(1)} %pad_clamp_fusion), kind=kCustom, calls=%fused_computation.6 | custom fusion | bytes 6297600 | tf_op jit(solution)/shard_map/gather | solution.py:110
  309.9 40.7 %all_to_all.38 = f32[1536,2,128]{2,1,0:T(2,128)} all-to-all(f32[1536,2,128]{2,1,0:T(2,128)S(1)} %get-tuple-element.36), channel_id=1, replica_groups=mesh['seq'=8,'head'=4] {'seq'}, dimensions={0} | all-to-all | bytes 3145728 | tf_op jit(solution)/shard_map/all_to_all | solution.py:123
  368.4 16.8 %collective-permute-done.1 = f32[1024,256]{1,0:T(8,128)} collective-permute-done((f32[1024,256]{1,0:T(8,128)}, f32[1024,256]{1,0:T(8,128)}, u32[]{:S(2)}, u32[]{:S(2)}) %collective-permute-start.1) | collective-permute-done | bytes 1048608 | tf_op jit(solution)/shard_map/ppermute | solution.py:128
  385.3 5.5 %convolution_add_fusion.1 = f32[1024,1024]{1,0:T(8,128)} fusion(f32[1024,1024]{1,0:T(8,128)S(1)} %fusion.19, f32[1024,256]{1,0:T(8,128)} %collective-permute-done.1, f32[2,512,1024]{2,1,0:T(8,128)} %collective-permute-done), kind=kOutput, calls=%fused_computation.26 | convolution fusion | flops 1611661312 | bytes 10485760 | tf_op jit(solution)/shard_map/dot_general | solution.py:118
  390.8 5.4 %convolution_add_fusion = f32[1024,1024]{1,0:T(8,128)} fusion(f32[1024,1024]{1,0:T(8,128)S(1)} %fusion.17, f32[1024,256]{1,0:T(8,128)} %collective-permute-done.1, f32[2,512,1024]{2,1,0:T(8,128)} %collective-permute-done), kind=kOutput, calls=%fused_computation.25 | convolution fusion | flops 1611661312 | bytes 10485760 | tf_op jit(solution)/shard_map/dot_general | solution.py:118
  405.7 18.9 %collective-permute-done.2 = f32[1024,256]{1,0:T(8,128)S(1)} collective-permute-done((f32[1024,256]{1,0:T(8,128)}, f32[1024,256]{1,0:T(8,128)S(1)}, u32[]{:S(2)}, u32[]{:S(2)}) %collective-permute-start.2) | collective-permute-done | bytes 1048608 | tf_op jit(solution)/shard_map/ppermute | solution.py:128
  435.2 6.2 %add_add_fusion.1 = f32[1024,1024]{1,0:T(8,128)} fusion(f32[1024,1024]{1,0:T(8,128)} %collective-permute-done.3, f32[1024,1024]{1,0:T(8,128)S(1)} %copy-done.2, f32[1024,1024]{1,0:T(8,128)S(1)} %fusion.15, f32[1024,1024]{1,0:T(8,128)S(1)} %fusion.22), kind=kLoop, calls=%fused_computation.23 | loop fusion | flops 3145728 | bytes 20971520 | tf_op jit(solution)/shard_map/add | solution.py:142
  (62 shorter events, 91.4 us)
Async XLA Ops:
  10.0 33.2 %all-to-all-start.1 = ((s32[8,192,1]{1,2,0:T(1,128)}), s32[8,192,1]{1,2,0:T(1,128)S(1)}, u32[]{:S(2)}, u32[]{:S(2)}) async-start(s32[8,192,1]{1,2,0:T(1,128)} %all_to_all.31), calls=%async_computation.1 | async-start | bytes 16384 | tf_op jit(solution)/shard_map/all_to_all | solution.py:90
  27.5 2.2 copy-start.1
  43.2 6.1 %copy-start.4 = (f32[1024,4,128]{2,1,0:T(4,128)S(1)}, f32[1024,4,128]{2,1,0:T(4,128)}, u32[]{:S(2)}) copy-start(f32[1024,4,128]{2,1,0:T(4,128)} %get-tuple-element.43) | copy-start | bytes 6291460
  43.2 76.4 %all-to-all-start.2 = ((f32[1536,4,128]{2,1,0:T(4,128)}), f32[1536,4,128]{2,1,0:T(4,128)}, u32[]{:S(2)}, u32[]{:S(2)}) async-start(f32[1536,4,128]{2,1,0:T(4,128)} %gather_fusion.2), calls=%async_computation.2 | async-start | bytes 6291456 | tf_op jit(solution)/shard_map/all_to_all | solution.py:102
  119.6 84.7 %all-to-all-start.3 = ((f32[1536,4,128]{2,1,0:T(4,128)}), f32[1536,4,128]{2,1,0:T(4,128)}, u32[]{:S(2)}, u32[]{:S(2)}) async-start(f32[1536,4,128]{2,1,0:T(4,128)} %gather_fusion.4), calls=%async_computation.3 | async-start | bytes 6291456 | tf_op jit(solution)/shard_map/all_to_all | solution.py:106
  139.2 91.5 %collective-permute-start = (f32[2,512,1024]{2,1,0:T(8,128)}, f32[2,512,1024]{2,1,0:T(8,128)}, u32[]{:S(2)}, u32[]{:S(2)}) collective-permute-start(f32[2,512,1024]{2,1,0:T(8,128)} %pad_maximum_fusion), channel_id=1, source_target_pairs={{0,2},{1,3},{2,0},{3,1},{4,6},{5,7},{6,4},{7,5},{8,10},{9,11},{10,... | collective-permute-start | bytes 12582920 | tf_op jit(solution)/shard_map/ppermute | solution.py:160
  204.4 74.4 %all-to-all-start = ((f32[1536,4,128]{2,1,0:T(4,128)}), f32[1536,4,128]{2,1,0:T(4,128)}, u32[]{:S(2)}, u32[]{:S(2)}) async-start(f32[1536,4,128]{2,1,0:T(4,128)} %gather_fusion), calls=%async_computation | async-start | bytes 6291456 | tf_op jit(solution)/shard_map/all_to_all | solution.py:107
  256.5 5.7 %copy-start = (f32[4,1024,1024]{1,2,0:T(8,128)}, f32[4,1024,1024]{1,2,0:T(8,128)S(1)}, u32[]{:S(2)}) copy-start(f32[4,1024,1024]{1,2,0:T(8,128)S(1)} %get-tuple-element.47) | copy-start | bytes 50331652
  350.6 45.6 %all-to-all-start.4 = ((f32[1536,2,128]{2,1,0:T(2,128)}), f32[1536,2,128]{2,1,0:T(2,128)S(1)}, u32[]{:S(2)}, u32[]{:S(2)}) async-start(f32[1536,2,128]{2,1,0:T(2,128)} %get-tuple-element.37), calls=%async_computation.4 | async-start | bytes 3145728 | tf_op jit(solution)/shard_map/all_to_all | solution.py:123
  360.7 24.6 %collective-permute-start.1 = (f32[1024,256]{1,0:T(8,128)}, f32[1024,256]{1,0:T(8,128)}, u32[]{:S(2)}, u32[]{:S(2)}) collective-permute-start(f32[1024,256]{1,0:T(8,128)} %bitcast.53), channel_id=1, source_target_pairs={{0,2},{1,3},{2,0},{3,1},{4,6},{5,7},{6,4},{7,5},{8,10},{9,11},{10,... | collective-permute-start | bytes 3145736 | tf_op jit(solution)/shard_map/ppermute | solution.py:128
  401.0 23.6 %collective-permute-start.2 = (f32[1024,256]{1,0:T(8,128)}, f32[1024,256]{1,0:T(8,128)S(1)}, u32[]{:S(2)}, u32[]{:S(2)}) collective-permute-start(f32[1024,256]{1,0:T(8,128)} %bitcast.52), channel_id=1, source_target_pairs={{0,2},{1,3},{2,0},{3,1},{4,6},{5,7},{6,4},{7,5},{8,10},{9,11},{10,... | collective-permute-start | bytes 3145736 | tf_op jit(solution)/shard_map/ppermute | solution.py:128
  402.5 22.0 %copy-start.3 = (f32[1024,1024]{1,0:T(8,128)S(1)}, f32[1024,1024]{1,0:T(8,128)}, u32[]{:S(2)}) copy-start(f32[1024,1024]{1,0:T(8,128)} %convolution_add_fusion.1) | copy-start | bytes 12582916
  427.9 7.4 %collective-permute-start.3 = (f32[1024,1024]{1,0:T(8,128)S(1)}, f32[1024,1024]{1,0:T(8,128)}, u32[]{:S(2)}, u32[]{:S(2)}) collective-permute-start(f32[1024,1024]{1,0:T(8,128)S(1)} %add_add_fusion), channel_id=1, source_target_pairs={{0,1},{1,0},{2,3},{3,2},{4,5},{5,4},{6,7},{7,6},{8,9},{9,8},{10,11... | collective-permute-start | bytes 12582920 | tf_op jit(solution)/shard_map/ppermute | solution.py:141
  431.0 4.2 copy-start.2

commit v11 on v10

--- a/solution.py
+++ b/solution.py
@@ -99,11 +99,12 @@
         return pieces[where_from]
 
     far_weights = fetch_far_weights(out_weight)
-    first_arrived = lax.all_to_all(send_q, "seq", split_axis=0, concat_axis=0, tiled=True)
-    first_arrived, far_weights = lax.optimization_barrier((first_arrived, far_weights))
+    send_qk = jnp.concatenate([send_q, send_k], 1)
+    arrived_qk = lax.all_to_all(send_qk, "seq", split_axis=0, concat_axis=0, tiled=True)
+    arrived_qk, far_weights = lax.optimization_barrier((arrived_qk, far_weights))
     received = (
-        first_arrived,
-        lax.all_to_all(send_k, "seq", split_axis=0, concat_axis=0, tiled=True),
+        arrived_qk[:, :heads_here],
+        arrived_qk[:, heads_here:],
         lax.all_to_all(send_v, "seq", split_axis=0, concat_axis=0, tiled=True),
     )
     result = attend_local(place(received[0]), place(received[1]), place(received[2]))

time: 441 us -> 452 us (1.025); the launches traced: 442 us -> 448 us
  starting transfers between devices: 41.2 us -> 27 us
  local copies, waits for them, and re-layouts: 93.3 us -> 104 us
    all_to_all x2 -> x1, waiting for transfers between devices: 121 us -> 40.9 us  [per_device(): lax.all_to_all(send_qk, 'seq', split_axis=0, concat_axis=0, tiled=True)]
    ppermute x1, waiting for transfers between devices: 15.2 us -> 73.5 us  [fetch_far_weights(): return lax.ppermute(outgoing, 'head', swap_pairs(head_count, 2))]
    all_to_all x1, waiting for transfers between devices: 13 us -> 38.9 us  [per_device(): lax.all_to_all(send_v, 'seq', split_axis=0, concat_axis=0, tiled=True)]
    all_to_all x2 -> x1, starting transfers between devices: 20.8 us -> 5.16 us  [per_device(): lax.all_to_all(send_qk, 'seq', split_axis=0, concat_axis=0, tiled=True)]
    gather x3, local copies, waits for them, and re-layouts: 20.7 us -> 29.4 us  [place(): return pieces[where_from]]
    slice x1 -> x2, local copies, waits for them, and re-layouts: 0.28 us -> 8.06 us  [the longest x1 7.78 us: per_device(): arrived_qk[:, :heads_here]]
    unnamed x12, local copies, waits for them, and re-layouts: 7.8 us -> 2.1 us
    concatenate x0 -> x1, other arithmetic: none -> 5.18 us  [per_device(): send_qk = jnp.concatenate([send_q, send_k], 1)]
  transfers between devices with their start and end apart: 9 -> 8, of which waited for: 7 -> 6; matrix products, arithmetic and copies ran while one was open for 25% -> 22% of each run, Pallas kernels for 0% -> 0%
where the time goes in v11:
time: 452 us; the launch traced here: 448 us
  waiting for transfers between devices  190 us (42%)
  local copies, waits for them, and re-layouts  104 us (23%)
  matrix products  54.3 us (12%)
  blocking collectives  40.6 us (9%)
  other arithmetic  31.4 us (7%)
  starting transfers between devices  27 us (6%)
    ppermute x1, waiting for transfers between devices, fetch_far_weights(): return lax.ppermute(outgoing, 'head', swap_pairs(head_count, 2))  73.5 us
    all_to_all x1, waiting for transfers between devices, per_device(): lax.all_to_all(send_qk, 'seq', split_axis=0, concat_axis=0, tiled=True)  40.9 us
    all_to_all x1, blocking collectives, exchange(): lax.all_to_all(outgoing[:, lo:hi], 'seq', split_axis=0, concat_axis=0, ti...  40.6 us
    all_to_all x1, waiting for transfers between devices, per_device(): lax.all_to_all(send_v, 'seq', split_axis=0, concat_axis=0, tiled=True)  38.9 us
    ppermute x2, waiting for transfers between devices, half_terms(): far_mixed = lax.ppermute(mixed, 'head', swap_pairs(head_count, 2))  35.7 us
    dot_general x8, matrix products, dot(): jnp.dot(lhs, weight, precision=lax.Precision.HIGH, preferred_element_type...  29.9 us
    gather x3, local copies, waits for them, and re-layouts, place(): return pieces[where_from]  29.4 us
    dot_general x1, matrix products, cluster_attention(): jnp.einsum('hqk,khd->qhd', weights, value_c, precision=lax.Precision.HIGH)  13.3 us
  transfers between devices with their start and end apart: 8, of which 6 were waited for; matrix products, arithmetic and copies ran while one was open for 22% of the time, Pallas kernels for 0%

profile of v11, /device:TPU:0, one launch (start us, length us, event | category | flops | bytes accessed | tf_op | source)
XLA Modules:
  0.0 448.0 jit_solution(11256143531191349441)
XLA Ops:
  10.0 7.3 %all-to-all-start.1 = ((s32[8,192,1]{1,2,0:T(1,128)}), s32[8,192,1]{1,2,0:T(1,128)S(1)}, u32[]{:S(2)}, u32[]{:S(2)}) async-start(s32[8,192,1]{1,2,0:T(1,128)} %all_to_all.27), calls=%async_computation.1 | async-start | bytes 16384 | tf_op jit(solution)/shard_map/all_to_all | solution.py:90
  23.6 5.6 %gather_fusion = f32[1536,4,128]{2,1,0:T(4,128)} fusion(f32[1024,4,128]{2,1,0:T(4,128)S(1)} %reshape.174, s32[2048]{0:T(1024)S(1)} %pad_clamp_fusion.1), kind=kCustom, calls=%fused_computation | custom fusion | bytes 6297600 | tf_op jit(solution)/shard_map/gather | solution.py:88
  29.2 6.4 %all-to-all-start = ((f32[1536,4,128]{2,1,0:T(4,128)}), f32[1536,4,128]{2,1,0:T(4,128)}, u32[]{:S(2)}, u32[]{:S(2)}) async-start(f32[1536,4,128]{2,1,0:T(4,128)} %gather_fusion), calls=%async_computation | async-start | bytes 6291456 | tf_op jit(solution)/shard_map/all_to_all | solution.py:108
  49.5 6.7 %gather_fusion.2 = f32[1536,4,128]{2,1,0:T(4,128)} fusion(f32[1024,4,128]{2,1,0:T(4,128)} %get-tuple-element.44, s32[2048]{0:T(1024)S(1)} %pad_clamp_fusion.1), kind=kCustom, calls=%fused_computation.2 | custom fusion | bytes 6297600 | tf_op jit(solution)/shard_map/gather | solution.py:86
  56.2 5.5 %gather_fusion.3 = f32[1536,4,128]{2,1,0:T(4,128)} fusion(f32[1024,4,128]{2,1,0:T(4,128)S(1)} %copy-done.3, s32[2048]{0:T(1024)S(1)} %pad_clamp_fusion.1), kind=kCustom, calls=%fused_computation.3 | custom fusion | bytes 6297600 | tf_op jit(solution)/shard_map/gather | solution.py:87
  61.7 5.2 %pad_maximum_fusion = f32[1536,8,128]{2,1,0:T(8,128)} fusion(f32[1536,4,128]{2,1,0:T(4,128)} %gather_fusion.3, f32[1536,4,128]{2,1,0:T(4,128)} %gather_fusion.2), kind=kLoop, calls=%fused_computation.21 | loop fusion | flops 1572864 | bytes 12582912 | tf_op jit(solution)/shard_map/concatenate | solution.py:102
  66.8 38.9 %all-to-all-done = f32[1536,4,128]{2,1,0:T(4,128)} async-done(((f32[1536,4,128]{2,1,0:T(4,128)}), f32[1536,4,128]{2,1,0:T(4,128)}, u32[]{:S(2)}, u32[]{:S(2)}) %all-to-all-start) | async-done | bytes 3145760 | tf_op jit(solution)/shard_map/all_to_all | solution.py:108
  117.8 6.2 %scatter_custom_fusion.2 = s32[1024]{0:T(1024)S(1)} fusion(s32[1536]{0:T(1024)S(1)} %get-tuple-element.31, s32[1536]{0:T(1024)S(1)} %iota.37, s32[]{:T(128)} %constant.52.clone.1), kind=kCustom, calls=%fused_computation.87 | custom fusion | bytes 4100 | tf_op jit(solution)/shard_map/scatter | solution.py:95
  124.0 9.8 %gather_fusion.1 = f32[1024,4,128]{2,1,0:T(4,128)} fusion(f32[1536,4,128]{2,1,0:T(4,128)} %all-to-all-done, s32[1024]{0:T(1024)S(1)} %fusion.37), kind=kCustom, calls=%fused_computation.1 | custom fusion | bytes 4198400 | tf_op jit(solution)/shard_map/gather | solution.py:99
  133.8 73.5 %collective-permute-done = f32[2,512,1024]{2,1,0:T(8,128)} collective-permute-done((f32[2,512,1024]{2,1,0:T(8,128)}, f32[2,512,1024]{2,1,0:T(8,128)}, u32[]{:S(2)}, u32[]{:S(2)}) %collective-permute-start) | collective-permute-done | bytes 4194336 | tf_op jit(solution)/shard_map/ppermute | solution.py:161
  207.3 40.9 %all-to-all-done.2 = f32[1536,8,128]{2,1,0:T(8,128)} async-done(((f32[1536,8,128]{2,1,0:T(8,128)}), f32[1536,8,128]{2,1,0:T(8,128)}, u32[]{:S(2)}, u32[]{:S(2)}) %all-to-all-start.2) | async-done | bytes 6291488 | tf_op jit(solution)/shard_map/all_to_all | solution.py:103
  248.2 7.8 %fusion.48 = (f32[1536,4,128]{2,1,0:T(4,128)}, f32[1536,4,128]{2,1,0:T(4,128)}) fusion(f32[1536,8,128]{2,1,0:T(8,128)} %all-to-all-done.2), kind=kLoop, calls=%fused_computation.94 | loop fusion | bytes 12582912 | tf_op jit(solution)/shard_map/slice | solution.py:106
  256.0 9.8 %gather_fusion.4 = f32[1024,4,128]{2,1,0:T(4,128)} fusion(f32[1536,4,128]{2,1,0:T(4,128)} %get-tuple-element.36, s32[1024]{0:T(1024)S(1)} %fusion.37), kind=kCustom, calls=%fused_computation.4 | custom fusion | bytes 4198400 | tf_op jit(solution)/shard_map/gather | solution.py:99
  265.8 9.8 %gather_fusion.5 = f32[1024,4,128]{2,1,0:T(4,128)} fusion(f32[1536,4,128]{2,1,0:T(4,128)} %get-tuple-element.37, s32[1024]{0:T(1024)S(1)} %fusion.37), kind=kCustom, calls=%fused_computation.5 | custom fusion | bytes 4198400 | tf_op jit(solution)/shard_map/gather | solution.py:99
  275.6 11.2 %fusion = (f32[4,1024]{1,0:T(4,128)S(1)}, f32[4,1024,1024]{1,2,0:T(8,128)S(1)}) fusion(pred[1024,1024]{0,1:T(8,128)(4,1)S(1)} %iota_compare_fusion, f32[1024,4,128]{2,1,0:T(4,128)} %gather_fusion.5, f32[1024,4,128]{2,1,0:T(4,128)} %gather_fusion.4), kind=kOutput, calls=%fused_computation.14 | convolution fusion | flops 3233804288 | bytes 22036480 | tf_op jit(solution)/shard_map/while/body/eval_jaxpr/qhd,khd->hqk/dot_general | solution.py:43
  290.5 13.3 %bitcast_divide_fusion = f32[1024,4,128]{0,2,1:T(8,128)} fusion(f32[1024,4]{0,1:T(4,128)S(1)} %bitcast.66, f32[4,1024,1024]{1,2,0:T(8,128)S(1)} %get-tuple-element.49, f32[4,1024]{1,0:T(4,128)S(1)} %get-tuple-element.48, pred[1024,1024]{0,1:T(8,128)(4,1)S(1)} %iota_compare_fusion, f32[1024,4,128]{2,1,0:T(4,128)} %gather_fusion.1), kind=kOutput, calls=%fused_computation.34 | convolution fusion | flops 3234332672 | bytes 22052864 | tf_op jit(solution)/shard_map/while/body/eval_jaxpr/hqk,khd->qhd/dot_general | solution.py:51
  305.8 5.5 %gather_fusion.6 = f32[1536,4,128]{2,1,0:T(4,128)} fusion(f32[1024,4,128]{2,1,0:T(4,128)S(1)} %copy.19, s32[2048]{0:T(1024)S(1)} %pad_clamp_fusion), kind=kCustom, calls=%fused_computation.6 | custom fusion | bytes 6297600 | tf_op jit(solution)/shard_map/gather | solution.py:111
  311.3 5.4 %fusion.49 = (f32[1536,2,128]{2,1,0:T(2,128)S(1)}, f32[1536,2,128]{2,1,0:T(2,128)}) fusion(f32[1536,4,128]{2,1,0:T(4,128)} %gather_fusion.6), kind=kLoop, calls=%fused_computation.95 | loop fusion | bytes 6291456 | tf_op jit(solution)/shard_map/slice | solution.py:124
  316.7 40.6 %all_to_all.33 = f32[1536,2,128]{2,1,0:T(2,128)} all-to-all(f32[1536,2,128]{2,1,0:T(2,128)S(1)} %get-tuple-element.38), channel_id=1, replica_groups=mesh['seq'=8,'head'=4] {'seq'}, dimensions={0} | all-to-all | bytes 3145728 | tf_op jit(solution)/shard_map/all_to_all | solution.py:124
  374.7 16.8 %collective-permute-done.1 = f32[1024,256]{1,0:T(8,128)} collective-permute-done((f32[1024,256]{1,0:T(8,128)}, f32[1024,256]{1,0:T(8,128)}, u32[]{:S(2)}, u32[]{:S(2)}) %collective-permute-start.1) | collective-permute-done | bytes 1048608 | tf_op jit(solution)/shard_map/ppermute | solution.py:129
  391.5 5.5 %convolution_add_fusion.1 = f32[1024,1024]{1,0:T(8,128)} fusion(f32[1024,1024]{1,0:T(8,128)S(1)} %fusion.19, f32[1024,256]{1,0:T(8,128)} %collective-permute-done.1, f32[2,512,1024]{2,1,0:T(8,128)} %collective-permute-done), kind=kOutput, calls=%fused_computation.27 | convolution fusion | flops 1611661312 | bytes 10485760 | tf_op jit(solution)/shard_map/dot_general | solution.py:119
  397.0 5.4 %convolution_add_fusion = f32[1024,1024]{1,0:T(8,128)} fusion(f32[1024,1024]{1,0:T(8,128)S(1)} %fusion.17, f32[1024,256]{1,0:T(8,128)} %collective-permute-done.1, f32[2,512,1024]{2,1,0:T(8,128)} %collective-permute-done), kind=kOutput, calls=%fused_computation.26 | convolution fusion | flops 1611661312 | bytes 10485760 | tf_op jit(solution)/shard_map/dot_general | solution.py:119
  412.0 18.8 %collective-permute-done.2 = f32[1024,256]{1,0:T(8,128)S(1)} collective-permute-done((f32[1024,256]{1,0:T(8,128)}, f32[1024,256]{1,0:T(8,128)S(1)}, u32[]{:S(2)}, u32[]{:S(2)}) %collective-permute-start.2) | collective-permute-done | bytes 1048608 | tf_op jit(solution)/shard_map/ppermute | solution.py:129
  441.5 6.2 %add_add_fusion.1 = f32[1024,1024]{1,0:T(8,128)} fusion(f32[1024,1024]{1,0:T(8,128)} %collective-permute-done.3, f32[1024,1024]{1,0:T(8,128)S(1)} %copy-done.1, f32[1024,1024]{1,0:T(8,128)S(1)} %fusion.15, f32[1024,1024]{1,0:T(8,128)S(1)} %fusion.22), kind=kLoop, calls=%fused_computation.24 | loop fusion | flops 3145728 | bytes 20971520 | tf_op jit(solution)/shard_map/add | solution.py:143
  (62 shorter events, 85.4 us)
Async XLA Ops:
  10.0 19.2 %all-to-all-start.1 = ((s32[8,192,1]{1,2,0:T(1,128)}), s32[8,192,1]{1,2,0:T(1,128)S(1)}, u32[]{:S(2)}, u32[]{:S(2)}) async-start(s32[8,192,1]{1,2,0:T(1,128)} %all_to_all.27), calls=%async_computation.1 | async-start | bytes 16384 | tf_op jit(solution)/shard_map/all_to_all | solution.py:90
  29.2 6.4 %copy-start.4 = (s32[1024]{0:T(1024)S(1)}, s32[1024]{0:T(1024)}, u32[]{:S(2)}) copy-start(s32[1024]{0:T(1024)} %param.10) | copy-start | bytes 12292
  29.2 76.5 %all-to-all-start = ((f32[1536,4,128]{2,1,0:T(4,128)}), f32[1536,4,128]{2,1,0:T(4,128)}, u32[]{:S(2)}, u32[]{:S(2)}) async-start(f32[1536,4,128]{2,1,0:T(4,128)} %gather_fusion), calls=%async_computation | async-start | bytes 6291456 | tf_op jit(solution)/shard_map/all_to_all | solution.py:108
  40.4 2.3 copy-start
  49.5 6.7 %copy-start.3 = (f32[1024,4,128]{2,1,0:T(4,128)S(1)}, f32[1024,4,128]{2,1,0:T(4,128)}, u32[]{:S(2)}) copy-start(f32[1024,4,128]{2,1,0:T(4,128)} %get-tuple-element.45) | copy-start | bytes 6291460
  105.8 142.5 %all-to-all-start.2 = ((f32[1536,8,128]{2,1,0:T(8,128)}), f32[1536,8,128]{2,1,0:T(8,128)}, u32[]{:S(2)}, u32[]{:S(2)}) async-start(f32[1536,8,128]{2,1,0:T(8,128)} %pad_maximum_fusion), calls=%async_computation.2 | async-start | bytes 12582912 | tf_op jit(solution)/shard_map/all_to_all | solution.py:103
  115.8 91.5 %collective-permute-start = (f32[2,512,1024]{2,1,0:T(8,128)}, f32[2,512,1024]{2,1,0:T(8,128)}, u32[]{:S(2)}, u32[]{:S(2)}) collective-permute-start(f32[2,512,1024]{2,1,0:T(8,128)} %pad_maximum_fusion.1), channel_id=1, source_target_pairs={{0,2},{1,3},{2,0},{3,1},{4,6},{5,7},{6,4},{7,5},{8,10},{9,11},{10,... | collective-permute-start | bytes 12582920 | tf_op jit(solution)/shard_map/ppermute | solution.py:161
  357.3 45.2 %all-to-all-start.3 = ((f32[1536,2,128]{2,1,0:T(2,128)}), f32[1536,2,128]{2,1,0:T(2,128)S(1)}, u32[]{:S(2)}, u32[]{:S(2)}) async-start(f32[1536,2,128]{2,1,0:T(2,128)} %get-tuple-element.39), calls=%async_computation.3 | async-start | bytes 3145728 | tf_op jit(solution)/shard_map/all_to_all | solution.py:124
  366.9 24.6 %collective-permute-start.1 = (f32[1024,256]{1,0:T(8,128)}, f32[1024,256]{1,0:T(8,128)}, u32[]{:S(2)}, u32[]{:S(2)}) collective-permute-start(f32[1024,256]{1,0:T(8,128)} %bitcast.53), channel_id=1, source_target_pairs={{0,2},{1,3},{2,0},{3,1},{4,6},{5,7},{6,4},{7,5},{8,10},{9,11},{10,... | collective-permute-start | bytes 3145736 | tf_op jit(solution)/shard_map/ppermute | solution.py:129
  407.3 23.6 %collective-permute-start.2 = (f32[1024,256]{1,0:T(8,128)}, f32[1024,256]{1,0:T(8,128)S(1)}, u32[]{:S(2)}, u32[]{:S(2)}) collective-permute-start(f32[1024,256]{1,0:T(8,128)} %bitcast.52), channel_id=1, source_target_pairs={{0,2},{1,3},{2,0},{3,1},{4,6},{5,7},{6,4},{7,5},{8,10},{9,11},{10,... | collective-permute-start | bytes 3145736 | tf_op jit(solution)/shard_map/ppermute | solution.py:129
  408.8 22.0 %copy-start.2 = (f32[1024,1024]{1,0:T(8,128)S(1)}, f32[1024,1024]{1,0:T(8,128)}, u32[]{:S(2)}) copy-start(f32[1024,1024]{1,0:T(8,128)} %convolution_add_fusion.1) | copy-start | bytes 12582916
  434.2 7.4 %collective-permute-start.3 = (f32[1024,1024]{1,0:T(8,128)S(1)}, f32[1024,1024]{1,0:T(8,128)}, u32[]{:S(2)}, u32[]{:S(2)}) collective-permute-start(f32[1024,1024]{1,0:T(8,128)S(1)} %add_add_fusion), channel_id=1, source_target_pairs={{0,1},{1,0},{2,3},{3,2},{4,5},{5,4},{6,7},{7,6},{8,9},{9,8},{10,11... | collective-permute-start | bytes 12582920 | tf_op jit(solution)/shard_map/ppermute | solution.py:142
  437.3 4.2 copy-start.1

commit v12 on v10

--- a/solution.py
+++ b/solution.py
@@ -78,16 +78,15 @@
         .at[send_row]
         .set(jnp.arange(row_count, dtype=jnp.int32))
     )
-    cos_table, sin_table = yarn_tables(positions, DH)
     shaped = (row_count, heads_here, DH)
-    rot_q = rotate(queries.reshape(shaped), cos_table, sin_table)
-    rot_k = rotate(keys.reshape(shaped), cos_table, sin_table)
     send_from = jnp.minimum(source_token, row_count - 1)
-    send_q = rot_q[send_from]
-    send_k = rot_k[send_from]
+    send_q = queries.reshape(shaped)[send_from]
+    send_k = keys.reshape(shaped)[send_from]
     send_v = values.reshape(shaped)[send_from]
     slot_rows = jnp.full((buffer_rows,), row_count, jnp.int32).at[send_row].set(target_row)
-    arrived = lax.all_to_all(slot_rows, "seq", split_axis=0, concat_axis=0, tiled=True)
+    index_rows = jnp.stack([slot_rows, positions[send_from]], 1)
+    arrived_index = lax.all_to_all(index_rows, "seq", split_axis=0, concat_axis=0, tiled=True)
+    arrived = arrived_index[:, 0]
     picked = jnp.minimum(arrived, row_count - 1)
     where_from = (
         jnp.zeros((row_count,), jnp.int32)
@@ -106,7 +105,12 @@
         lax.all_to_all(send_k, "seq", split_axis=0, concat_axis=0, tiled=True),
         lax.all_to_all(send_v, "seq", split_axis=0, concat_axis=0, tiled=True),
     )
-    result = attend_local(place(received[0]), place(received[1]), place(received[2]))
+    cos_table, sin_table = yarn_tables(place(arrived_index[:, 1]), DH)
+    result = attend_local(
+        rotate(place(received[0]), cos_table, sin_table),
+        rotate(place(received[1]), cos_table, sin_table),
+        place(received[2]),
+    )
     outgoing = result[picked]
     split = heads_here // 2
     head_count = lax.axis_size("head")

time: 441 us -> 432 us (0.980); the launches traced: 442 us -> 424 us
  waiting for transfers between devices: 186 us -> 167 us
  local copies, waits for them, and re-layouts: 93.3 us -> 104 us
  starting transfers between devices: 41.2 us -> 30.6 us
    all_to_all x1, starting transfers between devices: 14.7 us -> 4.44 us  [per_device(): lax.all_to_all(send_k, 'seq', split_axis=0, concat_axis=0, tiled=True)]
    ppermute x1, waiting for transfers between devices: 15.2 us -> 5.58 us  [fetch_far_weights(): return lax.ppermute(outgoing, 'head', swap_pairs(head_count, 2))]
    all_to_all x1, waiting for transfers between devices: 13 us -> 6.05 us  [per_device(): lax.all_to_all(send_v, 'seq', split_axis=0, concat_axis=0, tiled=True)]
    gather x3 -> x4, local copies, waits for them, and re-layouts: 20.7 us -> 26.8 us  [place(): return pieces[where_from]]
    gather x2 -> x3, local copies, waits for them, and re-layouts: 12.2 us -> 16.9 us  [the longest x1 5.84 us: per_device(): index_rows = jnp.stack([slot_rows, positions[send_from]], 1)]
  transfers between devices with their start and end apart: 9 -> 9, of which waited for: 7 -> 7; matrix products, arithmetic and copies ran while one was open for 25% -> 26% of each run, Pallas kernels for 0% -> 0%
where the time goes in v12:
time: 432 us; the launch traced here: 424 us
  waiting for transfers between devices  167 us (39%)
  local copies, waits for them, and re-layouts  104 us (24%)
  matrix products  52.6 us (12%)
  blocking collectives  40.7 us (9%)
  starting transfers between devices  30.6 us (7%)
  other arithmetic  28.5 us (7%)
    all_to_all x1, waiting for transfers between devices, per_device(): lax.all_to_all(send_q, 'seq', split_axis=0, concat_axis=0, tiled=True)  62.7 us
    all_to_all x1, waiting for transfers between devices, per_device(): lax.all_to_all(send_k, 'seq', split_axis=0, concat_axis=0, tiled=True)  56.3 us
    all_to_all x1, blocking collectives, exchange(): lax.all_to_all(outgoing[:, lo:hi], 'seq', split_axis=0, concat_axis=0, ti...  40.7 us
    ppermute x2, waiting for transfers between devices, half_terms(): far_mixed = lax.ppermute(mixed, 'head', swap_pairs(head_count, 2))  35.6 us
    dot_general x8, matrix products, dot(): jnp.dot(lhs, weight, precision=lax.Precision.HIGH, preferred_element_type...  30.4 us
    gather x4, local copies, waits for them, and re-layouts, place(): return pieces[where_from]  26.8 us
    dot_general x1, matrix products, cluster_attention(): jnp.einsum('hqk,khd->qhd', weights, value_c, precision=lax.Precision.HIGH)  13.2 us
    dot_general x1, matrix products, cluster_attention(): jnp.einsum('qhd,khd->hqk', query_c, key_c, precision=lax.Precision.HIGH)  9 us
  transfers between devices with their start and end apart: 9, of which 7 were waited for; matrix products, arithmetic and copies ran while one was open for 26% of the time, Pallas kernels for 0%

profile of v12, /device:TPU:0, one launch (start us, length us, event | category | flops | bytes accessed | tf_op | source)
XLA Modules:
  0.0 423.9 jit_solution(15850183737435868022)
XLA Ops:
  13.8 5.8 %gather_fusion.1 = s32[1536]{0:T(1024)S(1)} fusion(s32[1024]{0:T(1024)S(1)} %copy-done, s32[2048]{0:T(1024)S(1)} %pad_clamp_fusion.1), kind=kCustom, calls=%fused_computation.1 | custom fusion | bytes 18432 | tf_op jit(solution)/shard_map/gather | solution.py:87
  20.3 7.3 %all-to-all-start.1 = ((s32[8,192,2]{1,2,0:T(2,128)}), s32[8,192,2]{1,2,0:T(2,128)S(1)}, u32[]{:S(2)}, u32[]{:S(2)}) async-start(s32[8,192,2]{1,2,0:T(2,128)} %copy.20), calls=%async_computation.1 | async-start | bytes 32768 | tf_op jit(solution)/shard_map/all_to_all | solution.py:88
  29.5 5.5 %gather_fusion.3 = f32[1536,4,128]{2,1,0:T(4,128)} fusion(f32[1024,4,128]{2,1,0:T(4,128)S(1)} %reshape.135, s32[2048]{0:T(1024)S(1)} %pad_clamp_fusion.1), kind=kCustom, calls=%fused_computation.3 | custom fusion | bytes 6297600 | tf_op jit(solution)/shard_map/gather | solution.py:83
  35.0 6.0 %all-to-all-start.2 = ((f32[1536,4,128]{2,1,0:T(4,128)}), f32[1536,4,128]{2,1,0:T(4,128)}, u32[]{:S(2)}, u32[]{:S(2)}) async-start(f32[1536,4,128]{2,1,0:T(4,128)} %gather_fusion.3), calls=%async_computation.2 | async-start | bytes 6291456 | tf_op jit(solution)/shard_map/all_to_all | solution.py:101
  43.0 5.6 %gather_fusion.6 = f32[1536,4,128]{2,1,0:T(4,128)} fusion(f32[1024,4,128]{2,1,0:T(4,128)S(1)} %reshape.136, s32[2048]{0:T(1024)S(1)} %pad_clamp_fusion.1), kind=kCustom, calls=%fused_computation.6 | custom fusion | bytes 6297600 | tf_op jit(solution)/shard_map/gather | solution.py:84
  48.6 62.7 %all-to-all-done.2 = f32[1536,4,128]{2,1,0:T(4,128)} async-done(((f32[1536,4,128]{2,1,0:T(4,128)}), f32[1536,4,128]{2,1,0:T(4,128)}, u32[]{:S(2)}, u32[]{:S(2)}) %all-to-all-start.2) | async-done | bytes 3145760 | tf_op jit(solution)/shard_map/all_to_all | solution.py:101
  124.1 5.6 %gather_fusion = f32[1536,4,128]{2,1,0:T(4,128)} fusion(f32[1024,4,128]{2,1,0:T(4,128)S(1)} %reshape.133, s32[2048]{0:T(1024)S(1)} %pad_clamp_fusion.1), kind=kCustom, calls=%fused_computation | custom fusion | bytes 6297600 | tf_op jit(solution)/shard_map/gather | solution.py:85
  129.6 56.3 %all-to-all-done.3 = f32[1536,4,128]{2,1,0:T(4,128)} async-done(((f32[1536,4,128]{2,1,0:T(4,128)}), f32[1536,4,128]{2,1,0:T(4,128)}, u32[]{:S(2)}, u32[]{:S(2)}) %all-to-all-start.3) | async-done | bytes 3145760 | tf_op jit(solution)/shard_map/all_to_all | solution.py:105
  190.9 6.4 %scatter_custom_fusion.2 = s32[1024]{0:T(1024)S(1)} fusion(s32[1536]{0:T(1024)S(1)} %get-tuple-element.31, s32[1536]{0:T(1024)S(1)} %iota.37, s32[]{:T(128)} %constant.52.clone.1), kind=kCustom, calls=%fused_computation.90 | custom fusion | bytes 4100 | tf_op jit(solution)/shard_map/scatter | solution.py:94
  197.3 6.2 %gather_fusion.5 = s32[1024]{0:T(1024)S(1)} fusion(s32[1536]{0:T(1024)S(1)} %get-tuple-element.32, s32[1024]{0:T(1024)S(1)} %fusion.37), kind=kCustom, calls=%fused_computation.5 | custom fusion | bytes 12288 | tf_op jit(solution)/shard_map/gather | solution.py:98
  206.7 5.6 %collective-permute-done = f32[2,512,1024]{2,1,0:T(8,128)} collective-permute-done((f32[2,512,1024]{2,1,0:T(8,128)}, f32[2,512,1024]{2,1,0:T(8,128)}, u32[]{:S(2)}, u32[]{:S(2)}) %collective-permute-start) | collective-permute-done | bytes 4194336 | tf_op jit(solution)/shard_map/ppermute | solution.py:164
  212.3 5.4 %gather_fusion.4 = f32[1024,4,128]{2,1,0:T(4,128)S(1)} fusion(f32[1536,4,128]{2,1,0:T(4,128)} %all-to-all-done.2, s32[1024]{0:T(1024)S(1)} %fusion.37), kind=kCustom, calls=%fused_computation.4 | custom fusion | bytes 4198400 | tf_op jit(solution)/shard_map/gather | solution.py:98
  217.7 9.8 %gather_fusion.7 = f32[1024,4,128]{2,1,0:T(4,128)} fusion(f32[1536,4,128]{2,1,0:T(4,128)} %all-to-all-done.3, s32[1024]{0:T(1024)S(1)} %fusion.37), kind=kCustom, calls=%fused_computation.7 | custom fusion | bytes 4198400 | tf_op jit(solution)/shard_map/gather | solution.py:98
  236.2 9.0 %fusion = (f32[4,1024]{1,0:T(4,128)S(1)}, f32[4,1024,1024]{1,2,0:T(8,128)S(1)}) fusion(pred[1024,1024]{0,1:T(8,128)(4,1)S(1)} %iota_compare_fusion, f32[1024,4,128]{2,1,0:T(4,128)S(1)} %get-tuple-element.44, f32[1024,4,128]{2,1,0:T(4,128)S(1)} %get-tuple-element.43), kind=kOutput, calls=%fused_computation.16 | convolution fusion | flops 3233804288 | bytes 22036480 | tf_op jit(solution)/shard_map/while/body/eval_jaxpr/qhd,khd->hqk/dot_general | solution.py:43
  245.2 5.7 %copy-done.2 = f32[4,1024,1024]{1,2,0:T(8,128)} copy-done((f32[4,1024,1024]{1,2,0:T(8,128)}, f32[4,1024,1024]{1,2,0:T(8,128)S(1)}, u32[]{:S(2)}) %copy-start.2) | copy-done | bytes 16777240
  254.5 6.1 %all-to-all-done = f32[1536,4,128]{2,1,0:T(4,128)} async-done(((f32[1536,4,128]{2,1,0:T(4,128)}), f32[1536,4,128]{2,1,0:T(4,128)}, u32[]{:S(2)}, u32[]{:S(2)}) %all-to-all-start) | async-done | bytes 3145760 | tf_op jit(solution)/shard_map/all_to_all | solution.py:106
  266.0 13.2 %bitcast_divide_fusion = f32[1024,4,128]{0,2,1:T(8,128)} fusion(f32[1024,4]{0,1:T(4,128)S(1)} %bitcast.68, f32[4,1024,1024]{1,2,0:T(8,128)} %copy-done.2, f32[4,1024]{1,0:T(4,128)S(1)} %get-tuple-element.47, pred[1024,1024]{0,1:T(8,128)(4,1)S(1)} %iota_compare_fusion, f32[1024,4,128]{2,1,0:T(4,128)S(1)} %gather_fusion.2), kind=kOutput, calls=%fused_computation.35 | convolution fusion | flops 3234332672 | bytes 22052864 | tf_op jit(solution)/shard_map/while/body/eval_jaxpr/hqk,khd->qhd/dot_general | solution.py:51
  281.2 5.5 %gather_fusion.8 = f32[1536,4,128]{2,1,0:T(4,128)} fusion(f32[1024,4,128]{2,1,0:T(4,128)S(1)} %copy.26, s32[2048]{0:T(1024)S(1)} %pad_clamp_fusion), kind=kCustom, calls=%fused_computation.8 | custom fusion | bytes 6297600 | tf_op jit(solution)/shard_map/gather | solution.py:114
  292.0 40.7 %all_to_all.34 = f32[1536,2,128]{2,1,0:T(2,128)} all-to-all(f32[1536,2,128]{2,1,0:T(2,128)S(1)} %get-tuple-element.37), channel_id=1, replica_groups=mesh['seq'=8,'head'=4] {'seq'}, dimensions={0} | all-to-all | bytes 3145728 | tf_op jit(solution)/shard_map/all_to_all | solution.py:127
  350.2 16.8 %collective-permute-done.1 = f32[1024,256]{1,0:T(8,128)} collective-permute-done((f32[1024,256]{1,0:T(8,128)}, f32[1024,256]{1,0:T(8,128)}, u32[]{:S(2)}, u32[]{:S(2)}) %collective-permute-start.1) | collective-permute-done | bytes 1048608 | tf_op jit(solution)/shard_map/ppermute | solution.py:132
  367.0 5.5 %convolution_add_fusion.1 = f32[1024,1024]{1,0:T(8,128)} fusion(f32[1024,1024]{1,0:T(8,128)S(1)} %fusion.19, f32[1024,256]{1,0:T(8,128)} %collective-permute-done.1, f32[2,512,1024]{2,1,0:T(8,128)} %collective-permute-done), kind=kOutput, calls=%fused_computation.28 | convolution fusion | flops 1611661312 | bytes 10485760 | tf_op jit(solution)/shard_map/dot_general | solution.py:122
  372.6 5.4 %convolution_add_fusion = f32[1024,1024]{1,0:T(8,128)} fusion(f32[1024,1024]{1,0:T(8,128)S(1)} %fusion.17, f32[1024,256]{1,0:T(8,128)} %collective-permute-done.1, f32[2,512,1024]{2,1,0:T(8,128)} %collective-permute-done), kind=kOutput, calls=%fused_computation.27 | convolution fusion | flops 1611661312 | bytes 10485760 | tf_op jit(solution)/shard_map/dot_general | solution.py:122
  387.6 18.8 %collective-permute-done.2 = f32[1024,256]{1,0:T(8,128)S(1)} collective-permute-done((f32[1024,256]{1,0:T(8,128)}, f32[1024,256]{1,0:T(8,128)S(1)}, u32[]{:S(2)}, u32[]{:S(2)}) %collective-permute-start.2) | collective-permute-done | bytes 1048608 | tf_op jit(solution)/shard_map/ppermute | solution.py:132
  417.4 6.3 %add_add_fusion.1 = f32[1024,1024]{1,0:T(8,128)} fusion(f32[1024,1024]{1,0:T(8,128)} %collective-permute-done.3, f32[1024,1024]{1,0:T(8,128)S(1)} %copy-done.4, f32[1024,1024]{1,0:T(8,128)S(1)} %fusion.15, f32[1024,1024]{1,0:T(8,128)S(1)} %fusion.22), kind=kLoop, calls=%fused_computation.25 | loop fusion | flops 3145728 | bytes 20971520 | tf_op jit(solution)/shard_map/add | solution.py:146
  (74 shorter events, 102.2 us)
Async XLA Ops:
  0.0 13.8 %copy-start = (s32[1024]{0:T(1024)S(1)}, s32[1024]{0:T(1024)}, u32[]{:S(2)}) copy-start(s32[1024]{0:T(1024)} %param.10) | copy-start | bytes 12292
  20.3 14.7 %all-to-all-start.1 = ((s32[8,192,2]{1,2,0:T(2,128)}), s32[8,192,2]{1,2,0:T(2,128)S(1)}, u32[]{:S(2)}, u32[]{:S(2)}) async-start(s32[8,192,2]{1,2,0:T(2,128)} %copy.20), calls=%async_computation.1 | async-start | bytes 32768 | tf_op jit(solution)/shard_map/all_to_all | solution.py:88
  35.0 76.3 %all-to-all-start.2 = ((f32[1536,4,128]{2,1,0:T(4,128)}), f32[1536,4,128]{2,1,0:T(4,128)}, u32[]{:S(2)}, u32[]{:S(2)}) async-start(f32[1536,4,128]{2,1,0:T(4,128)} %gather_fusion.3), calls=%async_computation.2 | async-start | bytes 6291456 | tf_op jit(solution)/shard_map/all_to_all | solution.py:101
  111.3 74.6 %all-to-all-start.3 = ((f32[1536,4,128]{2,1,0:T(4,128)}), f32[1536,4,128]{2,1,0:T(4,128)}, u32[]{:S(2)}, u32[]{:S(2)}) async-start(f32[1536,4,128]{2,1,0:T(4,128)} %gather_fusion.6), calls=%async_computation.3 | async-start | bytes 6291456 | tf_op jit(solution)/shard_map/all_to_all | solution.py:105
  120.6 91.7 %collective-permute-start = (f32[2,512,1024]{2,1,0:T(8,128)}, f32[2,512,1024]{2,1,0:T(8,128)}, u32[]{:S(2)}, u32[]{:S(2)}) collective-permute-start(f32[2,512,1024]{2,1,0:T(8,128)} %pad_maximum_fusion), channel_id=1, source_target_pairs={{0,2},{1,3},{2,0},{3,1},{4,6},{5,7},{6,4},{7,5},{8,10},{9,11},{10,... | collective-permute-start | bytes 12582920 | tf_op jit(solution)/shard_map/ppermute | solution.py:164
  185.9 74.6 %all-to-all-start = ((f32[1536,4,128]{2,1,0:T(4,128)}), f32[1536,4,128]{2,1,0:T(4,128)}, u32[]{:S(2)}, u32[]{:S(2)}) async-start(f32[1536,4,128]{2,1,0:T(4,128)} %gather_fusion), calls=%async_computation | async-start | bytes 6291456 | tf_op jit(solution)/shard_map/all_to_all | solution.py:106
  231.0 1.6 copy-start.3
  231.0 1.7 copy-start.6
  231.0 1.8 copy-start.7
  245.2 5.7 %copy-start.2 = (f32[4,1024,1024]{1,2,0:T(8,128)}, f32[4,1024,1024]{1,2,0:T(8,128)S(1)}, u32[]{:S(2)}) copy-start(f32[4,1024,1024]{1,2,0:T(8,128)S(1)} %get-tuple-element.48) | copy-start | bytes 50331652
  332.6 45.4 %all-to-all-start.4 = ((f32[1536,2,128]{2,1,0:T(2,128)}), f32[1536,2,128]{2,1,0:T(2,128)S(1)}, u32[]{:S(2)}, u32[]{:S(2)}) async-start(f32[1536,2,128]{2,1,0:T(2,128)} %get-tuple-element.38), calls=%async_computation.4 | async-start | bytes 3145728 | tf_op jit(solution)/shard_map/all_to_all | solution.py:127
  342.5 24.6 %collective-permute-start.1 = (f32[1024,256]{1,0:T(8,128)}, f32[1024,256]{1,0:T(8,128)}, u32[]{:S(2)}, u32[]{:S(2)}) collective-permute-start(f32[1024,256]{1,0:T(8,128)} %bitcast.55), channel_id=1, source_target_pairs={{0,2},{1,3},{2,0},{3,1},{4,6},{5,7},{6,4},{7,5},{8,10},{9,11},{10,... | collective-permute-start | bytes 3145736 | tf_op jit(solution)/shard_map/ppermute | solution.py:132
  382.9 23.6 %collective-permute-start.2 = (f32[1024,256]{1,0:T(8,128)}, f32[1024,256]{1,0:T(8,128)S(1)}, u32[]{:S(2)}, u32[]{:S(2)}) collective-permute-start(f32[1024,256]{1,0:T(8,128)} %bitcast.54), channel_id=1, source_target_pairs={{0,2},{1,3},{2,0},{3,1},{4,6},{5,7},{6,4},{7,5},{8,10},{9,11},{10,... | collective-permute-start | bytes 3145736 | tf_op jit(solution)/shard_map/ppermute | solution.py:132
  384.4 22.0 %copy-start.5 = (f32[1024,1024]{1,0:T(8,128)S(1)}, f32[1024,1024]{1,0:T(8,128)}, u32[]{:S(2)}) copy-start(f32[1024,1024]{1,0:T(8,128)} %convolution_add_fusion.1) | copy-start | bytes 12582916
  410.0 7.4 %collective-permute-start.3 = (f32[1024,1024]{1,0:T(8,128)S(1)}, f32[1024,1024]{1,0:T(8,128)}, u32[]{:S(2)}, u32[]{:S(2)}) collective-permute-start(f32[1024,1024]{1,0:T(8,128)S(1)} %add_add_fusion), channel_id=1, source_target_pairs={{0,1},{1,0},{2,3},{3,2},{4,5},{5,4},{6,7},{7,6},{8,9},{9,8},{10,11... | collective-permute-start | bytes 12582920 | tf_op jit(solution)/shard_map/ppermute | solution.py:145
  413.2 4.2 copy-start.4
  417.4 6.3 %copy-start.1 = (s32[1024]{0:T(1024)S(1)}, s32[1024]{0:T(1024)}, u32[]{:S(2)}) copy-start(s32[1024]{0:T(1024)} %param.10) | copy-start | bytes 12292

commit v13 on v12

--- a/solution.py
+++ b/solution.py
@@ -83,8 +83,11 @@
     send_q = queries.reshape(shaped)[send_from]
     send_k = keys.reshape(shaped)[send_from]
     send_v = values.reshape(shaped)[send_from]
-    slot_rows = jnp.full((buffer_rows,), row_count, jnp.int32).at[send_row].set(target_row)
-    index_rows = jnp.stack([slot_rows, positions[send_from]], 1)
+    index_rows = (
+        jnp.full((buffer_rows, 2), row_count, jnp.int32)
+        .at[send_row]
+        .set(jnp.stack([target_row, positions], 1))
+    )
     arrived_index = lax.all_to_all(index_rows, "seq", split_axis=0, concat_axis=0, tiled=True)
     arrived = arrived_index[:, 0]
     picked = jnp.minimum(arrived, row_count - 1)

time: 432 us -> 425 us (0.984)
  local copies, waits for them, and re-layouts: 104 us -> 97.2 us
    gather x1 -> x0, local copies, waits for them, and re-layouts: 5.84 us -> none  [per_device(): index_rows = jnp.stack([slot_rows, positions[send_from]], 1)]
  transfers between devices with their start and end apart: 9 -> 9, of which waited for: 7 -> 7; matrix products, arithmetic and copies ran while one was open for 26% -> 28% of each run, Pallas kernels for 0% -> 0%
where the time goes in v13:
time: 425 us; the launch traced here: 418 us
  waiting for transfers between devices  167 us (39%)
  local copies, waits for them, and re-layouts  97.2 us (23%)
  matrix products  52 us (12%)
  blocking collectives  40.7 us (10%)
  starting transfers between devices  30.6 us (7%)
  other arithmetic  29.1 us (7%)
    all_to_all x1, waiting for transfers between devices, per_device(): lax.all_to_all(send_q, 'seq', split_axis=0, concat_axis=0, tiled=True)  62.7 us
    all_to_all x1, waiting for transfers between devices, per_device(): lax.all_to_all(send_k, 'seq', split_axis=0, concat_axis=0, tiled=True)  56.3 us
    all_to_all x1, blocking collectives, exchange(): lax.all_to_all(outgoing[:, lo:hi], 'seq', split_axis=0, concat_axis=0, ti...  40.7 us
    ppermute x2, waiting for transfers between devices, half_terms(): far_mixed = lax.ppermute(mixed, 'head', swap_pairs(head_count, 2))  35.7 us
    dot_general x8, matrix products, dot(): jnp.dot(lhs, weight, precision=lax.Precision.HIGH, preferred_element_type...  29.9 us
    gather x4, local copies, waits for them, and re-layouts, place(): return pieces[where_from]  26.8 us
    dot_general x1, matrix products, cluster_attention(): jnp.einsum('hqk,khd->qhd', weights, value_c, precision=lax.Precision.HIGH)  13.2 us
    dot_general x1, matrix products, cluster_attention(): jnp.einsum('qhd,khd->hqk', query_c, key_c, precision=lax.Precision.HIGH)  8.98 us
  transfers between devices with their start and end apart: 9, of which 7 were waited for; matrix products, arithmetic and copies ran while one was open for 28% of the time, Pallas kernels for 0%

profile of v13, /device:TPU:0, one launch (start us, length us, event | category | flops | bytes accessed | tf_op | source)
XLA Modules:
  0.0 417.5 jit_solution(3186655191582792988)
XLA Ops:
  10.0 7.3 %all-to-all-start.1 = ((s32[8,192,2]{1,2,0:T(2,128)}), s32[8,192,2]{1,2,0:T(2,128)S(1)}, u32[]{:S(2)}, u32[]{:S(2)}) async-start(s32[8,192,2]{1,2,0:T(2,128)} %copy.29), calls=%async_computation.1 | async-start | bytes 32768 | tf_op jit(solution)/shard_map/all_to_all | solution.py:91
  23.6 5.5 %gather_fusion.2 = f32[1536,4,128]{2,1,0:T(4,128)} fusion(f32[1024,4,128]{2,1,0:T(4,128)S(1)} %reshape.131, s32[2048]{0:T(1024)S(1)} %pad_clamp_fusion.1), kind=kCustom, calls=%fused_computation.2 | custom fusion | bytes 6297600 | tf_op jit(solution)/shard_map/gather | solution.py:83
  29.1 6.0 %all-to-all-start.2 = ((f32[1536,4,128]{2,1,0:T(4,128)}), f32[1536,4,128]{2,1,0:T(4,128)}, u32[]{:S(2)}, u32[]{:S(2)}) async-start(f32[1536,4,128]{2,1,0:T(4,128)} %gather_fusion.2), calls=%async_computation.2 | async-start | bytes 6291456 | tf_op jit(solution)/shard_map/all_to_all | solution.py:104
  37.0 5.6 %gather_fusion.5 = f32[1536,4,128]{2,1,0:T(4,128)} fusion(f32[1024,4,128]{2,1,0:T(4,128)S(1)} %reshape.132, s32[2048]{0:T(1024)S(1)} %pad_clamp_fusion.1), kind=kCustom, calls=%fused_computation.5 | custom fusion | bytes 6297600 | tf_op jit(solution)/shard_map/gather | solution.py:84
  42.6 62.7 %all-to-all-done.2 = f32[1536,4,128]{2,1,0:T(4,128)} async-done(((f32[1536,4,128]{2,1,0:T(4,128)}), f32[1536,4,128]{2,1,0:T(4,128)}, u32[]{:S(2)}, u32[]{:S(2)}) %all-to-all-start.2) | async-done | bytes 3145760 | tf_op jit(solution)/shard_map/all_to_all | solution.py:104
  118.1 5.6 %gather_fusion = f32[1536,4,128]{2,1,0:T(4,128)} fusion(f32[1024,4,128]{2,1,0:T(4,128)S(1)} %reshape.129, s32[2048]{0:T(1024)S(1)} %pad_clamp_fusion.1), kind=kCustom, calls=%fused_computation | custom fusion | bytes 6297600 | tf_op jit(solution)/shard_map/gather | solution.py:85
  123.7 56.3 %all-to-all-done.3 = f32[1536,4,128]{2,1,0:T(4,128)} async-done(((f32[1536,4,128]{2,1,0:T(4,128)}), f32[1536,4,128]{2,1,0:T(4,128)}, u32[]{:S(2)}, u32[]{:S(2)}) %all-to-all-start.3) | async-done | bytes 3145760 | tf_op jit(solution)/shard_map/all_to_all | solution.py:108
  184.9 6.4 %scatter_custom_fusion.2 = s32[1024]{0:T(1024)S(1)} fusion(s32[1536]{0:T(1024)S(1)} %get-tuple-element.31, s32[1536]{0:T(1024)S(1)} %iota.37, s32[]{:T(128)} %constant.47.clone.1), kind=kCustom, calls=%fused_computation.89 | custom fusion | bytes 4100 | tf_op jit(solution)/shard_map/scatter | solution.py:97
  191.4 6.2 %gather_fusion.4 = s32[1024]{0:T(1024)S(1)} fusion(s32[1536]{0:T(1024)S(1)} %get-tuple-element.32, s32[1024]{0:T(1024)S(1)} %fusion.39), kind=kCustom, calls=%fused_computation.4 | custom fusion | bytes 12288 | tf_op jit(solution)/shard_map/gather | solution.py:101
  200.8 5.6 %collective-permute-done = f32[2,512,1024]{2,1,0:T(8,128)} collective-permute-done((f32[2,512,1024]{2,1,0:T(8,128)}, f32[2,512,1024]{2,1,0:T(8,128)}, u32[]{:S(2)}, u32[]{:S(2)}) %collective-permute-start) | collective-permute-done | bytes 4194336 | tf_op jit(solution)/shard_map/ppermute | solution.py:167
  206.4 5.4 %gather_fusion.3 = f32[1024,4,128]{2,1,0:T(4,128)S(1)} fusion(f32[1536,4,128]{2,1,0:T(4,128)} %all-to-all-done.2, s32[1024]{0:T(1024)S(1)} %fusion.39), kind=kCustom, calls=%fused_computation.3 | custom fusion | bytes 4198400 | tf_op jit(solution)/shard_map/gather | solution.py:101
  211.8 9.8 %gather_fusion.6 = f32[1024,4,128]{2,1,0:T(4,128)} fusion(f32[1536,4,128]{2,1,0:T(4,128)} %all-to-all-done.3, s32[1024]{0:T(1024)S(1)} %fusion.39), kind=kCustom, calls=%fused_computation.6 | custom fusion | bytes 4198400 | tf_op jit(solution)/shard_map/gather | solution.py:101
  230.2 9.0 %fusion = (f32[4,1024]{1,0:T(4,128)S(1)}, f32[4,1024,1024]{1,2,0:T(8,128)S(1)}) fusion(pred[1024,1024]{0,1:T(8,128)(4,1)S(1)} %iota_compare_fusion, f32[1024,4,128]{2,1,0:T(4,128)S(1)} %get-tuple-element.44, f32[1024,4,128]{2,1,0:T(4,128)S(1)} %get-tuple-element.43), kind=kOutput, calls=%fused_computation.15 | convolution fusion | flops 3233804288 | bytes 22036480 | tf_op jit(solution)/shard_map/while/body/eval_jaxpr/qhd,khd->hqk/dot_general | solution.py:43
  239.2 5.7 %copy-done = f32[4,1024,1024]{1,2,0:T(8,128)} copy-done((f32[4,1024,1024]{1,2,0:T(8,128)}, f32[4,1024,1024]{1,2,0:T(8,128)S(1)}, u32[]{:S(2)}) %copy-start) | copy-done | bytes 16777240
  248.5 6.1 %all-to-all-done = f32[1536,4,128]{2,1,0:T(4,128)} async-done(((f32[1536,4,128]{2,1,0:T(4,128)}), f32[1536,4,128]{2,1,0:T(4,128)}, u32[]{:S(2)}, u32[]{:S(2)}) %all-to-all-start) | async-done | bytes 3145760 | tf_op jit(solution)/shard_map/all_to_all | solution.py:109
  254.6 5.4 %gather_fusion.1 = f32[1024,4,128]{2,1,0:T(4,128)S(1)} fusion(f32[1536,4,128]{2,1,0:T(4,128)} %all-to-all-done, s32[1024]{0:T(1024)S(1)} %fusion.39), kind=kCustom, calls=%fused_computation.1 | custom fusion | bytes 4198400 | tf_op jit(solution)/shard_map/gather | solution.py:101
  260.1 13.2 %bitcast_divide_fusion = f32[1024,4,128]{0,2,1:T(8,128)} fusion(f32[1024,4]{0,1:T(4,128)S(1)} %bitcast.72, f32[4,1024,1024]{1,2,0:T(8,128)} %copy-done, f32[4,1024]{1,0:T(4,128)S(1)} %get-tuple-element.47, pred[1024,1024]{0,1:T(8,128)(4,1)S(1)} %iota_compare_fusion, f32[1024,4,128]{2,1,0:T(4,128)S(1)} %gather_fusion.1), kind=kOutput, calls=%fused_computation.34 | convolution fusion | flops 3234332672 | bytes 22052864 | tf_op jit(solution)/shard_map/while/body/eval_jaxpr/hqk,khd->qhd/dot_general | solution.py:51
  275.3 5.5 %gather_fusion.7 = f32[1536,4,128]{2,1,0:T(4,128)} fusion(f32[1024,4,128]{2,1,0:T(4,128)S(1)} %copy.35, s32[2048]{0:T(1024)S(1)} %pad_clamp_fusion), kind=kCustom, calls=%fused_computation.7 | custom fusion | bytes 6297600 | tf_op jit(solution)/shard_map/gather | solution.py:117
  286.0 40.7 %all_to_all.37 = f32[1536,2,128]{2,1,0:T(2,128)} all-to-all(f32[1536,2,128]{2,1,0:T(2,128)S(1)} %get-tuple-element.37), channel_id=1, replica_groups=mesh['seq'=8,'head'=4] {'seq'}, dimensions={0} | all-to-all | bytes 3145728 | tf_op jit(solution)/shard_map/all_to_all | solution.py:130
  344.2 16.8 %collective-permute-done.1 = f32[1024,256]{1,0:T(8,128)} collective-permute-done((f32[1024,256]{1,0:T(8,128)}, f32[1024,256]{1,0:T(8,128)}, u32[]{:S(2)}, u32[]{:S(2)}) %collective-permute-start.1) | collective-permute-done | bytes 1048608 | tf_op jit(solution)/shard_map/ppermute | solution.py:135
  361.1 5.5 %convolution_add_fusion.1 = f32[1024,1024]{1,0:T(8,128)} fusion(f32[1024,1024]{1,0:T(8,128)S(1)} %fusion.19, f32[1024,256]{1,0:T(8,128)} %collective-permute-done.1, f32[2,512,1024]{2,1,0:T(8,128)} %collective-permute-done), kind=kOutput, calls=%fused_computation.27 | convolution fusion | flops 1611661312 | bytes 10485760 | tf_op jit(solution)/shard_map/dot_general | solution.py:125
  366.6 5.4 %convolution_add_fusion = f32[1024,1024]{1,0:T(8,128)} fusion(f32[1024,1024]{1,0:T(8,128)S(1)} %fusion.17, f32[1024,256]{1,0:T(8,128)} %collective-permute-done.1, f32[2,512,1024]{2,1,0:T(8,128)} %collective-permute-done), kind=kOutput, calls=%fused_computation.26 | convolution fusion | flops 1611661312 | bytes 10485760 | tf_op jit(solution)/shard_map/dot_general | solution.py:125
  381.6 18.8 %collective-permute-done.2 = f32[1024,256]{1,0:T(8,128)S(1)} collective-permute-done((f32[1024,256]{1,0:T(8,128)}, f32[1024,256]{1,0:T(8,128)S(1)}, u32[]{:S(2)}, u32[]{:S(2)}) %collective-permute-start.2) | collective-permute-done | bytes 1048608 | tf_op jit(solution)/shard_map/ppermute | solution.py:135
  411.1 6.2 %add_add_fusion.1 = f32[1024,1024]{1,0:T(8,128)} fusion(f32[1024,1024]{1,0:T(8,128)} %collective-permute-done.3, f32[1024,1024]{1,0:T(8,128)S(1)} %copy-done.2, f32[1024,1024]{1,0:T(8,128)S(1)} %fusion.15, f32[1024,1024]{1,0:T(8,128)S(1)} %fusion.22), kind=kLoop, calls=%fused_computation.24 | loop fusion | flops 3145728 | bytes 20971520 | tf_op jit(solution)/shard_map/add | solution.py:149
  (68 shorter events, 96.3 us)
Async XLA Ops:
  10.0 19.0 %all-to-all-start.1 = ((s32[8,192,2]{1,2,0:T(2,128)}), s32[8,192,2]{1,2,0:T(2,128)S(1)}, u32[]{:S(2)}, u32[]{:S(2)}) async-start(s32[8,192,2]{1,2,0:T(2,128)} %copy.29), calls=%async_computation.1 | async-start | bytes 32768 | tf_op jit(solution)/shard_map/all_to_all | solution.py:91
  29.1 76.2 %all-to-all-start.2 = ((f32[1536,4,128]{2,1,0:T(4,128)}), f32[1536,4,128]{2,1,0:T(4,128)}, u32[]{:S(2)}, u32[]{:S(2)}) async-start(f32[1536,4,128]{2,1,0:T(4,128)} %gather_fusion.2), calls=%async_computation.2 | async-start | bytes 6291456 | tf_op jit(solution)/shard_map/all_to_all | solution.py:104
  105.3 74.6 %all-to-all-start.3 = ((f32[1536,4,128]{2,1,0:T(4,128)}), f32[1536,4,128]{2,1,0:T(4,128)}, u32[]{:S(2)}, u32[]{:S(2)}) async-start(f32[1536,4,128]{2,1,0:T(4,128)} %gather_fusion.5), calls=%async_computation.3 | async-start | bytes 6291456 | tf_op jit(solution)/shard_map/all_to_all | solution.py:108
  114.7 91.7 %collective-permute-start = (f32[2,512,1024]{2,1,0:T(8,128)}, f32[2,512,1024]{2,1,0:T(8,128)}, u32[]{:S(2)}, u32[]{:S(2)}) collective-permute-start(f32[2,512,1024]{2,1,0:T(8,128)} %pad_maximum_fusion), channel_id=1, source_target_pairs={{0,2},{1,3},{2,0},{3,1},{4,6},{5,7},{6,4},{7,5},{8,10},{9,11},{10,... | collective-permute-start | bytes 12582920 | tf_op jit(solution)/shard_map/ppermute | solution.py:167
  180.0 74.6 %all-to-all-start = ((f32[1536,4,128]{2,1,0:T(4,128)}), f32[1536,4,128]{2,1,0:T(4,128)}, u32[]{:S(2)}, u32[]{:S(2)}) async-start(f32[1536,4,128]{2,1,0:T(4,128)} %gather_fusion), calls=%async_computation | async-start | bytes 6291456 | tf_op jit(solution)/shard_map/all_to_all | solution.py:109
  225.0 1.6 copy-start.1
  225.0 1.7 copy-start.4
  225.1 1.8 copy-start.5
  239.2 5.7 %copy-start = (f32[4,1024,1024]{1,2,0:T(8,128)}, f32[4,1024,1024]{1,2,0:T(8,128)S(1)}, u32[]{:S(2)}) copy-start(f32[4,1024,1024]{1,2,0:T(8,128)S(1)} %get-tuple-element.48) | copy-start | bytes 50331652
  326.6 45.4 %all-to-all-start.4 = ((f32[1536,2,128]{2,1,0:T(2,128)}), f32[1536,2,128]{2,1,0:T(2,128)S(1)}, u32[]{:S(2)}, u32[]{:S(2)}) async-start(f32[1536,2,128]{2,1,0:T(2,128)} %get-tuple-element.38), calls=%async_computation.4 | async-start | bytes 3145728 | tf_op jit(solution)/shard_map/all_to_all | solution.py:130
  336.5 24.6 %collective-permute-start.1 = (f32[1024,256]{1,0:T(8,128)}, f32[1024,256]{1,0:T(8,128)}, u32[]{:S(2)}, u32[]{:S(2)}) collective-permute-start(f32[1024,256]{1,0:T(8,128)} %bitcast.58), channel_id=1, source_target_pairs={{0,2},{1,3},{2,0},{3,1},{4,6},{5,7},{6,4},{7,5},{8,10},{9,11},{10,... | collective-permute-start | bytes 3145736 | tf_op jit(solution)/shard_map/ppermute | solution.py:135
  376.9 23.5 %collective-permute-start.2 = (f32[1024,256]{1,0:T(8,128)}, f32[1024,256]{1,0:T(8,128)S(1)}, u32[]{:S(2)}, u32[]{:S(2)}) collective-permute-start(f32[1024,256]{1,0:T(8,128)} %bitcast.57), channel_id=1, source_target_pairs={{0,2},{1,3},{2,0},{3,1},{4,6},{5,7},{6,4},{7,5},{8,10},{9,11},{10,... | collective-permute-start | bytes 3145736 | tf_op jit(solution)/shard_map/ppermute | solution.py:135
  378.4 22.0 %copy-start.3 = (f32[1024,1024]{1,0:T(8,128)S(1)}, f32[1024,1024]{1,0:T(8,128)}, u32[]{:S(2)}) copy-start(f32[1024,1024]{1,0:T(8,128)} %convolution_add_fusion.1) | copy-start | bytes 12582916
  403.7 7.4 %collective-permute-start.3 = (f32[1024,1024]{1,0:T(8,128)S(1)}, f32[1024,1024]{1,0:T(8,128)}, u32[]{:S(2)}, u32[]{:S(2)}) collective-permute-start(f32[1024,1024]{1,0:T(8,128)S(1)} %add_add_fusion), channel_id=1, source_target_pairs={{0,1},{1,0},{2,3},{3,2},{4,5},{5,4},{6,7},{7,6},{8,9},{9,8},{10,11... | collective-permute-start | bytes 12582920 | tf_op jit(solution)/shard_map/ppermute | solution.py:148
  406.8 4.2 %copy-start.2 = (f32[1024,1024]{1,0:T(8,128)S(1)}, f32[1024,1024]{1,0:T(8,128)}, u32[]{:S(2)}) copy-start(f32[1024,1024]{1,0:T(8,128)} %convolution_add_fusion) | copy-start | bytes 12582916

commit v14 on v13

--- a/solution.py
+++ b/solution.py
@@ -114,7 +114,6 @@
         rotate(place(received[1]), cos_table, sin_table),
         place(received[2]),
     )
-    outgoing = result[picked]
     split = heads_here // 2
     head_count = lax.axis_size("head")
     me = lax.axis_index("head")
@@ -127,7 +126,8 @@
         )
 
     def exchange(lo, hi):
-        back = lax.all_to_all(outgoing[:, lo:hi], "seq", split_axis=0, concat_axis=0, tiled=True)
+        part = result[:, lo:hi][picked]
+        back = lax.all_to_all(part, "seq", split_axis=0, concat_axis=0, tiled=True)
         return back
 
     def half_terms(back, lo, hi):

time: 425 us -> 422 us (level)
  blocking collectives: 40.7 us -> 0 us
  waiting for transfers between devices: 167 us -> 199 us
    all_to_all x1 -> x0, blocking collectives: 40.7 us -> none  [exchange(): lax.all_to_all(outgoing[:, lo:hi], 'seq', split_axis=0, concat_axis=0, ti...]
    all_to_all x1 -> x2, waiting for transfers between devices: 0.01 us -> 30.4 us  [exchange(): back = lax.all_to_all(part, 'seq', split_axis=0, concat_axis=0, tiled=True)]
    gather x1 -> x2, local copies, waits for them, and re-layouts: 5.49 us -> 10.4 us  [exchange(): part = result[:, lo:hi][picked]]
    unnamed x14 -> x16, local copies, waits for them, and re-layouts: 8.38 us -> 9.52 us
  transfers between devices with their start and end apart: 9 -> 10, of which waited for: 7 -> 8; matrix products, arithmetic and copies ran while one was open for 28% -> 30% of each run, Pallas kernels for 0% -> 0%
where the time goes in v14:
time: 422 us; the launch traced here: 414 us
  waiting for transfers between devices  199 us (47%)
  local copies, waits for them, and re-layouts  99.2 us (24%)
  matrix products  51.5 us (12%)
  starting transfers between devices  34.2 us (8%)
  other arithmetic  29.1 us (7%)
    all_to_all x1, waiting for transfers between devices, per_device(): lax.all_to_all(send_q, 'seq', split_axis=0, concat_axis=0, tiled=True)  62.7 us
    all_to_all x1, waiting for transfers between devices, per_device(): lax.all_to_all(send_k, 'seq', split_axis=0, concat_axis=0, tiled=True)  56.3 us
    ppermute x2, waiting for transfers between devices, half_terms(): far_mixed = lax.ppermute(mixed, 'head', swap_pairs(head_count, 2))  36.8 us
    all_to_all x2, waiting for transfers between devices, exchange(): back = lax.all_to_all(part, 'seq', split_axis=0, concat_axis=0, tiled=True)  30.4 us
    dot_general x8, matrix products, dot(): jnp.dot(lhs, weight, precision=lax.Precision.HIGH, preferred_element_type...  29.9 us
    gather x4, local copies, waits for them, and re-layouts, place(): return pieces[where_from]  26.8 us
    dot_general x1, matrix products, cluster_attention(): jnp.einsum('hqk,khd->qhd', weights, value_c, precision=lax.Precision.HIGH)  12.6 us
    gather x2, local copies, waits for them, and re-layouts, exchange(): part = result[:, lo:hi][picked]  10.4 us
  transfers between devices with their start and end apart: 10, of which 8 were waited for; matrix products, arithmetic and copies ran while one was open for 30% of the time, Pallas kernels for 0%

profile of v14, /device:TPU:0, one launch (start us, length us, event | category | flops | bytes accessed | tf_op | source)
XLA Modules:
  0.0 413.6 jit_solution(7801829085411656499)
XLA Ops:
  10.0 7.3 %all-to-all-start.1 = ((s32[8,192,2]{1,2,0:T(2,128)}), s32[8,192,2]{1,2,0:T(2,128)S(1)}, u32[]{:S(2)}, u32[]{:S(2)}) async-start(s32[8,192,2]{1,2,0:T(2,128)} %copy.32), calls=%async_computation.1 | async-start | bytes 32768 | tf_op jit(solution)/shard_map/all_to_all | solution.py:91
  23.6 5.5 %gather_fusion.2 = f32[1536,4,128]{2,1,0:T(4,128)} fusion(f32[1024,4,128]{2,1,0:T(4,128)S(1)} %reshape.131, s32[2048]{0:T(1024)S(1)} %pad_clamp_fusion.1), kind=kCustom, calls=%fused_computation.2 | custom fusion | bytes 6297600 | tf_op jit(solution)/shard_map/gather | solution.py:83
  29.1 6.0 %all-to-all-start.2 = ((f32[1536,4,128]{2,1,0:T(4,128)}), f32[1536,4,128]{2,1,0:T(4,128)}, u32[]{:S(2)}, u32[]{:S(2)}) async-start(f32[1536,4,128]{2,1,0:T(4,128)} %gather_fusion.2), calls=%async_computation.2 | async-start | bytes 6291456 | tf_op jit(solution)/shard_map/all_to_all | solution.py:104
  37.0 5.6 %gather_fusion.5 = f32[1536,4,128]{2,1,0:T(4,128)} fusion(f32[1024,4,128]{2,1,0:T(4,128)S(1)} %reshape.132, s32[2048]{0:T(1024)S(1)} %pad_clamp_fusion.1), kind=kCustom, calls=%fused_computation.5 | custom fusion | bytes 6297600 | tf_op jit(solution)/shard_map/gather | solution.py:84
  42.6 62.7 %all-to-all-done.2 = f32[1536,4,128]{2,1,0:T(4,128)} async-done(((f32[1536,4,128]{2,1,0:T(4,128)}), f32[1536,4,128]{2,1,0:T(4,128)}, u32[]{:S(2)}, u32[]{:S(2)}) %all-to-all-start.2) | async-done | bytes 3145760 | tf_op jit(solution)/shard_map/all_to_all | solution.py:104
  118.1 5.6 %gather_fusion = f32[1536,4,128]{2,1,0:T(4,128)} fusion(f32[1024,4,128]{2,1,0:T(4,128)S(1)} %reshape.129, s32[2048]{0:T(1024)S(1)} %pad_clamp_fusion.1), kind=kCustom, calls=%fused_computation | custom fusion | bytes 6297600 | tf_op jit(solution)/shard_map/gather | solution.py:85
  123.7 56.3 %all-to-all-done.3 = f32[1536,4,128]{2,1,0:T(4,128)} async-done(((f32[1536,4,128]{2,1,0:T(4,128)}), f32[1536,4,128]{2,1,0:T(4,128)}, u32[]{:S(2)}, u32[]{:S(2)}) %all-to-all-start.3) | async-done | bytes 3145760 | tf_op jit(solution)/shard_map/all_to_all | solution.py:108
  184.9 6.4 %scatter_custom_fusion.2 = s32[1024]{0:T(1024)S(1)} fusion(s32[1536]{0:T(1024)S(1)} %get-tuple-element.31, s32[1536]{0:T(1024)S(1)} %iota.37, s32[]{:T(128)} %constant.47.clone.1), kind=kCustom, calls=%fused_computation.90 | custom fusion | bytes 4100 | tf_op jit(solution)/shard_map/scatter | solution.py:97
  191.4 6.2 %gather_fusion.4 = s32[1024]{0:T(1024)S(1)} fusion(s32[1536]{0:T(1024)S(1)} %get-tuple-element.32, s32[1024]{0:T(1024)S(1)} %fusion.39), kind=kCustom, calls=%fused_computation.4 | custom fusion | bytes 12288 | tf_op jit(solution)/shard_map/gather | solution.py:101
  200.8 5.6 %collective-permute-done = f32[2,512,1024]{2,1,0:T(8,128)} collective-permute-done((f32[2,512,1024]{2,1,0:T(8,128)}, f32[2,512,1024]{2,1,0:T(8,128)}, u32[]{:S(2)}, u32[]{:S(2)}) %collective-permute-start) | collective-permute-done | bytes 4194336 | tf_op jit(solution)/shard_map/ppermute | solution.py:167
  206.4 5.4 %gather_fusion.3 = f32[1024,4,128]{2,1,0:T(4,128)S(1)} fusion(f32[1536,4,128]{2,1,0:T(4,128)} %all-to-all-done.2, s32[1024]{0:T(1024)S(1)} %fusion.39), kind=kCustom, calls=%fused_computation.3 | custom fusion | bytes 4198400 | tf_op jit(solution)/shard_map/gather | solution.py:101
  211.8 9.8 %gather_fusion.6 = f32[1024,4,128]{2,1,0:T(4,128)} fusion(f32[1536,4,128]{2,1,0:T(4,128)} %all-to-all-done.3, s32[1024]{0:T(1024)S(1)} %fusion.39), kind=kCustom, calls=%fused_computation.6 | custom fusion | bytes 4198400 | tf_op jit(solution)/shard_map/gather | solution.py:101
  230.2 9.0 %fusion = (f32[4,1024]{1,0:T(4,128)S(1)}, f32[4,1024,1024]{1,2,0:T(8,128)S(1)}) fusion(pred[1024,1024]{0,1:T(8,128)(4,1)S(1)} %iota_compare_fusion, f32[1024,4,128]{2,1,0:T(4,128)S(1)} %get-tuple-element.44, f32[1024,4,128]{2,1,0:T(4,128)S(1)} %get-tuple-element.43), kind=kOutput, calls=%fused_computation.16 | convolution fusion | flops 3233804288 | bytes 22036480 | tf_op jit(solution)/shard_map/while/body/eval_jaxpr/qhd,khd->hqk/dot_general | solution.py:43
  239.2 5.7 %copy-done = f32[4,1024,1024]{1,2,0:T(8,128)} copy-done((f32[4,1024,1024]{1,2,0:T(8,128)}, f32[4,1024,1024]{1,2,0:T(8,128)S(1)}, u32[]{:S(2)}) %copy-start) | copy-done | bytes 16777240
  248.5 6.1 %all-to-all-done = f32[1536,4,128]{2,1,0:T(4,128)} async-done(((f32[1536,4,128]{2,1,0:T(4,128)}), f32[1536,4,128]{2,1,0:T(4,128)}, u32[]{:S(2)}, u32[]{:S(2)}) %all-to-all-start) | async-done | bytes 3145760 | tf_op jit(solution)/shard_map/all_to_all | solution.py:109
  254.6 5.4 %gather_fusion.1 = f32[1024,4,128]{2,1,0:T(4,128)S(1)} fusion(f32[1536,4,128]{2,1,0:T(4,128)} %all-to-all-done, s32[1024]{0:T(1024)S(1)} %fusion.39), kind=kCustom, calls=%fused_computation.1 | custom fusion | bytes 4198400 | tf_op jit(solution)/shard_map/gather | solution.py:101
  260.1 12.6 %bitcast_divide_fusion = f32[1024,4,128]{0,2,1:T(8,128)S(1)} fusion(f32[1024,4]{0,1:T(4,128)S(1)} %bitcast.72, f32[4,1024,1024]{1,2,0:T(8,128)} %copy-done, f32[4,1024]{1,0:T(4,128)S(1)} %get-tuple-element.47, pred[1024,1024]{0,1:T(8,128)(4,1)S(1)} %iota_compare_fusion, f32[1024,4,128]{2,1,0:T(4,128)S(1)} %gather_fusion.1), kind=kOutput, calls=%fused_computation.35 | convolution fusion | flops 3234332672 | bytes 22052864 | tf_op jit(solution)/shard_map/while/body/eval_jaxpr/hqk,khd->qhd/dot_general | solution.py:51
  284.8 5.2 %gather_fusion.7 = f32[1536,2,128]{2,1,0:T(2,128)} fusion(f32[1024,2,128]{2,1,0:T(2,128)S(1)} %copy.38, s32[2048]{0:T(1024)S(1)} %pad_clamp_fusion), kind=kCustom, calls=%fused_computation.7 | custom fusion | bytes 3151872 | tf_op jit(solution)/shard_map/gather | solution.py:129
  290.0 30.4 %all-to-all-done.5 = f32[1536,2,128]{2,1,0:T(2,128)S(1)} async-done(((f32[1536,2,128]{2,1,0:T(2,128)}), f32[1536,2,128]{2,1,0:T(2,128)S(1)}, u32[]{:S(2)}, u32[]{:S(2)}) %all-to-all-start.5) | async-done | bytes 1572896 | tf_op jit(solution)/shard_map/all_to_all | solution.py:130
  339.2 17.4 %collective-permute-done.1 = f32[1024,256]{1,0:T(8,128)} collective-permute-done((f32[1024,256]{1,0:T(8,128)}, f32[1024,256]{1,0:T(8,128)}, u32[]{:S(2)}, u32[]{:S(2)}) %collective-permute-start.1) | collective-permute-done | bytes 1048608 | tf_op jit(solution)/shard_map/ppermute | solution.py:135
  356.5 5.5 %convolution_add_fusion.1 = f32[1024,1024]{1,0:T(8,128)} fusion(f32[1024,1024]{1,0:T(8,128)S(1)} %fusion.19, f32[1024,256]{1,0:T(8,128)} %collective-permute-done.1, f32[2,512,1024]{2,1,0:T(8,128)} %collective-permute-done), kind=kOutput, calls=%fused_computation.28 | convolution fusion | flops 1611661312 | bytes 10485760 | tf_op jit(solution)/shard_map/dot_general | solution.py:124
  362.1 5.4 %convolution_add_fusion = f32[1024,1024]{1,0:T(8,128)} fusion(f32[1024,1024]{1,0:T(8,128)S(1)} %fusion.17, f32[1024,256]{1,0:T(8,128)} %collective-permute-done.1, f32[2,512,1024]{2,1,0:T(8,128)} %collective-permute-done), kind=kOutput, calls=%fused_computation.27 | convolution fusion | flops 1611661312 | bytes 10485760 | tf_op jit(solution)/shard_map/dot_general | solution.py:124
  377.0 19.4 %collective-permute-done.2 = f32[1024,256]{1,0:T(8,128)S(1)} collective-permute-done((f32[1024,256]{1,0:T(8,128)}, f32[1024,256]{1,0:T(8,128)S(1)}, u32[]{:S(2)}, u32[]{:S(2)}) %collective-permute-start.2) | collective-permute-done | bytes 1048608 | tf_op jit(solution)/shard_map/ppermute | solution.py:135
  407.1 6.2 %add_add_fusion.1 = f32[1024,1024]{1,0:T(8,128)} fusion(f32[1024,1024]{1,0:T(8,128)} %collective-permute-done.3, f32[1024,1024]{1,0:T(8,128)S(1)} %copy-done.2, f32[1024,1024]{1,0:T(8,128)S(1)} %fusion.15, f32[1024,1024]{1,0:T(8,128)S(1)} %fusion.22), kind=kLoop, calls=%fused_computation.25 | loop fusion | flops 3145728 | bytes 20971520 | tf_op jit(solution)/shard_map/add | solution.py:149
  (73 shorter events, 102.2 us)
Async XLA Ops:
  10.0 19.0 %all-to-all-start.1 = ((s32[8,192,2]{1,2,0:T(2,128)}), s32[8,192,2]{1,2,0:T(2,128)S(1)}, u32[]{:S(2)}, u32[]{:S(2)}) async-start(s32[8,192,2]{1,2,0:T(2,128)} %copy.32), calls=%async_computation.1 | async-start | bytes 32768 | tf_op jit(solution)/shard_map/all_to_all | solution.py:91
  29.1 76.2 %all-to-all-start.2 = ((f32[1536,4,128]{2,1,0:T(4,128)}), f32[1536,4,128]{2,1,0:T(4,128)}, u32[]{:S(2)}, u32[]{:S(2)}) async-start(f32[1536,4,128]{2,1,0:T(4,128)} %gather_fusion.2), calls=%async_computation.2 | async-start | bytes 6291456 | tf_op jit(solution)/shard_map/all_to_all | solution.py:104
  105.3 74.7 %all-to-all-start.3 = ((f32[1536,4,128]{2,1,0:T(4,128)}), f32[1536,4,128]{2,1,0:T(4,128)}, u32[]{:S(2)}, u32[]{:S(2)}) async-start(f32[1536,4,128]{2,1,0:T(4,128)} %gather_fusion.5), calls=%async_computation.3 | async-start | bytes 6291456 | tf_op jit(solution)/shard_map/all_to_all | solution.py:108
  114.7 91.7 %collective-permute-start = (f32[2,512,1024]{2,1,0:T(8,128)}, f32[2,512,1024]{2,1,0:T(8,128)}, u32[]{:S(2)}, u32[]{:S(2)}) collective-permute-start(f32[2,512,1024]{2,1,0:T(8,128)} %pad_maximum_fusion), channel_id=1, source_target_pairs={{0,2},{1,3},{2,0},{3,1},{4,6},{5,7},{6,4},{7,5},{8,10},{9,11},{10,... | collective-permute-start | bytes 12582920 | tf_op jit(solution)/shard_map/ppermute | solution.py:167
  180.0 74.6 %all-to-all-start = ((f32[1536,4,128]{2,1,0:T(4,128)}), f32[1536,4,128]{2,1,0:T(4,128)}, u32[]{:S(2)}, u32[]{:S(2)}) async-start(f32[1536,4,128]{2,1,0:T(4,128)} %gather_fusion), calls=%async_computation | async-start | bytes 6291456 | tf_op jit(solution)/shard_map/all_to_all | solution.py:109
  225.0 1.6 copy-start.1
  225.0 1.7 copy-start.5
  225.1 1.8 copy-start.6
  239.2 5.7 %copy-start = (f32[4,1024,1024]{1,2,0:T(8,128)}, f32[4,1024,1024]{1,2,0:T(8,128)S(1)}, u32[]{:S(2)}) copy-start(f32[4,1024,1024]{1,2,0:T(8,128)S(1)} %get-tuple-element.48) | copy-start | bytes 50331652
  279.6 40.8 %all-to-all-start.5 = ((f32[1536,2,128]{2,1,0:T(2,128)}), f32[1536,2,128]{2,1,0:T(2,128)S(1)}, u32[]{:S(2)}, u32[]{:S(2)}) async-start(f32[1536,2,128]{2,1,0:T(2,128)} %gather_fusion.8), calls=%async_computation.5 | async-start | bytes 3145728 | tf_op jit(solution)/shard_map/all_to_all | solution.py:130
  320.4 1.1 copy-start.4
  321.6 45.9 %all-to-all-start.4 = ((f32[1536,2,128]{2,1,0:T(2,128)}), f32[1536,2,128]{2,1,0:T(2,128)S(1)}, u32[]{:S(2)}, u32[]{:S(2)}) async-start(f32[1536,2,128]{2,1,0:T(2,128)} %gather_fusion.7), calls=%async_computation.4 | async-start | bytes 3145728 | tf_op jit(solution)/shard_map/all_to_all | solution.py:130
  331.4 25.1 %collective-permute-start.1 = (f32[1024,256]{1,0:T(8,128)}, f32[1024,256]{1,0:T(8,128)}, u32[]{:S(2)}, u32[]{:S(2)}) collective-permute-start(f32[1024,256]{1,0:T(8,128)} %bitcast.58), channel_id=1, source_target_pairs={{0,2},{1,3},{2,0},{3,1},{4,6},{5,7},{6,4},{7,5},{8,10},{9,11},{10,... | collective-permute-start | bytes 3145736 | tf_op jit(solution)/shard_map/ppermute | solution.py:135
  372.3 24.1 %collective-permute-start.2 = (f32[1024,256]{1,0:T(8,128)}, f32[1024,256]{1,0:T(8,128)S(1)}, u32[]{:S(2)}, u32[]{:S(2)}) collective-permute-start(f32[1024,256]{1,0:T(8,128)} %bitcast.57), channel_id=1, source_target_pairs={{0,2},{1,3},{2,0},{3,1},{4,6},{5,7},{6,4},{7,5},{8,10},{9,11},{10,... | collective-permute-start | bytes 3145736 | tf_op jit(solution)/shard_map/ppermute | solution.py:135
  373.8 22.6 %copy-start.3 = (f32[1024,1024]{1,0:T(8,128)S(1)}, f32[1024,1024]{1,0:T(8,128)}, u32[]{:S(2)}) copy-start(f32[1024,1024]{1,0:T(8,128)} %convolution_add_fusion.1) | copy-start | bytes 12582916
  399.8 7.4 %collective-permute-start.3 = (f32[1024,1024]{1,0:T(8,128)S(1)}, f32[1024,1024]{1,0:T(8,128)}, u32[]{:S(2)}, u32[]{:S(2)}) collective-permute-start(f32[1024,1024]{1,0:T(8,128)S(1)} %add_add_fusion), channel_id=1, source_target_pairs={{0,1},{1,0},{2,3},{3,2},{4,5},{5,4},{6,7},{7,6},{8,9},{9,8},{10,11... | collective-permute-start | bytes 12582920 | tf_op jit(solution)/shard_map/ppermute | solution.py:148
  402.9 4.2 %copy-start.2 = (f32[1024,1024]{1,0:T(8,128)S(1)}, f32[1024,1024]{1,0:T(8,128)}, u32[]{:S(2)}) copy-start(f32[1024,1024]{1,0:T(8,128)} %convolution_add_fusion) | copy-start | bytes 12582916

commit v15 on v14

--- a/solution.py
+++ b/solution.py
@@ -48,8 +48,14 @@
     peak = jnp.max(scores, -1, keepdims=True)
     weights = jnp.exp(scores - peak)
     total = jnp.sum(weights, -1, keepdims=True)
-    summed = jnp.einsum("hqk,khd->qhd", weights, value_c, precision=lax.Precision.HIGH)
-    return summed / jnp.transpose(total, (1, 0, 2))
+    split = query_c.shape[1] // 2
+    parts = []
+    for lo, hi in ((0, split), (split, query_c.shape[1])):
+        summed = jnp.einsum(
+            "hqk,khd->qhd", weights[lo:hi], value_c[:, lo:hi], precision=lax.Precision.HIGH
+        )
+        parts.append(summed / jnp.transpose(total[lo:hi], (1, 0, 2)))
+    return tuple(parts)
 
 
 def attend_local(query_all, key_all, value_all):
@@ -59,7 +65,8 @@
         key_all.reshape(row_count // CS, CS, head_count, width),
         value_all.reshape(row_count // CS, CS, head_count, width),
     )
-    return lax.map(cluster_attention, grouped).reshape(row_count, head_count, width)
+    parts = lax.map(cluster_attention, grouped)
+    return [part.reshape(row_count, part.shape[2], width) for part in parts]
 
 
 def per_device(queries, keys, values, positions, cluster, slot, out_weight):
@@ -126,7 +133,7 @@
         )
 
     def exchange(lo, hi):
-        part = result[:, lo:hi][picked]
+        part = result[0 if lo == 0 else 1][picked]
         back = lax.all_to_all(part, "seq", split_axis=0, concat_axis=0, tiled=True)
         return back
 

time: 422 us -> 416 us (0.986)
  local copies, waits for them, and re-layouts: 99.2 us -> 94.4 us
    all_to_all x2, waiting for transfers between devices: 30.4 us -> 23.5 us  [exchange(): back = lax.all_to_all(part, 'seq', split_axis=0, concat_axis=0, tiled=True)]
    unnamed x16, local copies, waits for them, and re-layouts: 9.52 us -> 3.62 us
    all_to_all x1, waiting for transfers between devices: 6.08 us -> 10.7 us  [per_device(): lax.all_to_all(send_v, 'seq', split_axis=0, concat_axis=0, tiled=True)]
    dot_general x1 -> x2, matrix products: 12.6 us -> 13 us  [cluster_attention(): jnp.einsum('hqk,khd->qhd', weights[lo:hi], value_c[:, lo:hi], precision=l...]
  transfers between devices with their start and end apart: 10 -> 10, of which waited for: 8 -> 8; matrix products, arithmetic and copies ran while one was open for 30% -> 32% of each run, Pallas kernels for 0% -> 0%
where the time goes in v15:
time: 416 us; the launch traced here: 408 us
  waiting for transfers between devices  196 us (47%)
  local copies, waits for them, and re-layouts  94.4 us (23%)
  matrix products  51.8 us (12%)
  starting transfers between devices  34.6 us (8%)
  other arithmetic  30.4 us (7%)
    all_to_all x1, waiting for transfers between devices, per_device(): lax.all_to_all(send_q, 'seq', split_axis=0, concat_axis=0, tiled=True)  62.7 us
    all_to_all x1, waiting for transfers between devices, per_device(): lax.all_to_all(send_k, 'seq', split_axis=0, concat_axis=0, tiled=True)  56.3 us
    ppermute x2, waiting for transfers between devices, half_terms(): far_mixed = lax.ppermute(mixed, 'head', swap_pairs(head_count, 2))  36.8 us
    dot_general x8, matrix products, dot(): jnp.dot(lhs, weight, precision=lax.Precision.HIGH, preferred_element_type...  29.9 us
    gather x4, local copies, waits for them, and re-layouts, place(): return pieces[where_from]  27 us
    all_to_all x2, waiting for transfers between devices, exchange(): back = lax.all_to_all(part, 'seq', split_axis=0, concat_axis=0, tiled=True)  23.5 us
    dot_general x2, matrix products, cluster_attention(): jnp.einsum('hqk,khd->qhd', weights[lo:hi], value_c[:, lo:hi], precision=l...  13 us
    all_to_all x1, waiting for transfers between devices, per_device(): lax.all_to_all(send_v, 'seq', split_axis=0, concat_axis=0, tiled=True)  10.7 us
  transfers between devices with their start and end apart: 10, of which 8 were waited for; matrix products, arithmetic and copies ran while one was open for 32% of the time, Pallas kernels for 0%

profile of v15, /device:TPU:0, one launch (start us, length us, event | category | flops | bytes accessed | tf_op | source)
XLA Modules:
  0.0 408.2 jit_solution(8577537700455735929)
XLA Ops:
  10.1 7.3 %all-to-all-start.1 = ((s32[8,192,2]{1,2,0:T(2,128)}), s32[8,192,2]{1,2,0:T(2,128)S(1)}, u32[]{:S(2)}, u32[]{:S(2)}) async-start(s32[8,192,2]{1,2,0:T(2,128)} %copy.39), calls=%async_computation.1 | async-start | bytes 32768 | tf_op jit(solution)/shard_map/all_to_all | solution.py:98
  23.6 5.5 %gather_fusion.2 = f32[1536,4,128]{2,1,0:T(4,128)} fusion(f32[1024,4,128]{2,1,0:T(4,128)S(1)} %reshape.135, s32[2048]{0:T(1024)S(1)} %pad_clamp_fusion.1), kind=kCustom, calls=%fused_computation.2 | custom fusion | bytes 6297600 | tf_op jit(solution)/shard_map/gather | solution.py:90
  29.1 6.0 %all-to-all-start.2 = ((f32[1536,4,128]{2,1,0:T(4,128)}), f32[1536,4,128]{2,1,0:T(4,128)}, u32[]{:S(2)}, u32[]{:S(2)}) async-start(f32[1536,4,128]{2,1,0:T(4,128)} %gather_fusion.2), calls=%async_computation.2 | async-start | bytes 6291456 | tf_op jit(solution)/shard_map/all_to_all | solution.py:111
  37.0 5.6 %gather_fusion.5 = f32[1536,4,128]{2,1,0:T(4,128)} fusion(f32[1024,4,128]{2,1,0:T(4,128)S(1)} %reshape.136, s32[2048]{0:T(1024)S(1)} %pad_clamp_fusion.1), kind=kCustom, calls=%fused_computation.5 | custom fusion | bytes 6297600 | tf_op jit(solution)/shard_map/gather | solution.py:91
  42.6 62.7 %all-to-all-done.2 = f32[1536,4,128]{2,1,0:T(4,128)} async-done(((f32[1536,4,128]{2,1,0:T(4,128)}), f32[1536,4,128]{2,1,0:T(4,128)}, u32[]{:S(2)}, u32[]{:S(2)}) %all-to-all-start.2) | async-done | bytes 3145760 | tf_op jit(solution)/shard_map/all_to_all | solution.py:111
  118.1 5.5 %gather_fusion = f32[1536,4,128]{2,1,0:T(4,128)} fusion(f32[1024,4,128]{2,1,0:T(4,128)S(1)} %reshape.133, s32[2048]{0:T(1024)S(1)} %pad_clamp_fusion.1), kind=kCustom, calls=%fused_computation | custom fusion | bytes 6297600 | tf_op jit(solution)/shard_map/gather | solution.py:92
  123.7 56.3 %all-to-all-done.3 = f32[1536,4,128]{2,1,0:T(4,128)} async-done(((f32[1536,4,128]{2,1,0:T(4,128)}), f32[1536,4,128]{2,1,0:T(4,128)}, u32[]{:S(2)}, u32[]{:S(2)}) %all-to-all-start.3) | async-done | bytes 3145760 | tf_op jit(solution)/shard_map/all_to_all | solution.py:115
  185.0 6.6 %scatter_custom_fusion.2 = s32[1024]{0:T(1024)S(1)} fusion(s32[1536]{0:T(1024)S(1)} %get-tuple-element.34, s32[1536]{0:T(1024)S(1)} %iota.37, s32[]{:T(128)} %constant.53.clone.1), kind=kCustom, calls=%fused_computation.94 | custom fusion | bytes 4100 | tf_op jit(solution)/shard_map/scatter | solution.py:104
  191.6 6.2 %gather_fusion.4 = s32[1024]{0:T(1024)S(1)} fusion(s32[1536]{0:T(1024)S(1)} %get-tuple-element.35, s32[1024]{0:T(1024)S(1)} %fusion.48), kind=kCustom, calls=%fused_computation.4 | custom fusion | bytes 12288 | tf_op jit(solution)/shard_map/gather | solution.py:108
  201.0 5.3 %collective-permute-done = f32[2,512,1024]{2,1,0:T(8,128)} collective-permute-done((f32[2,512,1024]{2,1,0:T(8,128)}, f32[2,512,1024]{2,1,0:T(8,128)}, u32[]{:S(2)}, u32[]{:S(2)}) %collective-permute-start) | collective-permute-done | bytes 4194336 | tf_op jit(solution)/shard_map/ppermute | solution.py:174
  206.4 5.4 %gather_fusion.3 = f32[1024,4,128]{2,1,0:T(4,128)S(1)} fusion(f32[1536,4,128]{2,1,0:T(4,128)} %all-to-all-done.2, s32[1024]{0:T(1024)S(1)} %fusion.48), kind=kCustom, calls=%fused_computation.3 | custom fusion | bytes 4198400 | tf_op jit(solution)/shard_map/gather | solution.py:108
  211.8 9.8 %gather_fusion.6 = f32[1024,4,128]{2,1,0:T(4,128)} fusion(f32[1536,4,128]{2,1,0:T(4,128)} %all-to-all-done.3, s32[1024]{0:T(1024)S(1)} %fusion.48), kind=kCustom, calls=%fused_computation.6 | custom fusion | bytes 4198400 | tf_op jit(solution)/shard_map/gather | solution.py:108
  227.7 9.0 %fusion = (f32[4,1024]{1,0:T(4,128)S(1)}, f32[4,1024,1024]{1,2,0:T(8,128)S(1)}) fusion(pred[1024,1024]{0,1:T(8,128)(4,1)S(1)} %iota_compare_fusion, f32[1024,4,128]{2,1,0:T(4,128)S(1)} %get-tuple-element.49, f32[1024,4,128]{2,1,0:T(4,128)S(1)} %get-tuple-element.48), kind=kOutput, calls=%fused_computation.16 | convolution fusion | flops 3233804288 | bytes 22036480 | tf_op jit(solution)/shard_map/while/body/eval_jaxpr/qhd,khd->hqk/dot_general | solution.py:43
  236.7 7.2 %fusion.55 = (f32[4,1024]{1,0:T(4,128)S(1)}, f32[4,1024,1024]{1,2,0:T(8,128)}) fusion(f32[4,1024]{1,0:T(4,128)S(1)} %get-tuple-element.54, f32[4,1024,1024]{1,2,0:T(8,128)S(1)} %get-tuple-element.55, pred[1024,1024]{0,1:T(8,128)(4,1)S(1)} %iota_compare_fusion), kind=kLoop, calls=%fused_computation.99 | loop fusion | flops 16773120 | bytes 34635776 | tf_op jit(solution)/shard_map/while/body/eval_jaxpr/reduce_sum | solution.py:50
  243.9 10.7 %all-to-all-done = f32[1536,4,128]{2,1,0:T(4,128)} async-done(((f32[1536,4,128]{2,1,0:T(4,128)}), f32[1536,4,128]{2,1,0:T(4,128)}, u32[]{:S(2)}, u32[]{:S(2)}) %all-to-all-start) | async-done | bytes 3145760 | tf_op jit(solution)/shard_map/all_to_all | solution.py:116
  254.6 5.6 %gather_fusion.1 = f32[1024,4,128]{2,1,0:T(4,128)S(1)} fusion(f32[1536,4,128]{2,1,0:T(4,128)} %all-to-all-done, s32[1024]{0:T(1024)S(1)} %fusion.48), kind=kCustom, calls=%fused_computation.1 | custom fusion | bytes 4198400 | tf_op jit(solution)/shard_map/gather | solution.py:108
  262.1 6.1 %fusion.16 = f32[1024,2,128]{0,2,1:T(8,128)S(1)} fusion(f32[4,1024,1024]{1,2,0:T(8,128)} %get-tuple-element.39, f32[1024,2,128]{2,1,0:T(2,128)S(1)} %get-tuple-element.42, f32[1024,2]{0,1:T(2,128)S(1)} %get-tuple-element.50), kind=kOutput, calls=%fused_computation.40 | convolution fusion | flops 1610874880 | bytes 10493952 | tf_op jit(solution)/shard_map/while/body/eval_jaxpr/hqk,khd->qhd/dot_general | solution.py:54
  277.7 6.9 %fusion.19 = f32[1024,2,128]{0,2,1:T(8,128)} fusion(f32[4,1024,1024]{1,2,0:T(8,128)} %get-tuple-element.39, f32[1024,2,128]{2,1,0:T(2,128)S(1)} %copy-done.4, f32[1024,2]{0,1:T(2,128)S(1)} %get-tuple-element.51), kind=kOutput, calls=%fused_computation.41 | convolution fusion | flops 1610874880 | bytes 10493952 | tf_op jit(solution)/shard_map/while/body/eval_jaxpr/hqk,khd->qhd/dot_general | solution.py:54
  291.4 23.5 %all-to-all-done.5 = f32[1536,2,128]{2,1,0:T(2,128)S(1)} async-done(((f32[1536,2,128]{2,1,0:T(2,128)}), f32[1536,2,128]{2,1,0:T(2,128)S(1)}, u32[]{:S(2)}, u32[]{:S(2)}) %all-to-all-start.5) | async-done | bytes 1572896 | tf_op jit(solution)/shard_map/all_to_all | solution.py:137
  333.9 17.4 %collective-permute-done.1 = f32[1024,256]{1,0:T(8,128)} collective-permute-done((f32[1024,256]{1,0:T(8,128)}, f32[1024,256]{1,0:T(8,128)}, u32[]{:S(2)}, u32[]{:S(2)}) %collective-permute-start.1) | collective-permute-done | bytes 1048608 | tf_op jit(solution)/shard_map/ppermute | solution.py:142
  351.2 5.4 %convolution_add_fusion = f32[1024,1024]{1,0:T(8,128)} fusion(f32[1024,1024]{1,0:T(8,128)S(1)} %fusion.26, f32[1024,256]{1,0:T(8,128)} %collective-permute-done.1, f32[2,512,1024]{2,1,0:T(8,128)} %collective-permute-done), kind=kOutput, calls=%fused_computation.25 | convolution fusion | flops 1611661312 | bytes 10485760 | tf_op jit(solution)/shard_map/dot_general | solution.py:131
  356.7 5.5 %convolution_add_fusion.1 = f32[1024,1024]{1,0:T(8,128)} fusion(f32[1024,1024]{1,0:T(8,128)S(1)} %fusion.28, f32[1024,256]{1,0:T(8,128)} %collective-permute-done.1, f32[2,512,1024]{2,1,0:T(8,128)} %collective-permute-done), kind=kOutput, calls=%fused_computation.26 | convolution fusion | flops 1611661312 | bytes 10485760 | tf_op jit(solution)/shard_map/dot_general | solution.py:131
  371.7 19.4 %collective-permute-done.2 = f32[1024,256]{1,0:T(8,128)S(1)} collective-permute-done((f32[1024,256]{1,0:T(8,128)}, f32[1024,256]{1,0:T(8,128)S(1)}, u32[]{:S(2)}, u32[]{:S(2)}) %collective-permute-start.2) | collective-permute-done | bytes 1048608 | tf_op jit(solution)/shard_map/ppermute | solution.py:142
  401.8 6.2 %add_add_fusion.1 = f32[1024,1024]{1,0:T(8,128)} fusion(f32[1024,1024]{1,0:T(8,128)} %collective-permute-done.3, f32[1024,1024]{1,0:T(8,128)S(1)} %copy-done.1, f32[1024,1024]{1,0:T(8,128)S(1)} %fusion.24, f32[1024,1024]{1,0:T(8,128)S(1)} %fusion.33), kind=kLoop, calls=%fused_computation.23 | loop fusion | flops 3145728 | bytes 20971520 | tf_op jit(solution)/shard_map/add | solution.py:156
  (75 shorter events, 102.4 us)
Async XLA Ops:
  10.1 19.0 %all-to-all-start.1 = ((s32[8,192,2]{1,2,0:T(2,128)}), s32[8,192,2]{1,2,0:T(2,128)S(1)}, u32[]{:S(2)}, u32[]{:S(2)}) async-start(s32[8,192,2]{1,2,0:T(2,128)} %copy.39), calls=%async_computation.1 | async-start | bytes 32768 | tf_op jit(solution)/shard_map/all_to_all | solution.py:98
  29.1 76.2 %all-to-all-start.2 = ((f32[1536,4,128]{2,1,0:T(4,128)}), f32[1536,4,128]{2,1,0:T(4,128)}, u32[]{:S(2)}, u32[]{:S(2)}) async-start(f32[1536,4,128]{2,1,0:T(4,128)} %gather_fusion.2), calls=%async_computation.2 | async-start | bytes 6291456 | tf_op jit(solution)/shard_map/all_to_all | solution.py:111
  105.3 74.7 %all-to-all-start.3 = ((f32[1536,4,128]{2,1,0:T(4,128)}), f32[1536,4,128]{2,1,0:T(4,128)}, u32[]{:S(2)}, u32[]{:S(2)}) async-start(f32[1536,4,128]{2,1,0:T(4,128)} %gather_fusion.5), calls=%async_computation.3 | async-start | bytes 6291456 | tf_op jit(solution)/shard_map/all_to_all | solution.py:115
  114.7 91.7 %collective-permute-start = (f32[2,512,1024]{2,1,0:T(8,128)}, f32[2,512,1024]{2,1,0:T(8,128)}, u32[]{:S(2)}, u32[]{:S(2)}) collective-permute-start(f32[2,512,1024]{2,1,0:T(8,128)} %pad_maximum_fusion), channel_id=1, source_target_pairs={{0,2},{1,3},{2,0},{3,1},{4,6},{5,7},{6,4},{7,5},{8,10},{9,11},{10,... | collective-permute-start | bytes 12582920 | tf_op jit(solution)/shard_map/ppermute | solution.py:174
  180.0 74.6 %all-to-all-start = ((f32[1536,4,128]{2,1,0:T(4,128)}), f32[1536,4,128]{2,1,0:T(4,128)}, u32[]{:S(2)}, u32[]{:S(2)}) async-start(f32[1536,4,128]{2,1,0:T(4,128)} %gather_fusion), calls=%async_computation | async-start | bytes 6291456 | tf_op jit(solution)/shard_map/all_to_all | solution.py:116
  221.6 1.6 copy-start
  223.2 1.2 copy-start.5
  223.2 1.2 copy-start.6
  274.0 3.8 copy-start.4
  274.0 40.9 %all-to-all-start.5 = ((f32[1536,2,128]{2,1,0:T(2,128)}), f32[1536,2,128]{2,1,0:T(2,128)S(1)}, u32[]{:S(2)}, u32[]{:S(2)}) async-start(f32[1536,2,128]{2,1,0:T(2,128)} %gather_fusion.8), calls=%async_computation.5 | async-start | bytes 3145728 | tf_op jit(solution)/shard_map/all_to_all | solution.py:137
  314.9 1.1 copy-start.3
  316.0 46.2 %all-to-all-start.4 = ((f32[1536,2,128]{2,1,0:T(2,128)}), f32[1536,2,128]{2,1,0:T(2,128)S(1)}, u32[]{:S(2)}, u32[]{:S(2)}) async-start(f32[1536,2,128]{2,1,0:T(2,128)} %gather_fusion.7), calls=%async_computation.4 | async-start | bytes 3145728 | tf_op jit(solution)/shard_map/all_to_all | solution.py:137
  326.1 25.1 %collective-permute-start.1 = (f32[1024,256]{1,0:T(8,128)}, f32[1024,256]{1,0:T(8,128)}, u32[]{:S(2)}, u32[]{:S(2)}) collective-permute-start(f32[1024,256]{1,0:T(8,128)} %bitcast.71), channel_id=1, source_target_pairs={{0,2},{1,3},{2,0},{3,1},{4,6},{5,7},{6,4},{7,5},{8,10},{9,11},{10,... | collective-permute-start | bytes 3145736 | tf_op jit(solution)/shard_map/ppermute | solution.py:142
  367.0 24.1 %collective-permute-start.2 = (f32[1024,256]{1,0:T(8,128)}, f32[1024,256]{1,0:T(8,128)S(1)}, u32[]{:S(2)}, u32[]{:S(2)}) collective-permute-start(f32[1024,256]{1,0:T(8,128)} %bitcast.70), channel_id=1, source_target_pairs={{0,2},{1,3},{2,0},{3,1},{4,6},{5,7},{6,4},{7,5},{8,10},{9,11},{10,... | collective-permute-start | bytes 3145736 | tf_op jit(solution)/shard_map/ppermute | solution.py:142
  368.5 22.6 %copy-start.2 = (f32[1024,1024]{1,0:T(8,128)S(1)}, f32[1024,1024]{1,0:T(8,128)}, u32[]{:S(2)}) copy-start(f32[1024,1024]{1,0:T(8,128)} %convolution_add_fusion.1) | copy-start | bytes 12582916
  394.4 7.4 %collective-permute-start.3 = (f32[1024,1024]{1,0:T(8,128)S(1)}, f32[1024,1024]{1,0:T(8,128)}, u32[]{:S(2)}, u32[]{:S(2)}) collective-permute-start(f32[1024,1024]{1,0:T(8,128)S(1)} %add_add_fusion), channel_id=1, source_target_pairs={{0,1},{1,0},{2,3},{3,2},{4,5},{5,4},{6,7},{7,6},{8,9},{9,8},{10,11... | collective-permute-start | bytes 12582920 | tf_op jit(solution)/shard_map/ppermute | solution.py:155
  397.5 4.2 %copy-start.1 = (f32[1024,1024]{1,0:T(8,128)S(1)}, f32[1024,1024]{1,0:T(8,128)}, u32[]{:S(2)}) copy-start(f32[1024,1024]{1,0:T(8,128)} %convolution_add_fusion) | copy-start | bytes 12582916

commit v16 on v15

--- a/solution.py
+++ b/solution.py
@@ -137,23 +137,28 @@
         back = lax.all_to_all(part, "seq", split_axis=0, concat_axis=0, tiled=True)
         return back
 
-    def half_terms(back, lo, hi):
+    def half_terms(back, lo, hi, start_partner, start_own):
         mixed = back[send_row].reshape(row_count, (hi - lo) * DH)
         far_mixed = lax.ppermute(mixed, "head", swap_pairs(head_count, 2))
         rows = slice(lo * DH, hi * DH)
-        to_partner = dot(mixed, partner_w[rows]) + dot(far_mixed, far_weights[1, rows])
-        to_own = dot(mixed, own_w[rows]) + dot(far_mixed, far_weights[0, rows])
+        near_partner = start_partner + dot(mixed, partner_w[rows])
+        near_own = start_own + dot(mixed, own_w[rows])
+        far_mixed, near_partner, near_own = lax.optimization_barrier(
+            (far_mixed, near_partner, near_own)
+        )
+        to_partner = near_partner + dot(far_mixed, far_weights[1, rows])
+        to_own = near_own + dot(far_mixed, far_weights[0, rows])
         return to_partner, to_own
 
-    first_partner, first_own = half_terms(exchange(0, split), 0, split)
+    zero = jnp.zeros((row_count, partner_w.shape[1]), jnp.float32)
+    first_partner, first_own = half_terms(exchange(0, split), 0, split, zero, zero)
     second_back = exchange(split, heads_here)
     second_back, first_partner, first_own = lax.optimization_barrier(
         (second_back, first_partner, first_own)
     )
-    second_partner, second_own = half_terms(second_back, split, heads_here)
-    for_partner = first_partner + second_partner
+    for_partner, own = half_terms(second_back, split, heads_here, first_partner, first_own)
     from_partner = lax.ppermute(for_partner, "head", swap_pairs(head_count, 1))
-    return first_own + second_own + from_partner
+    return own + from_partner
 
 
 def swap_pairs(count, bit):

time: 416 us -> 415 us (level)
    ppermute x2, waiting for transfers between devices: 36.8 us -> 32 us  [half_terms(): far_mixed = lax.ppermute(mixed, 'head', swap_pairs(head_count, 2))]
    add x1 -> x4, other arithmetic: 6.22 us -> 10.2 us  [the longest x2 3.88 us: half_terms(): to_partner = near_partner + dot(far_mixed, far_weights[1, rows])]
  transfers between devices with their start and end apart: 10 -> 10, of which waited for: 8 -> 8; matrix products, arithmetic and copies ran while one was open for 32% -> 33% of each run, Pallas kernels for 0% -> 0%
where the time goes in v16:
time: 415 us; the launch traced here: 407 us
  waiting for transfers between devices  195 us (47%)
  local copies, waits for them, and re-layouts  93.4 us (23%)
  matrix products  49 us (12%)
  starting transfers between devices  34.7 us (8%)
  other arithmetic  34.3 us (8%)
    all_to_all x1, waiting for transfers between devices, per_device(): lax.all_to_all(send_q, 'seq', split_axis=0, concat_axis=0, tiled=True)  62.7 us
    all_to_all x1, waiting for transfers between devices, per_device(): lax.all_to_all(send_k, 'seq', split_axis=0, concat_axis=0, tiled=True)  56.3 us
    ppermute x2, waiting for transfers between devices, half_terms(): far_mixed = lax.ppermute(mixed, 'head', swap_pairs(head_count, 2))  32 us
    dot_general x8, matrix products, dot(): jnp.dot(lhs, weight, precision=lax.Precision.HIGH, preferred_element_type...  27.1 us
    gather x4, local copies, waits for them, and re-layouts, place(): return pieces[where_from]  27 us
    all_to_all x2, waiting for transfers between devices, exchange(): back = lax.all_to_all(part, 'seq', split_axis=0, concat_axis=0, tiled=True)  23.5 us
    dot_general x2, matrix products, cluster_attention(): jnp.einsum('hqk,khd->qhd', weights[lo:hi], value_c[:, lo:hi], precision=l...  13 us
    all_to_all x1, waiting for transfers between devices, per_device(): lax.all_to_all(send_v, 'seq', split_axis=0, concat_axis=0, tiled=True)  10.8 us
  transfers between devices with their start and end apart: 10, of which 8 were waited for; matrix products, arithmetic and copies ran while one was open for 33% of the time, Pallas kernels for 0%

profile of v16, /device:TPU:0, one launch (start us, length us, event | category | flops | bytes accessed | tf_op | source)
XLA Modules:
  0.0 406.7 jit_solution(8902380797766697329)
XLA Ops:
  10.0 7.3 %all-to-all-start.1 = ((s32[8,192,2]{1,2,0:T(2,128)}), s32[8,192,2]{1,2,0:T(2,128)S(1)}, u32[]{:S(2)}, u32[]{:S(2)}) async-start(s32[8,192,2]{1,2,0:T(2,128)} %copy.39), calls=%async_computation.1 | async-start | bytes 32768 | tf_op jit(solution)/shard_map/all_to_all | solution.py:98
  23.6 5.5 %gather_fusion.2 = f32[1536,4,128]{2,1,0:T(4,128)} fusion(f32[1024,4,128]{2,1,0:T(4,128)S(1)} %reshape.135, s32[2048]{0:T(1024)S(1)} %pad_clamp_fusion.1), kind=kCustom, calls=%fused_computation.2 | custom fusion | bytes 6297600 | tf_op jit(solution)/shard_map/gather | solution.py:90
  29.1 6.0 %all-to-all-start.2 = ((f32[1536,4,128]{2,1,0:T(4,128)}), f32[1536,4,128]{2,1,0:T(4,128)}, u32[]{:S(2)}, u32[]{:S(2)}) async-start(f32[1536,4,128]{2,1,0:T(4,128)} %gather_fusion.2), calls=%async_computation.2 | async-start | bytes 6291456 | tf_op jit(solution)/shard_map/all_to_all | solution.py:111
  37.0 5.6 %gather_fusion.5 = f32[1536,4,128]{2,1,0:T(4,128)} fusion(f32[1024,4,128]{2,1,0:T(4,128)S(1)} %reshape.136, s32[2048]{0:T(1024)S(1)} %pad_clamp_fusion.1), kind=kCustom, calls=%fused_computation.5 | custom fusion | bytes 6297600 | tf_op jit(solution)/shard_map/gather | solution.py:91
  42.6 62.7 %all-to-all-done.2 = f32[1536,4,128]{2,1,0:T(4,128)} async-done(((f32[1536,4,128]{2,1,0:T(4,128)}), f32[1536,4,128]{2,1,0:T(4,128)}, u32[]{:S(2)}, u32[]{:S(2)}) %all-to-all-start.2) | async-done | bytes 3145760 | tf_op jit(solution)/shard_map/all_to_all | solution.py:111
  118.1 5.5 %gather_fusion = f32[1536,4,128]{2,1,0:T(4,128)} fusion(f32[1024,4,128]{2,1,0:T(4,128)S(1)} %reshape.133, s32[2048]{0:T(1024)S(1)} %pad_clamp_fusion.1), kind=kCustom, calls=%fused_computation | custom fusion | bytes 6297600 | tf_op jit(solution)/shard_map/gather | solution.py:92
  123.7 56.3 %all-to-all-done.3 = f32[1536,4,128]{2,1,0:T(4,128)} async-done(((f32[1536,4,128]{2,1,0:T(4,128)}), f32[1536,4,128]{2,1,0:T(4,128)}, u32[]{:S(2)}, u32[]{:S(2)}) %all-to-all-start.3) | async-done | bytes 3145760 | tf_op jit(solution)/shard_map/all_to_all | solution.py:115
  185.0 6.6 %scatter_custom_fusion.2 = s32[1024]{0:T(1024)S(1)} fusion(s32[1536]{0:T(1024)S(1)} %get-tuple-element.46, s32[1536]{0:T(1024)S(1)} %iota.37, s32[]{:T(128)} %constant.53.clone.1), kind=kCustom, calls=%fused_computation.94 | custom fusion | bytes 4100 | tf_op jit(solution)/shard_map/scatter | solution.py:104
  191.6 6.2 %gather_fusion.4 = s32[1024]{0:T(1024)S(1)} fusion(s32[1536]{0:T(1024)S(1)} %get-tuple-element.47, s32[1024]{0:T(1024)S(1)} %fusion.49), kind=kCustom, calls=%fused_computation.4 | custom fusion | bytes 12288 | tf_op jit(solution)/shard_map/gather | solution.py:108
  201.0 5.3 %collective-permute-done = f32[2,512,1024]{2,1,0:T(8,128)} collective-permute-done((f32[2,512,1024]{2,1,0:T(8,128)}, f32[2,512,1024]{2,1,0:T(8,128)}, u32[]{:S(2)}, u32[]{:S(2)}) %collective-permute-start) | collective-permute-done | bytes 4194336 | tf_op jit(solution)/shard_map/ppermute | solution.py:179
  206.4 5.4 %gather_fusion.3 = f32[1024,4,128]{2,1,0:T(4,128)S(1)} fusion(f32[1536,4,128]{2,1,0:T(4,128)} %all-to-all-done.2, s32[1024]{0:T(1024)S(1)} %fusion.49), kind=kCustom, calls=%fused_computation.3 | custom fusion | bytes 4198400 | tf_op jit(solution)/shard_map/gather | solution.py:108
  211.8 9.8 %gather_fusion.6 = f32[1024,4,128]{2,1,0:T(4,128)} fusion(f32[1536,4,128]{2,1,0:T(4,128)} %all-to-all-done.3, s32[1024]{0:T(1024)S(1)} %fusion.49), kind=kCustom, calls=%fused_computation.6 | custom fusion | bytes 4198400 | tf_op jit(solution)/shard_map/gather | solution.py:108
  227.7 9.0 %fusion = (f32[4,1024]{1,0:T(4,128)S(1)}, f32[4,1024,1024]{1,2,0:T(8,128)S(1)}) fusion(pred[1024,1024]{0,1:T(8,128)(4,1)S(1)} %iota_compare_fusion, f32[1024,4,128]{2,1,0:T(4,128)S(1)} %get-tuple-element.61, f32[1024,4,128]{2,1,0:T(4,128)S(1)} %get-tuple-element.60), kind=kOutput, calls=%fused_computation.16 | convolution fusion | flops 3233804288 | bytes 22036480 | tf_op jit(solution)/shard_map/while/body/eval_jaxpr/qhd,khd->hqk/dot_general | solution.py:43
  236.7 7.2 %fusion.56 = (f32[4,1024]{1,0:T(4,128)S(1)}, f32[4,1024,1024]{1,2,0:T(8,128)}) fusion(f32[4,1024]{1,0:T(4,128)S(1)} %get-tuple-element.66, f32[4,1024,1024]{1,2,0:T(8,128)S(1)} %get-tuple-element.67, pred[1024,1024]{0,1:T(8,128)(4,1)S(1)} %iota_compare_fusion), kind=kLoop, calls=%fused_computation.99 | loop fusion | flops 16773120 | bytes 34635776 | tf_op jit(solution)/shard_map/while/body/eval_jaxpr/reduce_sum | solution.py:50
  243.9 10.8 %all-to-all-done = f32[1536,4,128]{2,1,0:T(4,128)} async-done(((f32[1536,4,128]{2,1,0:T(4,128)}), f32[1536,4,128]{2,1,0:T(4,128)}, u32[]{:S(2)}, u32[]{:S(2)}) %all-to-all-start) | async-done | bytes 3145760 | tf_op jit(solution)/shard_map/all_to_all | solution.py:116
  254.6 5.6 %gather_fusion.1 = f32[1024,4,128]{2,1,0:T(4,128)S(1)} fusion(f32[1536,4,128]{2,1,0:T(4,128)} %all-to-all-done, s32[1024]{0:T(1024)S(1)} %fusion.49), kind=kCustom, calls=%fused_computation.1 | custom fusion | bytes 4198400 | tf_op jit(solution)/shard_map/gather | solution.py:108
  262.1 6.1 %fusion.16 = f32[1024,2,128]{0,2,1:T(8,128)S(1)} fusion(f32[4,1024,1024]{1,2,0:T(8,128)} %get-tuple-element.51, f32[1024,2,128]{2,1,0:T(2,128)S(1)} %get-tuple-element.54, f32[1024,2]{0,1:T(2,128)S(1)} %get-tuple-element.62), kind=kOutput, calls=%fused_computation.39 | convolution fusion | flops 1610874880 | bytes 10493952 | tf_op jit(solution)/shard_map/while/body/eval_jaxpr/hqk,khd->qhd/dot_general | solution.py:54
  268.7 5.2 %gather_fusion.8 = f32[1536,2,128]{2,1,0:T(2,128)} fusion(f32[1024,2,128]{2,1,0:T(2,128)S(1)} %copy.48, s32[2048]{0:T(1024)S(1)} %pad_clamp_fusion), kind=kCustom, calls=%fused_computation.8 | custom fusion | bytes 3151872 | tf_op jit(solution)/shard_map/gather | solution.py:136
  277.7 6.9 %fusion.19 = f32[1024,2,128]{0,2,1:T(8,128)} fusion(f32[4,1024,1024]{1,2,0:T(8,128)} %get-tuple-element.51, f32[1024,2,128]{2,1,0:T(2,128)S(1)} %copy-done.3, f32[1024,2]{0,1:T(2,128)S(1)} %get-tuple-element.63), kind=kOutput, calls=%fused_computation.40 | convolution fusion | flops 1610874880 | bytes 10493952 | tf_op jit(solution)/shard_map/while/body/eval_jaxpr/hqk,khd->qhd/dot_general | solution.py:54
  286.1 5.2 %gather_fusion.7 = f32[1536,2,128]{2,1,0:T(2,128)} fusion(f32[1024,2,128]{2,1,0:T(2,128)S(1)} %copy.45, s32[2048]{0:T(1024)S(1)} %pad_clamp_fusion), kind=kCustom, calls=%fused_computation.7 | custom fusion | bytes 3151872 | tf_op jit(solution)/shard_map/gather | solution.py:136
  291.4 23.5 %all-to-all-done.5 = f32[1536,2,128]{2,1,0:T(2,128)S(1)} async-done(((f32[1536,2,128]{2,1,0:T(2,128)}), f32[1536,2,128]{2,1,0:T(2,128)S(1)}, u32[]{:S(2)}, u32[]{:S(2)}) %all-to-all-start.5) | async-done | bytes 1572896 | tf_op jit(solution)/shard_map/all_to_all | solution.py:137
  320.1 5.0 %gather_fusion.9 = f32[1024,2,128]{2,1,0:T(2,128)S(1)} fusion(f32[1536,2,128]{2,1,0:T(2,128)} %copy-done.2, s32[1024]{0:T(1024)S(1)} %get-tuple-element.48), kind=kCustom, calls=%fused_computation.9 | custom fusion | bytes 2101248 | tf_op jit(solution)/shard_map/gather | solution.py:141
  333.9 17.4 %collective-permute-done.1 = f32[1024,256]{1,0:T(8,128)} collective-permute-done((f32[1024,256]{1,0:T(8,128)}, f32[1024,256]{1,0:T(8,128)}, u32[]{:S(2)}, u32[]{:S(2)}) %collective-permute-start.1) | collective-permute-done | bytes 1048608 | tf_op jit(solution)/shard_map/ppermute | solution.py:142
  377.1 14.6 %collective-permute-done.2 = f32[1024,256]{1,0:T(8,128)S(1)} collective-permute-done((f32[1024,256]{1,0:T(8,128)S(1)}, f32[1024,256]{1,0:T(8,128)S(1)}, u32[]{:S(2)}, u32[]{:S(2)}) %collective-permute-start.2) | collective-permute-done | bytes 1048608 | tf_op jit(solution)/shard_map/ppermute | solution.py:142
  (76 shorter events, 107.4 us)
Async XLA Ops:
  10.0 19.0 %all-to-all-start.1 = ((s32[8,192,2]{1,2,0:T(2,128)}), s32[8,192,2]{1,2,0:T(2,128)S(1)}, u32[]{:S(2)}, u32[]{:S(2)}) async-start(s32[8,192,2]{1,2,0:T(2,128)} %copy.39), calls=%async_computation.1 | async-start | bytes 32768 | tf_op jit(solution)/shard_map/all_to_all | solution.py:98
  29.1 76.2 %all-to-all-start.2 = ((f32[1536,4,128]{2,1,0:T(4,128)}), f32[1536,4,128]{2,1,0:T(4,128)}, u32[]{:S(2)}, u32[]{:S(2)}) async-start(f32[1536,4,128]{2,1,0:T(4,128)} %gather_fusion.2), calls=%async_computation.2 | async-start | bytes 6291456 | tf_op jit(solution)/shard_map/all_to_all | solution.py:111
  105.3 74.6 %all-to-all-start.3 = ((f32[1536,4,128]{2,1,0:T(4,128)}), f32[1536,4,128]{2,1,0:T(4,128)}, u32[]{:S(2)}, u32[]{:S(2)}) async-start(f32[1536,4,128]{2,1,0:T(4,128)} %gather_fusion.5), calls=%async_computation.3 | async-start | bytes 6291456 | tf_op jit(solution)/shard_map/all_to_all | solution.py:115
  114.7 91.7 %collective-permute-start = (f32[2,512,1024]{2,1,0:T(8,128)}, f32[2,512,1024]{2,1,0:T(8,128)}, u32[]{:S(2)}, u32[]{:S(2)}) collective-permute-start(f32[2,512,1024]{2,1,0:T(8,128)} %pad_maximum_fusion), channel_id=1, source_target_pairs={{0,2},{1,3},{2,0},{3,1},{4,6},{5,7},{6,4},{7,5},{8,10},{9,11},{10,... | collective-permute-start | bytes 12582920 | tf_op jit(solution)/shard_map/ppermute | solution.py:179
  180.0 74.6 %all-to-all-start = ((f32[1536,4,128]{2,1,0:T(4,128)}), f32[1536,4,128]{2,1,0:T(4,128)}, u32[]{:S(2)}, u32[]{:S(2)}) async-start(f32[1536,4,128]{2,1,0:T(4,128)} %gather_fusion), calls=%async_computation | async-start | bytes 6291456 | tf_op jit(solution)/shard_map/all_to_all | solution.py:116
  221.6 1.6 copy-start
  223.2 1.2 copy-start.4
  223.2 1.2 copy-start.5
  273.9 3.8 copy-start.3
  273.9 40.9 %all-to-all-start.5 = ((f32[1536,2,128]{2,1,0:T(2,128)}), f32[1536,2,128]{2,1,0:T(2,128)S(1)}, u32[]{:S(2)}, u32[]{:S(2)}) async-start(f32[1536,2,128]{2,1,0:T(2,128)} %gather_fusion.8), calls=%async_computation.5 | async-start | bytes 3145728 | tf_op jit(solution)/shard_map/all_to_all | solution.py:137
  314.9 1.1 copy-start.2
  316.0 47.9 %all-to-all-start.4 = ((f32[1536,2,128]{2,1,0:T(2,128)}), f32[1536,2,128]{2,1,0:T(2,128)S(1)}, u32[]{:S(2)}, u32[]{:S(2)}) async-start(f32[1536,2,128]{2,1,0:T(2,128)} %gather_fusion.7), calls=%async_computation.4 | async-start | bytes 3145728 | tf_op jit(solution)/shard_map/all_to_all | solution.py:137
  326.1 25.1 %collective-permute-start.1 = (f32[1024,256]{1,0:T(8,128)}, f32[1024,256]{1,0:T(8,128)}, u32[]{:S(2)}, u32[]{:S(2)}) collective-permute-start(f32[1024,256]{1,0:T(8,128)} %bitcast.71), channel_id=1, source_target_pairs={{0,2},{1,3},{2,0},{3,1},{4,6},{5,7},{6,4},{7,5},{8,10},{9,11},{10,... | collective-permute-start | bytes 3145736 | tf_op jit(solution)/shard_map/ppermute | solution.py:142
  367.7 24.0 %collective-permute-start.2 = (f32[1024,256]{1,0:T(8,128)S(1)}, f32[1024,256]{1,0:T(8,128)S(1)}, u32[]{:S(2)}, u32[]{:S(2)}) collective-permute-start(f32[1024,256]{1,0:T(8,128)S(1)} %bitcast.80), channel_id=1, source_target_pairs={{0,2},{1,3},{2,0},{3,1},{4,6},{5,7},{6,4},{7,5},{8,10},{9,11},{10,... | collective-permute-start | bytes 3145736 | tf_op jit(solution)/shard_map/ppermute | solution.py:142
  369.3 4.7 %copy-start.1 = (f32[1024,1024]{1,0:T(8,128)S(1)}, f32[1024,1024]{1,0:T(8,128)}, u32[]{:S(2)}) copy-start(f32[1024,1024]{1,0:T(8,128)} %add.102) | copy-start | bytes 12582916
  395.8 7.2 %collective-permute-start.3 = (f32[1024,1024]{1,0:T(8,128)S(1)}, f32[1024,1024]{1,0:T(8,128)S(1)}, u32[]{:S(2)}, u32[]{:S(2)}) collective-permute-start(f32[1024,1024]{1,0:T(8,128)S(1)} %add.107), channel_id=1, source_target_pairs={{0,1},{1,0},{2,3},{3,2},{4,5},{5,4},{6,7},{7,6},{8,9},{9,8},{10,11... | collective-permute-start | bytes 12582920 | tf_op jit(solution)/shard_map/ppermute | solution.py:160

commit v17 on v16

--- a/solution.py
+++ b/solution.py
@@ -137,26 +137,31 @@
         back = lax.all_to_all(part, "seq", split_axis=0, concat_axis=0, tiled=True)
         return back
 
-    def half_terms(back, lo, hi, start_partner, start_own):
+    def half_terms(back, lo, hi, start_partner, start_own, hold):
         mixed = back[send_row].reshape(row_count, (hi - lo) * DH)
         far_mixed = lax.ppermute(mixed, "head", swap_pairs(head_count, 2))
         rows = slice(lo * DH, hi * DH)
-        near_partner = start_partner + dot(mixed, partner_w[rows])
-        near_own = start_own + dot(mixed, own_w[rows])
-        far_mixed, near_partner, near_own = lax.optimization_barrier(
-            (far_mixed, near_partner, near_own)
-        )
+        near_partner = dot(mixed, partner_w[rows])
+        near_own = dot(mixed, own_w[rows])
+        if start_partner is not None:
+            near_partner = start_partner + near_partner
+            near_own = start_own + near_own
+        if hold:
+            far_mixed, near_partner, near_own = lax.optimization_barrier(
+                (far_mixed, near_partner, near_own)
+            )
         to_partner = near_partner + dot(far_mixed, far_weights[1, rows])
         to_own = near_own + dot(far_mixed, far_weights[0, rows])
         return to_partner, to_own
 
-    zero = jnp.zeros((row_count, partner_w.shape[1]), jnp.float32)
-    first_partner, first_own = half_terms(exchange(0, split), 0, split, zero, zero)
+    first_partner, first_own = half_terms(exchange(0, split), 0, split, None, None, False)
     second_back = exchange(split, heads_here)
     second_back, first_partner, first_own = lax.optimization_barrier(
         (second_back, first_partner, first_own)
     )
-    for_partner, own = half_terms(second_back, split, heads_here, first_partner, first_own)
+    for_partner, own = half_terms(
+        second_back, split, heads_here, first_partner, first_own, True
+    )
     from_partner = lax.ppermute(for_partner, "head", swap_pairs(head_count, 1))
     return own + from_partner
 

time: 415 us -> 413 us (level)
  other arithmetic: 34.3 us -> 28.5 us
where the time goes in v17:
time: 413 us; the launch traced here: 405 us
  waiting for transfers between devices  195 us (47%)
  local copies, waits for them, and re-layouts  93.4 us (23%)
  matrix products  53.1 us (13%)
  starting transfers between devices  34.7 us (8%)
  other arithmetic  28.5 us (7%)
    all_to_all x1, waiting for transfers between devices, per_device(): lax.all_to_all(send_q, 'seq', split_axis=0, concat_axis=0, tiled=True)  62.7 us
    all_to_all x1, waiting for transfers between devices, per_device(): lax.all_to_all(send_k, 'seq', split_axis=0, concat_axis=0, tiled=True)  56.3 us
    ppermute x2, waiting for transfers between devices, half_terms(): far_mixed = lax.ppermute(mixed, 'head', swap_pairs(head_count, 2))  31.9 us
    dot_general x8, matrix products, dot(): jnp.dot(lhs, weight, precision=lax.Precision.HIGH, preferred_element_type...  31.2 us
    gather x4, local copies, waits for them, and re-layouts, place(): return pieces[where_from]  27 us
    all_to_all x2, waiting for transfers between devices, exchange(): back = lax.all_to_all(part, 'seq', split_axis=0, concat_axis=0, tiled=True)  23.5 us
    dot_general x2, matrix products, cluster_attention(): jnp.einsum('hqk,khd->qhd', weights[lo:hi], value_c[:, lo:hi], precision=l...  13 us
    all_to_all x1, waiting for transfers between devices, per_device(): lax.all_to_all(send_v, 'seq', split_axis=0, concat_axis=0, tiled=True)  10.8 us
  transfers between devices with their start and end apart: 10, of which 8 were waited for; matrix products, arithmetic and copies ran while one was open for 33% of the time, Pallas kernels for 0%

profile of v17, /device:TPU:0, one launch (start us, length us, event | category | flops | bytes accessed | tf_op | source)
XLA Modules:
  0.0 404.9 jit_solution(9370851255286004834)
XLA Ops:
  10.0 7.3 %all-to-all-start.1 = ((s32[8,192,2]{1,2,0:T(2,128)}), s32[8,192,2]{1,2,0:T(2,128)S(1)}, u32[]{:S(2)}, u32[]{:S(2)}) async-start(s32[8,192,2]{1,2,0:T(2,128)} %copy.39), calls=%async_computation.1 | async-start | bytes 32768 | tf_op jit(solution)/shard_map/all_to_all | solution.py:98
  23.6 5.5 %gather_fusion.2 = f32[1536,4,128]{2,1,0:T(4,128)} fusion(f32[1024,4,128]{2,1,0:T(4,128)S(1)} %reshape.135, s32[2048]{0:T(1024)S(1)} %pad_clamp_fusion.1), kind=kCustom, calls=%fused_computation.2 | custom fusion | bytes 6297600 | tf_op jit(solution)/shard_map/gather | solution.py:90
  29.1 6.0 %all-to-all-start.2 = ((f32[1536,4,128]{2,1,0:T(4,128)}), f32[1536,4,128]{2,1,0:T(4,128)}, u32[]{:S(2)}, u32[]{:S(2)}) async-start(f32[1536,4,128]{2,1,0:T(4,128)} %gather_fusion.2), calls=%async_computation.2 | async-start | bytes 6291456 | tf_op jit(solution)/shard_map/all_to_all | solution.py:111
  37.0 5.6 %gather_fusion.5 = f32[1536,4,128]{2,1,0:T(4,128)} fusion(f32[1024,4,128]{2,1,0:T(4,128)S(1)} %reshape.136, s32[2048]{0:T(1024)S(1)} %pad_clamp_fusion.1), kind=kCustom, calls=%fused_computation.5 | custom fusion | bytes 6297600 | tf_op jit(solution)/shard_map/gather | solution.py:91
  42.6 62.7 %all-to-all-done.2 = f32[1536,4,128]{2,1,0:T(4,128)} async-done(((f32[1536,4,128]{2,1,0:T(4,128)}), f32[1536,4,128]{2,1,0:T(4,128)}, u32[]{:S(2)}, u32[]{:S(2)}) %all-to-all-start.2) | async-done | bytes 3145760 | tf_op jit(solution)/shard_map/all_to_all | solution.py:111
  118.1 5.5 %gather_fusion = f32[1536,4,128]{2,1,0:T(4,128)} fusion(f32[1024,4,128]{2,1,0:T(4,128)S(1)} %reshape.133, s32[2048]{0:T(1024)S(1)} %pad_clamp_fusion.1), kind=kCustom, calls=%fused_computation | custom fusion | bytes 6297600 | tf_op jit(solution)/shard_map/gather | solution.py:92
  123.7 56.3 %all-to-all-done.3 = f32[1536,4,128]{2,1,0:T(4,128)} async-done(((f32[1536,4,128]{2,1,0:T(4,128)}), f32[1536,4,128]{2,1,0:T(4,128)}, u32[]{:S(2)}, u32[]{:S(2)}) %all-to-all-start.3) | async-done | bytes 3145760 | tf_op jit(solution)/shard_map/all_to_all | solution.py:115
  185.0 6.6 %scatter_custom_fusion.2 = s32[1024]{0:T(1024)S(1)} fusion(s32[1536]{0:T(1024)S(1)} %get-tuple-element.40, s32[1536]{0:T(1024)S(1)} %iota.37, s32[]{:T(128)} %constant.53.clone.1), kind=kCustom, calls=%fused_computation.94 | custom fusion | bytes 4100 | tf_op jit(solution)/shard_map/scatter | solution.py:104
  191.6 6.2 %gather_fusion.4 = s32[1024]{0:T(1024)S(1)} fusion(s32[1536]{0:T(1024)S(1)} %get-tuple-element.41, s32[1024]{0:T(1024)S(1)} %fusion.47), kind=kCustom, calls=%fused_computation.4 | custom fusion | bytes 12288 | tf_op jit(solution)/shard_map/gather | solution.py:108
  201.0 5.3 %collective-permute-done = f32[2,512,1024]{2,1,0:T(8,128)} collective-permute-done((f32[2,512,1024]{2,1,0:T(8,128)}, f32[2,512,1024]{2,1,0:T(8,128)}, u32[]{:S(2)}, u32[]{:S(2)}) %collective-permute-start) | collective-permute-done | bytes 4194336 | tf_op jit(solution)/shard_map/ppermute | solution.py:184
  206.4 5.4 %gather_fusion.3 = f32[1024,4,128]{2,1,0:T(4,128)S(1)} fusion(f32[1536,4,128]{2,1,0:T(4,128)} %all-to-all-done.2, s32[1024]{0:T(1024)S(1)} %fusion.47), kind=kCustom, calls=%fused_computation.3 | custom fusion | bytes 4198400 | tf_op jit(solution)/shard_map/gather | solution.py:108
  211.8 9.8 %gather_fusion.6 = f32[1024,4,128]{2,1,0:T(4,128)} fusion(f32[1536,4,128]{2,1,0:T(4,128)} %all-to-all-done.3, s32[1024]{0:T(1024)S(1)} %fusion.47), kind=kCustom, calls=%fused_computation.6 | custom fusion | bytes 4198400 | tf_op jit(solution)/shard_map/gather | solution.py:108
  227.7 9.0 %fusion = (f32[4,1024]{1,0:T(4,128)S(1)}, f32[4,1024,1024]{1,2,0:T(8,128)S(1)}) fusion(pred[1024,1024]{0,1:T(8,128)(4,1)S(1)} %iota_compare_fusion, f32[1024,4,128]{2,1,0:T(4,128)S(1)} %get-tuple-element.55, f32[1024,4,128]{2,1,0:T(4,128)S(1)} %get-tuple-element.54), kind=kOutput, calls=%fused_computation.16 | convolution fusion | flops 3233804288 | bytes 22036480 | tf_op jit(solution)/shard_map/while/body/eval_jaxpr/qhd,khd->hqk/dot_general | solution.py:43
  236.7 7.2 %fusion.54 = (f32[4,1024]{1,0:T(4,128)S(1)}, f32[4,1024,1024]{1,2,0:T(8,128)}) fusion(f32[4,1024]{1,0:T(4,128)S(1)} %get-tuple-element.60, f32[4,1024,1024]{1,2,0:T(8,128)S(1)} %get-tuple-element.61, pred[1024,1024]{0,1:T(8,128)(4,1)S(1)} %iota_compare_fusion), kind=kLoop, calls=%fused_computation.99 | loop fusion | flops 16773120 | bytes 34635776 | tf_op jit(solution)/shard_map/while/body/eval_jaxpr/reduce_sum | solution.py:50
  243.8 10.8 %all-to-all-done = f32[1536,4,128]{2,1,0:T(4,128)} async-done(((f32[1536,4,128]{2,1,0:T(4,128)}), f32[1536,4,128]{2,1,0:T(4,128)}, u32[]{:S(2)}, u32[]{:S(2)}) %all-to-all-start) | async-done | bytes 3145760 | tf_op jit(solution)/shard_map/all_to_all | solution.py:116
  254.6 5.6 %gather_fusion.1 = f32[1024,4,128]{2,1,0:T(4,128)S(1)} fusion(f32[1536,4,128]{2,1,0:T(4,128)} %all-to-all-done, s32[1024]{0:T(1024)S(1)} %fusion.47), kind=kCustom, calls=%fused_computation.1 | custom fusion | bytes 4198400 | tf_op jit(solution)/shard_map/gather | solution.py:108
  262.0 6.1 %fusion.16 = f32[1024,2,128]{0,2,1:T(8,128)S(1)} fusion(f32[4,1024,1024]{1,2,0:T(8,128)} %get-tuple-element.45, f32[1024,2,128]{2,1,0:T(2,128)S(1)} %get-tuple-element.48, f32[1024,2]{0,1:T(2,128)S(1)} %get-tuple-element.56), kind=kOutput, calls=%fused_computation.41 | convolution fusion | flops 1610874880 | bytes 10493952 | tf_op jit(solution)/shard_map/while/body/eval_jaxpr/hqk,khd->qhd/dot_general | solution.py:54
  277.7 6.9 %fusion.19 = f32[1024,2,128]{0,2,1:T(8,128)} fusion(f32[4,1024,1024]{1,2,0:T(8,128)} %get-tuple-element.45, f32[1024,2,128]{2,1,0:T(2,128)S(1)} %copy-done.3, f32[1024,2]{0,1:T(2,128)S(1)} %get-tuple-element.57), kind=kOutput, calls=%fused_computation.42 | convolution fusion | flops 1610874880 | bytes 10493952 | tf_op jit(solution)/shard_map/while/body/eval_jaxpr/hqk,khd->qhd/dot_general | solution.py:54
  286.1 5.2 %gather_fusion.7 = f32[1536,2,128]{2,1,0:T(2,128)} fusion(f32[1024,2,128]{2,1,0:T(2,128)S(1)} %copy.45, s32[2048]{0:T(1024)S(1)} %pad_clamp_fusion), kind=kCustom, calls=%fused_computation.7 | custom fusion | bytes 3151872 | tf_op jit(solution)/shard_map/gather | solution.py:136
  291.4 23.5 %all-to-all-done.5 = f32[1536,2,128]{2,1,0:T(2,128)S(1)} async-done(((f32[1536,2,128]{2,1,0:T(2,128)}), f32[1536,2,128]{2,1,0:T(2,128)S(1)}, u32[]{:S(2)}, u32[]{:S(2)}) %all-to-all-start.5) | async-done | bytes 1572896 | tf_op jit(solution)/shard_map/all_to_all | solution.py:137
  333.9 17.4 %collective-permute-done.1 = f32[1024,256]{1,0:T(8,128)} collective-permute-done((f32[1024,256]{1,0:T(8,128)}, f32[1024,256]{1,0:T(8,128)}, u32[]{:S(2)}, u32[]{:S(2)}) %collective-permute-start.1) | collective-permute-done | bytes 1048608 | tf_op jit(solution)/shard_map/ppermute | solution.py:142
  351.2 5.4 %convolution_add_fusion.2 = f32[1024,1024]{1,0:T(8,128)} fusion(f32[1024,1024]{1,0:T(8,128)S(1)} %fusion.24, f32[1024,256]{1,0:T(8,128)} %collective-permute-done.1, f32[2,512,1024]{2,1,0:T(8,128)} %collective-permute-done), kind=kOutput, calls=%fused_computation.26 | convolution fusion | flops 1611661312 | bytes 10485760 | tf_op jit(solution)/shard_map/dot_general | solution.py:131
  356.7 5.5 %convolution_add_fusion.3 = f32[1024,1024]{1,0:T(8,128)} fusion(f32[1024,1024]{1,0:T(8,128)S(1)} %fusion.26, f32[1024,256]{1,0:T(8,128)} %collective-permute-done.1, f32[2,512,1024]{2,1,0:T(8,128)} %collective-permute-done), kind=kOutput, calls=%fused_computation.27 | convolution fusion | flops 1611661312 | bytes 10485760 | tf_op jit(solution)/shard_map/dot_general | solution.py:131
  375.4 14.6 %collective-permute-done.2 = f32[1024,256]{1,0:T(8,128)S(1)} collective-permute-done((f32[1024,256]{1,0:T(8,128)S(1)}, f32[1024,256]{1,0:T(8,128)S(1)}, u32[]{:S(2)}, u32[]{:S(2)}) %collective-permute-start.2) | collective-permute-done | bytes 1048608 | tf_op jit(solution)/shard_map/ppermute | solution.py:142
  (74 shorter events, 104.9 us)
Async XLA Ops:
  10.0 19.0 %all-to-all-start.1 = ((s32[8,192,2]{1,2,0:T(2,128)}), s32[8,192,2]{1,2,0:T(2,128)S(1)}, u32[]{:S(2)}, u32[]{:S(2)}) async-start(s32[8,192,2]{1,2,0:T(2,128)} %copy.39), calls=%async_computation.1 | async-start | bytes 32768 | tf_op jit(solution)/shard_map/all_to_all | solution.py:98
  29.1 76.2 %all-to-all-start.2 = ((f32[1536,4,128]{2,1,0:T(4,128)}), f32[1536,4,128]{2,1,0:T(4,128)}, u32[]{:S(2)}, u32[]{:S(2)}) async-start(f32[1536,4,128]{2,1,0:T(4,128)} %gather_fusion.2), calls=%async_computation.2 | async-start | bytes 6291456 | tf_op jit(solution)/shard_map/all_to_all | solution.py:111
  105.3 74.6 %all-to-all-start.3 = ((f32[1536,4,128]{2,1,0:T(4,128)}), f32[1536,4,128]{2,1,0:T(4,128)}, u32[]{:S(2)}, u32[]{:S(2)}) async-start(f32[1536,4,128]{2,1,0:T(4,128)} %gather_fusion.5), calls=%async_computation.3 | async-start | bytes 6291456 | tf_op jit(solution)/shard_map/all_to_all | solution.py:115
  114.7 91.7 %collective-permute-start = (f32[2,512,1024]{2,1,0:T(8,128)}, f32[2,512,1024]{2,1,0:T(8,128)}, u32[]{:S(2)}, u32[]{:S(2)}) collective-permute-start(f32[2,512,1024]{2,1,0:T(8,128)} %pad_maximum_fusion), channel_id=1, source_target_pairs={{0,2},{1,3},{2,0},{3,1},{4,6},{5,7},{6,4},{7,5},{8,10},{9,11},{10,... | collective-permute-start | bytes 12582920 | tf_op jit(solution)/shard_map/ppermute | solution.py:184
  180.0 74.6 %all-to-all-start = ((f32[1536,4,128]{2,1,0:T(4,128)}), f32[1536,4,128]{2,1,0:T(4,128)}, u32[]{:S(2)}, u32[]{:S(2)}) async-start(f32[1536,4,128]{2,1,0:T(4,128)} %gather_fusion), calls=%async_computation | async-start | bytes 6291456 | tf_op jit(solution)/shard_map/all_to_all | solution.py:116
  221.6 1.6 copy-start
  223.2 1.2 copy-start.4
  223.2 1.2 copy-start.5
  273.9 3.8 copy-start.3
  273.9 40.9 %all-to-all-start.5 = ((f32[1536,2,128]{2,1,0:T(2,128)}), f32[1536,2,128]{2,1,0:T(2,128)S(1)}, u32[]{:S(2)}, u32[]{:S(2)}) async-start(f32[1536,2,128]{2,1,0:T(2,128)} %gather_fusion.8), calls=%async_computation.5 | async-start | bytes 3145728 | tf_op jit(solution)/shard_map/all_to_all | solution.py:137
  314.9 1.1 copy-start.2
  316.0 46.2 %all-to-all-start.4 = ((f32[1536,2,128]{2,1,0:T(2,128)}), f32[1536,2,128]{2,1,0:T(2,128)S(1)}, u32[]{:S(2)}, u32[]{:S(2)}) async-start(f32[1536,2,128]{2,1,0:T(2,128)} %gather_fusion.7), calls=%async_computation.4 | async-start | bytes 3145728 | tf_op jit(solution)/shard_map/all_to_all | solution.py:137
  326.1 25.1 %collective-permute-start.1 = (f32[1024,256]{1,0:T(8,128)}, f32[1024,256]{1,0:T(8,128)}, u32[]{:S(2)}, u32[]{:S(2)}) collective-permute-start(f32[1024,256]{1,0:T(8,128)} %bitcast.71), channel_id=1, source_target_pairs={{0,2},{1,3},{2,0},{3,1},{4,6},{5,7},{6,4},{7,5},{8,10},{9,11},{10,... | collective-permute-start | bytes 3145736 | tf_op jit(solution)/shard_map/ppermute | solution.py:142
  366.0 24.0 %collective-permute-start.2 = (f32[1024,256]{1,0:T(8,128)S(1)}, f32[1024,256]{1,0:T(8,128)S(1)}, u32[]{:S(2)}, u32[]{:S(2)}) collective-permute-start(f32[1024,256]{1,0:T(8,128)S(1)} %bitcast.80), channel_id=1, source_target_pairs={{0,2},{1,3},{2,0},{3,1},{4,6},{5,7},{6,4},{7,5},{8,10},{9,11},{10,... | collective-permute-start | bytes 3145736 | tf_op jit(solution)/shard_map/ppermute | solution.py:142
  367.6 4.7 %copy-start.1 = (f32[1024,1024]{1,0:T(8,128)S(1)}, f32[1024,1024]{1,0:T(8,128)}, u32[]{:S(2)}) copy-start(f32[1024,1024]{1,0:T(8,128)} %convolution_add_fusion.3) | copy-start | bytes 12582916
  394.0 7.2 %collective-permute-start.3 = (f32[1024,1024]{1,0:T(8,128)S(1)}, f32[1024,1024]{1,0:T(8,128)S(1)}, u32[]{:S(2)}, u32[]{:S(2)}) collective-permute-start(f32[1024,1024]{1,0:T(8,128)S(1)} %add.107), channel_id=1, source_target_pairs={{0,1},{1,0},{2,3},{3,2},{4,5},{5,4},{6,7},{7,6},{8,9},{9,8},{10,11... | collective-permute-start | bytes 12582920 | tf_op jit(solution)/shard_map/ppermute | solution.py:165

commit v18 on v17

--- a/solution.py
+++ b/solution.py
@@ -50,9 +50,9 @@
     total = jnp.sum(weights, -1, keepdims=True)
     split = query_c.shape[1] // 2
     parts = []
-    for lo, hi in ((0, split), (split, query_c.shape[1])):
+    for (lo, hi), value_part in zip(((0, split), (split, query_c.shape[1])), value_c):
         summed = jnp.einsum(
-            "hqk,khd->qhd", weights[lo:hi], value_c[:, lo:hi], precision=lax.Precision.HIGH
+            "hqk,khd->qhd", weights[lo:hi], value_part, precision=lax.Precision.HIGH
         )
         parts.append(summed / jnp.transpose(total[lo:hi], (1, 0, 2)))
     return tuple(parts)
@@ -63,7 +63,9 @@
     grouped = (
         query_all.reshape(row_count // CS, CS, head_count, width),
         key_all.reshape(row_count // CS, CS, head_count, width),
-        value_all.reshape(row_count // CS, CS, head_count, width),
+        tuple(
+            part.reshape(row_count // CS, CS, part.shape[1], width) for part in value_all
+        ),
     )
     parts = lax.map(cluster_attention, grouped)
     return [part.reshape(row_count, part.shape[2], width) for part in parts]
@@ -113,13 +115,16 @@
     received = (
         first_arrived,
         lax.all_to_all(send_k, "seq", split_axis=0, concat_axis=0, tiled=True),
-        lax.all_to_all(send_v, "seq", split_axis=0, concat_axis=0, tiled=True),
+        tuple(
+            lax.all_to_all(send_v[:, lo:hi], "seq", split_axis=0, concat_axis=0, tiled=True)
+            for lo, hi in ((0, heads_here // 2), (heads_here // 2, heads_here))
+        ),
     )
     cos_table, sin_table = yarn_tables(place(arrived_index[:, 1]), DH)
     result = attend_local(
         rotate(place(received[0]), cos_table, sin_table),
         rotate(place(received[1]), cos_table, sin_table),
-        place(received[2]),
+        tuple(place(part) for part in received[2]),
     )
     split = heads_here // 2
     head_count = lax.axis_size("head")

time: 413 us -> 452 us (1.094)
  waiting for transfers between devices: 195 us -> 208 us
  local copies, waits for them, and re-layouts: 93.4 us -> 106 us
  starting transfers between devices: 34.7 us -> 42.4 us
  other arithmetic: 28.5 us -> 33.1 us
    ppermute x1, waiting for transfers between devices: 5.33 us -> 64.7 us  [fetch_far_weights(): return lax.ppermute(outgoing, 'head', swap_pairs(head_count, 2))]
    all_to_all x1, waiting for transfers between devices: 56.3 us -> 0.01 us  [per_device(): lax.all_to_all(send_k, 'seq', split_axis=0, concat_axis=0, tiled=True)]
    all_to_all x1 -> x2, waiting for transfers between devices: 10.8 us -> 29.1 us  [per_device(): lax.all_to_all(send_v[:, lo:hi], 'seq', split_axis=0, concat_axis=0, tile...]
    gather x4 -> x5, local copies, waits for them, and re-layouts: 27 us -> 35.2 us  [place(): return pieces[where_from]]
    all_to_all x2, waiting for transfers between devices: 23.5 us -> 16 us  [exchange(): back = lax.all_to_all(part, 'seq', split_axis=0, concat_axis=0, tiled=True)]
    all_to_all x1 -> x2, starting transfers between devices: 4.45 us -> 11.7 us  [per_device(): lax.all_to_all(send_v[:, lo:hi], 'seq', split_axis=0, concat_axis=0, tile...]
  transfers between devices with their start and end apart: 10 -> 11, of which waited for: 8 -> 7; matrix products, arithmetic and copies ran while one was open for 33% -> 38% of each run, Pallas kernels for 0% -> 0%
where the time goes in v18:
time: 452 us; the launch traced here: 443 us
  waiting for transfers between devices  208 us (46%)
  local copies, waits for them, and re-layouts  106 us (23%)
  matrix products  53.1 us (12%)
  starting transfers between devices  42.4 us (9%)
  other arithmetic  33.1 us (7%)
    ppermute x1, waiting for transfers between devices, fetch_far_weights(): return lax.ppermute(outgoing, 'head', swap_pairs(head_count, 2))  64.7 us
    all_to_all x1, waiting for transfers between devices, per_device(): lax.all_to_all(send_q, 'seq', split_axis=0, concat_axis=0, tiled=True)  62.8 us
    gather x5, local copies, waits for them, and re-layouts, place(): return pieces[where_from]  35.2 us
    ppermute x2, waiting for transfers between devices, half_terms(): far_mixed = lax.ppermute(mixed, 'head', swap_pairs(head_count, 2))  31.6 us
    dot_general x8, matrix products, dot(): jnp.dot(lhs, weight, precision=lax.Precision.HIGH, preferred_element_type...  31.2 us
    all_to_all x2, waiting for transfers between devices, per_device(): lax.all_to_all(send_v[:, lo:hi], 'seq', split_axis=0, concat_axis=0, tile...  29.1 us
    all_to_all x2, waiting for transfers between devices, exchange(): back = lax.all_to_all(part, 'seq', split_axis=0, concat_axis=0, tiled=True)  16 us
    dot_general x2, matrix products, cluster_attention(): jnp.einsum('hqk,khd->qhd', weights[lo:hi], value_part, precision=lax.Prec...  13 us
  transfers between devices with their start and end apart: 11, of which 7 were waited for; matrix products, arithmetic and copies ran while one was open for 38% of the time, Pallas kernels for 0%

profile of v18, /device:TPU:0, one launch (start us, length us, event | category | flops | bytes accessed | tf_op | source)
XLA Modules:
  0.0 443.3 jit_solution(1256945651924630246)
XLA Ops:
  10.1 7.3 %all-to-all-start.1 = ((s32[8,192,2]{1,2,0:T(2,128)}), s32[8,192,2]{1,2,0:T(2,128)S(1)}, u32[]{:S(2)}, u32[]{:S(2)}) async-start(s32[8,192,2]{1,2,0:T(2,128)} %copy.39), calls=%async_computation.1 | async-start | bytes 32768 | tf_op jit(solution)/shard_map/all_to_all | solution.py:100
  23.6 5.5 %gather_fusion = f32[1536,4,128]{2,1,0:T(4,128)} fusion(f32[1024,4,128]{2,1,0:T(4,128)S(1)} %reshape.136, s32[2048]{0:T(1024)S(1)} %pad_clamp_fusion.1), kind=kCustom, calls=%fused_computation | custom fusion | bytes 6297600 | tf_op jit(solution)/shard_map/gather | solution.py:94
  34.5 6.0 %all-to-all-start.5 = ((f32[1536,2,128]{2,1,0:T(2,128)}), f32[1536,2,128]{2,1,0:T(2,128)}, u32[]{:S(2)}, u32[]{:S(2)}) async-start(f32[1536,2,128]{2,1,0:T(2,128)} %get-tuple-element.51), calls=%async_computation.5 | async-start | bytes 3145728 | tf_op jit(solution)/shard_map/all_to_all | solution.py:119
  42.4 5.5 %gather_fusion.2 = f32[1536,4,128]{2,1,0:T(4,128)} fusion(f32[1024,4,128]{2,1,0:T(4,128)S(1)} %reshape.138, s32[2048]{0:T(1024)S(1)} %pad_clamp_fusion.1), kind=kCustom, calls=%fused_computation.2 | custom fusion | bytes 6297600 | tf_op jit(solution)/shard_map/gather | solution.py:92
  47.9 29.1 %all-to-all-done.5 = f32[1536,2,128]{2,1,0:T(2,128)} async-done(((f32[1536,2,128]{2,1,0:T(2,128)}), f32[1536,2,128]{2,1,0:T(2,128)}, u32[]{:S(2)}, u32[]{:S(2)}) %all-to-all-start.5) | async-done | bytes 1572896 | tf_op jit(solution)/shard_map/all_to_all | solution.py:119
  83.4 5.5 %gather_fusion.5 = f32[1536,4,128]{2,1,0:T(4,128)} fusion(f32[1024,4,128]{2,1,0:T(4,128)S(1)} %reshape.139, s32[2048]{0:T(1024)S(1)} %pad_clamp_fusion.1), kind=kCustom, calls=%fused_computation.5 | custom fusion | bytes 6297600 | tf_op jit(solution)/shard_map/gather | solution.py:93
  88.9 62.8 %all-to-all-done.2 = f32[1536,4,128]{2,1,0:T(4,128)} async-done(((f32[1536,4,128]{2,1,0:T(4,128)}), f32[1536,4,128]{2,1,0:T(4,128)}, u32[]{:S(2)}, u32[]{:S(2)}) %all-to-all-start.2) | async-done | bytes 3145760 | tf_op jit(solution)/shard_map/all_to_all | solution.py:113
  163.0 6.6 %scatter_custom_fusion.2 = s32[1024]{0:T(1024)S(1)} fusion(s32[1536]{0:T(1024)S(1)} %get-tuple-element.43, s32[1536]{0:T(1024)S(1)} %iota.37, s32[]{:T(128)} %constant.55.clone.1), kind=kCustom, calls=%fused_computation.95 | custom fusion | bytes 4100 | tf_op jit(solution)/shard_map/scatter | solution.py:106
  169.7 6.2 %gather_fusion.4 = s32[1024]{0:T(1024)S(1)} fusion(s32[1536]{0:T(1024)S(1)} %get-tuple-element.44, s32[1024]{0:T(1024)S(1)} %fusion.47), kind=kCustom, calls=%fused_computation.4 | custom fusion | bytes 12288 | tf_op jit(solution)/shard_map/gather | solution.py:110
  179.1 8.9 %gather_fusion.8 = f32[1024,2,128]{2,1,0:T(2,128)} fusion(f32[1536,2,128]{2,1,0:T(2,128)} %all-to-all-done.5, s32[1024]{0:T(1024)S(1)} %fusion.47), kind=kCustom, calls=%fused_computation.8 | custom fusion | bytes 2101248 | tf_op jit(solution)/shard_map/gather | solution.py:110
  188.0 64.7 %collective-permute-done = f32[2,512,1024]{2,1,0:T(8,128)} collective-permute-done((f32[2,512,1024]{2,1,0:T(8,128)}, f32[2,512,1024]{2,1,0:T(8,128)}, u32[]{:S(2)}, u32[]{:S(2)}) %collective-permute-start) | collective-permute-done | bytes 4194336 | tf_op jit(solution)/shard_map/ppermute | solution.py:189
  252.7 5.4 %gather_fusion.3 = f32[1024,4,128]{2,1,0:T(4,128)S(1)} fusion(f32[1536,4,128]{2,1,0:T(4,128)} %all-to-all-done.2, s32[1024]{0:T(1024)S(1)} %fusion.47), kind=kCustom, calls=%fused_computation.3 | custom fusion | bytes 4198400 | tf_op jit(solution)/shard_map/gather | solution.py:110
  261.3 5.7 %all-to-all-start = ((f32[1536,2,128]{2,1,0:T(2,128)}), f32[1536,2,128]{2,1,0:T(2,128)}, u32[]{:S(2)}, u32[]{:S(2)}) async-start(f32[1536,2,128]{2,1,0:T(2,128)} %get-tuple-element.52), calls=%async_computation | async-start | bytes 3145728 | tf_op jit(solution)/shard_map/all_to_all | solution.py:119
  267.1 9.8 %gather_fusion.6 = f32[1024,4,128]{2,1,0:T(4,128)} fusion(f32[1536,4,128]{2,1,0:T(4,128)} %all-to-all-done.3, s32[1024]{0:T(1024)S(1)} %fusion.47), kind=kCustom, calls=%fused_computation.6 | custom fusion | bytes 4198400 | tf_op jit(solution)/shard_map/gather | solution.py:110
  284.4 9.0 %fusion = (f32[4,1024]{1,0:T(4,128)S(1)}, f32[4,1024,1024]{1,2,0:T(8,128)S(1)}) fusion(pred[1024,1024]{0,1:T(8,128)(4,1)S(1)} %iota_compare_fusion, f32[1024,4,128]{2,1,0:T(4,128)S(1)} %get-tuple-element.58, f32[1024,4,128]{2,1,0:T(4,128)S(1)} %get-tuple-element.57), kind=kOutput, calls=%fused_computation.17 | convolution fusion | flops 3233804288 | bytes 22036480 | tf_op jit(solution)/shard_map/while/body/eval_jaxpr/qhd,khd->hqk/dot_general | solution.py:43
  293.4 7.3 %fusion.54 = (f32[4,1024]{1,0:T(4,128)S(1)}, f32[4,1024,1024]{1,2,0:T(8,128)}) fusion(f32[4,1024]{1,0:T(4,128)S(1)} %get-tuple-element.63, f32[4,1024,1024]{1,2,0:T(8,128)S(1)} %get-tuple-element.64, pred[1024,1024]{0,1:T(8,128)(4,1)S(1)} %iota_compare_fusion), kind=kLoop, calls=%fused_computation.100 | loop fusion | flops 16773120 | bytes 34635776 | tf_op jit(solution)/shard_map/while/body/eval_jaxpr/reduce_sum | solution.py:50
  300.8 6.1 %fusion.16 = f32[1024,2,128]{0,2,1:T(8,128)S(1)} fusion(f32[4,1024,1024]{1,2,0:T(8,128)} %get-tuple-element.48, f32[1024,2,128]{2,1,0:T(2,128)S(1)} %copy-done.5, f32[1024,2]{0,1:T(2,128)S(1)} %get-tuple-element.59), kind=kOutput, calls=%fused_computation.42 | convolution fusion | flops 1610874880 | bytes 10493952 | tf_op jit(solution)/shard_map/while/body/eval_jaxpr/hqk,khd->qhd/dot_general | solution.py:54
  312.7 6.0 %all-to-all-start.6 = ((f32[1536,2,128]{2,1,0:T(2,128)}), f32[1536,2,128]{2,1,0:T(2,128)S(1)}, u32[]{:S(2)}, u32[]{:S(2)}) async-start(f32[1536,2,128]{2,1,0:T(2,128)} %gather_fusion.9), calls=%async_computation.6 | async-start | bytes 3145728 | tf_op jit(solution)/shard_map/all_to_all | solution.py:142
  323.6 6.9 %fusion.19 = f32[1024,2,128]{0,2,1:T(8,128)} fusion(f32[4,1024,1024]{1,2,0:T(8,128)} %get-tuple-element.48, f32[1024,2,128]{2,1,0:T(2,128)S(1)} %gather_fusion.1, f32[1024,2]{0,1:T(2,128)S(1)} %get-tuple-element.60), kind=kOutput, calls=%fused_computation.43 | convolution fusion | flops 1610874880 | bytes 10493952 | tf_op jit(solution)/shard_map/while/body/eval_jaxpr/hqk,khd->qhd/dot_general | solution.py:54
  337.3 16.0 %all-to-all-done.6 = f32[1536,2,128]{2,1,0:T(2,128)S(1)} async-done(((f32[1536,2,128]{2,1,0:T(2,128)}), f32[1536,2,128]{2,1,0:T(2,128)S(1)}, u32[]{:S(2)}, u32[]{:S(2)}) %all-to-all-start.6) | async-done | bytes 1572896 | tf_op jit(solution)/shard_map/all_to_all | solution.py:142
  372.0 17.2 %collective-permute-done.1 = f32[1024,256]{1,0:T(8,128)} collective-permute-done((f32[1024,256]{1,0:T(8,128)}, f32[1024,256]{1,0:T(8,128)}, u32[]{:S(2)}, u32[]{:S(2)}) %collective-permute-start.1) | collective-permute-done | bytes 1048608 | tf_op jit(solution)/shard_map/ppermute | solution.py:147
  389.3 5.5 %convolution_add_fusion.2 = f32[1024,1024]{1,0:T(8,128)} fusion(f32[1024,1024]{1,0:T(8,128)S(1)} %fusion.24, f32[1024,256]{1,0:T(8,128)} %collective-permute-done.1, f32[2,512,1024]{2,1,0:T(8,128)} %collective-permute-done), kind=kOutput, calls=%fused_computation.27 | convolution fusion | flops 1611661312 | bytes 10485760 | tf_op jit(solution)/shard_map/dot_general | solution.py:136
  394.7 5.5 %convolution_add_fusion.3 = f32[1024,1024]{1,0:T(8,128)} fusion(f32[1024,1024]{1,0:T(8,128)S(1)} %fusion.26, f32[1024,256]{1,0:T(8,128)} %collective-permute-done.1, f32[2,512,1024]{2,1,0:T(8,128)} %collective-permute-done), kind=kOutput, calls=%fused_computation.28 | convolution fusion | flops 1611661312 | bytes 10485760 | tf_op jit(solution)/shard_map/dot_general | solution.py:136
  413.6 14.4 %collective-permute-done.2 = f32[1024,256]{1,0:T(8,128)S(1)} collective-permute-done((f32[1024,256]{1,0:T(8,128)S(1)}, f32[1024,256]{1,0:T(8,128)S(1)}, u32[]{:S(2)}, u32[]{:S(2)}) %collective-permute-start.2) | collective-permute-done | bytes 1048608 | tf_op jit(solution)/shard_map/ppermute | solution.py:147
  (81 shorter events, 119.5 us)
Async XLA Ops:
  10.1 24.4 %all-to-all-start.1 = ((s32[8,192,2]{1,2,0:T(2,128)}), s32[8,192,2]{1,2,0:T(2,128)S(1)}, u32[]{:S(2)}, u32[]{:S(2)}) async-start(s32[8,192,2]{1,2,0:T(2,128)} %copy.39), calls=%async_computation.1 | async-start | bytes 32768 | tf_op jit(solution)/shard_map/all_to_all | solution.py:100
  34.5 42.5 %all-to-all-start.5 = ((f32[1536,2,128]{2,1,0:T(2,128)}), f32[1536,2,128]{2,1,0:T(2,128)}, u32[]{:S(2)}, u32[]{:S(2)}) async-start(f32[1536,2,128]{2,1,0:T(2,128)} %get-tuple-element.51), calls=%async_computation.5 | async-start | bytes 3145728 | tf_op jit(solution)/shard_map/all_to_all | solution.py:119
  77.0 74.7 %all-to-all-start.2 = ((f32[1536,4,128]{2,1,0:T(4,128)}), f32[1536,4,128]{2,1,0:T(4,128)}, u32[]{:S(2)}, u32[]{:S(2)}) async-start(f32[1536,4,128]{2,1,0:T(4,128)} %gather_fusion.2), calls=%async_computation.2 | async-start | bytes 6291456 | tf_op jit(solution)/shard_map/all_to_all | solution.py:113
  151.7 109.7 %all-to-all-start.3 = ((f32[1536,4,128]{2,1,0:T(4,128)}), f32[1536,4,128]{2,1,0:T(4,128)}, u32[]{:S(2)}, u32[]{:S(2)}) async-start(f32[1536,4,128]{2,1,0:T(4,128)} %gather_fusion.5), calls=%async_computation.3 | async-start | bytes 6291456 | tf_op jit(solution)/shard_map/all_to_all | solution.py:117
  161.0 91.7 %collective-permute-start = (f32[2,512,1024]{2,1,0:T(8,128)}, f32[2,512,1024]{2,1,0:T(8,128)}, u32[]{:S(2)}, u32[]{:S(2)}) collective-permute-start(f32[2,512,1024]{2,1,0:T(8,128)} %pad_maximum_fusion), channel_id=1, source_target_pairs={{0,2},{1,3},{2,0},{3,1},{4,6},{5,7},{6,4},{7,5},{8,10},{9,11},{10,... | collective-permute-start | bytes 12582920 | tf_op jit(solution)/shard_map/ppermute | solution.py:189
  261.3 51.3 %all-to-all-start = ((f32[1536,2,128]{2,1,0:T(2,128)}), f32[1536,2,128]{2,1,0:T(2,128)}, u32[]{:S(2)}, u32[]{:S(2)}) async-start(f32[1536,2,128]{2,1,0:T(2,128)} %get-tuple-element.52), calls=%async_computation | async-start | bytes 3145728 | tf_op jit(solution)/shard_map/all_to_all | solution.py:119
  276.8 3.6 copy-start
  276.8 3.6 copy-start.2
  276.8 4.1 copy-start.3
  276.9 4.2 copy-start.6
  276.9 4.3 copy-start.7
  293.4 7.4 %copy-start.5 = (f32[1024,2,128]{2,1,0:T(2,128)S(1)}, f32[1024,2,128]{2,1,0:T(2,128)}, u32[]{:S(2)}) copy-start(f32[1024,2,128]{2,1,0:T(2,128)} %gather_fusion.8) | copy-start | bytes 3145732
  312.7 40.6 %all-to-all-start.6 = ((f32[1536,2,128]{2,1,0:T(2,128)}), f32[1536,2,128]{2,1,0:T(2,128)S(1)}, u32[]{:S(2)}, u32[]{:S(2)}) async-start(f32[1536,2,128]{2,1,0:T(2,128)} %gather_fusion.9), calls=%async_computation.6 | async-start | bytes 3145728 | tf_op jit(solution)/shard_map/all_to_all | solution.py:142
  353.3 1.1 copy-start.4
  354.5 45.8 %all-to-all-start.4 = ((f32[1536,2,128]{2,1,0:T(2,128)}), f32[1536,2,128]{2,1,0:T(2,128)S(1)}, u32[]{:S(2)}, u32[]{:S(2)}) async-start(f32[1536,2,128]{2,1,0:T(2,128)} %gather_fusion.7), calls=%async_computation.4 | async-start | bytes 3145728 | tf_op jit(solution)/shard_map/all_to_all | solution.py:142
  364.3 25.0 %collective-permute-start.1 = (f32[1024,256]{1,0:T(8,128)}, f32[1024,256]{1,0:T(8,128)}, u32[]{:S(2)}, u32[]{:S(2)}) collective-permute-start(f32[1024,256]{1,0:T(8,128)} %bitcast.71), channel_id=1, source_target_pairs={{0,2},{1,3},{2,0},{3,1},{4,6},{5,7},{6,4},{7,5},{8,10},{9,11},{10,... | collective-permute-start | bytes 3145736 | tf_op jit(solution)/shard_map/ppermute | solution.py:147
  404.2 23.8 %collective-permute-start.2 = (f32[1024,256]{1,0:T(8,128)S(1)}, f32[1024,256]{1,0:T(8,128)S(1)}, u32[]{:S(2)}, u32[]{:S(2)}) collective-permute-start(f32[1024,256]{1,0:T(8,128)S(1)} %bitcast.80), channel_id=1, source_target_pairs={{0,2},{1,3},{2,0},{3,1},{4,6},{5,7},{6,4},{7,5},{8,10},{9,11},{10,... | collective-permute-start | bytes 3145736 | tf_op jit(solution)/shard_map/ppermute | solution.py:147
  405.8 4.7 %copy-start.1 = (f32[1024,1024]{1,0:T(8,128)S(1)}, f32[1024,1024]{1,0:T(8,128)}, u32[]{:S(2)}) copy-start(f32[1024,1024]{1,0:T(8,128)} %convolution_add_fusion.3) | copy-start | bytes 12582916
  432.1 7.2 %collective-permute-start.3 = (f32[1024,1024]{1,0:T(8,128)S(1)}, f32[1024,1024]{1,0:T(8,128)S(1)}, u32[]{:S(2)}, u32[]{:S(2)}) collective-permute-start(f32[1024,1024]{1,0:T(8,128)S(1)} %add.108), channel_id=1, source_target_pairs={{0,1},{1,0},{2,3},{3,2},{4,5},{5,4},{6,7},{7,6},{8,9},{9,8},{10,11... | collective-permute-start | bytes 12582920 | tf_op jit(solution)/shard_map/ppermute | solution.py:170

commit v19 on v18

--- a/solution.py
+++ b/solution.py
@@ -115,16 +115,14 @@
     received = (
         first_arrived,
         lax.all_to_all(send_k, "seq", split_axis=0, concat_axis=0, tiled=True),
-        tuple(
-            lax.all_to_all(send_v[:, lo:hi], "seq", split_axis=0, concat_axis=0, tiled=True)
-            for lo, hi in ((0, heads_here // 2), (heads_here // 2, heads_here))
-        ),
-    )
+        lax.all_to_all(send_v, "seq", split_axis=0, concat_axis=0, tiled=True),
+    )
+    split = heads_here // 2
     cos_table, sin_table = yarn_tables(place(arrived_index[:, 1]), DH)
     result = attend_local(
         rotate(place(received[0]), cos_table, sin_table),
         rotate(place(received[1]), cos_table, sin_table),
-        tuple(place(part) for part in received[2]),
+        tuple(place(received[2][:, lo:hi]) for lo, hi in ((0, split), (split, heads_here))),
     )
     split = heads_here // 2
     head_count = lax.axis_size("head")

time: 452 us -> 416 us (0.920)
  waiting for transfers between devices: 208 us -> 190 us
  starting transfers between devices: 42.4 us -> 34.5 us
  local copies, waits for them, and re-layouts: 106 us -> 101 us
    ppermute x1, waiting for transfers between devices: 64.7 us -> 5.34 us  [fetch_far_weights(): return lax.ppermute(outgoing, 'head', swap_pairs(head_count, 2))]
    all_to_all x1, waiting for transfers between devices: 0.01 us -> 56.3 us  [per_device(): lax.all_to_all(send_k, 'seq', split_axis=0, concat_axis=0, tiled=True)]
    all_to_all x2 -> x1, waiting for transfers between devices: 29.1 us -> 10.7 us  [per_device(): lax.all_to_all(send_v, 'seq', split_axis=0, concat_axis=0, tiled=True)]
    all_to_all x2 -> x1, starting transfers between devices: 11.7 us -> 4.44 us  [per_device(): lax.all_to_all(send_v, 'seq', split_axis=0, concat_axis=0, tiled=True)]
    gather x5, local copies, waits for them, and re-layouts: 35.2 us -> 30.1 us  [place(): return pieces[where_from]]
  transfers between devices with their start and end apart: 11 -> 10, of which waited for: 7 -> 8; matrix products, arithmetic and copies ran while one was open for 38% -> 34% of each run, Pallas kernels for 0% -> 0%
where the time goes in v19:
time: 416 us; the launch traced here: 408 us
  waiting for transfers between devices  190 us (46%)
  local copies, waits for them, and re-layouts  101 us (24%)
  matrix products  53.9 us (13%)
  starting transfers between devices  34.5 us (8%)
  other arithmetic  28.6 us (7%)
    all_to_all x1, waiting for transfers between devices, per_device(): lax.all_to_all(send_q, 'seq', split_axis=0, concat_axis=0, tiled=True)  62.7 us
    all_to_all x1, waiting for transfers between devices, per_device(): lax.all_to_all(send_k, 'seq', split_axis=0, concat_axis=0, tiled=True)  56.3 us
    ppermute x2, waiting for transfers between devices, half_terms(): far_mixed = lax.ppermute(mixed, 'head', swap_pairs(head_count, 2))  32 us
    dot_general x8, matrix products, dot(): jnp.dot(lhs, weight, precision=lax.Precision.HIGH, preferred_element_type...  31.2 us
    gather x5, local copies, waits for them, and re-layouts, place(): return pieces[where_from]  30.1 us
    all_to_all x2, waiting for transfers between devices, exchange(): back = lax.all_to_all(part, 'seq', split_axis=0, concat_axis=0, tiled=True)  18.6 us
    dot_general x2, matrix products, cluster_attention(): jnp.einsum('hqk,khd->qhd', weights[lo:hi], value_part, precision=lax.Prec...  13.8 us
    all_to_all x1, waiting for transfers between devices, per_device(): lax.all_to_all(send_v, 'seq', split_axis=0, concat_axis=0, tiled=True)  10.7 us
  transfers between devices with their start and end apart: 10, of which 8 were waited for; matrix products, arithmetic and copies ran while one was open for 34% of the time, Pallas kernels for 0%

profile of v19, /device:TPU:0, one launch (start us, length us, event | category | flops | bytes accessed | tf_op | source)
XLA Modules:
  0.0 408.4 jit_solution(12198435898482006179)
XLA Ops:
  10.0 7.3 %all-to-all-start.1 = ((s32[8,192,2]{1,2,0:T(2,128)}), s32[8,192,2]{1,2,0:T(2,128)S(1)}, u32[]{:S(2)}, u32[]{:S(2)}) async-start(s32[8,192,2]{1,2,0:T(2,128)} %copy.39), calls=%async_computation.1 | async-start | bytes 32768 | tf_op jit(solution)/shard_map/all_to_all | solution.py:100
  23.6 5.5 %gather_fusion.2 = f32[1536,4,128]{2,1,0:T(4,128)} fusion(f32[1024,4,128]{2,1,0:T(4,128)S(1)} %reshape.138, s32[2048]{0:T(1024)S(1)} %pad_clamp_fusion.1), kind=kCustom, calls=%fused_computation.2 | custom fusion | bytes 6297600 | tf_op jit(solution)/shard_map/gather | solution.py:92
  29.1 6.0 %all-to-all-start.2 = ((f32[1536,4,128]{2,1,0:T(4,128)}), f32[1536,4,128]{2,1,0:T(4,128)}, u32[]{:S(2)}, u32[]{:S(2)}) async-start(f32[1536,4,128]{2,1,0:T(4,128)} %gather_fusion.2), calls=%async_computation.2 | async-start | bytes 6291456 | tf_op jit(solution)/shard_map/all_to_all | solution.py:113
  37.0 5.6 %gather_fusion.5 = f32[1536,4,128]{2,1,0:T(4,128)} fusion(f32[1024,4,128]{2,1,0:T(4,128)S(1)} %reshape.139, s32[2048]{0:T(1024)S(1)} %pad_clamp_fusion.1), kind=kCustom, calls=%fused_computation.5 | custom fusion | bytes 6297600 | tf_op jit(solution)/shard_map/gather | solution.py:93
  42.6 62.7 %all-to-all-done.2 = f32[1536,4,128]{2,1,0:T(4,128)} async-done(((f32[1536,4,128]{2,1,0:T(4,128)}), f32[1536,4,128]{2,1,0:T(4,128)}, u32[]{:S(2)}, u32[]{:S(2)}) %all-to-all-start.2) | async-done | bytes 3145760 | tf_op jit(solution)/shard_map/all_to_all | solution.py:113
  118.1 5.6 %gather_fusion = f32[1536,4,128]{2,1,0:T(4,128)} fusion(f32[1024,4,128]{2,1,0:T(4,128)S(1)} %reshape.136, s32[2048]{0:T(1024)S(1)} %pad_clamp_fusion.1), kind=kCustom, calls=%fused_computation | custom fusion | bytes 6297600 | tf_op jit(solution)/shard_map/gather | solution.py:94
  123.7 56.3 %all-to-all-done.3 = f32[1536,4,128]{2,1,0:T(4,128)} async-done(((f32[1536,4,128]{2,1,0:T(4,128)}), f32[1536,4,128]{2,1,0:T(4,128)}, u32[]{:S(2)}, u32[]{:S(2)}) %all-to-all-start.3) | async-done | bytes 3145760 | tf_op jit(solution)/shard_map/all_to_all | solution.py:117
  184.9 6.6 %scatter_custom_fusion.2 = s32[1024]{0:T(1024)S(1)} fusion(s32[1536]{0:T(1024)S(1)} %get-tuple-element.43, s32[1536]{0:T(1024)S(1)} %iota.37, s32[]{:T(128)} %constant.55.clone.1), kind=kCustom, calls=%fused_computation.95 | custom fusion | bytes 4100 | tf_op jit(solution)/shard_map/scatter | solution.py:106
  191.6 6.2 %gather_fusion.4 = s32[1024]{0:T(1024)S(1)} fusion(s32[1536]{0:T(1024)S(1)} %get-tuple-element.44, s32[1024]{0:T(1024)S(1)} %fusion.47), kind=kCustom, calls=%fused_computation.4 | custom fusion | bytes 12288 | tf_op jit(solution)/shard_map/gather | solution.py:110
  201.0 5.3 %collective-permute-done = f32[2,512,1024]{2,1,0:T(8,128)} collective-permute-done((f32[2,512,1024]{2,1,0:T(8,128)}, f32[2,512,1024]{2,1,0:T(8,128)}, u32[]{:S(2)}, u32[]{:S(2)}) %collective-permute-start) | collective-permute-done | bytes 4194336 | tf_op jit(solution)/shard_map/ppermute | solution.py:187
  206.4 5.4 %gather_fusion.3 = f32[1024,4,128]{2,1,0:T(4,128)S(1)} fusion(f32[1536,4,128]{2,1,0:T(4,128)} %all-to-all-done.2, s32[1024]{0:T(1024)S(1)} %fusion.47), kind=kCustom, calls=%fused_computation.3 | custom fusion | bytes 4198400 | tf_op jit(solution)/shard_map/gather | solution.py:110
  211.8 9.8 %gather_fusion.6 = f32[1024,4,128]{2,1,0:T(4,128)} fusion(f32[1536,4,128]{2,1,0:T(4,128)} %all-to-all-done.3, s32[1024]{0:T(1024)S(1)} %fusion.47), kind=kCustom, calls=%fused_computation.6 | custom fusion | bytes 4198400 | tf_op jit(solution)/shard_map/gather | solution.py:110
  227.7 9.0 %fusion = (f32[4,1024]{1,0:T(4,128)S(1)}, f32[4,1024,1024]{1,2,0:T(8,128)S(1)}) fusion(pred[1024,1024]{0,1:T(8,128)(4,1)S(1)} %iota_compare_fusion, f32[1024,4,128]{2,1,0:T(4,128)S(1)} %get-tuple-element.58, f32[1024,4,128]{2,1,0:T(4,128)S(1)} %get-tuple-element.57), kind=kOutput, calls=%fused_computation.17 | convolution fusion | flops 3233804288 | bytes 22036480 | tf_op jit(solution)/shard_map/while/body/eval_jaxpr/qhd,khd->hqk/dot_general | solution.py:43
  236.7 7.2 %fusion.54 = (f32[4,1024]{1,0:T(4,128)S(1)}, f32[4,1024,1024]{1,2,0:T(8,128)}) fusion(f32[4,1024]{1,0:T(4,128)S(1)} %get-tuple-element.63, f32[4,1024,1024]{1,2,0:T(8,128)S(1)} %get-tuple-element.64, pred[1024,1024]{0,1:T(8,128)(4,1)S(1)} %iota_compare_fusion), kind=kLoop, calls=%fused_computation.100 | loop fusion | flops 16773120 | bytes 34635776 | tf_op jit(solution)/shard_map/while/body/eval_jaxpr/reduce_sum | solution.py:50
  243.9 10.7 %all-to-all-done = f32[1536,4,128]{2,1,0:T(4,128)} async-done(((f32[1536,4,128]{2,1,0:T(4,128)}), f32[1536,4,128]{2,1,0:T(4,128)}, u32[]{:S(2)}, u32[]{:S(2)}) %all-to-all-start) | async-done | bytes 3145760 | tf_op jit(solution)/shard_map/all_to_all | solution.py:118
  254.6 5.4 %fusion.55 = (f32[1536,2,128]{2,1,0:T(2,128)S(1)}, f32[1536,2,128]{2,1,0:T(2,128)}) fusion(f32[1536,4,128]{2,1,0:T(4,128)} %all-to-all-done), kind=kLoop, calls=%fused_computation.101 | loop fusion | bytes 6291456 | tf_op jit(solution)/shard_map/slice | solution.py:125
  263.8 6.9 %fusion.16 = f32[1024,2,128]{0,2,1:T(8,128)} fusion(f32[4,1024,1024]{1,2,0:T(8,128)} %get-tuple-element.48, f32[1024,2,128]{2,1,0:T(2,128)S(1)} %gather_fusion.8, f32[1024,2]{0,1:T(2,128)S(1)} %get-tuple-element.59), kind=kOutput, calls=%fused_computation.42 | convolution fusion | flops 1610874880 | bytes 10493952 | tf_op jit(solution)/shard_map/while/body/eval_jaxpr/hqk,khd->qhd/dot_general | solution.py:54
  286.1 6.9 %fusion.19 = f32[1024,2,128]{0,2,1:T(8,128)} fusion(f32[4,1024,1024]{1,2,0:T(8,128)} %get-tuple-element.48, f32[1024,2,128]{2,1,0:T(2,128)S(1)} %gather_fusion.1, f32[1024,2]{0,1:T(2,128)S(1)} %get-tuple-element.60), kind=kOutput, calls=%fused_computation.43 | convolution fusion | flops 1610874880 | bytes 10493952 | tf_op jit(solution)/shard_map/while/body/eval_jaxpr/hqk,khd->qhd/dot_general | solution.py:54
  294.5 5.2 %gather_fusion.7 = f32[1536,2,128]{2,1,0:T(2,128)} fusion(f32[1024,2,128]{2,1,0:T(2,128)S(1)} %copy.45, s32[2048]{0:T(1024)S(1)} %pad_clamp_fusion), kind=kCustom, calls=%fused_computation.7 | custom fusion | bytes 3151872 | tf_op jit(solution)/shard_map/gather | solution.py:139
  299.7 18.6 %all-to-all-done.5 = f32[1536,2,128]{2,1,0:T(2,128)S(1)} async-done(((f32[1536,2,128]{2,1,0:T(2,128)}), f32[1536,2,128]{2,1,0:T(2,128)S(1)}, u32[]{:S(2)}, u32[]{:S(2)}) %all-to-all-start.5) | async-done | bytes 1572896 | tf_op jit(solution)/shard_map/all_to_all | solution.py:140
  337.2 17.4 %collective-permute-done.1 = f32[1024,256]{1,0:T(8,128)} collective-permute-done((f32[1024,256]{1,0:T(8,128)}, f32[1024,256]{1,0:T(8,128)}, u32[]{:S(2)}, u32[]{:S(2)}) %collective-permute-start.1) | collective-permute-done | bytes 1048608 | tf_op jit(solution)/shard_map/ppermute | solution.py:145
  354.6 5.5 %convolution_add_fusion.2 = f32[1024,1024]{1,0:T(8,128)} fusion(f32[1024,1024]{1,0:T(8,128)S(1)} %fusion.24, f32[1024,256]{1,0:T(8,128)} %collective-permute-done.1, f32[2,512,1024]{2,1,0:T(8,128)} %collective-permute-done), kind=kOutput, calls=%fused_computation.27 | convolution fusion | flops 1611661312 | bytes 10485760 | tf_op jit(solution)/shard_map/dot_general | solution.py:134
  360.1 5.5 %convolution_add_fusion.3 = f32[1024,1024]{1,0:T(8,128)} fusion(f32[1024,1024]{1,0:T(8,128)S(1)} %fusion.26, f32[1024,256]{1,0:T(8,128)} %collective-permute-done.1, f32[2,512,1024]{2,1,0:T(8,128)} %collective-permute-done), kind=kOutput, calls=%fused_computation.28 | convolution fusion | flops 1611661312 | bytes 10485760 | tf_op jit(solution)/shard_map/dot_general | solution.py:134
  378.8 14.6 %collective-permute-done.2 = f32[1024,256]{1,0:T(8,128)S(1)} collective-permute-done((f32[1024,256]{1,0:T(8,128)S(1)}, f32[1024,256]{1,0:T(8,128)S(1)}, u32[]{:S(2)}, u32[]{:S(2)}) %collective-permute-start.2) | collective-permute-done | bytes 1048608 | tf_op jit(solution)/shard_map/ppermute | solution.py:145
  (73 shorter events, 112.7 us)
Async XLA Ops:
  10.0 19.0 %all-to-all-start.1 = ((s32[8,192,2]{1,2,0:T(2,128)}), s32[8,192,2]{1,2,0:T(2,128)S(1)}, u32[]{:S(2)}, u32[]{:S(2)}) async-start(s32[8,192,2]{1,2,0:T(2,128)} %copy.39), calls=%async_computation.1 | async-start | bytes 32768 | tf_op jit(solution)/shard_map/all_to_all | solution.py:100
  29.1 76.2 %all-to-all-start.2 = ((f32[1536,4,128]{2,1,0:T(4,128)}), f32[1536,4,128]{2,1,0:T(4,128)}, u32[]{:S(2)}, u32[]{:S(2)}) async-start(f32[1536,4,128]{2,1,0:T(4,128)} %gather_fusion.2), calls=%async_computation.2 | async-start | bytes 6291456 | tf_op jit(solution)/shard_map/all_to_all | solution.py:113
  105.3 74.7 %all-to-all-start.3 = ((f32[1536,4,128]{2,1,0:T(4,128)}), f32[1536,4,128]{2,1,0:T(4,128)}, u32[]{:S(2)}, u32[]{:S(2)}) async-start(f32[1536,4,128]{2,1,0:T(4,128)} %gather_fusion.5), calls=%async_computation.3 | async-start | bytes 6291456 | tf_op jit(solution)/shard_map/all_to_all | solution.py:117
  114.7 91.7 %collective-permute-start = (f32[2,512,1024]{2,1,0:T(8,128)}, f32[2,512,1024]{2,1,0:T(8,128)}, u32[]{:S(2)}, u32[]{:S(2)}) collective-permute-start(f32[2,512,1024]{2,1,0:T(8,128)} %pad_maximum_fusion), channel_id=1, source_target_pairs={{0,2},{1,3},{2,0},{3,1},{4,6},{5,7},{6,4},{7,5},{8,10},{9,11},{10,... | collective-permute-start | bytes 12582920 | tf_op jit(solution)/shard_map/ppermute | solution.py:187
  180.0 74.6 %all-to-all-start = ((f32[1536,4,128]{2,1,0:T(4,128)}), f32[1536,4,128]{2,1,0:T(4,128)}, u32[]{:S(2)}, u32[]{:S(2)}) async-start(f32[1536,4,128]{2,1,0:T(4,128)} %gather_fusion), calls=%async_computation | async-start | bytes 6291456 | tf_op jit(solution)/shard_map/all_to_all | solution.py:118
  221.6 1.6 copy-start
  223.2 1.2 copy-start.3
  223.2 1.2 copy-start.4
  277.5 40.8 %all-to-all-start.5 = ((f32[1536,2,128]{2,1,0:T(2,128)}), f32[1536,2,128]{2,1,0:T(2,128)S(1)}, u32[]{:S(2)}, u32[]{:S(2)}) async-start(f32[1536,2,128]{2,1,0:T(2,128)} %gather_fusion.9), calls=%async_computation.5 | async-start | bytes 3145728 | tf_op jit(solution)/shard_map/all_to_all | solution.py:140
  318.3 1.1 copy-start.2
  319.4 46.2 %all-to-all-start.4 = ((f32[1536,2,128]{2,1,0:T(2,128)}), f32[1536,2,128]{2,1,0:T(2,128)S(1)}, u32[]{:S(2)}, u32[]{:S(2)}) async-start(f32[1536,2,128]{2,1,0:T(2,128)} %gather_fusion.7), calls=%async_computation.4 | async-start | bytes 3145728 | tf_op jit(solution)/shard_map/all_to_all | solution.py:140
  329.5 25.1 %collective-permute-start.1 = (f32[1024,256]{1,0:T(8,128)}, f32[1024,256]{1,0:T(8,128)}, u32[]{:S(2)}, u32[]{:S(2)}) collective-permute-start(f32[1024,256]{1,0:T(8,128)} %bitcast.71), channel_id=1, source_target_pairs={{0,2},{1,3},{2,0},{3,1},{4,6},{5,7},{6,4},{7,5},{8,10},{9,11},{10,... | collective-permute-start | bytes 3145736 | tf_op jit(solution)/shard_map/ppermute | solution.py:145
  369.4 24.0 %collective-permute-start.2 = (f32[1024,256]{1,0:T(8,128)S(1)}, f32[1024,256]{1,0:T(8,128)S(1)}, u32[]{:S(2)}, u32[]{:S(2)}) collective-permute-start(f32[1024,256]{1,0:T(8,128)S(1)} %bitcast.80), channel_id=1, source_target_pairs={{0,2},{1,3},{2,0},{3,1},{4,6},{5,7},{6,4},{7,5},{8,10},{9,11},{10,... | collective-permute-start | bytes 3145736 | tf_op jit(solution)/shard_map/ppermute | solution.py:145
  371.0 4.7 %copy-start.1 = (f32[1024,1024]{1,0:T(8,128)S(1)}, f32[1024,1024]{1,0:T(8,128)}, u32[]{:S(2)}) copy-start(f32[1024,1024]{1,0:T(8,128)} %convolution_add_fusion.3) | copy-start | bytes 12582916
  397.4 7.2 %collective-permute-start.3 = (f32[1024,1024]{1,0:T(8,128)S(1)}, f32[1024,1024]{1,0:T(8,128)S(1)}, u32[]{:S(2)}, u32[]{:S(2)}) collective-permute-start(f32[1024,1024]{1,0:T(8,128)S(1)} %add.108), channel_id=1, source_target_pairs={{0,1},{1,0},{2,3},{3,2},{4,5},{5,4},{6,7},{7,6},{8,9},{9,8},{10,11... | collective-permute-start | bytes 12582920 | tf_op jit(solution)/shard_map/ppermute | solution.py:168

commit v20 on v17

--- a/solution.py
+++ b/solution.py
@@ -151,19 +151,21 @@
                 (far_mixed, near_partner, near_own)
             )
         to_partner = near_partner + dot(far_mixed, far_weights[1, rows])
-        to_own = near_own + dot(far_mixed, far_weights[0, rows])
-        return to_partner, to_own
-
-    first_partner, first_own = half_terms(exchange(0, split), 0, split, None, None, False)
+        return to_partner, near_own, far_mixed, rows
+
+    first_partner, first_near, first_far, first_rows = half_terms(
+        exchange(0, split), 0, split, None, None, False
+    )
+    first_own = first_near + dot(first_far, far_weights[0, first_rows])
     second_back = exchange(split, heads_here)
     second_back, first_partner, first_own = lax.optimization_barrier(
         (second_back, first_partner, first_own)
     )
-    for_partner, own = half_terms(
+    for_partner, near_own, far_mixed, rows = half_terms(
         second_back, split, heads_here, first_partner, first_own, True
     )
     from_partner = lax.ppermute(for_partner, "head", swap_pairs(head_count, 1))
-    return own + from_partner
+    return (near_own + from_partner) + dot(far_mixed, far_weights[0, rows])
 
 
 def swap_pairs(count, bit):

time: 413 us -> 416 us (level)
  transfers between devices with their start and end apart: 10 -> 10, of which waited for: 8 -> 8; matrix products, arithmetic and copies ran while one was open for 33% -> 32% of each run, Pallas kernels for 0% -> 0%
where the time goes in v20:
time: 416 us; the launch traced here: 408 us
  waiting for transfers between devices  198 us (48%)
  local copies, waits for them, and re-layouts  93.4 us (22%)
  matrix products  55.6 us (13%)
  starting transfers between devices  34.4 us (8%)
  other arithmetic  25.5 us (6%)
    all_to_all x1, waiting for transfers between devices, per_device(): lax.all_to_all(send_q, 'seq', split_axis=0, concat_axis=0, tiled=True)  62.7 us
    all_to_all x1, waiting for transfers between devices, per_device(): lax.all_to_all(send_k, 'seq', split_axis=0, concat_axis=0, tiled=True)  56.3 us
    dot_general x8, matrix products, dot(): jnp.dot(lhs, weight, precision=lax.Precision.HIGH, preferred_element_type...  33.6 us
    ppermute x2, waiting for transfers between devices, half_terms(): far_mixed = lax.ppermute(mixed, 'head', swap_pairs(head_count, 2))  31.9 us
    gather x4, local copies, waits for them, and re-layouts, place(): return pieces[where_from]  27.3 us
    all_to_all x2, waiting for transfers between devices, exchange(): back = lax.all_to_all(part, 'seq', split_axis=0, concat_axis=0, tiled=True)  23.5 us
    dot_general x2, matrix products, cluster_attention(): jnp.einsum('hqk,khd->qhd', weights[lo:hi], value_c[:, lo:hi], precision=l...  13 us
    all_to_all x1, waiting for transfers between devices, per_device(): lax.all_to_all(send_v, 'seq', split_axis=0, concat_axis=0, tiled=True)  10.7 us
  transfers between devices with their start and end apart: 10, of which 8 were waited for; matrix products, arithmetic and copies ran while one was open for 32% of the time, Pallas kernels for 0%

profile of v20, /device:TPU:0, one launch (start us, length us, event | category | flops | bytes accessed | tf_op | source)
XLA Modules:
  0.0 407.5 jit_solution(2353805612491719926)
XLA Ops:
  10.0 7.3 %all-to-all-start.1 = ((s32[8,192,2]{1,2,0:T(2,128)}), s32[8,192,2]{1,2,0:T(2,128)S(1)}, u32[]{:S(2)}, u32[]{:S(2)}) async-start(s32[8,192,2]{1,2,0:T(2,128)} %copy.39), calls=%async_computation.1 | async-start | bytes 32768 | tf_op jit(solution)/shard_map/all_to_all | solution.py:98
  23.6 5.5 %gather_fusion.2 = f32[1536,4,128]{2,1,0:T(4,128)} fusion(f32[1024,4,128]{2,1,0:T(4,128)S(1)} %reshape.135, s32[2048]{0:T(1024)S(1)} %pad_clamp_fusion.1), kind=kCustom, calls=%fused_computation.2 | custom fusion | bytes 6297600 | tf_op jit(solution)/shard_map/gather | solution.py:90
  29.1 6.0 %all-to-all-start.2 = ((f32[1536,4,128]{2,1,0:T(4,128)}), f32[1536,4,128]{2,1,0:T(4,128)}, u32[]{:S(2)}, u32[]{:S(2)}) async-start(f32[1536,4,128]{2,1,0:T(4,128)} %gather_fusion.2), calls=%async_computation.2 | async-start | bytes 6291456 | tf_op jit(solution)/shard_map/all_to_all | solution.py:111
  37.0 5.6 %gather_fusion.5 = f32[1536,4,128]{2,1,0:T(4,128)} fusion(f32[1024,4,128]{2,1,0:T(4,128)S(1)} %reshape.136, s32[2048]{0:T(1024)S(1)} %pad_clamp_fusion.1), kind=kCustom, calls=%fused_computation.5 | custom fusion | bytes 6297600 | tf_op jit(solution)/shard_map/gather | solution.py:91
  42.6 62.7 %all-to-all-done.2 = f32[1536,4,128]{2,1,0:T(4,128)} async-done(((f32[1536,4,128]{2,1,0:T(4,128)}), f32[1536,4,128]{2,1,0:T(4,128)}, u32[]{:S(2)}, u32[]{:S(2)}) %all-to-all-start.2) | async-done | bytes 3145760 | tf_op jit(solution)/shard_map/all_to_all | solution.py:111
  118.1 5.5 %gather_fusion = f32[1536,4,128]{2,1,0:T(4,128)} fusion(f32[1024,4,128]{2,1,0:T(4,128)S(1)} %reshape.133, s32[2048]{0:T(1024)S(1)} %pad_clamp_fusion.1), kind=kCustom, calls=%fused_computation | custom fusion | bytes 6297600 | tf_op jit(solution)/shard_map/gather | solution.py:92
  123.7 56.3 %all-to-all-done.3 = f32[1536,4,128]{2,1,0:T(4,128)} async-done(((f32[1536,4,128]{2,1,0:T(4,128)}), f32[1536,4,128]{2,1,0:T(4,128)}, u32[]{:S(2)}, u32[]{:S(2)}) %all-to-all-start.3) | async-done | bytes 3145760 | tf_op jit(solution)/shard_map/all_to_all | solution.py:115
  185.0 6.4 %scatter_custom_fusion.2 = s32[1024]{0:T(1024)S(1)} fusion(s32[1536]{0:T(1024)S(1)} %get-tuple-element.40, s32[1536]{0:T(1024)S(1)} %iota.37, s32[]{:T(128)} %constant.53.clone.1), kind=kCustom, calls=%fused_computation.94 | custom fusion | bytes 4100 | tf_op jit(solution)/shard_map/scatter | solution.py:104
  191.4 6.2 %gather_fusion.4 = s32[1024]{0:T(1024)S(1)} fusion(s32[1536]{0:T(1024)S(1)} %get-tuple-element.41, s32[1024]{0:T(1024)S(1)} %fusion.49), kind=kCustom, calls=%fused_computation.4 | custom fusion | bytes 12288 | tf_op jit(solution)/shard_map/gather | solution.py:108
  200.8 5.6 %collective-permute-done = f32[2,512,1024]{2,1,0:T(8,128)} collective-permute-done((f32[2,512,1024]{2,1,0:T(8,128)}, f32[2,512,1024]{2,1,0:T(8,128)}, u32[]{:S(2)}, u32[]{:S(2)}) %collective-permute-start) | collective-permute-done | bytes 4194336 | tf_op jit(solution)/shard_map/ppermute | solution.py:186
  211.8 9.8 %gather_fusion.6 = f32[1024,4,128]{2,1,0:T(4,128)} fusion(f32[1536,4,128]{2,1,0:T(4,128)} %all-to-all-done.3, s32[1024]{0:T(1024)S(1)} %fusion.49), kind=kCustom, calls=%fused_computation.6 | custom fusion | bytes 4198400 | tf_op jit(solution)/shard_map/gather | solution.py:108
  227.8 9.0 %fusion = (f32[4,1024]{1,0:T(4,128)S(1)}, f32[4,1024,1024]{1,2,0:T(8,128)S(1)}) fusion(pred[1024,1024]{0,1:T(8,128)(4,1)S(1)} %iota_compare_fusion, f32[1024,4,128]{2,1,0:T(4,128)S(1)} %get-tuple-element.55, f32[1024,4,128]{2,1,0:T(4,128)S(1)} %get-tuple-element.54), kind=kOutput, calls=%fused_computation.16 | convolution fusion | flops 3233804288 | bytes 22036480 | tf_op jit(solution)/shard_map/while/body/eval_jaxpr/qhd,khd->hqk/dot_general | solution.py:43
  236.8 7.2 %fusion.56 = (f32[4,1024]{1,0:T(4,128)S(1)}, f32[4,1024,1024]{1,2,0:T(8,128)}) fusion(f32[4,1024]{1,0:T(4,128)S(1)} %get-tuple-element.60, f32[4,1024,1024]{1,2,0:T(8,128)S(1)} %get-tuple-element.61, pred[1024,1024]{0,1:T(8,128)(4,1)S(1)} %iota_compare_fusion), kind=kLoop, calls=%fused_computation.99 | loop fusion | flops 16773120 | bytes 34635776 | tf_op jit(solution)/shard_map/while/body/eval_jaxpr/reduce_sum | solution.py:50
  243.9 10.7 %all-to-all-done = f32[1536,4,128]{2,1,0:T(4,128)} async-done(((f32[1536,4,128]{2,1,0:T(4,128)}), f32[1536,4,128]{2,1,0:T(4,128)}, u32[]{:S(2)}, u32[]{:S(2)}) %all-to-all-start) | async-done | bytes 3145760 | tf_op jit(solution)/shard_map/all_to_all | solution.py:116
  254.6 5.9 %gather_fusion.1 = f32[1024,4,128]{2,1,0:T(4,128)S(1)} fusion(f32[1536,4,128]{2,1,0:T(4,128)} %all-to-all-done, s32[1024]{0:T(1024)S(1)} %fusion.49), kind=kCustom, calls=%fused_computation.1 | custom fusion | bytes 4198400 | tf_op jit(solution)/shard_map/gather | solution.py:108
  262.3 6.1 %fusion.16 = f32[1024,2,128]{0,2,1:T(8,128)S(1)} fusion(f32[4,1024,1024]{1,2,0:T(8,128)} %get-tuple-element.45, f32[1024,2,128]{2,1,0:T(2,128)S(1)} %get-tuple-element.48, f32[1024,2]{0,1:T(2,128)S(1)} %get-tuple-element.56), kind=kOutput, calls=%fused_computation.41 | convolution fusion | flops 1610874880 | bytes 10493952 | tf_op jit(solution)/shard_map/while/body/eval_jaxpr/hqk,khd->qhd/dot_general | solution.py:54
  278.0 6.9 %fusion.19 = f32[1024,2,128]{0,2,1:T(8,128)} fusion(f32[4,1024,1024]{1,2,0:T(8,128)} %get-tuple-element.45, f32[1024,2,128]{2,1,0:T(2,128)S(1)} %copy-done.3, f32[1024,2]{0,1:T(2,128)S(1)} %get-tuple-element.57), kind=kOutput, calls=%fused_computation.42 | convolution fusion | flops 1610874880 | bytes 10493952 | tf_op jit(solution)/shard_map/while/body/eval_jaxpr/hqk,khd->qhd/dot_general | solution.py:54
  291.6 23.5 %all-to-all-done.5 = f32[1536,2,128]{2,1,0:T(2,128)S(1)} async-done(((f32[1536,2,128]{2,1,0:T(2,128)}), f32[1536,2,128]{2,1,0:T(2,128)S(1)}, u32[]{:S(2)}, u32[]{:S(2)}) %all-to-all-start.5) | async-done | bytes 1572896 | tf_op jit(solution)/shard_map/all_to_all | solution.py:137
  333.9 17.4 %collective-permute-done.1 = f32[1024,256]{1,0:T(8,128)} collective-permute-done((f32[1024,256]{1,0:T(8,128)}, f32[1024,256]{1,0:T(8,128)}, u32[]{:S(2)}, u32[]{:S(2)}) %collective-permute-start.1) | collective-permute-done | bytes 1048608 | tf_op jit(solution)/shard_map/ppermute | solution.py:142
  351.2 5.5 %convolution_add_fusion.2 = f32[1024,1024]{1,0:T(8,128)} fusion(f32[1024,1024]{1,0:T(8,128)S(1)} %fusion.24, f32[1024,256]{1,0:T(8,128)} %collective-permute-done.1, f32[2,512,1024]{2,1,0:T(8,128)} %collective-permute-done), kind=kOutput, calls=%fused_computation.26 | convolution fusion | flops 1611661312 | bytes 10485760 | tf_op jit(solution)/shard_map/dot_general | solution.py:131
  356.8 5.5 %convolution_add_fusion.3 = f32[1024,1024]{1,0:T(8,128)} fusion(f32[1024,1024]{1,0:T(8,128)S(1)} %fusion.26, f32[1024,256]{1,0:T(8,128)} %collective-permute-done.1, f32[2,512,1024]{2,1,0:T(8,128)} %collective-permute-done), kind=kOutput, calls=%fused_computation.27 | convolution fusion | flops 1611661312 | bytes 10485760 | tf_op jit(solution)/shard_map/dot_general | solution.py:131
  375.5 14.6 %collective-permute-done.2 = f32[1024,256]{1,0:T(8,128)S(1)} collective-permute-done((f32[1024,256]{1,0:T(8,128)S(1)}, f32[1024,256]{1,0:T(8,128)S(1)}, u32[]{:S(2)}, u32[]{:S(2)}) %collective-permute-start.2) | collective-permute-done | bytes 1048608 | tf_op jit(solution)/shard_map/ppermute | solution.py:142
  394.6 7.1 %collective-permute-done.3 = f32[1024,1024]{1,0:T(8,128)S(1)} collective-permute-done((f32[1024,1024]{1,0:T(8,128)S(1)}, f32[1024,1024]{1,0:T(8,128)S(1)}, u32[]{:S(2)}, u32[]{:S(2)}) %collective-permute-start.3) | collective-permute-done | bytes 4194336 | tf_op jit(solution)/shard_map/ppermute | solution.py:167
  401.7 5.5 %add_add_fusion = f32[1024,1024]{1,0:T(8,128)} fusion(f32[1024,1024]{1,0:T(8,128)S(1)} %convolution_add_fusion, f32[1024,1024]{1,0:T(8,128)S(1)} %collective-permute-done.3, f32[1024,256]{1,0:T(8,128)S(1)} %collective-permute-done.2, f32[2,512,1024]{2,1,0:T(8,128)} %collective-permute-done), kind=kOutput, calls=%fused_computation.22 | convolution fusion | flops 1612709888 | bytes 14680064 | tf_op jit(solution)/shard_map/dot_general | solution.py:131
  (73 shorter events, 105.3 us)
Async XLA Ops:
  10.0 19.0 %all-to-all-start.1 = ((s32[8,192,2]{1,2,0:T(2,128)}), s32[8,192,2]{1,2,0:T(2,128)S(1)}, u32[]{:S(2)}, u32[]{:S(2)}) async-start(s32[8,192,2]{1,2,0:T(2,128)} %copy.39), calls=%async_computation.1 | async-start | bytes 32768 | tf_op jit(solution)/shard_map/all_to_all | solution.py:98
  29.1 76.2 %all-to-all-start.2 = ((f32[1536,4,128]{2,1,0:T(4,128)}), f32[1536,4,128]{2,1,0:T(4,128)}, u32[]{:S(2)}, u32[]{:S(2)}) async-start(f32[1536,4,128]{2,1,0:T(4,128)} %gather_fusion.2), calls=%async_computation.2 | async-start | bytes 6291456 | tf_op jit(solution)/shard_map/all_to_all | solution.py:111
  105.3 74.6 %all-to-all-start.3 = ((f32[1536,4,128]{2,1,0:T(4,128)}), f32[1536,4,128]{2,1,0:T(4,128)}, u32[]{:S(2)}, u32[]{:S(2)}) async-start(f32[1536,4,128]{2,1,0:T(4,128)} %gather_fusion.5), calls=%async_computation.3 | async-start | bytes 6291456 | tf_op jit(solution)/shard_map/all_to_all | solution.py:115
  114.7 91.7 %collective-permute-start = (f32[2,512,1024]{2,1,0:T(8,128)}, f32[2,512,1024]{2,1,0:T(8,128)}, u32[]{:S(2)}, u32[]{:S(2)}) collective-permute-start(f32[2,512,1024]{2,1,0:T(8,128)} %pad_maximum_fusion), channel_id=1, source_target_pairs={{0,2},{1,3},{2,0},{3,1},{4,6},{5,7},{6,4},{7,5},{8,10},{9,11},{10,... | collective-permute-start | bytes 12582920 | tf_op jit(solution)/shard_map/ppermute | solution.py:186
  180.0 74.6 %all-to-all-start = ((f32[1536,4,128]{2,1,0:T(4,128)}), f32[1536,4,128]{2,1,0:T(4,128)}, u32[]{:S(2)}, u32[]{:S(2)}) async-start(f32[1536,4,128]{2,1,0:T(4,128)} %gather_fusion), calls=%async_computation | async-start | bytes 6291456 | tf_op jit(solution)/shard_map/all_to_all | solution.py:116
  221.6 1.6 copy-start
  223.2 1.2 copy-start.4
  223.2 1.2 copy-start.5
  274.2 3.8 copy-start.3
  274.2 40.9 %all-to-all-start.5 = ((f32[1536,2,128]{2,1,0:T(2,128)}), f32[1536,2,128]{2,1,0:T(2,128)S(1)}, u32[]{:S(2)}, u32[]{:S(2)}) async-start(f32[1536,2,128]{2,1,0:T(2,128)} %gather_fusion.8), calls=%async_computation.5 | async-start | bytes 3145728 | tf_op jit(solution)/shard_map/all_to_all | solution.py:137
  315.1 1.1 copy-start.2
  316.3 45.9 %all-to-all-start.4 = ((f32[1536,2,128]{2,1,0:T(2,128)}), f32[1536,2,128]{2,1,0:T(2,128)S(1)}, u32[]{:S(2)}, u32[]{:S(2)}) async-start(f32[1536,2,128]{2,1,0:T(2,128)} %gather_fusion.7), calls=%async_computation.4 | async-start | bytes 3145728 | tf_op jit(solution)/shard_map/all_to_all | solution.py:137
  326.1 25.1 %collective-permute-start.1 = (f32[1024,256]{1,0:T(8,128)}, f32[1024,256]{1,0:T(8,128)}, u32[]{:S(2)}, u32[]{:S(2)}) collective-permute-start(f32[1024,256]{1,0:T(8,128)} %bitcast.73), channel_id=1, source_target_pairs={{0,2},{1,3},{2,0},{3,1},{4,6},{5,7},{6,4},{7,5},{8,10},{9,11},{10,... | collective-permute-start | bytes 3145736 | tf_op jit(solution)/shard_map/ppermute | solution.py:142
  366.1 24.0 %collective-permute-start.2 = (f32[1024,256]{1,0:T(8,128)S(1)}, f32[1024,256]{1,0:T(8,128)S(1)}, u32[]{:S(2)}, u32[]{:S(2)}) collective-permute-start(f32[1024,256]{1,0:T(8,128)S(1)} %bitcast.82), channel_id=1, source_target_pairs={{0,2},{1,3},{2,0},{3,1},{4,6},{5,7},{6,4},{7,5},{8,10},{9,11},{10,... | collective-permute-start | bytes 3145736 | tf_op jit(solution)/shard_map/ppermute | solution.py:142
  367.7 4.7 %copy-start.1 = (f32[1024,1024]{1,0:T(8,128)S(1)}, f32[1024,1024]{1,0:T(8,128)}, u32[]{:S(2)}) copy-start(f32[1024,1024]{1,0:T(8,128)} %convolution_add_fusion.3) | copy-start | bytes 12582916
  394.5 7.2 %collective-permute-start.3 = (f32[1024,1024]{1,0:T(8,128)S(1)}, f32[1024,1024]{1,0:T(8,128)S(1)}, u32[]{:S(2)}, u32[]{:S(2)}) collective-permute-start(f32[1024,1024]{1,0:T(8,128)S(1)} %add.106), channel_id=1, source_target_pairs={{0,1},{1,0},{2,3},{3,2},{4,5},{5,4},{6,7},{7,6},{8,9},{9,8},{10,11... | collective-permute-start | bytes 12582920 | tf_op jit(solution)/shard_map/ppermute | solution.py:167
